TPU v7x, 32 devices: a whole 2x2x4 slice. The times are simulated.
32 devices in a mesh: groups: 2 (over x), stream: 8 (over z, y), section: 2 (over core).
Axes of the slice: x: 2, y: 2, z: 4, core: 2. Of those that a mesh axis runs over, the one named last changes fastest.
Arguments:
- new_frames: bfloat16 [256, 16, 1024], P(('groups', 'stream')), parts along dimension 0, may hold values from -6 to 6
- valid_counts: int32 [256], P('groups'), parts along dimension 0, may hold values from 1 to 16
- anchor: int32 [256], P('groups'), parts along dimension 0, may hold values from 0 to 127, as said below
- context_cache: bfloat16 [2, 256, 12, 2048], P('section', ('groups', 'stream')), parts along dimension 1, may hold values from -240 to 240
- conv_state: bfloat16 [2, 256, 30, 1024], P('section', ('groups', 'stream')), parts along dimension 1, may hold values from -6 to 6
- qkv_weight: bfloat16 [2, 1024, 3072], P('section'), may hold values from -0.1875 to 0.1875
- out_weight: bfloat16 [2, 1024, 1024], P('section'), may hold values from -0.1875 to 0.1875
- conv_weight: float32 [2, 31, 1024], P('section'), may hold values from -1 to 1
Outputs:
- layer_outputs: bfloat16 [2, 256, 16, 1024], P('section', ('groups', 'stream')), parts along dimension 1
There are 2 independent parts, one for each index of `groups`. A program takes and returns all parts, laid end to end along the dimension named above; an argument that names none is the same for every part. Nothing has to cross between parts.
Inputs may be any that keep to these rules, and one draw needn't show every extreme that they name: anchor is a permutation of the 128 slots. New slot j lies on host j // 16, old slot o on host o // 16. Exactly 7 streams leave each host and 7 arrive at it; from one old host to one other new host moves at most one stream. A stream that stays on its host keeps its slot.
All inputs are finite; a program needn't handle non-finite values.
Results may differ from a plain program's by a relative error of at most 0.0094.
Values may be sent and summed in bfloat16 or wider, within the bound.
No kernel may reach another device: no remote copies, remote signals or barrier semaphores. Data moves between devices by JAX's collectives and lax.ppermute only.
A program may use at most 128 MiB of HBM per device.

v0:
```python
import jax
import jax.numpy as jnp
from jax import lax
from jax.sharding import PartitionSpec as P

HEADS = 16


def shifted(value, axis, steps):
    count = lax.axis_size(axis)
    leading, last = (max(0, -steps), min(count, count - steps))
    return lax.ppermute(value, axis, [(source, source + steps) for source in range(leading, last)])


def encoder_layer(inputs, valid_counts, context, conv_state, qkv_weight, out_weight, conv_weight):
    stream_count, frame_count, model_width = inputs.shape
    head_size = model_width // HEADS
    live_mask = jnp.arange(frame_count, dtype=jnp.int32)[None, :] < valid_counts[:, None]
    floats = inputs.astype(jnp.float32)
    centred = floats - jnp.mean(floats, axis=-1, keepdims=True)
    variance = jnp.mean(centred * centred, axis=-1, keepdims=True)
    normed = (centred * lax.rsqrt(variance + 1e-05)).astype(jnp.bfloat16)
    projected = jnp.dot(
        normed.reshape(-1, model_width), qkv_weight, preferred_element_type=jnp.float32
    )
    projected = projected.reshape(stream_count, frame_count, 3 * model_width)
    queries = (projected[:, :, :model_width] * head_size ** (-0.5)).astype(jnp.bfloat16)
    new_keys = projected[:, :, model_width : 2 * model_width].astype(jnp.bfloat16)
    new_values = projected[:, :, 2 * model_width :].astype(jnp.bfloat16)
    keys_all = jnp.concatenate([context[:, :, :model_width], new_keys], axis=1)
    values_all = jnp.concatenate([context[:, :, model_width:], new_values], axis=1)
    key_total = keys_all.shape[1]
    queries_split = queries.reshape(stream_count, frame_count, HEADS, head_size)
    keys_split = keys_all.reshape(stream_count, key_total, HEADS, head_size)
    values_split = values_all.reshape(stream_count, key_total, HEADS, head_size)
    scores = jnp.einsum(
        "bqhd,bkhd->bhqk", queries_split, keys_split, preferred_element_type=jnp.float32
    )
    key_mask = jnp.concatenate(
        [jnp.ones((stream_count, key_total - frame_count), dtype=bool), live_mask], axis=1
    )
    scores = jnp.where(key_mask[:, None, None, :], scores, jnp.float32(-1e30))
    top_score = jnp.max(scores, axis=-1, keepdims=True)
    exponent = jnp.exp(scores - top_score)
    softmax_weights = (exponent / jnp.sum(exponent, axis=-1, keepdims=True)).astype(jnp.bfloat16)
    attended = jnp.einsum(
        "bhqk,bkhd->bqhd", softmax_weights, values_split, preferred_element_type=jnp.float32
    )
    attended = attended.reshape(stream_count * frame_count, model_width).astype(jnp.bfloat16)
    mixed = jnp.dot(attended, out_weight, preferred_element_type=jnp.float32)
    residual_sum = floats + mixed.reshape(stream_count, frame_count, model_width)
    rounded = lax.optimization_barrier(residual_sum.astype(jnp.bfloat16))
    padded_input = jnp.concatenate([conv_state, rounded], axis=1).astype(jnp.float32)
    convolved = jnp.zeros((stream_count, frame_count, model_width), jnp.float32)
    for tap_index in range(conv_weight.shape[0]):
        convolved = (
            convolved
            + conv_weight[tap_index][None, None, :]
            * padded_input[:, tap_index : tap_index + frame_count, :]
        )
    output = (residual_sum + jax.nn.silu(convolved)) * live_mask[:, :, None].astype(jnp.float32)
    return output.astype(jnp.bfloat16)


def routing(anchor, own_index, local_count):
    stream_total = anchor.shape[0]
    every_slot = jnp.arange(stream_total, dtype=jnp.int32)
    newpos = jnp.sum(
        jnp.where(anchor[None, :] == every_slot[:, None], every_slot[None, :], 0), axis=1
    )
    mine_new = lax.dynamic_slice_in_dim(newpos, own_index * local_count, local_count)
    mine_old = lax.dynamic_slice_in_dim(anchor, own_index * local_count, local_count)
    return (mine_new // local_count, mine_old // local_count, mine_new, mine_old)


def pack_rows(rows, hosts, own_index, slot_total):
    places = jnp.where(hosts == own_index, slot_total, hosts)
    return jnp.zeros((slot_total,) + rows.shape[1:], rows.dtype).at[places].set(rows, mode="drop")


def pick_rows(buffer, local_rows, hosts, own_index, local_index):
    from_buffer = jnp.take(buffer, hosts, axis=0)
    from_local = jnp.take(local_rows, local_index, axis=0)
    staying = (hosts == own_index).reshape((-1,) + (1,) * (buffer.ndim - 1))
    return jnp.where(staying, from_local, from_buffer)


def run_sections(inputs, valid_counts, context, conv_state, qkv_weight, out_weight, conv_weight):
    local_count = inputs.shape[0]
    block_total = 1
    block_rows = local_count // block_total
    section_total = lax.axis_size("section")
    section_index = lax.axis_index("section")
    inbound = jnp.zeros((block_rows,) + inputs.shape[1:], jnp.bfloat16)
    result = jnp.zeros_like(inputs)
    turn_total = block_total + section_total - 1
    for turn_index in range(turn_total):
        own_block = turn_index - section_index
        first_row = jnp.clip(own_block, 0, block_total - 1) * block_rows
        layer_input = jnp.where(section_index == 0, inputs, inbound)
        produced = encoder_layer(
            layer_input, valid_counts, context, conv_state, qkv_weight, out_weight, conv_weight
        )
        active = (own_block >= 0) & (own_block < block_total)
        previous = result
        result = jnp.where(active, produced, previous)
        if turn_index + 1 < turn_total:
            inbound = shifted(produced, "section", 1)
    return result


def body(
    new_frames, valid_counts, anchor, context_cache, conv_state, qkv_weight, out_weight, conv_weight
):
    local_count = new_frames.shape[0]
    own_index = lax.axis_index("stream")
    slot_total = lax.axis_size("stream")
    context_here = context_cache[0]
    conv_here = conv_state[0]
    target_host, source_host, mine_new, mine_old = routing(anchor, own_index, local_count)
    old_local = jnp.clip(mine_old - own_index * local_count, 0, local_count - 1)
    outgoing = (
        pack_rows(context_here, target_host, own_index, slot_total),
        pack_rows(conv_here, target_host, own_index, slot_total),
    )
    got_context, got_conv = (
        lax.all_to_all(outgoing[0], "stream", split_axis=0, concat_axis=0, tiled=True),
        lax.all_to_all(outgoing[1], "stream", split_axis=0, concat_axis=0, tiled=True),
    )
    valid_here = lax.dynamic_slice_in_dim(valid_counts, own_index * local_count, local_count)
    context_new = pick_rows(got_context, context_here, source_host, own_index, old_local)
    conv_new = pick_rows(got_conv, conv_here, source_host, own_index, old_local)
    section_output = run_sections(
        new_frames, valid_here, context_new, conv_new, qkv_weight[0], out_weight[0], conv_weight[0]
    )
    return section_output[None]


def solution(mesh):
    return jax.shard_map(
        body,
        mesh=mesh,
        in_specs=(
            P(("groups", "stream"), None, None),
            P("groups"),
            P("groups"),
            P("section", ("groups", "stream"), None, None),
            P("section", ("groups", "stream"), None, None),
            P("section", None, None),
            P("section", None, None),
            P("section", None, None),
        ),
        out_specs=P("section", ("groups", "stream"), None, None),
        check_vma=False,
    )
```

profile of v0, /device:TPU:1, one launch (start us, length us, event | category | flops | bytes accessed | tf_op | source)
XLA Modules:
  0.0 129.3 jit_solution(17258690904083255207)
XLA Ops:
  3.7 3.0 %scatter_fusion = bf16[8,12,2048]{2,1,0:T(8,128)(2,1)} fusion(bf16[8,12,2048]{2,1,0:T(8,128)(2,1)} %broadcast_in_dim.124, s32[16]{0:T(128)S(1)} %compare_select_fusion, bf16[16,12,2048]{2,1,0:T(8,128)(2,1)S(1)} %bitcast.73), kind=kCustom, calls=%fused_computation.4 | custom fusion | bytes 2359360 | tf_op jit(solution)/shard_map/scatter | solution.py:78
  6.8 6.5 %all-to-all-start = ((bf16[8,12,2048]{2,1,0:T(8,128)(2,1)}), bf16[8,12,2048]{2,1,0:T(8,128)(2,1)S(1)}, u32[]{:S(2)}, u32[]{:S(2)}) async-start(bf16[8,12,2048]{2,1,0:T(8,128)(2,1)} %scatter_fusion), calls=%async_computation | async-start | bytes 1048576 | tf_op jit(solution)/shard_map/all_to_all | solution.py:127
  13.4 2.8 %gather_fusion = bf16[16,12,2048]{2,1,0:T(8,128)(2,1)} fusion(bf16[16,12,2048]{2,1,0:T(8,128)(2,1)} %bitcast.74, s32[1024]{0:T(1024)S(1)} %pad_clamp_fusion.1), kind=kCustom, calls=%fused_computation | custom fusion | bytes 1572928 | tf_op jit(solution)/shard_map/jit(_take)/gather | solution.py:83
  16.7 5.8 %fusion.132 = (bf16[16,16,3072]{2,1,0:T(8,128)(2,1)}, f32[16,16,3072]{2,1,0:T(8,128)S(1)}) fusion(bf16[1,1024,3072]{2,1,0:T(8,128)(2,1)} %param.13, f32[16,16]{1,0:T(8,128)S(1)} %add_rsqrt_fusion.1, f32[16,16]{1,0:T(8,128)S(1)} %broadcast_multiply_fusion.1, bf16[16,16,1024]{2,1,0:T(8,128)(2,1)S(1)} %copy-done.1, pred[]{:T(512)S(6)} %eq.14), kind=kOutput, calls=%fused_computation.239 | convolution fusion | flops 1612709888 | bytes 11536385 | tf_op jit(solution)/shard_map/dot_general | solution.py:23
  23.4 2.5 %reshape.164 = bf16[16,16,16,64]{3,2,1,0:T(8,128)(2,1)} reshape(bf16[16,16,1024]{2,1,0:T(8,128)(2,1)} %fusion.107) | data formatting | bytes 1048576 | tf_op jit(solution)/shard_map/reshape | solution.py:33
  26.1 2.7 %copy.89 = bf16[1,16,30,1024]{3,2,1,0:T(8,128)(2,1)} copy(bf16[1,16,30,1024]{3,1,2,0:T(8,128)(2,1)} %param.12) | data formatting | bytes 1966080 | tf_op args[4]
  28.8 2.8 %gather_fusion.2 = bf16[16,30,1024]{2,1,0:T(8,128)(2,1)} fusion(bf16[16,30,1024]{2,1,0:T(8,128)(2,1)} %bitcast.75, s32[1024]{0:T(1024)S(1)} %pad_clamp_fusion.1), kind=kCustom, calls=%fused_computation.2 | custom fusion | bytes 1966144 | tf_op jit(solution)/shard_map/jit(_take)/gather | solution.py:83
  32.5 3.3 %scatter_fusion.1 = bf16[8,30,1024]{2,1,0:T(8,128)(2,1)} fusion(bf16[8,30,1024]{2,1,0:T(8,128)(2,1)} %broadcast_in_dim.135, s32[16]{0:T(128)S(1)} %compare_select_fusion, bf16[16,30,1024]{2,1,0:T(8,128)(2,1)} %bitcast.76), kind=kCustom, calls=%fused_computation.5 | custom fusion | bytes 2949184 | tf_op jit(solution)/shard_map/scatter | solution.py:78
  36.0 2.3 %fusion.128 = (bf16[16,16,1024]{2,1,0:T(8,128)(2,1)}, bf16[16,16,1024]{2,1,0:T(8,128)(2,1)}) fusion(bf16[16,16,3072]{2,1,0:T(8,128)(2,1)} %get-tuple-element.52), kind=kLoop, calls=%fused_computation.235 | loop fusion | bytes 2097152 | tf_op jit(solution)/shard_map/slice | solution.py:28
  38.3 5.5 %all-to-all-start.1 = ((bf16[8,30,1024]{2,1,0:T(8,128)(2,1)}), bf16[8,30,1024]{2,1,0:T(8,128)(2,1)}, u32[]{:S(2)}, u32[]{:S(2)}) async-start(bf16[8,30,1024]{2,1,0:T(8,128)(2,1)} %scatter_fusion.1), calls=%async_computation.1 | async-start | bytes 1048576 | tf_op jit(solution)/shard_map/all_to_all | solution.py:128
  45.3 1.9 %select_select_fusion.1 = bf16[16,12,2048]{2,1,0:T(8,128)(2,1)S(1)} fusion(bf16[16,12,2048]{2,1,0:T(8,128)(2,1)} %gather_fusion.1, bf16[16,12,2048]{2,1,0:T(8,128)(2,1)} %gather_fusion, pred[16]{0:T(512)(128)(4,1)S(1)} %compare_and_fusion, pred[16]{0:T(512)(128)(4,1)S(1)} %get-tuple-element.9, pred[16]{0:T(512)(128)(4,1)S(1)} %get-tuple-element.50), kind=kLoop, calls=%fused_computation.195 | loop fusion | flops 1179648 | bytes 2359344 | tf_op jit(solution)/shard_map/jit(_where)/select_n | solution.py:85
  49.4 3.7 %reshape.226 = bf16[16,28,16,64]{3,2,1,0:T(8,128)(2,1)} reshape(bf16[16,28,1024]{2,1,0:T(8,128)(2,1)} %pad_maximum_fusion.5) | data formatting | bytes 1835008 | tf_op jit(solution)/shard_map/reshape | solution.py:34
  53.1 5.2 %fusion.133 = (f32[16,16,16]{2,1,0:T(8,128)}, f32[16,16,16,28]{3,2,1,0:T(8,128)}) fusion(pred[16,28]{1,0:T(8,128)(4,1)S(1)} %concatenate.23, bf16[16,28,16,64]{3,2,1,0:T(8,128)(2,1)} %reshape.226, bf16[16,16,16,64]{3,2,1,0:T(8,128)(2,1)} %reshape.164), kind=kOutput, calls=%fused_computation.240 | convolution fusion | flops 15024155 | bytes 1917376 | tf_op jit(solution)/shard_map/sub | solution.py:44
  58.3 2.3 %pad_maximum_fusion.3 = bf16[16,28,1024]{2,1,0:T(8,128)(2,1)} fusion(bf16[16,12,1024]{2,1,0:T(8,128)(2,1)S(1)} %get-tuple-element.16, bf16[16,16,1024]{2,1,0:T(8,128)(2,1)} %get-tuple-element.14), kind=kLoop, calls=%fused_computation.51 | loop fusion | flops 1835008 | bytes 1835008 | tf_op jit(solution)/shard_map/concatenate | solution.py:31
  60.6 3.8 %reshape.225 = bf16[16,28,16,64]{3,2,1,0:T(8,128)(2,1)} reshape(bf16[16,28,1024]{2,1,0:T(8,128)(2,1)} %pad_maximum_fusion.3) | data formatting | bytes 1835008 | tf_op jit(solution)/shard_map/reshape | solution.py:35
  64.4 2.9 %fusion.31 = bf16[16,16,16,64]{3,1,2,0:T(8,128)(2,1)S(1)} fusion(bf16[16,28,16,64]{3,2,1,0:T(8,128)(2,1)} %reshape.225, f32[16,16,16,28]{3,2,1,0:T(8,128)} %get-tuple-element.55, f32[16,16,16]{2,1,0:T(8,128)S(1)} %copy-done.15), kind=kOutput, calls=%fused_computation.45 | convolution fusion | flops 15171584 | bytes 1916928 | tf_op jit(solution)/shard_map/bhqk,bkhd->bqhd/dot_general | solution.py:46
  68.5 2.6 %convert_element_type.81 = bf16[16,16,1024]{2,1,0:T(8,128)(2,1)} reshape(bf16[16,16,16,64]{3,2,1,0:T(8,128)(2,1)} %copy.35) | data formatting | bytes 1048576 | tf_op jit(solution)/shard_map/convert_element_type | solution.py:49
  71.1 2.8 %fusion.134 = (bf16[16,16,1024]{2,1,0:T(8,128)(2,1)S(1)}, f32[16,16,1024]{2,1,0:T(8,128)}) fusion(bf16[16,16,1024]{2,1,0:T(8,128)(2,1)} %convert_element_type.81, bf16[1,1024,1024]{2,1,0:T(8,128)(2,1)S(1)} %copy-done, bf16[16,16,1024]{2,1,0:T(8,128)(2,1)S(1)} %copy-done.1, pred[]{:T(512)S(6)} %eq.14), kind=kOutput, calls=%fused_computation.241 | convolution fusion | flops 537919488 | bytes 4718593 | tf_op jit(solution)/shard_map/dot_general | solution.py:50
  73.9 2.6 %gather_fusion.3 = bf16[16,30,1024]{2,1,0:T(8,128)(2,1)} fusion(bf16[8,30,1024]{2,1,0:T(8,128)(2,1)} %all-to-all-done.1, s32[1024]{0:T(1024)S(1)} %pad_clamp_fusion), kind=kCustom, calls=%fused_computation.3 | custom fusion | bytes 1966144 | tf_op jit(solution)/shard_map/jit(_take)/gather | solution.py:82
  76.5 1.8 %select_select_fusion = bf16[16,30,1024]{2,1,0:T(8,128)(2,1)S(1)} fusion(bf16[16,30,1024]{2,1,0:T(8,128)(2,1)} %gather_fusion.3, bf16[16,30,1024]{2,1,0:T(8,128)(2,1)} %gather_fusion.2, pred[16]{0:T(512)(128)(4,1)S(1)} %compare_and_fusion, pred[16]{0:T(512)(128)(4,1)S(1)} %get-tuple-element.9, pred[16]{0:T(512)(128)(4,1)S(1)} %get-tuple-element.50), kind=kLoop, calls=%fused_computation.191 | loop fusion | flops 1474560 | bytes 2949168 | tf_op jit(solution)/shard_map/jit(_where)/select_n | solution.py:85
  79.3 5.4 %multiply_convert_fusion.1 = bf16[16,16,1024]{2,1,0:T(8,128)(2,1)S(1)} fusion(f32[16,16,1024]{2,1,0:T(8,128)} %get-tuple-element.57, f32[16,46,1024]{2,1,0:T(8,128)S(1)} %fusion.20, f32[16,16]{1,0:T(8,128)S(1)} %get-tuple-element.48, f32[1024]{0:T(1024)S(1)} %bitcast.97, f32[1024]{0:T(1024)S(1)} %bitcast.99, f32[1024]{0:T(1024)S(1)} %bitcast.103, ...), kind=kLoop, calls=%fused_computation.190 | loop fusion | flops 17825792 | bytes 34206720 | tf_op jit(solution)/shard_map/convert_element_type | solution.py:62
  86.2 2.8 %collective-permute-done = bf16[16,16,1024]{2,1,0:T(8,128)(2,1)} collective-permute-done((bf16[16,16,1024]{2,1,0:T(8,128)(2,1)S(1)}, bf16[16,16,1024]{2,1,0:T(8,128)(2,1)}, u32[]{:S(2)}, u32[]{:S(2)}) %collective-permute-start) | collective-permute-done | bytes 524320 | tf_op jit(solution)/shard_map/ppermute | solution.py:12
  90.5 6.4 %fusion.135 = (bf16[16,16,3072]{2,1,0:T(8,128)(2,1)S(1)}, f32[16,16,3072]{2,1,0:T(8,128)}) fusion(bf16[1,1024,3072]{2,1,0:T(8,128)(2,1)} %param.13, bf16[16,16,1024]{2,1,0:T(8,128)(2,1)S(1)} %get-tuple-element.6, f32[16,16]{1,0:T(8,128)S(1)} %add_rsqrt_fusion, f32[16,16]{1,0:T(8,128)S(1)} %broadcast_multiply_fusion), kind=kOutput, calls=%fused_computation.242 | convolution fusion | flops 1612447744 | bytes 11536384 | tf_op jit(solution)/shard_map/dot_general | solution.py:23
  98.1 2.1 %pad_maximum_fusion.2 = (bf16[16,28,1024]{2,1,0:T(8,128)(2,1)}, bf16[16,28,1024]{2,1,0:T(8,128)(2,1)}) fusion(bf16[16,12,1024]{2,1,0:T(8,128)(2,1)S(1)} %copy-done.8, bf16[16,16,1024]{2,1,0:T(8,128)(2,1)S(1)} %get-tuple-element.12, bf16[16,16,1024]{2,1,0:T(8,128)(2,1)S(1)} %get-tuple-element.11, bf16[16,12,1024]{2,1,0:T(8,128)(2,1)S(1)} %copy-done.6), kind=kLoop, calls=%fused_computation.50 | loop fusion | flops 3670016 | bytes 3670016 | tf_op jit(solution)/shard_map/concatenate | solution.py:31
  100.2 3.8 %reshape.228 = bf16[16,28,16,64]{3,2,1,0:T(8,128)(2,1)} reshape(bf16[16,28,1024]{2,1,0:T(8,128)(2,1)} %get-tuple-element.65) | data formatting | bytes 1835008 | tf_op jit(solution)/shard_map/reshape | solution.py:34
  105.2 1.7 %reshape.167 = bf16[16,16,16,64]{3,2,1,0:T(8,128)(2,1)} reshape(bf16[16,16,1024]{2,1,0:T(8,128)(2,1)S(1)} %fusion.76) | data formatting | bytes 1048576 | tf_op jit(solution)/shard_map/reshape | solution.py:33
  106.9 3.8 %reshape.227 = bf16[16,28,16,64]{3,2,1,0:T(8,128)(2,1)} reshape(bf16[16,28,1024]{2,1,0:T(8,128)(2,1)} %get-tuple-element.64) | data formatting | bytes 1835008 | tf_op jit(solution)/shard_map/reshape | solution.py:35
  110.7 4.5 %fusion.136 = (f32[16,16,16]{2,1,0:T(8,128)S(1)}, f32[16,16,16,28]{3,2,1,0:T(8,128)}) fusion(pred[16,28]{1,0:T(8,128)(4,1)S(1)} %concatenate.23, bf16[16,28,16,64]{3,2,1,0:T(8,128)(2,1)} %reshape.228, bf16[16,16,16,64]{3,2,1,0:T(8,128)(2,1)} %reshape.167), kind=kOutput, calls=%fused_computation.243 | convolution fusion | flops 15024155 | bytes 1917376 | tf_op jit(solution)/shard_map/sub | solution.py:44
  115.2 2.9 %fusion.28 = bf16[16,16,16,64]{3,1,2,0:T(8,128)(2,1)S(1)} fusion(bf16[16,28,16,64]{3,2,1,0:T(8,128)(2,1)} %reshape.227, f32[16,16,16,28]{3,2,1,0:T(8,128)} %get-tuple-element.61, f32[16,16,16]{2,1,0:T(8,128)S(1)} %get-tuple-element.60), kind=kOutput, calls=%fused_computation.44 | convolution fusion | flops 15171584 | bytes 1916928 | tf_op jit(solution)/shard_map/bhqk,bkhd->bqhd/dot_general | solution.py:46
  119.3 1.9 %convert_element_type.92 = bf16[16,16,1024]{2,1,0:T(8,128)(2,1)S(1)} reshape(bf16[16,16,16,64]{3,2,1,0:T(8,128)(2,1)} %copy.42) | data formatting | bytes 1048576 | tf_op jit(solution)/shard_map/convert_element_type | solution.py:49
  121.3 1.7 %fusion.137 = (bf16[16,16,1024]{2,1,0:T(8,128)(2,1)S(1)}, f32[16,16,1024]{2,1,0:T(8,128)}) fusion(bf16[16,16,1024]{2,1,0:T(8,128)(2,1)S(1)} %convert_element_type.92, bf16[1,1024,1024]{2,1,0:T(8,128)(2,1)S(1)} %copy-done, bf16[16,16,1024]{2,1,0:T(8,128)(2,1)S(1)} %get-tuple-element.6), kind=kOutput, calls=%fused_computation.244 | convolution fusion | flops 537657344 | bytes 4718592 | tf_op jit(solution)/shard_map/dot_general | solution.py:50
  124.2 5.1 %select_bitcast_fusion = bf16[1,16,16,1024]{3,2,1,0:T(8,128)(2,1)} fusion(bf16[16,16,1024]{2,1,0:T(8,128)(2,1)} %copy-done.10, pred[]{:T(512)S(6)} %and.36, pred[]{:T(512)S(6)} %and.31, f32[16,16]{1,0:T(8,128)S(1)} %get-tuple-element.48, f32[16,16,1024]{2,1,0:T(8,128)S(1)} %copy-done.9, f32[16,46,1024]{2,1,0:T(8,128)S(1)} %fusion.21, f32[1024]{0:T(1024)S(1)} %bitcast.98, ...), kind=kLoop, calls=%fused_computation.198 | loop fusion | flops 18350080 | bytes 34731008 | tf_op jit(solution)/shard_map/broadcast_in_dim | solution.py:136
  (68 shorter events, 20.3 us)
Async XLA Ops:
  0.0 71.1 %copy-start = (bf16[1,1024,1024]{2,1,0:T(8,128)(2,1)S(1)}, bf16[1,1024,1024]{2,1,0:T(8,128)(2,1)}, u32[]{:S(2)}) copy-start(bf16[1,1024,1024]{2,1,0:T(8,128)(2,1)} %param.14) | copy-start | bytes 6291460
  2.5 1.2 copy-start.2
  3.7 9.6 %copy-start.13 = (s32[128]{0:T(128)S(1)}, s32[128]{0:T(128)}, u32[]{:S(2)}) copy-start(s32[128]{0:T(128)} %param.10) | copy-start | bytes 1540
  6.8 9.5 %copy-start.1 = (bf16[16,16,1024]{2,1,0:T(8,128)(2,1)S(1)}, bf16[16,16,1024]{2,1,0:T(8,128)(2,1)}, u32[]{:S(2)}) copy-start(bf16[16,16,1024]{2,1,0:T(8,128)(2,1)} %param.8) | copy-start | bytes 1572868
  6.8 31.5 %all-to-all-start = ((bf16[8,12,2048]{2,1,0:T(8,128)(2,1)}), bf16[8,12,2048]{2,1,0:T(8,128)(2,1)S(1)}, u32[]{:S(2)}, u32[]{:S(2)}) async-start(bf16[8,12,2048]{2,1,0:T(8,128)(2,1)} %scatter_fusion), calls=%async_computation | async-start | bytes 1048576 | tf_op jit(solution)/shard_map/all_to_all | solution.py:127
  22.5 3.4 %copy-start.14 = (s32[128]{0:T(128)S(1)}, s32[128]{0:T(128)}, u32[]{:S(2)}) copy-start(s32[128]{0:T(128)} %param.9) | copy-start | bytes 1540
  31.6 4.2 %copy-start.12 = (f32[1,31,1024]{2,0,1:T(1,128)S(1)}, f32[1,31,1024]{2,0,1:T(1,128)}, u32[]{:S(2)}) copy-start(f32[1,31,1024]{2,0,1:T(1,128)} %param.15) | copy-start | bytes 380932
  38.3 35.6 %all-to-all-start.1 = ((bf16[8,30,1024]{2,1,0:T(8,128)(2,1)}), bf16[8,30,1024]{2,1,0:T(8,128)(2,1)}, u32[]{:S(2)}, u32[]{:S(2)}) async-start(bf16[8,30,1024]{2,1,0:T(8,128)(2,1)} %scatter_fusion.1), calls=%async_computation.1 | async-start | bytes 1048576 | tf_op jit(solution)/shard_map/all_to_all | solution.py:128
  45.3 2.8 %copy-start.11 = (bf16[16,16,1024]{2,1,0:T(8,128)(2,1)S(1)}, bf16[16,16,1024]{2,1,0:T(8,128)(2,1)}, u32[]{:S(2)}) copy-start(bf16[16,16,1024]{2,1,0:T(8,128)(2,1)} %get-tuple-element.13) | copy-start | bytes 1572868
  47.3 0.8 copy-start.5
  47.3 11.0 %copy-start.7 = (bf16[16,12,1024]{2,1,0:T(8,128)(2,1)}, bf16[16,12,1024]{2,1,0:T(8,128)(2,1)S(1)}, u32[]{:S(2)}) copy-start(bf16[16,12,1024]{2,1,0:T(8,128)(2,1)S(1)} %get-tuple-element.16) | copy-start | bytes 1179652
  60.6 3.8 %copy-start.15 = (f32[16,16,16]{2,1,0:T(8,128)S(1)}, f32[16,16,16]{2,1,0:T(8,128)}, u32[]{:S(2)}) copy-start(f32[16,16,16]{2,1,0:T(8,128)} %get-tuple-element.54) | copy-start | bytes 49156
  78.3 1.0 copy-start.3
  84.6 1.5 %copy-start.10 = (bf16[16,16,1024]{2,1,0:T(8,128)(2,1)}, bf16[16,16,1024]{2,1,0:T(8,128)(2,1)S(1)}, u32[]{:S(2)}) copy-start(bf16[16,16,1024]{2,1,0:T(8,128)(2,1)S(1)} %multiply_convert_fusion.1) | copy-start | bytes 1572868
  84.7 4.3 %collective-permute-start = (bf16[16,16,1024]{2,1,0:T(8,128)(2,1)S(1)}, bf16[16,16,1024]{2,1,0:T(8,128)(2,1)}, u32[]{:S(2)}, u32[]{:S(2)}) collective-permute-start(bf16[16,16,1024]{2,1,0:T(8,128)(2,1)S(1)} %multiply_convert_fusion.1), channel_id=1, source_target_pairs={{0,1},{2,3},{4,5},{6,7},{8,9},{10,11},{12,13},{14,15},{16,17},{18,... | collective-permute-start | bytes 1572872 | tf_op jit(solution)/shard_map/ppermute | solution.py:12
  96.9 1.0 copy-start.6
  96.9 1.2 copy-start.8
  121.2 1.7 %copy-start.4 = (bf16[16,30,1024]{2,1,0:T(8,128)(2,1)S(1)}, bf16[16,30,1024]{2,1,0:T(8,128)(2,1)}, u32[]{:S(2)}) copy-start(bf16[16,30,1024]{2,1,0:T(8,128)(2,1)} %copy-done.3) | copy-start | bytes 2949124
  122.9 1.2 copy-start.9
where the time goes:
time: 131 us; the launch traced here: 129 us
  local copies, waits for them, and re-layouts  54.7 us (42%)
  matrix products  32 us (24%)
  other arithmetic  26.1 us (20%)
  starting transfers between devices  13.5 us (10%)
  waiting for transfers between devices  2.79 us (2%)
    dot_general x2, matrix products, encoder_layer(): jnp.dot(normed.reshape(-1, model_width), qkv_weight, preferred_element_ty...  12.2 us
    sub x2, matrix products, encoder_layer(): exponent = jnp.exp(scores - top_score)  9.65 us
    unnamed x34, local copies, waits for them, and re-layouts  7.75 us
    reshape x2, local copies, waits for them, and re-layouts, encoder_layer(): values_split = values_all.reshape(stream_count, key_total, HEADS, head_size)  7.54 us
    reshape x2, local copies, waits for them, and re-layouts, encoder_layer(): keys_split = keys_all.reshape(stream_count, key_total, HEADS, head_size)  7.5 us
    convert_element_type x4, local copies, waits for them, and re-layouts, encoder_layer(): attended.reshape(stream_count * frame_count, model_width)  7.05 us
    all_to_all x1, starting transfers between devices, body(): lax.all_to_all(outgoing[0], 'stream', split_axis=0, concat_axis=0, tiled=...  6.53 us
    scatter x2, local copies, waits for them, and re-layouts, pack_rows(): jnp.zeros((slot_total,) + rows.shape[1:], rows.dtype).at[places]  6.34 us
  transfers between devices with their start and end apart: 3, of which 1 were waited for; matrix products, arithmetic and copies ran while one was open for 42% of the time, Pallas kernels for 0%

commit v1 on v0

--- a/solution.py
+++ b/solution.py
@@ -1,6 +1,10 @@
+import functools
+
 import jax
 import jax.numpy as jnp
 from jax import lax
+from jax.experimental import pallas as pl
+from jax.experimental.pallas import tpu as pltpu
 from jax.sharding import PartitionSpec as P
 
 HEADS = 16
@@ -12,54 +16,130 @@
     return lax.ppermute(value, axis, [(source, source + steps) for source in range(leading, last)])
 
 
+def layer_kernel(x_ref, klive_ref, rlive_ref, ck_ref, cv_ref, cst_ref, wq_ref, wk_ref, wv_ref,
+                 wo_ref, cw_ref, out_ref, nrm_ref, acc_ref, bc_ref, bn_ref, pad_ref,
+                 *, streams, frames, ctx, head_size):
+    step = pl.program_id(0)
+    tokens = streams * frames
+    width = x_ref.shape[1]
+    pair = wq_ref.shape[1]
+
+    @pl.when(step == 0)
+    def _():
+        floats = x_ref[...].astype(jnp.float32)
+        centred = floats - jnp.mean(floats, axis=-1, keepdims=True)
+        variance = jnp.mean(centred * centred, axis=-1, keepdims=True)
+        nrm_ref[...] = (centred * lax.rsqrt(variance + 1e-05)).astype(jnp.bfloat16)
+        acc_ref[...] = jnp.zeros_like(acc_ref)
+        q_stream = lax.broadcasted_iota(jnp.int32, (tokens, streams * ctx), 0) // frames
+        c_col = lax.broadcasted_iota(jnp.int32, (tokens, streams * ctx), 1)
+        same_c = (c_col >= q_stream * ctx) & (c_col < q_stream * ctx + ctx)
+        bc_ref[...] = jnp.where(same_c, 0.0, -1e30).astype(jnp.float32)
+        q_stream_n = lax.broadcasted_iota(jnp.int32, (tokens, tokens), 0) // frames
+        k_stream_n = lax.broadcasted_iota(jnp.int32, (tokens, tokens), 1) // frames
+        same_n = (q_stream_n == k_stream_n) & (klive_ref[...] > 0.0)
+        bn_ref[...] = jnp.where(same_n, 0.0, -1e30).astype(jnp.float32)
+
+    normed = nrm_ref[...]
+    q = jnp.dot(normed, wq_ref[...], preferred_element_type=jnp.float32)
+    q = (q * (head_size ** -0.5)).astype(jnp.bfloat16)
+    k = jnp.dot(normed, wk_ref[...], preferred_element_type=jnp.float32).astype(jnp.bfloat16)
+    v = jnp.dot(normed, wv_ref[...], preferred_element_type=jnp.float32).astype(jnp.bfloat16)
+    ck = ck_ref[...]
+    cv = cv_ref[...]
+    lane = lax.broadcasted_iota(jnp.int32, (tokens, pair), 1)
+    nt = (((1,), (1,)), ((), ()))
+    outs = []
+    for half in range(pair // head_size):
+        mine = (lane >= half * head_size) & (lane < (half + 1) * head_size)
+        qh = jnp.where(mine, q, jnp.zeros_like(q))
+        sc = lax.dot_general(qh, ck, nt, preferred_element_type=jnp.float32) + bc_ref[...]
+        sn = lax.dot_general(qh, k, nt, preferred_element_type=jnp.float32) + bn_ref[...]
+        top = jnp.maximum(jnp.max(sc, axis=-1, keepdims=True), jnp.max(sn, axis=-1, keepdims=True))
+        ec = jnp.exp(sc - top)
+        en = jnp.exp(sn - top)
+        total = jnp.sum(ec, axis=-1, keepdims=True) + jnp.sum(en, axis=-1, keepdims=True)
+        pc = (ec / total).astype(jnp.bfloat16)
+        pn = (en / total).astype(jnp.bfloat16)
+        oh = jnp.dot(pc, cv, preferred_element_type=jnp.float32) + jnp.dot(
+            pn, v, preferred_element_type=jnp.float32)
+        outs.append((mine, oh))
+    attended = outs[-1][1]
+    for mine, oh in outs[:-1]:
+        attended = jnp.where(mine, oh, attended)
+    attended = attended.astype(jnp.bfloat16)
+    acc_ref[...] += jnp.dot(attended, wo_ref[...], preferred_element_type=jnp.float32)
+
+    @pl.when(step == pl.num_programs(0) - 1)
+    def _():
+        kept = cst_ref.shape[1]
+        lead = pad_ref.shape[1] - frames - kept
+        residual = x_ref[...].astype(jnp.float32) + acc_ref[...]
+        acc_ref[...] = residual
+        rounded = residual.astype(jnp.bfloat16).astype(jnp.float32)
+        pad_ref[:, lead:lead + kept, :] = cst_ref[...].astype(jnp.float32)
+        pad_ref[:, lead + kept:, :] = rounded.reshape(streams, frames, width)
+        taps = cw_ref.shape[0]
+        chunk = 128
+        for c in range(width // chunk):
+            cols = slice(c * chunk, (c + 1) * chunk)
+            conv = jnp.zeros((streams, frames, chunk), jnp.float32)
+            for j in range(taps):
+                conv = conv + cw_ref[j:j + 1, cols].reshape(1, 1, chunk) * pad_ref[
+                    :, lead + j:lead + j + frames, cols]
+            res = acc_ref[:, cols].reshape(streams, frames, chunk)
+            silu = conv / (1.0 + jnp.exp(-conv))
+            live = rlive_ref[...].reshape(streams, frames, 1)
+            out = (res + silu) * live
+            out_ref[:, cols] = out.reshape(tokens, chunk).astype(out_ref.dtype)
+
+
 def encoder_layer(inputs, valid_counts, context, conv_state, qkv_weight, out_weight, conv_weight):
-    stream_count, frame_count, model_width = inputs.shape
-    head_size = model_width // HEADS
-    live_mask = jnp.arange(frame_count, dtype=jnp.int32)[None, :] < valid_counts[:, None]
-    floats = inputs.astype(jnp.float32)
-    centred = floats - jnp.mean(floats, axis=-1, keepdims=True)
-    variance = jnp.mean(centred * centred, axis=-1, keepdims=True)
-    normed = (centred * lax.rsqrt(variance + 1e-05)).astype(jnp.bfloat16)
-    projected = jnp.dot(
-        normed.reshape(-1, model_width), qkv_weight, preferred_element_type=jnp.float32
-    )
-    projected = projected.reshape(stream_count, frame_count, 3 * model_width)
-    queries = (projected[:, :, :model_width] * head_size ** (-0.5)).astype(jnp.bfloat16)
-    new_keys = projected[:, :, model_width : 2 * model_width].astype(jnp.bfloat16)
-    new_values = projected[:, :, 2 * model_width :].astype(jnp.bfloat16)
-    keys_all = jnp.concatenate([context[:, :, :model_width], new_keys], axis=1)
-    values_all = jnp.concatenate([context[:, :, model_width:], new_values], axis=1)
-    key_total = keys_all.shape[1]
-    queries_split = queries.reshape(stream_count, frame_count, HEADS, head_size)
-    keys_split = keys_all.reshape(stream_count, key_total, HEADS, head_size)
-    values_split = values_all.reshape(stream_count, key_total, HEADS, head_size)
-    scores = jnp.einsum(
-        "bqhd,bkhd->bhqk", queries_split, keys_split, preferred_element_type=jnp.float32
-    )
-    key_mask = jnp.concatenate(
-        [jnp.ones((stream_count, key_total - frame_count), dtype=bool), live_mask], axis=1
-    )
-    scores = jnp.where(key_mask[:, None, None, :], scores, jnp.float32(-1e30))
-    top_score = jnp.max(scores, axis=-1, keepdims=True)
-    exponent = jnp.exp(scores - top_score)
-    softmax_weights = (exponent / jnp.sum(exponent, axis=-1, keepdims=True)).astype(jnp.bfloat16)
-    attended = jnp.einsum(
-        "bhqk,bkhd->bqhd", softmax_weights, values_split, preferred_element_type=jnp.float32
-    )
-    attended = attended.reshape(stream_count * frame_count, model_width).astype(jnp.bfloat16)
-    mixed = jnp.dot(attended, out_weight, preferred_element_type=jnp.float32)
-    residual_sum = floats + mixed.reshape(stream_count, frame_count, model_width)
-    rounded = lax.optimization_barrier(residual_sum.astype(jnp.bfloat16))
-    padded_input = jnp.concatenate([conv_state, rounded], axis=1).astype(jnp.float32)
-    convolved = jnp.zeros((stream_count, frame_count, model_width), jnp.float32)
-    for tap_index in range(conv_weight.shape[0]):
-        convolved = (
-            convolved
-            + conv_weight[tap_index][None, None, :]
-            * padded_input[:, tap_index : tap_index + frame_count, :]
-        )
-    output = (residual_sum + jax.nn.silu(convolved)) * live_mask[:, :, None].astype(jnp.float32)
-    return output.astype(jnp.bfloat16)
+    streams, frames, width = inputs.shape
+    ctx = context.shape[1]
+    kept = conv_state.shape[1]
+    head_size = width // HEADS
+    pair = 2 * head_size
+    pairs = width // pair
+    tokens = streams * frames
+    live = (jnp.arange(frames, dtype=jnp.int32)[None, :] < valid_counts[:, None]).astype(jnp.float32)
+    klive = live.reshape(1, tokens)
+    rlive = live.reshape(tokens, 1)
+    x = inputs.reshape(tokens, width)
+    ctx2 = context.reshape(streams * ctx, 2 * width)
+    lead = (-(kept + frames)) % 8
+    kernel = functools.partial(layer_kernel, streams=streams, frames=frames, ctx=ctx,
+                               head_size=head_size)
+    const = lambda p: (0, 0)
+    out = pl.pallas_call(
+        kernel,
+        out_shape=jax.ShapeDtypeStruct((tokens, width), jnp.bfloat16),
+        grid=(pairs,),
+        in_specs=[
+            pl.BlockSpec((tokens, width), const),
+            pl.BlockSpec((1, tokens), const),
+            pl.BlockSpec((tokens, 1), const),
+            pl.BlockSpec((streams * ctx, pair), lambda p: (0, p)),
+            pl.BlockSpec((streams * ctx, pair), lambda p: (0, pairs + p)),
+            pl.BlockSpec((streams, kept, width), lambda p: (0, 0, 0)),
+            pl.BlockSpec((width, pair), lambda p: (0, p)),
+            pl.BlockSpec((width, pair), lambda p: (0, pairs + p)),
+            pl.BlockSpec((width, pair), lambda p: (0, 2 * pairs + p)),
+            pl.BlockSpec((pair, width), lambda p: (p, 0)),
+            pl.BlockSpec(conv_weight.shape, const),
+        ],
+        out_specs=pl.BlockSpec((tokens, width), const),
+        scratch_shapes=[
+            pltpu.VMEM((tokens, width), jnp.bfloat16),
+            pltpu.VMEM((tokens, width), jnp.float32),
+            pltpu.VMEM((tokens, streams * ctx), jnp.float32),
+            pltpu.VMEM((tokens, tokens), jnp.float32),
+            pltpu.VMEM((streams, lead + kept + frames, width), jnp.float32),
+        ],
+        compiler_params=pltpu.CompilerParams(dimension_semantics=("arbitrary",)),
+    )(x, klive, rlive, ctx2, ctx2, conv_state, qkv_weight, qkv_weight, qkv_weight, out_weight,
+      conv_weight)
+    return out.reshape(streams, frames, width)
 
 
 def routing(anchor, own_index, local_count):

time: 131 us -> 106 us (0.81); the launches traced: 129 us -> 106 us
  Pallas kernels: 0 us -> 51.5 us
  local copies, waits for them, and re-layouts: 54.7 us -> 18.4 us
  matrix products: 32 us -> 0 us
  other arithmetic: 26.1 us -> 8.44 us
  waiting for transfers between devices: 2.79 us -> 14.6 us
    pallas_call x0 -> x2, Pallas kernels: none -> 51.5 us  [encoder_layer(): pl.pallas_call(kernel, out_shape=jax.ShapeDtypeStruct((tokens, width), jn...]
    dot_general x6 -> x0, matrix products: 22.4 us -> none  [the longest x2 12.2 us: encoder_layer(): jnp.dot(normed.reshape(-1, model_width), qkv_weight, preferred_element_ty...]
    reshape x6 -> x0, local copies, waits for them, and re-layouts: 19.2 us -> none  [the longest x2 7.54 us: encoder_layer(): values_split = values_all.reshape(stream_count, key_total, HEADS, head_size)]
    sub x2 -> x0, matrix products: 9.65 us -> none  [encoder_layer(): exponent = jnp.exp(scores - top_score)]
    all_to_all x1, waiting for transfers between devices: 0.01 us -> 8.43 us  [body(): lax.all_to_all(outgoing[1], 'stream', split_axis=0, concat_axis=0, tiled=...]
    convert_element_type x6 -> x1, other arithmetic: 8.48 us -> 0.07 us  [encoder_layer(): (jnp.arange(frames, dtype=jnp.int32)[None, :] < valid_counts[:, None]).as...]
    convert_element_type x4 -> x2, local copies, waits for them, and re-layouts: 7.05 us -> 1.42 us  [encoder_layer(): (jnp.arange(frames, dtype=jnp.int32)[None, :] < valid_counts[:, None]).as...]
    concatenate x3 -> x0, other arithmetic: 5.61 us -> none  [the longest x2 4.37 us: encoder_layer(): jnp.concatenate([context[:, :, model_width:], new_values], axis=1)]
  transfers between devices with their start and end apart: 3 -> 3, of which waited for: 1 -> 3; matrix products, arithmetic and copies ran while one was open for 42% -> 15% of each run, Pallas kernels for 0% -> 0%
where the time goes in v1:
time: 106 us
  Pallas kernels  51.5 us (49%)
  local copies, waits for them, and re-layouts  18.4 us (17%)
  waiting for transfers between devices  14.6 us (14%)
  starting transfers between devices  12.7 us (12%)
  other arithmetic  8.44 us (8%)
    pallas_call x2, Pallas kernels, encoder_layer(): pl.pallas_call(kernel, out_shape=jax.ShapeDtypeStruct((tokens, width), jn...  51.5 us
    all_to_all x1, waiting for transfers between devices, body(): lax.all_to_all(outgoing[1], 'stream', split_axis=0, concat_axis=0, tiled=...  8.43 us
    all_to_all x1, starting transfers between devices, body(): lax.all_to_all(outgoing[0], 'stream', split_axis=0, concat_axis=0, tiled=...  6.55 us
    scatter x2, local copies, waits for them, and re-layouts, pack_rows(): jnp.zeros((slot_total,) + rows.shape[1:], rows.dtype).at[places]  6.04 us
    all_to_all x1, starting transfers between devices, body(): lax.all_to_all(outgoing[1], 'stream', split_axis=0, concat_axis=0, tiled=...  4.88 us
    unnamed x15, local copies, waits for them, and re-layouts  4.03 us
    select_n x2, other arithmetic, pick_rows(): return jnp.where(staying, from_local, from_buffer)  3.76 us
    ppermute x1, waiting for transfers between devices, shifted(): lax.ppermute(value, axis, [(source, source + steps) for source in range(l...  3.54 us
  transfers between devices with their start and end apart: 3, of which 3 were waited for; matrix products, arithmetic and copies ran while one was open for 15% of the time, Pallas kernels for 0%

profile of v1, /device:TPU:1, one launch (start us, length us, event | category | flops | bytes accessed | tf_op | source)
XLA Modules:
  0.0 105.7 jit_solution(5091577445284995008)
XLA Ops:
  0.0 0.8 select_reduce_fusion
  0.8 1.6 %copy.23 = bf16[1,16,12,2048]{3,2,1,0:T(8,128)(2,1)S(1)} copy(bf16[1,16,12,2048]{3,1,2,0:T(8,128)(2,1)} %param.11) | data formatting | bytes 1572864 | tf_op args[3]
  2.5 0.8 broadcast_in_dim.112
  3.4 3.1 %scatter_fusion = bf16[8,12,2048]{2,1,0:T(8,128)(2,1)} fusion(bf16[8,12,2048]{2,1,0:T(8,128)(2,1)} %broadcast_in_dim.112, s32[16]{0:T(128)S(1)} %compare_select_fusion, bf16[16,12,2048]{2,1,0:T(8,128)(2,1)S(1)} %bitcast.21), kind=kCustom, calls=%fused_computation.4 | custom fusion | bytes 2359360 | tf_op jit(solution)/shard_map/scatter | solution.py:158
  6.5 6.6 %all-to-all-start = ((bf16[8,12,2048]{2,1,0:T(8,128)(2,1)}), bf16[8,12,2048]{2,1,0:T(8,128)(2,1)S(1)}, u32[]{:S(2)}, u32[]{:S(2)}) async-start(bf16[8,12,2048]{2,1,0:T(8,128)(2,1)} %scatter_fusion), calls=%async_computation | async-start | bytes 1048576 | tf_op jit(solution)/shard_map/all_to_all | solution.py:207
  13.2 0.8 reshape.174.rlive_ref
  13.9 0.7 reshape.118.klive_ref
  14.7 0.6 gather_fusion
  15.3 1.1 %gather.21 = bf16[192,2048]{1,0:T(8,128)(2,1)} reshape(bf16[16,12,2048]{2,1,0:T(8,128)(2,1)S(1)} %gather_fusion) | data formatting | bytes 1572864 | tf_op jit(solution)/shard_map/jit(_take)/gather | solution.py:163
  16.5 0.1 broadcast_in_dim.110
  16.7 0.1 broadcast_in_dim.102
  16.8 0.1 broadcast_in_dim.105
  16.9 1.7 %copy.22 = bf16[1,16,30,1024]{3,2,1,0:T(8,128)(2,1)S(1)} copy(bf16[1,16,30,1024]{3,1,2,0:T(8,128)(2,1)} %param.12) | data formatting | bytes 1966080 | tf_op args[4]
  18.7 0.6 gather_fusion.2
  19.3 0.9 broadcast_in_dim.121
  20.2 3.0 %scatter_fusion.1 = bf16[8,30,1024]{2,1,0:T(8,128)(2,1)} fusion(bf16[8,30,1024]{2,1,0:T(8,128)(2,1)} %broadcast_in_dim.121, s32[16]{0:T(128)S(1)} %compare_select_fusion, bf16[16,30,1024]{2,1,0:T(8,128)(2,1)S(1)} %bitcast.24), kind=kCustom, calls=%fused_computation.5 | custom fusion | bytes 2949184 | tf_op jit(solution)/shard_map/scatter | solution.py:158
  23.1 0.7 copy.24
  23.8 2.6 %all-to-all-done = bf16[8,12,2048]{2,1,0:T(8,128)(2,1)S(1)} async-done(((bf16[8,12,2048]{2,1,0:T(8,128)(2,1)}), bf16[8,12,2048]{2,1,0:T(8,128)(2,1)S(1)}, u32[]{:S(2)}, u32[]{:S(2)}) %all-to-all-start) | async-done | bytes 393248 | tf_op jit(solution)/shard_map/all_to_all | solution.py:207
  26.4 4.9 %all-to-all-start.1 = ((bf16[8,30,1024]{2,1,0:T(8,128)(2,1)}), bf16[8,30,1024]{2,1,0:T(8,128)(2,1)S(1)}, u32[]{:S(2)}, u32[]{:S(2)}) async-start(bf16[8,30,1024]{2,1,0:T(8,128)(2,1)} %scatter_fusion.1), calls=%async_computation.1 | async-start | bytes 1048576 | tf_op jit(solution)/shard_map/all_to_all | solution.py:208
  31.3 0.8 broadcast_select_fusion.1
  32.2 0.6 gather_fusion.1
  32.8 1.1 %gather.23 = bf16[192,2048]{1,0:T(8,128)(2,1)} reshape(bf16[16,12,2048]{2,1,0:T(8,128)(2,1)S(1)} %gather_fusion.1) | data formatting | bytes 1572864 | tf_op jit(solution)/shard_map/jit(_take)/gather | solution.py:162
  33.9 2.5 %select_select_fusion.1.ck_ref.cv_ref = bf16[192,2048]{1,0:T(8,128)(2,1)} fusion(bf16[192,2048]{1,0:T(8,128)(2,1)} %gather.23, bf16[192,2048]{1,0:T(8,128)(2,1)} %gather.21, pred[192]{0:T(512)(128)(4,1)S(1)} %broadcast_in_dim.110, pred[192]{0:T(512)(128)(4,1)S(1)} %broadcast_in_dim.105, pred[192]{0:T(512)(128)(4,1)S(1)} %broadcast_in_dim.102), kind=kLoop, calls=%fused_computation.9 | loop fusion | flops 1179648 | bytes 2359872 | tf_op jit(solution)/shard_map/jit(_where)/select_n | solution.py:165
  36.4 8.4 %all-to-all-done.1 = bf16[8,30,1024]{2,1,0:T(8,128)(2,1)S(1)} async-done(((bf16[8,30,1024]{2,1,0:T(8,128)(2,1)}), bf16[8,30,1024]{2,1,0:T(8,128)(2,1)S(1)}, u32[]{:S(2)}, u32[]{:S(2)}) %all-to-all-start.1) | async-done | bytes 491552 | tf_op jit(solution)/shard_map/all_to_all | solution.py:208
  44.8 0.6 gather_fusion.3
  45.4 1.3 %select_select_fusion.cst_ref = bf16[16,30,1024]{2,1,0:T(8,128)(2,1)} fusion(bf16[16,30,1024]{2,1,0:T(8,128)(2,1)S(1)} %gather_fusion.3, bf16[16,30,1024]{2,1,0:T(8,128)(2,1)S(1)} %gather_fusion.2, pred[16]{0:T(512)(128)(4,1)S(1)} %compare_and_fusion, pred[16]{0:T(512)(128)(4,1)S(1)} %get-tuple-element.7, pred[16]{0:T(512)(128)(4,1)S(1)} %get-tuple-element.9), kind=kLoop, calls=%fused_computation.8 | loop fusion | flops 1474560 | bytes 2949168 | tf_op jit(solution)/shard_map/jit(_where)/select_n | solution.py:165
  46.7 25.7 %shard_map.82 = bf16[256,1024]{1,0:T(8,128)(2,1)} custom-call(bf16[256,1024]{1,0:T(8,128)(2,1)} %bitcast.28, f32[1,256]{1,0:T(1,128)} %reshape.118.klive_ref, f32[256,1]{1,0:T(8,128)} %reshape.174.rlive_ref, bf16[192,2048]{1,0:T(8,128)(2,1)} %select_select_fusion.1.ck_ref.cv_ref, bf16[192,2048]{1,0:T(8,128)(2,1)} %select_select_fusion.1.ck_ref.cv_ref, ...), custom_call_target="tpu_custom_call" | custom-call | tf_op jit(solution)/shard_map/pallas_call | solution.py:114
  72.4 1.3 %collective-permute-start = (bf16[16,16,1024]{2,1,0:T(8,128)(2,1)}, bf16[16,16,1024]{2,1,0:T(8,128)(2,1)S(1)}, u32[]{:S(2)}, u32[]{:S(2)}) collective-permute-start(bf16[16,16,1024]{2,1,0:T(8,128)(2,1)} %bitcast.29), channel_id=1, source_target_pairs={{0,1},{2,3},{4,5},{6,7},{8,9},{10,11},{12,13},{14,15},{16,17},{18,... | collective-permute-start | bytes 1572872 | tf_op jit(solution)/shard_map/ppermute | solution.py:16
  73.7 3.5 %collective-permute-done = bf16[16,16,1024]{2,1,0:T(8,128)(2,1)S(1)} collective-permute-done((bf16[16,16,1024]{2,1,0:T(8,128)(2,1)}, bf16[16,16,1024]{2,1,0:T(8,128)(2,1)S(1)}, u32[]{:S(2)}, u32[]{:S(2)}) %collective-permute-start) | collective-permute-done | bytes 524320 | tf_op jit(solution)/shard_map/ppermute | solution.py:16
  77.2 0.8 broadcast_select_fusion
  78.1 25.7 %shard_map.83 = bf16[256,1024]{1,0:T(8,128)(2,1)} custom-call(bf16[256,1024]{1,0:T(8,128)(2,1)} %bitcast.27, f32[1,256]{1,0:T(1,128)} %reshape.118.klive_ref, f32[256,1]{1,0:T(8,128)} %reshape.174.rlive_ref, bf16[192,2048]{1,0:T(8,128)(2,1)} %select_select_fusion.1.ck_ref.cv_ref, bf16[192,2048]{1,0:T(8,128)(2,1)} %select_select_fusion.1.ck_ref.cv_ref, ...), custom_call_target="tpu_custom_call" | custom-call | tf_op jit(solution)/shard_map/pallas_call | solution.py:114
  103.8 1.9 %select_select_fusion.2 = bf16[256,1024]{1,0:T(8,128)(2,1)} fusion(bf16[256,1024]{1,0:T(8,128)(2,1)} %shard_map.83, bf16[256,1024]{1,0:T(8,128)(2,1)S(1)} %copy-done.2, pred[]{:T(512)S(6)} %and.36, pred[]{:T(512)S(6)} %and.31), kind=kLoop, calls=%fused_computation.10 | loop fusion | flops 524288 | bytes 1572866 | tf_op jit(solution)/shard_map/jit(_where)/select_n | solution.py:186
  (23 shorter events, 0.6 us)
Async XLA Ops:
  0.0 14.6 %copy-start.4 = (s32[128]{0:T(128)S(1)}, s32[128]{0:T(128)}, u32[]{:S(2)}) copy-start(s32[128]{0:T(128)} %param.10) | copy-start | bytes 1540
  0.0 13.0 %copy-start.5 = (s32[128]{0:T(128)S(1)}, s32[128]{0:T(128)}, u32[]{:S(2)}) copy-start(s32[128]{0:T(128)} %param.9) | copy-start | bytes 1540
  6.5 16.7 %copy-start.3 = (f32[1,31,1024]{2,0,1:T(1,128)S(1)}, f32[1,31,1024]{2,0,1:T(1,128)}, u32[]{:S(2)}) copy-start(f32[1,31,1024]{2,0,1:T(1,128)} %param.15) | copy-start | bytes 380932
  6.5 20.0 %all-to-all-start = ((bf16[8,12,2048]{2,1,0:T(8,128)(2,1)}), bf16[8,12,2048]{2,1,0:T(8,128)(2,1)S(1)}, u32[]{:S(2)}, u32[]{:S(2)}) async-start(bf16[8,12,2048]{2,1,0:T(8,128)(2,1)} %scatter_fusion), calls=%async_computation | async-start | bytes 1048576 | tf_op jit(solution)/shard_map/all_to_all | solution.py:207
  14.7 16.6 %copy-start = (bf16[16,16,1024]{2,1,0:T(8,128)(2,1)S(1)}, bf16[16,16,1024]{2,1,0:T(8,128)(2,1)}, u32[]{:S(2)}) copy-start(bf16[16,16,1024]{2,1,0:T(8,128)(2,1)} %param.8) | copy-start | bytes 1572868
  26.4 18.4 %all-to-all-start.1 = ((bf16[8,30,1024]{2,1,0:T(8,128)(2,1)}), bf16[8,30,1024]{2,1,0:T(8,128)(2,1)S(1)}, u32[]{:S(2)}, u32[]{:S(2)}) async-start(bf16[8,30,1024]{2,1,0:T(8,128)(2,1)} %scatter_fusion.1), calls=%async_computation.1 | async-start | bytes 1048576 | tf_op jit(solution)/shard_map/all_to_all | solution.py:208
  46.7 30.6 %copy-start.1 = (bf16[16,16,1024]{2,1,0:T(8,128)(2,1)S(1)}, bf16[16,16,1024]{2,1,0:T(8,128)(2,1)}, u32[]{:S(2)}) copy-start(bf16[16,16,1024]{2,1,0:T(8,128)(2,1)} %param.8) | copy-start | bytes 1572868
  72.4 4.8 %collective-permute-start = (bf16[16,16,1024]{2,1,0:T(8,128)(2,1)}, bf16[16,16,1024]{2,1,0:T(8,128)(2,1)S(1)}, u32[]{:S(2)}, u32[]{:S(2)}) collective-permute-start(bf16[16,16,1024]{2,1,0:T(8,128)(2,1)} %bitcast.29), channel_id=1, source_target_pairs={{0,1},{2,3},{4,5},{6,7},{8,9},{10,11},{12,13},{14,15},{16,17},{18,... | collective-permute-start | bytes 1572872 | tf_op jit(solution)/shard_map/ppermute | solution.py:16
  78.1 25.7 %copy-start.2 = (bf16[256,1024]{1,0:T(8,128)(2,1)S(1)}, bf16[256,1024]{1,0:T(8,128)(2,1)}, u32[]{:S(2)}) copy-start(bf16[256,1024]{1,0:T(8,128)(2,1)} %shard_map.82) | copy-start | bytes 1572868

commit v2 on v0

v2 whole, which is shorter than its diff:
```python
import functools

import jax
import jax.numpy as jnp
from jax import lax
from jax.experimental import pallas as pl
from jax.experimental.pallas import tpu as pltpu
from jax.sharding import PartitionSpec as P

HEADS = 16
GROUP = 8


def shifted(value, axis, steps):
    count = lax.axis_size(axis)
    leading, last = (max(0, -steps), min(count, count - steps))
    return lax.ppermute(value, axis, [(source, source + steps) for source in range(leading, last)])


def layer_kernel(sel_ref, x_ref, klive_ref, rlive_ref, cw_ref, wqkv_hbm, wo_hbm, ctxl_hbm,
                 ctxr_hbm, cstl_hbm, cstr_hbm, out_ref, wbuf, ctxv, cstv, qkv, acc_ref, pad_ref,
                 wsem, gsem, *, streams, frames, ctx, head_size):
    tokens = streams * frames
    width = x_ref.shape[1]
    slot = ctxv.shape[0] // streams
    copies = [
        pltpu.make_async_copy(wqkv_hbm.at[:, pl.ds(i * width, width)], wbuf.at[i], wsem.at[i])
        for i in range(3)
    ]
    copies.append(pltpu.make_async_copy(wo_hbm, wbuf.at[3], wsem.at[3]))
    for c in copies:
        c.start()
    for j in range(streams):
        kind = sel_ref[j]
        idx = sel_ref[streams + j]

        @pl.when(kind == 0)
        def _():
            pltpu.make_async_copy(ctxl_hbm.at[idx], ctxv.at[pl.ds(slot * j, slot)],
                                  gsem.at[0, j]).start()
            pltpu.make_async_copy(cstl_hbm.at[idx], cstv.at[j], gsem.at[1, j]).start()

        @pl.when(kind != 0)
        def _():
            pltpu.make_async_copy(ctxr_hbm.at[idx], ctxv.at[pl.ds(slot * j, slot)],
                                  gsem.at[0, j]).start()
            pltpu.make_async_copy(cstr_hbm.at[idx], cstv.at[j], gsem.at[1, j]).start()

    floats = x_ref[...].astype(jnp.float32)
    centred = floats - jnp.mean(floats, axis=-1, keepdims=True)
    variance = jnp.mean(centred * centred, axis=-1, keepdims=True)
    normed = (centred * lax.rsqrt(variance + 1e-05)).astype(jnp.bfloat16)
    for i in range(3):
        copies[i].wait()
        part = jnp.dot(normed, wbuf[i], preferred_element_type=jnp.float32)
        if i == 0:
            part = part * (head_size ** -0.5)
        qkv[i] = part.astype(jnp.bfloat16)
    for j in range(streams):
        pltpu.make_async_copy(ctxl_hbm.at[0], ctxv.at[pl.ds(slot * j, slot)], gsem.at[0, j]).wait()

    rows_g = GROUP * frames
    cols_g = GROUP * slot
    q_stream = lax.broadcasted_iota(jnp.int32, (rows_g, cols_g), 0) // frames
    c_col = lax.broadcasted_iota(jnp.int32, (rows_g, cols_g), 1)
    bias_c = jnp.where((c_col // slot == q_stream) & (c_col % slot < ctx), 0.0, -1e30)
    k_stream = lax.broadcasted_iota(jnp.int32, (rows_g, rows_g), 1) // frames
    q_stream_n = lax.broadcasted_iota(jnp.int32, (rows_g, rows_g), 0) // frames
    same_n = q_stream_n == k_stream
    pair = 2 * head_size
    lane = lax.broadcasted_iota(jnp.int32, (rows_g, pair), 1)
    nt = (((1,), (1,)), ((), ()))
    for g in range(streams // GROUP):
        rows = pl.ds(g * rows_g, rows_g)
        crow = pl.ds(g * cols_g, cols_g)
        bias_n = jnp.where(same_n & (klive_ref[:, pl.ds(g * rows_g, rows_g)] > 0.0), 0.0, -1e30)
        def head_pair(p, carry):
            cols = pl.ds(pl.multiple_of(p * pair, pair), pair)
            q = qkv[0, rows, cols]
            k = qkv[1, rows, cols]
            v = qkv[2, rows, cols]
            ck = ctxv[crow, cols]
            cv = ctxv[crow, pl.ds(pl.multiple_of(width + p * pair, pair), pair)]
            attended = None
            for half in range(pair // head_size):
                mine = (lane >= half * head_size) & (lane < (half + 1) * head_size)
                qh = jnp.where(mine, q, jnp.zeros_like(q))
                sc = lax.dot_general(qh, ck, nt, preferred_element_type=jnp.float32) + bias_c
                sn = lax.dot_general(qh, k, nt, preferred_element_type=jnp.float32) + bias_n
                top = jnp.maximum(jnp.max(sc, axis=-1, keepdims=True),
                                  jnp.max(sn, axis=-1, keepdims=True))
                ec = jnp.exp(sc - top)
                en = jnp.exp(sn - top)
                total = jnp.sum(ec, axis=-1, keepdims=True) + jnp.sum(en, axis=-1, keepdims=True)
                pc = (ec / total).astype(jnp.bfloat16)
                pn = (en / total).astype(jnp.bfloat16)
                oh = jnp.dot(pc, cv, preferred_element_type=jnp.float32) + jnp.dot(
                    pn, v, preferred_element_type=jnp.float32)
                attended = oh if attended is None else jnp.where(mine, oh, attended)
            qkv[0, rows, cols] = attended.astype(jnp.bfloat16)
            return carry

        lax.fori_loop(0, width // pair, head_pair, 0)

    copies[3].wait()
    mixed = jnp.dot(qkv[0], wbuf[3], preferred_element_type=jnp.float32)
    residual = x_ref[...].astype(jnp.float32) + mixed
    acc_ref[...] = residual
    for j in range(streams):
        pltpu.make_async_copy(cstl_hbm.at[0], cstv.at[j], gsem.at[1, j]).wait()
    kept = cstv.shape[1]
    lead = pad_ref.shape[1] - frames - kept
    rounded = residual.astype(jnp.bfloat16).astype(jnp.float32)
    pad_ref[:, lead:lead + kept, :] = cstv[...].astype(jnp.float32)
    pad_ref[:, lead + kept:, :] = rounded.reshape(streams, frames, width)
    taps = cw_ref.shape[0]
    chunk = 128
    live = rlive_ref[...].reshape(streams, frames, 1)
    def conv_chunk(c, carry):
        cols = pl.ds(pl.multiple_of(c * chunk, chunk), chunk)
        conv = jnp.zeros((streams, frames, chunk), jnp.float32)
        for j in range(taps):
            conv = conv + cw_ref[pl.ds(j, 1), cols].reshape(1, 1, chunk) * pad_ref[
                :, pl.ds(lead + j, frames), cols]
        res = acc_ref[:, cols].reshape(streams, frames, chunk)
        silu = conv / (1.0 + jnp.exp(-conv))
        out = (res + silu) * live
        out_ref[:, cols] = out.reshape(tokens, chunk).astype(out_ref.dtype)
        return carry

    lax.fori_loop(0, width // chunk, conv_chunk, 0)


def encoder_layer(inputs, valid_counts, sel, ctx_local, ctx_recv, cst_local, cst_recv,
                  qkv_weight, out_weight, conv_weight, ctx):
    streams, frames, width = inputs.shape
    kept = cst_local.shape[1]
    head_size = width // HEADS
    tokens = streams * frames
    slot = -(-ctx // 16) * 16
    live = (jnp.arange(frames, dtype=jnp.int32)[None, :] < valid_counts[:, None]).astype(jnp.float32)
    klive = live.reshape(1, tokens)
    rlive = live.reshape(tokens, 1)
    x = inputs.reshape(tokens, width)
    lead = (-(kept + frames)) % 8
    kernel = functools.partial(layer_kernel, streams=streams, frames=frames, ctx=ctx,
                               head_size=head_size)
    vmem = pl.BlockSpec(memory_space=pltpu.VMEM)
    hbm = pl.BlockSpec(memory_space=pl.ANY)
    out = pl.pallas_call(
        kernel,
        out_shape=jax.ShapeDtypeStruct((tokens, width), jnp.bfloat16),
        in_specs=[pl.BlockSpec(memory_space=pltpu.SMEM), vmem, vmem, vmem, vmem,
                  hbm, hbm, hbm, hbm, hbm, hbm],
        out_specs=vmem,
        scratch_shapes=[
            pltpu.VMEM((4, width, width), jnp.bfloat16),
            pltpu.VMEM((streams * slot, 2 * width), jnp.bfloat16),
            pltpu.VMEM((streams, kept, width), jnp.bfloat16),
            pltpu.VMEM((3, tokens, width), jnp.bfloat16),
            pltpu.VMEM((tokens, width), jnp.float32),
            pltpu.VMEM((streams, lead + kept + frames, width), jnp.float32),
            pltpu.SemaphoreType.DMA((4,)),
            pltpu.SemaphoreType.DMA((2, streams)),
        ],
    )(sel, x, klive, rlive, conv_weight, qkv_weight, out_weight, ctx_local, ctx_recv, cst_local,
      cst_recv)
    return out.reshape(streams, frames, width)


def migrate(anchor, own, count, local_count, ctx_local, cst_local):
    total = anchor.shape[0]
    every_slot = jnp.arange(total, dtype=jnp.int32)
    newpos = jnp.sum(jnp.where(anchor[None, :] == every_slot[:, None], every_slot[None, :], 0),
                     axis=1)
    mine_new = lax.dynamic_slice_in_dim(newpos, own * local_count, local_count)
    target = mine_new // local_count
    shifts = jnp.arange(1, count, dtype=jnp.int32)
    dest = (own + shifts) % count
    match = target[None, :] == dest[:, None]
    send_slot = jnp.sum(jnp.where(match, jnp.arange(local_count, dtype=jnp.int32)[None, :], 0),
                        axis=1)
    ctx_recv, cst_recv = [], []
    for k in range(1, count):
        perm = [(i, (i + k) % count) for i in range(count)]
        row = send_slot[k - 1]
        ctx_recv.append(lax.ppermute(ctx_local[row], "stream", perm))
        cst_recv.append(lax.ppermute(cst_local[row], "stream", perm))
    mine_old = lax.dynamic_slice_in_dim(anchor, own * local_count, local_count)
    source = mine_old // local_count
    staying = source == own
    local_idx = jnp.clip(mine_old - own * local_count, 0, local_count - 1)
    recv_idx = jnp.clip((own - source) % count - 1, 0, count - 2)
    sel = jnp.concatenate([jnp.where(staying, 0, 1), jnp.where(staying, local_idx, recv_idx)])
    return sel.astype(jnp.int32), jnp.stack(ctx_recv), jnp.stack(cst_recv)


def body(
    new_frames, valid_counts, anchor, context_cache, conv_state, qkv_weight, out_weight, conv_weight
):
    local_count = new_frames.shape[0]
    own = lax.axis_index("stream")
    count = lax.axis_size("stream")
    ctx = context_cache.shape[2]
    slot = -(-ctx // 16) * 16
    ctx_local = jnp.pad(context_cache[0], ((0, 0), (0, slot - ctx), (0, 0)))
    cst_local = conv_state[0]
    sel, ctx_recv, cst_recv = migrate(anchor, own, count, local_count, ctx_local, cst_local)
    valid_here = lax.dynamic_slice_in_dim(valid_counts, own * local_count, local_count)
    section_index = lax.axis_index("section")
    layer = functools.partial(encoder_layer, valid_counts=valid_here, sel=sel, ctx_local=ctx_local,
                              ctx_recv=ctx_recv, cst_local=cst_local, cst_recv=cst_recv,
                              qkv_weight=qkv_weight[0], out_weight=out_weight[0],
                              conv_weight=conv_weight[0], ctx=ctx)
    first = layer(new_frames)
    inbound = shifted(first, "section", 1)
    second = layer(inbound)
    result = jnp.where(section_index == 0, first, second)
    return result[None]


def solution(mesh):
    return jax.shard_map(
        body,
        mesh=mesh,
        in_specs=(
            P(("groups", "stream"), None, None),
            P("groups"),
            P("groups"),
            P("section", ("groups", "stream"), None, None),
            P("section", ("groups", "stream"), None, None),
            P("section", None, None),
            P("section", None, None),
            P("section", None, None),
        ),
        out_specs=P("section", ("groups", "stream"), None, None),
        check_vma=False,
    )
```

time: 131 us -> 139 us (1.061); the launches traced: 129 us -> 139 us
  Pallas kernels: 0 us -> 60 us
  local copies, waits for them, and re-layouts: 54.7 us -> 10.6 us
  waiting for transfers between devices: 2.79 us -> 34.8 us
  matrix products: 32 us -> 0 us
  other arithmetic: 26.1 us -> 5.05 us
  between operations: 0.27 us -> 13.3 us
  starting transfers between devices: 13.5 us -> 15.2 us
    pallas_call x0 -> x2, Pallas kernels: none -> 60 us  [encoder_layer(): pl.pallas_call(kernel, out_shape=jax.ShapeDtypeStruct((tokens, width), jn...]
    ppermute x0 -> x14, waiting for transfers between devices: none -> 25.4 us  [the longest x7 15.6 us: migrate(): ctx_recv.append(lax.ppermute(ctx_local[row], 'stream', perm))]
    dot_general x6 -> x0, matrix products: 22.4 us -> none  [the longest x2 12.2 us: encoder_layer(): jnp.dot(normed.reshape(-1, model_width), qkv_weight, preferred_element_ty...]
    reshape x6 -> x0, local copies, waits for them, and re-layouts: 19.2 us -> none  [the longest x2 7.54 us: encoder_layer(): values_split = values_all.reshape(stream_count, key_total, HEADS, head_size)]
    ppermute x0 -> x14, starting transfers between devices: none -> 13.7 us  [the longest x7 9 us: migrate(): cst_recv.append(lax.ppermute(cst_local[row], 'stream', perm))]
    all_to_all x2 -> x0, starting transfers between devices: 12 us -> none  [the longest x1 6.53 us: body(): lax.all_to_all(outgoing[0], 'stream', split_axis=0, concat_axis=0, tiled=...]
    gather x4 -> x0, local copies, waits for them, and re-layouts: 9.86 us -> none  [the longest x2 5.63 us: pick_rows(): from_local = jnp.take(local_rows, local_index, axis=0)]
    sub x2 -> x0, matrix products: 9.65 us -> none  [encoder_layer(): exponent = jnp.exp(scores - top_score)]
  transfers between devices with their start and end apart: 3 -> 15, of which waited for: 1 -> 6; matrix products, arithmetic and copies ran while one was open for 42% -> 6% of each run, Pallas kernels for 0% -> 0%
where the time goes in v2:
time: 139 us
  Pallas kernels  60 us (43%)
  waiting for transfers between devices  34.8 us (25%)
  starting transfers between devices  15.2 us (11%)
  between operations  13.3 us (10%)
  local copies, waits for them, and re-layouts  10.6 us (8%)
  other arithmetic  5.05 us (4%)
    pallas_call x2, Pallas kernels, encoder_layer(): pl.pallas_call(kernel, out_shape=jax.ShapeDtypeStruct((tokens, width), jn...  60 us
    ppermute x7, waiting for transfers between devices, migrate(): ctx_recv.append(lax.ppermute(ctx_local[row], 'stream', perm))  15.6 us
    ppermute x7, waiting for transfers between devices, migrate(): cst_recv.append(lax.ppermute(cst_local[row], 'stream', perm))  9.82 us
    ppermute x1, waiting for transfers between devices, shifted(): lax.ppermute(value, axis, [(source, source + steps) for source in range(l...  9.39 us
    ppermute x7, starting transfers between devices, migrate(): cst_recv.append(lax.ppermute(cst_local[row], 'stream', perm))  9 us
    unnamed x25, local copies, waits for them, and re-layouts  6.56 us
    ppermute x7, starting transfers between devices, migrate(): ctx_recv.append(lax.ppermute(ctx_local[row], 'stream', perm))  4.68 us
  transfers between devices with their start and end apart: 15, of which 6 were waited for; matrix products, arithmetic and copies ran while one was open for 6% of the time, Pallas kernels for 0%

profile of v2, /device:TPU:1, one launch (start us, length us, event | category | flops | bytes accessed | tf_op | source)
XLA Modules:
  0.0 138.9 jit_solution(1678942337225370200)
XLA Ops:
  0.0 0.8 select_reduce_fusion
  0.8 0.7 compare_select_fusion.11
  1.5 0.2 select_reduce_fusion.1
  1.7 0.7 fusion.6
  11.1 1.7 %copy.40 = bf16[1,16,30,1024]{3,2,1,0:T(8,128)(2,1)S(1)} copy(bf16[1,16,30,1024]{3,1,2,0:T(8,128)(2,1)} %param.12) | data formatting | bytes 1966080 | tf_op args[4]
  17.2 5.2 %collective-permute-start.13 = (bf16[30,1024]{1,0:T(8,128)(2,1)S(1)}, bf16[30,1024]{1,0:T(8,128)(2,1)S(1)}, u32[]{:S(2)}, u32[]{:S(2)}) collective-permute-start(bf16[30,1024]{1,0:T(8,128)(2,1)S(1)} %get-tuple-element.7), channel_id=1, source_target_pairs={{0,14},{2,0},{4,2},{6,4},{8,6},{10,8},{12,10},{14,12},{1,15},{3,1}... | collective-permute-start | bytes 184328 | tf_op jit(solution)/shard_map/ppermute | solution.py:188
  22.6 2.4 %collective-permute-start.10 = (bf16[30,1024]{1,0:T(8,128)(2,1)S(1)}, bf16[30,1024]{1,0:T(8,128)(2,1)S(1)}, u32[]{:S(2)}, u32[]{:S(2)}) collective-permute-start(bf16[30,1024]{1,0:T(8,128)(2,1)S(1)} %get-tuple-element.10), channel_id=1, source_target_pairs={{0,8},{2,10},{4,12},{6,14},{8,0},{10,2},{12,4},{14,6},{1,9},{3,11}... | collective-permute-start | bytes 184328 | tf_op jit(solution)/shard_map/ppermute | solution.py:188
  25.0 1.2 collective-permute-start.7
  26.2 0.7 dynamic_slice.52
  27.0 0.6 reshape.123.klive_ref
  27.7 0.7 reshape.125.rlive_ref
  28.4 0.7 compare_select_fusion.10
  29.1 1.6 %copy.39 = f32[1,31,1024]{2,1,0:T(8,128)} copy(f32[1,31,1024]{2,0,1:T(1,128)} %param.15) | data formatting | bytes 253952
  30.7 1.6 %copy.38 = bf16[1,16,12,2048]{3,2,1,0:T(8,128)(2,1)S(1)} copy(bf16[1,16,12,2048]{3,1,2,0:T(8,128)(2,1)} %param.11) | data formatting | bytes 1572864 | tf_op args[3]
  32.4 1.1 pad.4.ctxl_hbm
  33.5 0.6 pad_add_fusion.sel_ref
  34.2 4.9 %collective-permute-done.8 = bf16[30,1024]{1,0:T(8,128)(2,1)S(1)} collective-permute-done((bf16[30,1024]{1,0:T(8,128)(2,1)S(1)}, bf16[30,1024]{1,0:T(8,128)(2,1)S(1)}, u32[]{:S(2)}, u32[]{:S(2)}) %collective-permute-start.8) | collective-permute-done | bytes 61472 | tf_op jit(solution)/shard_map/ppermute | solution.py:188
  39.1 4.9 %collective-permute-done.9 = bf16[30,1024]{1,0:T(8,128)(2,1)S(1)} collective-permute-done((bf16[30,1024]{1,0:T(8,128)(2,1)S(1)}, bf16[30,1024]{1,0:T(8,128)(2,1)S(1)}, u32[]{:S(2)}, u32[]{:S(2)}) %collective-permute-start.9) | collective-permute-done | bytes 61472 | tf_op jit(solution)/shard_map/ppermute | solution.py:188
  44.0 0.2 collective-permute-start.6
  44.2 0.7 collective-permute-start.5
  45.0 3.1 %collective-permute-start.3 = (bf16[16,2048]{1,0:T(8,128)(2,1)S(1)}, bf16[16,2048]{1,0:T(8,128)(2,1)S(1)}, u32[]{:S(2)}, u32[]{:S(2)}) collective-permute-start(bf16[16,2048]{1,0:T(8,128)(2,1)S(1)} %get-tuple-element.17), channel_id=1, source_target_pairs={{0,8},{2,10},{4,12},{6,14},{8,0},{10,2},{12,4},{14,6},{1,9},{3,11}... | collective-permute-start | bytes 196616 | tf_op jit(solution)/shard_map/ppermute | solution.py:187
  48.2 0.6 collective-permute-start
  48.8 5.4 %collective-permute-done = bf16[16,2048]{1,0:T(8,128)(2,1)S(1)} collective-permute-done((bf16[16,2048]{1,0:T(8,128)(2,1)S(1)}, bf16[16,2048]{1,0:T(8,128)(2,1)S(1)}, u32[]{:S(2)}, u32[]{:S(2)}) %collective-permute-start) | collective-permute-done | bytes 65568 | tf_op jit(solution)/shard_map/ppermute | solution.py:187
  54.1 5.2 %collective-permute-done.1 = bf16[16,2048]{1,0:T(8,128)(2,1)S(1)} collective-permute-done((bf16[16,2048]{1,0:T(8,128)(2,1)S(1)}, bf16[16,2048]{1,0:T(8,128)(2,1)S(1)}, u32[]{:S(2)}, u32[]{:S(2)}) %collective-permute-start.1) | collective-permute-done | bytes 65568 | tf_op jit(solution)/shard_map/ppermute | solution.py:187
  59.3 5.0 %collective-permute-done.2 = bf16[16,2048]{1,0:T(8,128)(2,1)S(1)} collective-permute-done((bf16[16,2048]{1,0:T(8,128)(2,1)S(1)}, bf16[16,2048]{1,0:T(8,128)(2,1)S(1)}, u32[]{:S(2)}, u32[]{:S(2)}) %collective-permute-start.2) | collective-permute-done | bytes 65568 | tf_op jit(solution)/shard_map/ppermute | solution.py:187
  64.5 0.8 copy-done.2
  65.3 30.0 %shard_map.82 = bf16[256,1024]{1,0:T(8,128)(2,1)} custom-call(s32[32]{0:T(128)} %pad_add_fusion.sel_ref, bf16[256,1024]{1,0:T(8,128)(2,1)} %bitcast.88, f32[1,256]{1,0:T(1,128)} %reshape.123.klive_ref, f32[256,1]{1,0:T(8,128)} %reshape.125.rlive_ref, f32[31,1024]{1,0:T(8,128)} %bitcast.86, bf16[1024,3072]{1,0:T(8,128)(2,1)} %bitcast.77, ...), custom_call_target="tpu_custom_call" | custom-call | tf_op jit(solution)/shard_map/pallas_call | solution.py:150
  95.3 1.5 %collective-permute-start.14 = (bf16[16,16,1024]{2,1,0:T(8,128)(2,1)}, bf16[16,16,1024]{2,1,0:T(8,128)(2,1)S(1)}, u32[]{:S(2)}, u32[]{:S(2)}) collective-permute-start(bf16[16,16,1024]{2,1,0:T(8,128)(2,1)} %bitcast.85), channel_id=1, source_target_pairs={{0,1},{2,3},{4,5},{6,7},{8,9},{10,11},{12,13},{14,15},{16,17},{18,... | collective-permute-start | bytes 1572872 | tf_op jit(solution)/shard_map/ppermute | solution.py:17
  96.7 9.4 %collective-permute-done.14 = bf16[16,16,1024]{2,1,0:T(8,128)(2,1)S(1)} collective-permute-done((bf16[16,16,1024]{2,1,0:T(8,128)(2,1)}, bf16[16,16,1024]{2,1,0:T(8,128)(2,1)S(1)}, u32[]{:S(2)}, u32[]{:S(2)}) %collective-permute-start.14) | collective-permute-done | bytes 524320 | tf_op jit(solution)/shard_map/ppermute | solution.py:17
  106.1 0.8 copy-done.4
  106.9 30.0 %shard_map.83 = bf16[256,1024]{1,0:T(8,128)(2,1)} custom-call(s32[32]{0:T(128)} %pad_add_fusion.sel_ref, bf16[256,1024]{1,0:T(8,128)(2,1)} %bitcast.89, f32[1,256]{1,0:T(1,128)} %reshape.123.klive_ref, f32[256,1]{1,0:T(8,128)} %reshape.125.rlive_ref, f32[31,1024]{1,0:T(8,128)} %bitcast.87, bf16[1024,3072]{1,0:T(8,128)(2,1)} %bitcast.78, ...), custom_call_target="tpu_custom_call" | custom-call | tf_op jit(solution)/shard_map/pallas_call | solution.py:150
  137.0 1.9 %broadcast_select_fusion = bf16[256,1024]{1,0:T(8,128)(2,1)} fusion(bf16[256,1024]{1,0:T(8,128)(2,1)S(1)} %copy-done.3, bf16[256,1024]{1,0:T(8,128)(2,1)} %shard_map.83, pred[]{:T(512)S(6)} %eq.39), kind=kLoop, calls=%fused_computation.1 | loop fusion | flops 262144 | bytes 1572865 | tf_op jit(solution)/shard_map/jit(_where)/select_n | solution.py:218
  (42 shorter events, 0.5 us)
Async XLA Ops:
  12.8 51.7 %copy-start = (bf16[1,16,30,1024]{3,2,1,0:T(8,128)(2,1)}, bf16[1,16,30,1024]{3,2,1,0:T(8,128)(2,1)S(1)}, u32[]{:S(2)}) copy-start(bf16[1,16,30,1024]{3,2,1,0:T(8,128)(2,1)S(1)} %copy.40) | copy-start | bytes 2949124
  17.2 30.9 %collective-permute-start.13 = (bf16[30,1024]{1,0:T(8,128)(2,1)S(1)}, bf16[30,1024]{1,0:T(8,128)(2,1)S(1)}, u32[]{:S(2)}, u32[]{:S(2)}) collective-permute-start(bf16[30,1024]{1,0:T(8,128)(2,1)S(1)} %get-tuple-element.7), channel_id=1, source_target_pairs={{0,14},{2,0},{4,2},{6,4},{8,6},{10,8},{12,10},{14,12},{1,15},{3,1}... | collective-permute-start | bytes 184328 | tf_op jit(solution)/shard_map/ppermute | solution.py:188
  22.4 22.6 %collective-permute-start.12 = (bf16[30,1024]{1,0:T(8,128)(2,1)S(1)}, bf16[30,1024]{1,0:T(8,128)(2,1)S(1)}, u32[]{:S(2)}, u32[]{:S(2)}) collective-permute-start(bf16[30,1024]{1,0:T(8,128)(2,1)S(1)} %get-tuple-element.8), channel_id=1, source_target_pairs={{0,12},{2,14},{4,0},{6,2},{8,4},{10,6},{12,8},{14,10},{1,13},{3,15... | collective-permute-start | bytes 184328 | tf_op jit(solution)/shard_map/ppermute | solution.py:188
  22.6 22.4 %collective-permute-start.11 = (bf16[30,1024]{1,0:T(8,128)(2,1)S(1)}, bf16[30,1024]{1,0:T(8,128)(2,1)S(1)}, u32[]{:S(2)}, u32[]{:S(2)}) collective-permute-start(bf16[30,1024]{1,0:T(8,128)(2,1)S(1)} %get-tuple-element.9), channel_id=1, source_target_pairs={{0,10},{2,12},{4,14},{6,0},{8,2},{10,4},{12,6},{14,8},{1,11},{3,13... | collective-permute-start | bytes 184328 | tf_op jit(solution)/shard_map/ppermute | solution.py:188
  22.6 21.7 %collective-permute-start.10 = (bf16[30,1024]{1,0:T(8,128)(2,1)S(1)}, bf16[30,1024]{1,0:T(8,128)(2,1)S(1)}, u32[]{:S(2)}, u32[]{:S(2)}) collective-permute-start(bf16[30,1024]{1,0:T(8,128)(2,1)S(1)} %get-tuple-element.10), channel_id=1, source_target_pairs={{0,8},{2,10},{4,12},{6,14},{8,0},{10,2},{12,4},{14,6},{1,9},{3,11}... | collective-permute-start | bytes 184328 | tf_op jit(solution)/shard_map/ppermute | solution.py:188
  25.0 9.2 %collective-permute-start.7 = (bf16[30,1024]{1,0:T(8,128)(2,1)S(1)}, bf16[30,1024]{1,0:T(8,128)(2,1)S(1)}, u32[]{:S(2)}, u32[]{:S(2)}) collective-permute-start(bf16[30,1024]{1,0:T(8,128)(2,1)S(1)} %get-tuple-element.13), channel_id=1, source_target_pairs={{0,2},{2,4},{4,6},{6,8},{8,10},{10,12},{12,14},{14,0},{1,3},{3,5},... | collective-permute-start | bytes 184328 | tf_op jit(solution)/shard_map/ppermute | solution.py:188
  34.2 4.9 %collective-permute-start.8 = (bf16[30,1024]{1,0:T(8,128)(2,1)S(1)}, bf16[30,1024]{1,0:T(8,128)(2,1)S(1)}, u32[]{:S(2)}, u32[]{:S(2)}) collective-permute-start(bf16[30,1024]{1,0:T(8,128)(2,1)S(1)} %get-tuple-element.12), channel_id=1, source_target_pairs={{0,4},{2,6},{4,8},{6,10},{8,12},{10,14},{12,0},{14,2},{1,5},{3,7},... | collective-permute-start | bytes 184328 | tf_op jit(solution)/shard_map/ppermute | solution.py:188
  39.1 4.9 %collective-permute-start.9 = (bf16[30,1024]{1,0:T(8,128)(2,1)S(1)}, bf16[30,1024]{1,0:T(8,128)(2,1)S(1)}, u32[]{:S(2)}, u32[]{:S(2)}) collective-permute-start(bf16[30,1024]{1,0:T(8,128)(2,1)S(1)} %get-tuple-element.11), channel_id=1, source_target_pairs={{0,6},{2,8},{4,10},{6,12},{8,14},{10,0},{12,2},{14,4},{1,7},{3,9},... | collective-permute-start | bytes 184328 | tf_op jit(solution)/shard_map/ppermute | solution.py:188
  44.0 20.5 %collective-permute-start.6 = (bf16[16,2048]{1,0:T(8,128)(2,1)S(1)}, bf16[16,2048]{1,0:T(8,128)(2,1)S(1)}, u32[]{:S(2)}, u32[]{:S(2)}) collective-permute-start(bf16[16,2048]{1,0:T(8,128)(2,1)S(1)} %get-tuple-element.14), channel_id=1, source_target_pairs={{0,14},{2,0},{4,2},{6,4},{8,6},{10,8},{12,10},{14,12},{1,15},{3,1}... | collective-permute-start | bytes 196616 | tf_op jit(solution)/shard_map/ppermute | solution.py:187
  44.2 20.2 %collective-permute-start.5 = (bf16[16,2048]{1,0:T(8,128)(2,1)S(1)}, bf16[16,2048]{1,0:T(8,128)(2,1)S(1)}, u32[]{:S(2)}, u32[]{:S(2)}) collective-permute-start(bf16[16,2048]{1,0:T(8,128)(2,1)S(1)} %get-tuple-element.15), channel_id=1, source_target_pairs={{0,12},{2,14},{4,0},{6,2},{8,4},{10,6},{12,8},{14,10},{1,13},{3,15... | collective-permute-start | bytes 196616 | tf_op jit(solution)/shard_map/ppermute | solution.py:187
  44.9 19.5 %collective-permute-start.4 = (bf16[16,2048]{1,0:T(8,128)(2,1)S(1)}, bf16[16,2048]{1,0:T(8,128)(2,1)S(1)}, u32[]{:S(2)}, u32[]{:S(2)}) collective-permute-start(bf16[16,2048]{1,0:T(8,128)(2,1)S(1)} %get-tuple-element.16), channel_id=1, source_target_pairs={{0,10},{2,12},{4,14},{6,0},{8,2},{10,4},{12,6},{14,8},{1,11},{3,13... | collective-permute-start | bytes 196616 | tf_op jit(solution)/shard_map/ppermute | solution.py:187
  45.0 19.4 %collective-permute-start.3 = (bf16[16,2048]{1,0:T(8,128)(2,1)S(1)}, bf16[16,2048]{1,0:T(8,128)(2,1)S(1)}, u32[]{:S(2)}, u32[]{:S(2)}) collective-permute-start(bf16[16,2048]{1,0:T(8,128)(2,1)S(1)} %get-tuple-element.17), channel_id=1, source_target_pairs={{0,8},{2,10},{4,12},{6,14},{8,0},{10,2},{12,4},{14,6},{1,9},{3,11}... | collective-permute-start | bytes 196616 | tf_op jit(solution)/shard_map/ppermute | solution.py:187
  48.2 6.0 %collective-permute-start = (bf16[16,2048]{1,0:T(8,128)(2,1)S(1)}, bf16[16,2048]{1,0:T(8,128)(2,1)S(1)}, u32[]{:S(2)}, u32[]{:S(2)}) collective-permute-start(bf16[16,2048]{1,0:T(8,128)(2,1)S(1)} %get-tuple-element.20), channel_id=1, source_target_pairs={{0,2},{2,4},{4,6},{6,8},{8,10},{10,12},{12,14},{14,0},{1,3},{3,5},... | collective-permute-start | bytes 196616 | tf_op jit(solution)/shard_map/ppermute | solution.py:187
  48.8 15.8 %copy-start.1 = (bf16[7,30,1024]{2,1,0:T(8,128)(2,1)}, bf16[7,30,1024]{2,1,0:T(8,128)(2,1)S(1)}, u32[]{:S(2)}) copy-start(bf16[7,30,1024]{2,1,0:T(8,128)(2,1)S(1)} %bitcast_dynamic-update-slice_fusion.cstr_hbm) | copy-start | bytes 1290244
  54.1 5.2 %collective-permute-start.1 = (bf16[16,2048]{1,0:T(8,128)(2,1)S(1)}, bf16[16,2048]{1,0:T(8,128)(2,1)S(1)}, u32[]{:S(2)}, u32[]{:S(2)}) collective-permute-start(bf16[16,2048]{1,0:T(8,128)(2,1)S(1)} %get-tuple-element.19), channel_id=1, source_target_pairs={{0,4},{2,6},{4,8},{6,10},{8,12},{10,14},{12,0},{14,2},{1,5},{3,7},... | collective-permute-start | bytes 196616 | tf_op jit(solution)/shard_map/ppermute | solution.py:187
  59.3 5.1 %collective-permute-start.2 = (bf16[16,2048]{1,0:T(8,128)(2,1)S(1)}, bf16[16,2048]{1,0:T(8,128)(2,1)S(1)}, u32[]{:S(2)}, u32[]{:S(2)}) collective-permute-start(bf16[16,2048]{1,0:T(8,128)(2,1)S(1)} %get-tuple-element.18), channel_id=1, source_target_pairs={{0,6},{2,8},{4,10},{6,12},{8,14},{10,0},{12,2},{14,4},{1,7},{3,9},... | collective-permute-start | bytes 196616 | tf_op jit(solution)/shard_map/ppermute | solution.py:187
  64.5 0.8 copy-start.2
  95.3 10.9 %collective-permute-start.14 = (bf16[16,16,1024]{2,1,0:T(8,128)(2,1)}, bf16[16,16,1024]{2,1,0:T(8,128)(2,1)S(1)}, u32[]{:S(2)}, u32[]{:S(2)}) collective-permute-start(bf16[16,16,1024]{2,1,0:T(8,128)(2,1)} %bitcast.85), channel_id=1, source_target_pairs={{0,1},{2,3},{4,5},{6,7},{8,9},{10,11},{12,13},{14,15},{16,17},{18,... | collective-permute-start | bytes 1572872 | tf_op jit(solution)/shard_map/ppermute | solution.py:17
  106.1 0.8 copy-start.4
  106.9 30.0 %copy-start.3 = (bf16[256,1024]{1,0:T(8,128)(2,1)S(1)}, bf16[256,1024]{1,0:T(8,128)(2,1)}, u32[]{:S(2)}) copy-start(bf16[256,1024]{1,0:T(8,128)(2,1)} %shard_map.82) | copy-start | bytes 1572868

commit v3 on v2

--- a/solution.py
+++ b/solution.py
@@ -8,7 +8,8 @@
 from jax.sharding import PartitionSpec as P
 
 HEADS = 16
-GROUP = 8
+GROUP = 16
+CHUNK_ROWS = 128
 
 
 def shifted(value, axis, steps):
@@ -18,46 +19,89 @@
 
 
 def layer_kernel(sel_ref, x_ref, klive_ref, rlive_ref, cw_ref, wqkv_hbm, wo_hbm, ctxl_hbm,
-                 ctxr_hbm, cstl_hbm, cstr_hbm, out_ref, wbuf, ctxv, cstv, qkv, acc_ref, pad_ref,
-                 wsem, gsem, *, streams, frames, ctx, head_size):
+                 ctxr_hbm, cstl_hbm, cstr_hbm, out_ref, wbuf, wobuf, ctxv, cstv, qkv, conv_ref,
+                 pad_ref, res_ref, wsem, gsem, *, streams, frames, ctx, head_size):
     tokens = streams * frames
     width = x_ref.shape[1]
     slot = ctxv.shape[0] // streams
-    copies = [
-        pltpu.make_async_copy(wqkv_hbm.at[:, pl.ds(i * width, width)], wbuf.at[i], wsem.at[i])
-        for i in range(3)
-    ]
-    copies.append(pltpu.make_async_copy(wo_hbm, wbuf.at[3], wsem.at[3]))
+    kept = cstv.shape[1]
+    lead = pad_ref.shape[1] - frames - kept
+    taps = cw_ref.shape[0]
+    chunk = 128
+
+    def gather(j, which):
+        kind = sel_ref[j]
+        idx = sel_ref[streams + j]
+        if which == 0:
+            dst, local, remote = cstv.at[j], cstl_hbm, cstr_hbm
+        else:
+            dst, local, remote = ctxv.at[pl.ds(slot * j, slot)], ctxl_hbm, ctxr_hbm
+
+        @pl.when(kind == 0)
+        def _():
+            pltpu.make_async_copy(local.at[idx], dst, gsem.at[which, j]).start()
+
+        @pl.when(kind != 0)
+        def _():
+            pltpu.make_async_copy(remote.at[idx], dst, gsem.at[which, j]).start()
+
+    def gather_wait(j, which):
+        if which == 0:
+            pltpu.make_async_copy(cstl_hbm.at[0], cstv.at[j], gsem.at[0, j]).wait()
+        else:
+            pltpu.make_async_copy(ctxl_hbm.at[0], ctxv.at[pl.ds(slot * j, slot)],
+                                  gsem.at[1, j]).wait()
+
+    for j in range(streams):
+        gather(j, 0)
+    for j in range(streams):
+        gather(j, 1)
+    rows_w = wqkv_hbm.shape[0]
+    copies = []
+    for r in range(rows_w // CHUNK_ROWS):
+        part = pl.ds(r * CHUNK_ROWS, CHUNK_ROWS)
+        copies.append(pltpu.make_async_copy(wqkv_hbm.at[part], wbuf.at[part], wsem.at[0, r]))
+    for r in range(rows_w // CHUNK_ROWS):
+        part = pl.ds(r * CHUNK_ROWS, CHUNK_ROWS)
+        copies.append(pltpu.make_async_copy(wo_hbm.at[part], wobuf.at[part], wsem.at[1, r]))
     for c in copies:
         c.start()
-    for j in range(streams):
-        kind = sel_ref[j]
-        idx = sel_ref[streams + j]
-
-        @pl.when(kind == 0)
-        def _():
-            pltpu.make_async_copy(ctxl_hbm.at[idx], ctxv.at[pl.ds(slot * j, slot)],
-                                  gsem.at[0, j]).start()
-            pltpu.make_async_copy(cstl_hbm.at[idx], cstv.at[j], gsem.at[1, j]).start()
-
-        @pl.when(kind != 0)
-        def _():
-            pltpu.make_async_copy(ctxr_hbm.at[idx], ctxv.at[pl.ds(slot * j, slot)],
-                                  gsem.at[0, j]).start()
-            pltpu.make_async_copy(cstr_hbm.at[idx], cstv.at[j], gsem.at[1, j]).start()
 
     floats = x_ref[...].astype(jnp.float32)
     centred = floats - jnp.mean(floats, axis=-1, keepdims=True)
     variance = jnp.mean(centred * centred, axis=-1, keepdims=True)
     normed = (centred * lax.rsqrt(variance + 1e-05)).astype(jnp.bfloat16)
+
+    for j in range(streams):
+        gather_wait(j, 0)
+    pad_ref[:, 0:lead, :] = jnp.zeros((streams, lead, width), jnp.float32)
+    pad_ref[:, lead:lead + kept, :] = cstv[...].astype(jnp.float32)
+    pad_ref[:, lead + kept:, :] = jnp.zeros((streams, frames, width), jnp.float32)
+
+    def conv_taps(first):
+        def conv_chunk(c, carry):
+            cols = pl.ds(pl.multiple_of(c * chunk, chunk), chunk)
+            conv = conv_ref[:, :, cols]
+            for j in range(first, taps):
+                conv = conv + cw_ref[pl.ds(j, 1), cols].reshape(1, 1, chunk) * pad_ref[
+                    :, pl.ds(lead + j, frames), cols]
+            conv_ref[:, :, cols] = conv
+            return carry
+
+        lax.fori_loop(0, width // chunk, conv_chunk, 0)
+
+    conv_ref[...] = jnp.zeros_like(conv_ref)
+    conv_taps(0)
+
+    for c in copies[:rows_w // CHUNK_ROWS]:
+        c.wait()
     for i in range(3):
-        copies[i].wait()
-        part = jnp.dot(normed, wbuf[i], preferred_element_type=jnp.float32)
+        part = jnp.dot(normed, wbuf[:, pl.ds(i * width, width)], preferred_element_type=jnp.float32)
         if i == 0:
             part = part * (head_size ** -0.5)
         qkv[i] = part.astype(jnp.bfloat16)
     for j in range(streams):
-        pltpu.make_async_copy(ctxl_hbm.at[0], ctxv.at[pl.ds(slot * j, slot)], gsem.at[0, j]).wait()
+        gather_wait(j, 1)
 
     rows_g = GROUP * frames
     cols_g = GROUP * slot
@@ -74,6 +118,7 @@
         rows = pl.ds(g * rows_g, rows_g)
         crow = pl.ds(g * cols_g, cols_g)
         bias_n = jnp.where(same_n & (klive_ref[:, pl.ds(g * rows_g, rows_g)] > 0.0), 0.0, -1e30)
+
         def head_pair(p, carry):
             cols = pl.ds(pl.multiple_of(p * pair, pair), pair)
             q = qkv[0, rows, cols]
@@ -102,33 +147,28 @@
 
         lax.fori_loop(0, width // pair, head_pair, 0)
 
-    copies[3].wait()
-    mixed = jnp.dot(qkv[0], wbuf[3], preferred_element_type=jnp.float32)
+    for c in copies[rows_w // CHUNK_ROWS:]:
+        c.wait()
+    mixed = jnp.dot(qkv[0], wobuf[...], preferred_element_type=jnp.float32)
     residual = x_ref[...].astype(jnp.float32) + mixed
-    acc_ref[...] = residual
-    for j in range(streams):
-        pltpu.make_async_copy(cstl_hbm.at[0], cstv.at[j], gsem.at[1, j]).wait()
-    kept = cstv.shape[1]
-    lead = pad_ref.shape[1] - frames - kept
-    rounded = residual.astype(jnp.bfloat16).astype(jnp.float32)
-    pad_ref[:, lead:lead + kept, :] = cstv[...].astype(jnp.float32)
-    pad_ref[:, lead + kept:, :] = rounded.reshape(streams, frames, width)
-    taps = cw_ref.shape[0]
-    chunk = 128
+    res_ref[...] = residual
+    pad_ref[:, lead:lead + kept, :] = jnp.zeros((streams, kept, width), jnp.float32)
+    pad_ref[:, lead + kept:, :] = residual.astype(jnp.bfloat16).astype(jnp.float32).reshape(
+        streams, frames, width)
+    first = taps - frames
+    conv_taps(first)
     live = rlive_ref[...].reshape(streams, frames, 1)
-    def conv_chunk(c, carry):
+
+    def finish(c, carry):
         cols = pl.ds(pl.multiple_of(c * chunk, chunk), chunk)
-        conv = jnp.zeros((streams, frames, chunk), jnp.float32)
-        for j in range(taps):
-            conv = conv + cw_ref[pl.ds(j, 1), cols].reshape(1, 1, chunk) * pad_ref[
-                :, pl.ds(lead + j, frames), cols]
-        res = acc_ref[:, cols].reshape(streams, frames, chunk)
+        conv = conv_ref[:, :, cols]
+        res = res_ref[:, cols]
         silu = conv / (1.0 + jnp.exp(-conv))
-        out = (res + silu) * live
+        out = (res.reshape(streams, frames, chunk) + silu) * live
         out_ref[:, cols] = out.reshape(tokens, chunk).astype(out_ref.dtype)
         return carry
 
-    lax.fori_loop(0, width // chunk, conv_chunk, 0)
+    lax.fori_loop(0, width // chunk, finish, 0)
 
 
 def encoder_layer(inputs, valid_counts, sel, ctx_local, ctx_recv, cst_local, cst_recv,
@@ -154,13 +194,15 @@
                   hbm, hbm, hbm, hbm, hbm, hbm],
         out_specs=vmem,
         scratch_shapes=[
-            pltpu.VMEM((4, width, width), jnp.bfloat16),
+            pltpu.VMEM((width, 3 * width), jnp.bfloat16),
+            pltpu.VMEM((width, width), jnp.bfloat16),
             pltpu.VMEM((streams * slot, 2 * width), jnp.bfloat16),
             pltpu.VMEM((streams, kept, width), jnp.bfloat16),
             pltpu.VMEM((3, tokens, width), jnp.bfloat16),
+            pltpu.VMEM((streams, frames, width), jnp.float32),
+            pltpu.VMEM((streams, lead + kept + frames, width), jnp.float32),
             pltpu.VMEM((tokens, width), jnp.float32),
-            pltpu.VMEM((streams, lead + kept + frames, width), jnp.float32),
-            pltpu.SemaphoreType.DMA((4,)),
+            pltpu.SemaphoreType.DMA((2, width // CHUNK_ROWS)),
             pltpu.SemaphoreType.DMA((2, streams)),
         ],
     )(sel, x, klive, rlive, conv_weight, qkv_weight, out_weight, ctx_local, ctx_recv, cst_local,
@@ -175,24 +217,19 @@
                      axis=1)
     mine_new = lax.dynamic_slice_in_dim(newpos, own * local_count, local_count)
     target = mine_new // local_count
-    shifts = jnp.arange(1, count, dtype=jnp.int32)
-    dest = (own + shifts) % count
-    match = target[None, :] == dest[:, None]
+    hosts = jnp.arange(count, dtype=jnp.int32)
+    match = target[None, :] == hosts[:, None]
     send_slot = jnp.sum(jnp.where(match, jnp.arange(local_count, dtype=jnp.int32)[None, :], 0),
                         axis=1)
-    ctx_recv, cst_recv = [], []
-    for k in range(1, count):
-        perm = [(i, (i + k) % count) for i in range(count)]
-        row = send_slot[k - 1]
-        ctx_recv.append(lax.ppermute(ctx_local[row], "stream", perm))
-        cst_recv.append(lax.ppermute(cst_local[row], "stream", perm))
+    ctx_recv = lax.all_to_all(jnp.take(ctx_local, send_slot, axis=0), "stream", 0, 0, tiled=True)
+    cst_recv = lax.all_to_all(jnp.take(cst_local, send_slot, axis=0), "stream", 0, 0, tiled=True)
     mine_old = lax.dynamic_slice_in_dim(anchor, own * local_count, local_count)
     source = mine_old // local_count
     staying = source == own
     local_idx = jnp.clip(mine_old - own * local_count, 0, local_count - 1)
-    recv_idx = jnp.clip((own - source) % count - 1, 0, count - 2)
+    recv_idx = jnp.clip(source, 0, count - 1)
     sel = jnp.concatenate([jnp.where(staying, 0, 1), jnp.where(staying, local_idx, recv_idx)])
-    return sel.astype(jnp.int32), jnp.stack(ctx_recv), jnp.stack(cst_recv)
+    return sel.astype(jnp.int32), ctx_recv, cst_recv
 
 
 def body(

time: 139 us -> 99.7 us (0.72)
  between operations: 13.3 us -> 0.12 us
  Pallas kernels: 60 us -> 47.7 us
  waiting for transfers between devices: 34.8 us -> 23.1 us
  starting transfers between devices: 15.2 us -> 12.7 us
    ppermute x14 -> x0, waiting for transfers between devices: 25.4 us -> none  [the longest x7 15.6 us: migrate(): ctx_recv.append(lax.ppermute(ctx_local[row], 'stream', perm))]
    all_to_all x0 -> x2, waiting for transfers between devices: none -> 19.7 us  [the longest x1 10.3 us: migrate(): lax.all_to_all(jnp.take(cst_local, send_slot, axis=0), 'stream', 0, 0, ti...]
    ppermute x14 -> x0, starting transfers between devices: 13.7 us -> none  [the longest x7 9 us: migrate(): cst_recv.append(lax.ppermute(cst_local[row], 'stream', perm))]
    pallas_call x2, Pallas kernels: 60 us -> 47.7 us  [encoder_layer(): pl.pallas_call(kernel, out_shape=jax.ShapeDtypeStruct((tokens, width), jn...]
    all_to_all x0 -> x2, starting transfers between devices: none -> 11.3 us  [the longest x1 6.38 us: migrate(): lax.all_to_all(jnp.take(cst_local, send_slot, axis=0), 'stream', 0, 0, ti...]
    ppermute x1, waiting for transfers between devices: 9.39 us -> 3.37 us  [shifted(): lax.ppermute(value, axis, [(source, source + steps) for source in range(l...]
    select_n x1 -> x3, other arithmetic: 0.01 us -> 1.88 us  [the longest x2 0.95 us: migrate(): jnp.take(ctx_local, send_slot, axis=0)]
    unnamed x25 -> x19, local copies, waits for them, and re-layouts: 6.56 us -> 5.62 us
  transfers between devices with their start and end apart: 15 -> 3, of which waited for: 6 -> 3; matrix products, arithmetic and copies ran while one was open for 6% -> 7% of each run, Pallas kernels for 0% -> 0%
where the time goes in v3:
time: 99.7 us; the launch traced here: 99.2 us
  Pallas kernels  47.7 us (48%)
  waiting for transfers between devices  23.1 us (23%)
  starting transfers between devices  12.7 us (13%)
  local copies, waits for them, and re-layouts  9.43 us (9%)
  other arithmetic  6.2 us (6%)
    pallas_call x2, Pallas kernels, encoder_layer(): pl.pallas_call(kernel, out_shape=jax.ShapeDtypeStruct((tokens, width), jn...  47.7 us
    all_to_all x1, waiting for transfers between devices, migrate(): lax.all_to_all(jnp.take(cst_local, send_slot, axis=0), 'stream', 0, 0, ti...  10.3 us
    all_to_all x1, waiting for transfers between devices, migrate(): lax.all_to_all(jnp.take(ctx_local, send_slot, axis=0), 'stream', 0, 0, ti...  9.38 us
    all_to_all x1, starting transfers between devices, migrate(): lax.all_to_all(jnp.take(cst_local, send_slot, axis=0), 'stream', 0, 0, ti...  6.38 us
    unnamed x19, local copies, waits for them, and re-layouts  5.62 us
    all_to_all x1, starting transfers between devices, migrate(): lax.all_to_all(jnp.take(ctx_local, send_slot, axis=0), 'stream', 0, 0, ti...  4.88 us
    ppermute x1, waiting for transfers between devices, shifted(): lax.ppermute(value, axis, [(source, source + steps) for source in range(l...  3.37 us
  transfers between devices with their start and end apart: 3, of which 3 were waited for; matrix products, arithmetic and copies ran while one was open for 7% of the time, Pallas kernels for 0%

profile of v3, /device:TPU:1, one launch (start us, length us, event | category | flops | bytes accessed | tf_op | source)
XLA Modules:
  0.0 99.2 jit_solution(2482559268670316637)
XLA Ops:
  0.0 0.8 select_reduce_fusion
  0.8 0.7 compare_select_fusion.9
  1.6 0.1 select_reduce_fusion.1
  1.7 0.0 copy-start.6
  1.7 1.8 %copy.23 = bf16[1,16,30,1024]{3,2,1,0:T(8,128)(2,1)S(1)} copy(bf16[1,16,30,1024]{3,1,2,0:T(8,128)(2,1)} %param.12) | data formatting | bytes 1966080 | tf_op args[4]
  3.5 0.0 copy-start
  3.5 0.6 gather_fusion.1
  4.1 0.9 broadcast_select_fusion
  5.0 6.4 %all-to-all-start.1 = ((bf16[8,30,1024]{2,1,0:T(8,128)(2,1)}), bf16[8,30,1024]{2,1,0:T(8,128)(2,1)S(1)}, u32[]{:S(2)}, u32[]{:S(2)}) async-start(bf16[8,30,1024]{2,1,0:T(8,128)(2,1)} %broadcast_select_fusion), calls=%async_computation.1 | async-start | bytes 1048576 | tf_op jit(solution)/shard_map/all_to_all | solution.py:225
  11.4 1.6 %copy.24 = bf16[1,16,12,2048]{3,2,1,0:T(8,128)(2,1)S(1)} copy(bf16[1,16,12,2048]{3,1,2,0:T(8,128)(2,1)} %param.11) | data formatting | bytes 1572864 | tf_op args[3]
  13.0 0.6 gather_fusion
  13.5 0.9 pad_select_fusion
  14.5 10.3 %all-to-all-done.1.cstr_hbm = bf16[8,30,1024]{2,1,0:T(8,128)(2,1)S(1)} async-done(((bf16[8,30,1024]{2,1,0:T(8,128)(2,1)}), bf16[8,30,1024]{2,1,0:T(8,128)(2,1)S(1)}, u32[]{:S(2)}, u32[]{:S(2)}) %all-to-all-start.1) | async-done | bytes 491552 | tf_op jit(solution)/shard_map/all_to_all | solution.py:225
  24.8 4.9 %all-to-all-start = ((bf16[8,16,2048]{2,1,0:T(8,128)(2,1)}), bf16[8,16,2048]{2,1,0:T(8,128)(2,1)S(1)}, u32[]{:S(2)}, u32[]{:S(2)}) async-start(bf16[8,16,2048]{2,1,0:T(8,128)(2,1)} %pad_select_fusion), calls=%async_computation | async-start | bytes 1048576 | tf_op jit(solution)/shard_map/all_to_all | solution.py:224
  29.7 0.1 dynamic_slice.10
  29.8 0.1 fusion
  29.8 0.7 reshape.111.klive_ref
  30.5 0.7 reshape.129.rlive_ref
  31.2 0.0 copy-done.5
  31.3 0.7 copy.25
  31.9 1.2 %pad.5.ctxl_hbm = bf16[16,16,2048]{2,1,0:T(8,128)(2,1)} pad(bf16[16,12,2048]{2,1,0:T(8,128)(2,1)S(1)} %bitcast.27, bf16[]{:T(256)} %constant.64.clone.1), padding=0_0x0_4x0_0 | pad | bytes 1835010 | tf_op jit(solution)/shard_map/jit(_pad)/pad | solution.py:243
  33.1 0.1 compare_select_fusion.8
  33.2 0.6 pad_add_fusion.sel_ref
  33.8 9.4 %all-to-all-done.ctxr_hbm = bf16[8,16,2048]{2,1,0:T(8,128)(2,1)S(1)} async-done(((bf16[8,16,2048]{2,1,0:T(8,128)(2,1)}), bf16[8,16,2048]{2,1,0:T(8,128)(2,1)S(1)}, u32[]{:S(2)}, u32[]{:S(2)}) %all-to-all-start) | async-done | bytes 524320 | tf_op jit(solution)/shard_map/all_to_all | solution.py:224
  43.2 0.0 copy-done
  43.2 0.8 copy-done.2
  44.0 23.8 %shard_map.82 = bf16[256,1024]{1,0:T(8,128)(2,1)} custom-call(s32[32]{0:T(128)} %pad_add_fusion.sel_ref, bf16[256,1024]{1,0:T(8,128)(2,1)} %bitcast.31, f32[1,256]{1,0:T(1,128)} %reshape.111.klive_ref, f32[256,1]{1,0:T(8,128)} %reshape.129.rlive_ref, f32[31,1024]{1,0:T(8,128)} %bitcast.29, bf16[1024,3072]{1,0:T(8,128)(2,1)} %bitcast.19, ...), custom_call_target="tpu_custom_call" | custom-call | tf_op jit(solution)/shard_map/pallas_call | solution.py:190
  67.8 1.5 %collective-permute-start = (bf16[16,16,1024]{2,1,0:T(8,128)(2,1)}, bf16[16,16,1024]{2,1,0:T(8,128)(2,1)S(1)}, u32[]{:S(2)}, u32[]{:S(2)}) collective-permute-start(bf16[16,16,1024]{2,1,0:T(8,128)(2,1)} %bitcast.28), channel_id=1, source_target_pairs={{0,1},{2,3},{4,5},{6,7},{8,9},{10,11},{12,13},{14,15},{16,17},{18,... | collective-permute-start | bytes 1572872 | tf_op jit(solution)/shard_map/ppermute | solution.py:18
  69.3 3.4 %collective-permute-done = bf16[16,16,1024]{2,1,0:T(8,128)(2,1)S(1)} collective-permute-done((bf16[16,16,1024]{2,1,0:T(8,128)(2,1)}, bf16[16,16,1024]{2,1,0:T(8,128)(2,1)S(1)}, u32[]{:S(2)}, u32[]{:S(2)}) %collective-permute-start) | collective-permute-done | bytes 524320 | tf_op jit(solution)/shard_map/ppermute | solution.py:18
  72.6 0.8 copy-done.4
  73.4 23.9 %shard_map.83 = bf16[256,1024]{1,0:T(8,128)(2,1)} custom-call(s32[32]{0:T(128)} %pad_add_fusion.sel_ref, bf16[256,1024]{1,0:T(8,128)(2,1)} %bitcast.32, f32[1,256]{1,0:T(1,128)} %reshape.111.klive_ref, f32[256,1]{1,0:T(8,128)} %reshape.129.rlive_ref, f32[31,1024]{1,0:T(8,128)} %bitcast.30, bf16[1024,3072]{1,0:T(8,128)(2,1)} %bitcast.20, ...), custom_call_target="tpu_custom_call" | custom-call | tf_op jit(solution)/shard_map/pallas_call | solution.py:190
  97.3 1.9 %broadcast_select_fusion.1 = bf16[256,1024]{1,0:T(8,128)(2,1)} fusion(bf16[256,1024]{1,0:T(8,128)(2,1)S(1)} %copy-done.3, bf16[256,1024]{1,0:T(8,128)(2,1)} %shard_map.83, pred[]{:T(512)S(6)} %eq.35), kind=kLoop, calls=%fused_computation.6 | loop fusion | flops 262144 | bytes 1572865 | tf_op jit(solution)/shard_map/jit(_where)/select_n | solution.py:255
  (13 shorter events, 0.0 us)
Async XLA Ops:
  0.0 29.7 %copy-start.7 = (s32[128]{0:T(128)S(1)}, s32[128]{0:T(128)}, u32[]{:S(2)}) copy-start(s32[128]{0:T(128)} %param.9) | copy-start | bytes 1540
  0.0 31.2 %copy-start.5 = (f32[1,31,1024]{2,0,1:T(1,128)S(1)}, f32[1,31,1024]{2,0,1:T(1,128)}, u32[]{:S(2)}) copy-start(f32[1,31,1024]{2,0,1:T(1,128)} %param.15) | copy-start | bytes 380932
  1.7 31.4 %copy-start.6 = (s32[128]{0:T(128)S(1)}, s32[128]{0:T(128)}, u32[]{:S(2)}) copy-start(s32[128]{0:T(128)} %param.10) | copy-start | bytes 1540
  3.5 39.7 %copy-start = (bf16[1,16,30,1024]{3,2,1,0:T(8,128)(2,1)}, bf16[1,16,30,1024]{3,2,1,0:T(8,128)(2,1)S(1)}, u32[]{:S(2)}) copy-start(bf16[1,16,30,1024]{3,2,1,0:T(8,128)(2,1)S(1)} %copy.23) | copy-start | bytes 2949124
  5.0 19.8 %all-to-all-start.1 = ((bf16[8,30,1024]{2,1,0:T(8,128)(2,1)}), bf16[8,30,1024]{2,1,0:T(8,128)(2,1)S(1)}, u32[]{:S(2)}, u32[]{:S(2)}) async-start(bf16[8,30,1024]{2,1,0:T(8,128)(2,1)} %broadcast_select_fusion), calls=%async_computation.1 | async-start | bytes 1048576 | tf_op jit(solution)/shard_map/all_to_all | solution.py:225
  24.8 18.4 %copy-start.1 = (bf16[8,30,1024]{2,1,0:T(8,128)(2,1)}, bf16[8,30,1024]{2,1,0:T(8,128)(2,1)S(1)}, u32[]{:S(2)}) copy-start(bf16[8,30,1024]{2,1,0:T(8,128)(2,1)S(1)} %all-to-all-done.1.cstr_hbm) | copy-start | bytes 1474564
  24.8 18.4 %all-to-all-start = ((bf16[8,16,2048]{2,1,0:T(8,128)(2,1)}), bf16[8,16,2048]{2,1,0:T(8,128)(2,1)S(1)}, u32[]{:S(2)}, u32[]{:S(2)}) async-start(bf16[8,16,2048]{2,1,0:T(8,128)(2,1)} %pad_select_fusion), calls=%async_computation | async-start | bytes 1048576 | tf_op jit(solution)/shard_map/all_to_all | solution.py:224
  43.2 0.8 copy-start.2
  67.8 4.9 %collective-permute-start = (bf16[16,16,1024]{2,1,0:T(8,128)(2,1)}, bf16[16,16,1024]{2,1,0:T(8,128)(2,1)S(1)}, u32[]{:S(2)}, u32[]{:S(2)}) collective-permute-start(bf16[16,16,1024]{2,1,0:T(8,128)(2,1)} %bitcast.28), channel_id=1, source_target_pairs={{0,1},{2,3},{4,5},{6,7},{8,9},{10,11},{12,13},{14,15},{16,17},{18,... | collective-permute-start | bytes 1572872 | tf_op jit(solution)/shard_map/ppermute | solution.py:18
  72.6 0.8 copy-start.4
  73.4 23.9 %copy-start.3 = (bf16[256,1024]{1,0:T(8,128)(2,1)S(1)}, bf16[256,1024]{1,0:T(8,128)(2,1)}, u32[]{:S(2)}) copy-start(bf16[256,1024]{1,0:T(8,128)(2,1)} %shard_map.82) | copy-start | bytes 1572868

commit v4 on v3

--- a/solution.py
+++ b/solution.py
@@ -18,44 +18,28 @@
     return lax.ppermute(value, axis, [(source, source + steps) for source in range(leading, last)])
 
 
-def layer_kernel(sel_ref, x_ref, klive_ref, rlive_ref, cw_ref, wqkv_hbm, wo_hbm, ctxl_hbm,
-                 ctxr_hbm, cstl_hbm, cstr_hbm, out_ref, wbuf, wobuf, ctxv, cstv, qkv, conv_ref,
-                 pad_ref, res_ref, wsem, gsem, *, streams, frames, ctx, head_size):
+def layer_kernel(sel_ref, x_ref, klive_ref, rlive_ref, cw_ref, wqkv_hbm, wo_hbm, state_hbm,
+                 recv_hbm, out_ref, wbuf, wobuf, stv, qkv, conv_ref, pad_ref, res_ref, wsem, gsem,
+                 *, streams, frames, ctx, head_size):
     tokens = streams * frames
     width = x_ref.shape[1]
-    slot = ctxv.shape[0] // streams
-    kept = cstv.shape[1]
-    lead = pad_ref.shape[1] - frames - kept
+    slot = -(-ctx // 16) * 16
+    kept = pad_ref.shape[1] - frames
     taps = cw_ref.shape[0]
     chunk = 128
 
-    def gather(j, which):
+    for j in range(streams):
         kind = sel_ref[j]
         idx = sel_ref[streams + j]
-        if which == 0:
-            dst, local, remote = cstv.at[j], cstl_hbm, cstr_hbm
-        else:
-            dst, local, remote = ctxv.at[pl.ds(slot * j, slot)], ctxl_hbm, ctxr_hbm
 
         @pl.when(kind == 0)
         def _():
-            pltpu.make_async_copy(local.at[idx], dst, gsem.at[which, j]).start()
+            pltpu.make_async_copy(state_hbm.at[idx], stv.at[j], gsem.at[j]).start()
 
         @pl.when(kind != 0)
         def _():
-            pltpu.make_async_copy(remote.at[idx], dst, gsem.at[which, j]).start()
-
-    def gather_wait(j, which):
-        if which == 0:
-            pltpu.make_async_copy(cstl_hbm.at[0], cstv.at[j], gsem.at[0, j]).wait()
-        else:
-            pltpu.make_async_copy(ctxl_hbm.at[0], ctxv.at[pl.ds(slot * j, slot)],
-                                  gsem.at[1, j]).wait()
-
-    for j in range(streams):
-        gather(j, 0)
-    for j in range(streams):
-        gather(j, 1)
+            pltpu.make_async_copy(recv_hbm.at[idx], stv.at[j], gsem.at[j]).start()
+
     rows_w = wqkv_hbm.shape[0]
     copies = []
     for r in range(rows_w // CHUNK_ROWS):
@@ -73,10 +57,9 @@
     normed = (centred * lax.rsqrt(variance + 1e-05)).astype(jnp.bfloat16)
 
     for j in range(streams):
-        gather_wait(j, 0)
-    pad_ref[:, 0:lead, :] = jnp.zeros((streams, lead, width), jnp.float32)
-    pad_ref[:, lead:lead + kept, :] = cstv[...].astype(jnp.float32)
-    pad_ref[:, lead + kept:, :] = jnp.zeros((streams, frames, width), jnp.float32)
+        pltpu.make_async_copy(state_hbm.at[0], stv.at[j], gsem.at[j]).wait()
+    pad_ref[:, 0:kept, :] = stv[:, pl.ds(2 * slot, kept), :].astype(jnp.float32)
+    pad_ref[:, kept:, :] = jnp.zeros((streams, frames, width), jnp.float32)
 
     def conv_taps(first):
         def conv_chunk(c, carry):
@@ -84,7 +67,7 @@
             conv = conv_ref[:, :, cols]
             for j in range(first, taps):
                 conv = conv + cw_ref[pl.ds(j, 1), cols].reshape(1, 1, chunk) * pad_ref[
-                    :, pl.ds(lead + j, frames), cols]
+                    :, pl.ds(kept - taps + 1 + j, frames), cols]
             conv_ref[:, :, cols] = conv
             return carry
 
@@ -100,8 +83,6 @@
         if i == 0:
             part = part * (head_size ** -0.5)
         qkv[i] = part.astype(jnp.bfloat16)
-    for j in range(streams):
-        gather_wait(j, 1)
 
     rows_g = GROUP * frames
     cols_g = GROUP * slot
@@ -116,7 +97,7 @@
     nt = (((1,), (1,)), ((), ()))
     for g in range(streams // GROUP):
         rows = pl.ds(g * rows_g, rows_g)
-        crow = pl.ds(g * cols_g, cols_g)
+        srow = pl.ds(g * GROUP, GROUP)
         bias_n = jnp.where(same_n & (klive_ref[:, pl.ds(g * rows_g, rows_g)] > 0.0), 0.0, -1e30)
 
         def head_pair(p, carry):
@@ -124,8 +105,8 @@
             q = qkv[0, rows, cols]
             k = qkv[1, rows, cols]
             v = qkv[2, rows, cols]
-            ck = ctxv[crow, cols]
-            cv = ctxv[crow, pl.ds(pl.multiple_of(width + p * pair, pair), pair)]
+            ck = stv[srow, pl.ds(0, slot), cols].reshape(cols_g, pair)
+            cv = stv[srow, pl.ds(slot, slot), cols].reshape(cols_g, pair)
             attended = None
             for half in range(pair // head_size):
                 mine = (lane >= half * head_size) & (lane < (half + 1) * head_size)
@@ -152,8 +133,8 @@
     mixed = jnp.dot(qkv[0], wobuf[...], preferred_element_type=jnp.float32)
     residual = x_ref[...].astype(jnp.float32) + mixed
     res_ref[...] = residual
-    pad_ref[:, lead:lead + kept, :] = jnp.zeros((streams, kept, width), jnp.float32)
-    pad_ref[:, lead + kept:, :] = residual.astype(jnp.bfloat16).astype(jnp.float32).reshape(
+    pad_ref[:, 0:kept, :] = jnp.zeros((streams, kept, width), jnp.float32)
+    pad_ref[:, kept:, :] = residual.astype(jnp.bfloat16).astype(jnp.float32).reshape(
         streams, frames, width)
     first = taps - frames
     conv_taps(first)
@@ -171,10 +152,10 @@
     lax.fori_loop(0, width // chunk, finish, 0)
 
 
-def encoder_layer(inputs, valid_counts, sel, ctx_local, ctx_recv, cst_local, cst_recv,
-                  qkv_weight, out_weight, conv_weight, ctx):
+def encoder_layer(inputs, valid_counts, sel, state, recv, qkv_weight, out_weight, conv_weight,
+                  ctx):
     streams, frames, width = inputs.shape
-    kept = cst_local.shape[1]
+    taps = conv_weight.shape[0]
     head_size = width // HEADS
     tokens = streams * frames
     slot = -(-ctx // 16) * 16
@@ -182,7 +163,7 @@
     klive = live.reshape(1, tokens)
     rlive = live.reshape(tokens, 1)
     x = inputs.reshape(tokens, width)
-    lead = (-(kept + frames)) % 8
+    kept = state.shape[1] - 2 * slot
     kernel = functools.partial(layer_kernel, streams=streams, frames=frames, ctx=ctx,
                                head_size=head_size)
     vmem = pl.BlockSpec(memory_space=pltpu.VMEM)
@@ -191,26 +172,24 @@
         kernel,
         out_shape=jax.ShapeDtypeStruct((tokens, width), jnp.bfloat16),
         in_specs=[pl.BlockSpec(memory_space=pltpu.SMEM), vmem, vmem, vmem, vmem,
-                  hbm, hbm, hbm, hbm, hbm, hbm],
+                  hbm, hbm, hbm, hbm],
         out_specs=vmem,
         scratch_shapes=[
             pltpu.VMEM((width, 3 * width), jnp.bfloat16),
             pltpu.VMEM((width, width), jnp.bfloat16),
-            pltpu.VMEM((streams * slot, 2 * width), jnp.bfloat16),
-            pltpu.VMEM((streams, kept, width), jnp.bfloat16),
+            pltpu.VMEM((streams,) + state.shape[1:], jnp.bfloat16),
             pltpu.VMEM((3, tokens, width), jnp.bfloat16),
             pltpu.VMEM((streams, frames, width), jnp.float32),
-            pltpu.VMEM((streams, lead + kept + frames, width), jnp.float32),
+            pltpu.VMEM((streams, kept + frames, width), jnp.float32),
             pltpu.VMEM((tokens, width), jnp.float32),
             pltpu.SemaphoreType.DMA((2, width // CHUNK_ROWS)),
-            pltpu.SemaphoreType.DMA((2, streams)),
+            pltpu.SemaphoreType.DMA((streams,)),
         ],
-    )(sel, x, klive, rlive, conv_weight, qkv_weight, out_weight, ctx_local, ctx_recv, cst_local,
-      cst_recv)
+    )(sel, x, klive, rlive, conv_weight, qkv_weight, out_weight, state, recv)
     return out.reshape(streams, frames, width)
 
 
-def migrate(anchor, own, count, local_count, ctx_local, cst_local):
+def migrate(anchor, own, count, local_count, state):
     total = anchor.shape[0]
     every_slot = jnp.arange(total, dtype=jnp.int32)
     newpos = jnp.sum(jnp.where(anchor[None, :] == every_slot[:, None], every_slot[None, :], 0),
@@ -221,15 +200,14 @@
     match = target[None, :] == hosts[:, None]
     send_slot = jnp.sum(jnp.where(match, jnp.arange(local_count, dtype=jnp.int32)[None, :], 0),
                         axis=1)
-    ctx_recv = lax.all_to_all(jnp.take(ctx_local, send_slot, axis=0), "stream", 0, 0, tiled=True)
-    cst_recv = lax.all_to_all(jnp.take(cst_local, send_slot, axis=0), "stream", 0, 0, tiled=True)
+    recv = lax.all_to_all(jnp.take(state, send_slot, axis=0), "stream", 0, 0, tiled=True)
     mine_old = lax.dynamic_slice_in_dim(anchor, own * local_count, local_count)
     source = mine_old // local_count
     staying = source == own
     local_idx = jnp.clip(mine_old - own * local_count, 0, local_count - 1)
     recv_idx = jnp.clip(source, 0, count - 1)
     sel = jnp.concatenate([jnp.where(staying, 0, 1), jnp.where(staying, local_idx, recv_idx)])
-    return sel.astype(jnp.int32), ctx_recv, cst_recv
+    return sel.astype(jnp.int32), recv
 
 
 def body(
@@ -239,15 +217,21 @@
     own = lax.axis_index("stream")
     count = lax.axis_size("stream")
     ctx = context_cache.shape[2]
+    width = conv_state.shape[3]
     slot = -(-ctx // 16) * 16
-    ctx_local = jnp.pad(context_cache[0], ((0, 0), (0, slot - ctx), (0, 0)))
-    cst_local = conv_state[0]
-    sel, ctx_recv, cst_recv = migrate(anchor, own, count, local_count, ctx_local, cst_local)
+    kept = conv_state.shape[2]
+    lead = (-kept) % 16
+    context = context_cache[0]
+    state = jnp.concatenate([
+        jnp.pad(context[:, :, :width], ((0, 0), (0, slot - ctx), (0, 0))),
+        jnp.pad(context[:, :, width:], ((0, 0), (0, slot - ctx), (0, 0))),
+        jnp.pad(conv_state[0], ((0, 0), (lead, 0), (0, 0))),
+    ], axis=1)
+    sel, recv = migrate(anchor, own, count, local_count, state)
     valid_here = lax.dynamic_slice_in_dim(valid_counts, own * local_count, local_count)
     section_index = lax.axis_index("section")
-    layer = functools.partial(encoder_layer, valid_counts=valid_here, sel=sel, ctx_local=ctx_local,
-                              ctx_recv=ctx_recv, cst_local=cst_local, cst_recv=cst_recv,
-                              qkv_weight=qkv_weight[0], out_weight=out_weight[0],
+    layer = functools.partial(encoder_layer, valid_counts=valid_here, sel=sel, state=state,
+                              recv=recv, qkv_weight=qkv_weight[0], out_weight=out_weight[0],
                               conv_weight=conv_weight[0], ctx=ctx)
     first = layer(new_frames)
     inbound = shifted(first, "section", 1)

time: 99.7 us -> 98.8 us (level)
  starting transfers between devices: 12.7 us -> 7.68 us
  Pallas kernels: 47.7 us -> 52.5 us
  local copies, waits for them, and re-layouts: 9.43 us -> 6.79 us
  waiting for transfers between devices: 23.1 us -> 25.3 us
    all_to_all x2 -> x1, starting transfers between devices: 11.3 us -> 6.38 us  [migrate(): lax.all_to_all(jnp.take(state, send_slot, axis=0), 'stream', 0, 0, tiled=...]
    pallas_call x2, Pallas kernels: 47.7 us -> 52.5 us  [encoder_layer(): pl.pallas_call(kernel, out_shape=jax.ShapeDtypeStruct((tokens, width), jn...]
    all_to_all x2 -> x1, waiting for transfers between devices: 19.7 us -> 21.6 us  [migrate(): lax.all_to_all(jnp.take(state, send_slot, axis=0), 'stream', 0, 0, tiled=...]
    pad x1 -> x0, local copies, waits for them, and re-layouts: 1.17 us -> none  [body(): ctx_local = jnp.pad(context_cache[0], ((0, 0), (0, slot - ctx), (0, 0)))]
    unnamed x19, local copies, waits for them, and re-layouts: 5.62 us -> 4.6 us
  transfers between devices with their start and end apart: 3 -> 2, of which waited for: 3 -> 2; matrix products, arithmetic and copies ran while one was open for 7% -> 3% of each run, Pallas kernels for 0% -> 0%
where the time goes in v4:
time: 98.8 us; the launch traced here: 98.5 us
  Pallas kernels  52.5 us (53%)
  waiting for transfers between devices  25.3 us (26%)
  starting transfers between devices  7.68 us (8%)
  local copies, waits for them, and re-layouts  6.79 us (7%)
  other arithmetic  6.07 us (6%)
    pallas_call x2, Pallas kernels, encoder_layer(): pl.pallas_call(kernel, out_shape=jax.ShapeDtypeStruct((tokens, width), jn...  52.5 us
    all_to_all x1, waiting for transfers between devices, migrate(): lax.all_to_all(jnp.take(state, send_slot, axis=0), 'stream', 0, 0, tiled=...  21.6 us
    all_to_all x1, starting transfers between devices, migrate(): lax.all_to_all(jnp.take(state, send_slot, axis=0), 'stream', 0, 0, tiled=...  6.38 us
    unnamed x19, local copies, waits for them, and re-layouts  4.6 us
    ppermute x1, waiting for transfers between devices, shifted(): lax.ppermute(value, axis, [(source, source + steps) for source in range(l...  3.7 us
  transfers between devices with their start and end apart: 2, of which 2 were waited for; matrix products, arithmetic and copies ran while one was open for 3% of the time, Pallas kernels for 0%

profile of v4, /device:TPU:1, one launch (start us, length us, event | category | flops | bytes accessed | tf_op | source)
XLA Modules:
  0.0 98.5 jit_solution(4557678597840677073)
XLA Ops:
  0.0 0.8 select_reduce_fusion
  0.8 0.7 compare_select_fusion.9
  1.6 0.1 select_reduce_fusion.1
  1.7 1.6 %copy.24 = bf16[1,16,12,2048]{3,2,1,0:T(8,128)(2,1)S(1)} copy(bf16[1,16,12,2048]{3,1,2,0:T(8,128)(2,1)} %param.11) | data formatting | bytes 1572864 | tf_op args[3]
  3.3 0.1 fusion.8
  3.4 0.0 copy-done.3
  3.4 0.5 copy.23
  4.0 0.5 fusion.5.state_hbm
  4.5 0.0 copy-start
  4.5 0.0 copy-start.7
  4.5 0.0 copy-start.5
  4.5 0.0 copy-start.6
  4.5 0.6 gather_fusion
  5.2 1.2 %broadcast_select_fusion = bf16[8,64,1024]{2,1,0:T(8,128)(2,1)} fusion(bf16[8,64,1024]{2,1,0:T(8,128)(2,1)S(1)} %gather_fusion, pred[8]{0:T(512)(128)(4,1)S(1)} %compare_and_fusion), kind=kLoop, calls=%fused_computation.13 | loop fusion | flops 524288 | bytes 2097160 | tf_op jit(solution)/shard_map/jit(_take)/select_n | solution.py:203
  6.3 6.4 %all-to-all-start = ((bf16[8,64,1024]{2,1,0:T(8,128)(2,1)}), bf16[8,64,1024]{2,1,0:T(8,128)(2,1)S(1)}, u32[]{:S(2)}, u32[]{:S(2)}) async-start(bf16[8,64,1024]{2,1,0:T(8,128)(2,1)} %broadcast_select_fusion), calls=%async_computation | async-start | bytes 2097152 | tf_op jit(solution)/shard_map/all_to_all | solution.py:203
  12.7 0.1 dynamic_slice.10
  12.8 0.1 fusion.6
  12.9 0.7 reshape.111.klive_ref
  13.5 0.7 reshape.121.rlive_ref
  14.3 0.7 copy.25
  14.9 0.0 copy-done.6
  14.9 0.1 compare_select_fusion.8
  15.0 0.7 pad_add_fusion.sel_ref
  15.7 21.6 %all-to-all-done.recv_hbm = bf16[8,64,1024]{2,1,0:T(8,128)(2,1)S(1)} async-done(((bf16[8,64,1024]{2,1,0:T(8,128)(2,1)}), bf16[8,64,1024]{2,1,0:T(8,128)(2,1)S(1)}, u32[]{:S(2)}, u32[]{:S(2)}) %all-to-all-start) | async-done | bytes 1048608 | tf_op jit(solution)/shard_map/all_to_all | solution.py:203
  37.3 0.0 copy-done
  37.3 1.0 copy-done.1
  38.3 26.2 %shard_map.82 = bf16[256,1024]{1,0:T(8,128)(2,1)} custom-call(s32[32]{0:T(128)} %pad_add_fusion.sel_ref, bf16[256,1024]{1,0:T(8,128)(2,1)} %bitcast.28, f32[1,256]{1,0:T(1,128)} %reshape.111.klive_ref, f32[256,1]{1,0:T(8,128)} %reshape.121.rlive_ref, f32[31,1024]{1,0:T(8,128)} %bitcast.26, bf16[1024,3072]{1,0:T(8,128)(2,1)} %bitcast.19, ...), custom_call_target="tpu_custom_call" | custom-call | tf_op jit(solution)/shard_map/pallas_call | solution.py:171
  64.5 1.3 %collective-permute-start = (bf16[16,16,1024]{2,1,0:T(8,128)(2,1)}, bf16[16,16,1024]{2,1,0:T(8,128)(2,1)S(1)}, u32[]{:S(2)}, u32[]{:S(2)}) collective-permute-start(bf16[16,16,1024]{2,1,0:T(8,128)(2,1)} %bitcast.25), channel_id=1, source_target_pairs={{0,1},{2,3},{4,5},{6,7},{8,9},{10,11},{12,13},{14,15},{16,17},{18,... | collective-permute-start | bytes 1572872 | tf_op jit(solution)/shard_map/ppermute | solution.py:18
  65.8 3.7 %collective-permute-done = bf16[16,16,1024]{2,1,0:T(8,128)(2,1)S(1)} collective-permute-done((bf16[16,16,1024]{2,1,0:T(8,128)(2,1)}, bf16[16,16,1024]{2,1,0:T(8,128)(2,1)S(1)}, u32[]{:S(2)}, u32[]{:S(2)}) %collective-permute-start) | collective-permute-done | bytes 524320 | tf_op jit(solution)/shard_map/ppermute | solution.py:18
  69.5 0.8 copy-done.4
  70.3 26.3 %shard_map.83 = bf16[256,1024]{1,0:T(8,128)(2,1)} custom-call(s32[32]{0:T(128)} %pad_add_fusion.sel_ref, bf16[256,1024]{1,0:T(8,128)(2,1)} %bitcast.29, f32[1,256]{1,0:T(1,128)} %reshape.111.klive_ref, f32[256,1]{1,0:T(8,128)} %reshape.121.rlive_ref, f32[31,1024]{1,0:T(8,128)} %bitcast.27, bf16[1024,3072]{1,0:T(8,128)(2,1)} %bitcast.20, ...), custom_call_target="tpu_custom_call" | custom-call | tf_op jit(solution)/shard_map/pallas_call | solution.py:171
  96.6 1.9 %broadcast_select_fusion.1 = bf16[256,1024]{1,0:T(8,128)(2,1)} fusion(bf16[256,1024]{1,0:T(8,128)(2,1)S(1)} %copy-done.2, bf16[256,1024]{1,0:T(8,128)(2,1)} %shard_map.83, pred[]{:T(512)S(6)} %eq.35), kind=kLoop, calls=%fused_computation.14 | loop fusion | flops 262144 | bytes 1572865 | tf_op jit(solution)/shard_map/jit(_where)/select_n | solution.py:239
  (10 shorter events, 0.0 us)
Async XLA Ops:
  0.0 3.4 %copy-start.3 = (bf16[1,16,30,1024]{3,1,2,0:T(8,128)(2,1)S(1)}, bf16[1,16,30,1024]{3,1,2,0:T(8,128)(2,1)}, u32[]{:S(2)}) copy-start(bf16[1,16,30,1024]{3,1,2,0:T(8,128)(2,1)} %param.12) | copy-start | bytes 2949124
  4.5 32.8 %copy-start = (bf16[16,64,1024]{2,1,0:T(8,128)(2,1)}, bf16[16,64,1024]{2,1,0:T(8,128)(2,1)S(1)}, u32[]{:S(2)}) copy-start(bf16[16,64,1024]{2,1,0:T(8,128)(2,1)S(1)} %fusion.5.state_hbm) | copy-start | bytes 6291460
  4.5 8.2 %copy-start.7 = (s32[128]{0:T(128)S(1)}, s32[128]{0:T(128)}, u32[]{:S(2)}) copy-start(s32[128]{0:T(128)} %param.9) | copy-start | bytes 1540
  4.5 9.8 %copy-start.5 = (f32[1,31,1024]{2,0,1:T(1,128)S(1)}, f32[1,31,1024]{2,0,1:T(1,128)}, u32[]{:S(2)}) copy-start(f32[1,31,1024]{2,0,1:T(1,128)} %param.15) | copy-start | bytes 380932
  4.5 10.4 %copy-start.6 = (s32[128]{0:T(128)S(1)}, s32[128]{0:T(128)}, u32[]{:S(2)}) copy-start(s32[128]{0:T(128)} %param.10) | copy-start | bytes 1540
  6.3 31.0 %all-to-all-start = ((bf16[8,64,1024]{2,1,0:T(8,128)(2,1)}), bf16[8,64,1024]{2,1,0:T(8,128)(2,1)S(1)}, u32[]{:S(2)}, u32[]{:S(2)}) async-start(bf16[8,64,1024]{2,1,0:T(8,128)(2,1)} %broadcast_select_fusion), calls=%async_computation | async-start | bytes 2097152 | tf_op jit(solution)/shard_map/all_to_all | solution.py:203
  37.3 1.0 %copy-start.1 = (bf16[8,64,1024]{2,1,0:T(8,128)(2,1)}, bf16[8,64,1024]{2,1,0:T(8,128)(2,1)S(1)}, u32[]{:S(2)}) copy-start(bf16[8,64,1024]{2,1,0:T(8,128)(2,1)S(1)} %all-to-all-done.recv_hbm) | copy-start | bytes 3145732
  64.5 5.0 %collective-permute-start = (bf16[16,16,1024]{2,1,0:T(8,128)(2,1)}, bf16[16,16,1024]{2,1,0:T(8,128)(2,1)S(1)}, u32[]{:S(2)}, u32[]{:S(2)}) collective-permute-start(bf16[16,16,1024]{2,1,0:T(8,128)(2,1)} %bitcast.25), channel_id=1, source_target_pairs={{0,1},{2,3},{4,5},{6,7},{8,9},{10,11},{12,13},{14,15},{16,17},{18,... | collective-permute-start | bytes 1572872 | tf_op jit(solution)/shard_map/ppermute | solution.py:18
  69.5 0.8 copy-start.4
  70.3 26.3 %copy-start.2 = (bf16[256,1024]{1,0:T(8,128)(2,1)S(1)}, bf16[256,1024]{1,0:T(8,128)(2,1)}, u32[]{:S(2)}) copy-start(bf16[256,1024]{1,0:T(8,128)(2,1)} %shard_map.82) | copy-start | bytes 1572868

commit v5 on v4

--- a/solution.py
+++ b/solution.py
@@ -18,8 +18,23 @@
     return lax.ppermute(value, axis, [(source, source + steps) for source in range(leading, last)])
 
 
-def layer_kernel(sel_ref, x_ref, klive_ref, rlive_ref, cw_ref, wqkv_hbm, wo_hbm, state_hbm,
-                 recv_hbm, out_ref, wbuf, wobuf, stv, qkv, conv_ref, pad_ref, res_ref, wsem, gsem,
+def projection_kernel(x_ref, w_ref, out_ref, nrm_ref, *, head_size):
+    step = pl.program_id(0)
+
+    @pl.when(step == 0)
+    def _():
+        floats = x_ref[...].astype(jnp.float32)
+        centred = floats - jnp.mean(floats, axis=-1, keepdims=True)
+        variance = jnp.mean(centred * centred, axis=-1, keepdims=True)
+        nrm_ref[...] = (centred * lax.rsqrt(variance + 1e-05)).astype(jnp.bfloat16)
+
+    part = jnp.dot(nrm_ref[...], w_ref[...], preferred_element_type=jnp.float32)
+    scale = jnp.where(step == 0, head_size ** -0.5, 1.0).astype(jnp.float32)
+    out_ref[0] = (part * scale).astype(out_ref.dtype)
+
+
+def layer_kernel(sel_ref, x_ref, klive_ref, rlive_ref, cw_ref, qkv_hbm, wo_hbm, state_hbm,
+                 recv_hbm, out_ref, wobuf, stv, qkv, conv_ref, pad_ref, res_ref, wsem, gsem,
                  *, streams, frames, ctx, head_size):
     tokens = streams * frames
     width = x_ref.shape[1]
@@ -40,21 +55,13 @@
         def _():
             pltpu.make_async_copy(recv_hbm.at[idx], stv.at[j], gsem.at[j]).start()
 
-    rows_w = wqkv_hbm.shape[0]
-    copies = []
-    for r in range(rows_w // CHUNK_ROWS):
-        part = pl.ds(r * CHUNK_ROWS, CHUNK_ROWS)
-        copies.append(pltpu.make_async_copy(wqkv_hbm.at[part], wbuf.at[part], wsem.at[0, r]))
+    rows_w = wo_hbm.shape[0]
+    copies = [pltpu.make_async_copy(qkv_hbm, qkv, wsem.at[0, 0])]
     for r in range(rows_w // CHUNK_ROWS):
         part = pl.ds(r * CHUNK_ROWS, CHUNK_ROWS)
         copies.append(pltpu.make_async_copy(wo_hbm.at[part], wobuf.at[part], wsem.at[1, r]))
     for c in copies:
         c.start()
-
-    floats = x_ref[...].astype(jnp.float32)
-    centred = floats - jnp.mean(floats, axis=-1, keepdims=True)
-    variance = jnp.mean(centred * centred, axis=-1, keepdims=True)
-    normed = (centred * lax.rsqrt(variance + 1e-05)).astype(jnp.bfloat16)
 
     for j in range(streams):
         pltpu.make_async_copy(state_hbm.at[0], stv.at[j], gsem.at[j]).wait()
@@ -76,13 +83,7 @@
     conv_ref[...] = jnp.zeros_like(conv_ref)
     conv_taps(0)
 
-    for c in copies[:rows_w // CHUNK_ROWS]:
-        c.wait()
-    for i in range(3):
-        part = jnp.dot(normed, wbuf[:, pl.ds(i * width, width)], preferred_element_type=jnp.float32)
-        if i == 0:
-            part = part * (head_size ** -0.5)
-        qkv[i] = part.astype(jnp.bfloat16)
+    copies[0].wait()
 
     rows_g = GROUP * frames
     cols_g = GROUP * slot
@@ -128,7 +129,7 @@
 
         lax.fori_loop(0, width // pair, head_pair, 0)
 
-    for c in copies[rows_w // CHUNK_ROWS:]:
+    for c in copies[1:]:
         c.wait()
     mixed = jnp.dot(qkv[0], wobuf[...], preferred_element_type=jnp.float32)
     residual = x_ref[...].astype(jnp.float32) + mixed
@@ -150,6 +151,23 @@
         return carry
 
     lax.fori_loop(0, width // chunk, finish, 0)
+
+
+def project(inputs, qkv_weight):
+    streams, frames, width = inputs.shape
+    tokens = streams * frames
+    x = inputs.reshape(tokens, width)
+    kernel = functools.partial(projection_kernel, head_size=width // HEADS)
+    return pl.pallas_call(
+        kernel,
+        out_shape=jax.ShapeDtypeStruct((3, tokens, width), jnp.bfloat16),
+        grid=(3,),
+        in_specs=[pl.BlockSpec((tokens, width), lambda i: (0, 0)),
+                  pl.BlockSpec((width, width), lambda i: (0, i))],
+        out_specs=pl.BlockSpec((1, tokens, width), lambda i: (i, 0, 0)),
+        scratch_shapes=[pltpu.VMEM((tokens, width), jnp.bfloat16)],
+        compiler_params=pltpu.CompilerParams(dimension_semantics=("arbitrary",)),
+    )(x, qkv_weight)
 
 
 def encoder_layer(inputs, valid_counts, sel, state, recv, qkv_weight, out_weight, conv_weight,
@@ -175,7 +193,6 @@
                   hbm, hbm, hbm, hbm],
         out_specs=vmem,
         scratch_shapes=[
-            pltpu.VMEM((width, 3 * width), jnp.bfloat16),
             pltpu.VMEM((width, width), jnp.bfloat16),
             pltpu.VMEM((streams,) + state.shape[1:], jnp.bfloat16),
             pltpu.VMEM((3, tokens, width), jnp.bfloat16),
@@ -185,7 +202,7 @@
             pltpu.SemaphoreType.DMA((2, width // CHUNK_ROWS)),
             pltpu.SemaphoreType.DMA((streams,)),
         ],
-    )(sel, x, klive, rlive, conv_weight, qkv_weight, out_weight, state, recv)
+    )(sel, x, klive, rlive, conv_weight, project(inputs, qkv_weight), out_weight, state, recv)
     return out.reshape(streams, frames, width)
 
 

time: 98.8 us -> 99.1 us (level)
  Pallas kernels: 52.5 us -> 58.9 us
  waiting for transfers between devices: 25.3 us -> 19.2 us
    pallas_call x0 -> x2, Pallas kernels: none -> 12.4 us  [project(): pl.pallas_call(kernel, out_shape=jax.ShapeDtypeStruct((3, tokens, width),...]
    all_to_all x1, waiting for transfers between devices: 21.6 us -> 15.5 us  [migrate(): lax.all_to_all(jnp.take(state, send_slot, axis=0), 'stream', 0, 0, tiled=...]
    pallas_call x2, Pallas kernels: 52.5 us -> 46.4 us  [encoder_layer(): pl.pallas_call(kernel, out_shape=jax.ShapeDtypeStruct((tokens, width), jn...]
  transfers between devices with their start and end apart: 2 -> 2, of which waited for: 2 -> 2; matrix products, arithmetic and copies ran while one was open for 3% -> 3% of each run, Pallas kernels for 0% -> 6%
where the time goes in v5:
time: 99.1 us; the launch traced here: 98.7 us
  Pallas kernels  58.9 us (59%)
  waiting for transfers between devices  19.2 us (19%)
  starting transfers between devices  7.68 us (8%)
  local copies, waits for them, and re-layouts  6.74 us (7%)
  other arithmetic  6.03 us (6%)
    pallas_call x2, Pallas kernels, encoder_layer(): pl.pallas_call(kernel, out_shape=jax.ShapeDtypeStruct((tokens, width), jn...  46.4 us
    all_to_all x1, waiting for transfers between devices, migrate(): lax.all_to_all(jnp.take(state, send_slot, axis=0), 'stream', 0, 0, tiled=...  15.5 us
    pallas_call x2, Pallas kernels, project(): pl.pallas_call(kernel, out_shape=jax.ShapeDtypeStruct((3, tokens, width),...  12.4 us
    all_to_all x1, starting transfers between devices, migrate(): lax.all_to_all(jnp.take(state, send_slot, axis=0), 'stream', 0, 0, tiled=...  6.38 us
    unnamed x19, local copies, waits for them, and re-layouts  4.62 us
    ppermute x1, waiting for transfers between devices, shifted(): lax.ppermute(value, axis, [(source, source + steps) for source in range(l...  3.7 us
  transfers between devices with their start and end apart: 2, of which 2 were waited for; matrix products, arithmetic and copies ran while one was open for 3% of the time, Pallas kernels for 6%

profile of v5, /device:TPU:1, one launch (start us, length us, event | category | flops | bytes accessed | tf_op | source)
XLA Modules:
  0.0 98.7 jit_solution(10004269578375606887)
XLA Ops:
  0.0 0.8 select_reduce_fusion
  0.8 0.7 compare_select_fusion.9
  1.6 0.1 select_reduce_fusion.1
  1.7 1.6 %copy.24 = bf16[1,16,12,2048]{3,2,1,0:T(8,128)(2,1)S(1)} copy(bf16[1,16,12,2048]{3,1,2,0:T(8,128)(2,1)} %param.11) | data formatting | bytes 1572864 | tf_op args[3]
  3.3 0.1 fusion.8
  3.4 0.0 copy-done.4
  3.4 0.5 copy.23
  4.0 0.5 fusion.5.state_hbm
  4.5 0.0 copy-start
  4.5 0.6 gather_fusion
  5.1 0.0 copy-start.7
  5.1 0.0 copy-start.5
  5.1 1.2 %broadcast_select_fusion = bf16[8,64,1024]{2,1,0:T(8,128)(2,1)} fusion(bf16[8,64,1024]{2,1,0:T(8,128)(2,1)S(1)} %gather_fusion, pred[8]{0:T(512)(128)(4,1)S(1)} %compare_and_fusion), kind=kLoop, calls=%fused_computation.13 | loop fusion | flops 524288 | bytes 2097160 | tf_op jit(solution)/shard_map/jit(_take)/select_n | solution.py:220
  6.3 6.4 %all-to-all-start = ((bf16[8,64,1024]{2,1,0:T(8,128)(2,1)}), bf16[8,64,1024]{2,1,0:T(8,128)(2,1)S(1)}, u32[]{:S(2)}, u32[]{:S(2)}) async-start(bf16[8,64,1024]{2,1,0:T(8,128)(2,1)} %broadcast_select_fusion), calls=%async_computation | async-start | bytes 2097152 | tf_op jit(solution)/shard_map/all_to_all | solution.py:220
  12.7 0.1 dynamic_slice.10
  12.8 0.1 fusion.6
  12.9 0.6 reshape.113.klive_ref
  13.4 0.8 reshape.123.rlive_ref
  14.2 0.0 copy-done.5
  14.2 0.7 copy.25
  14.9 6.2 %shard_map.82.qkv_hbm = bf16[3,256,1024]{2,1,0:T(8,128)(2,1)} custom-call(bf16[256,1024]{1,0:T(8,128)(2,1)} %bitcast.25, bf16[1024,3072]{1,0:T(8,128)(2,1)} %bitcast.19), custom_call_target="tpu_custom_call" | custom-call | tf_op jit(solution)/shard_map/pallas_call | solution.py:161
  21.1 0.1 compare_select_fusion.8
  21.2 0.6 pad_add_fusion.sel_ref
  21.8 15.5 %all-to-all-done.recv_hbm = bf16[8,64,1024]{2,1,0:T(8,128)(2,1)S(1)} async-done(((bf16[8,64,1024]{2,1,0:T(8,128)(2,1)}), bf16[8,64,1024]{2,1,0:T(8,128)(2,1)S(1)}, u32[]{:S(2)}, u32[]{:S(2)}) %all-to-all-start) | async-done | bytes 1048608 | tf_op jit(solution)/shard_map/all_to_all | solution.py:220
  37.3 1.0 %copy-done.1 = bf16[8,64,1024]{2,1,0:T(8,128)(2,1)} copy-done((bf16[8,64,1024]{2,1,0:T(8,128)(2,1)}, bf16[8,64,1024]{2,1,0:T(8,128)(2,1)S(1)}, u32[]{:S(2)}) %copy-start.1) | copy-done | bytes 1048600
  38.3 23.2 %shard_map.83 = bf16[256,1024]{1,0:T(8,128)(2,1)} custom-call(s32[32]{0:T(128)} %pad_add_fusion.sel_ref, bf16[256,1024]{1,0:T(8,128)(2,1)} %bitcast.26, f32[1,256]{1,0:T(1,128)} %reshape.113.klive_ref, f32[256,1]{1,0:T(8,128)} %reshape.123.rlive_ref, f32[31,1024]{1,0:T(8,128)} %bitcast.30, bf16[3,256,1024]{2,1,0:T(8,128)(2,1)} %shard_map.82.qkv_hbm, ...), custom_call_target="tpu_custom_call" | custom-call | tf_op jit(solution)/shard_map/pallas_call | solution.py:189
  61.5 1.3 %collective-permute-start = (bf16[16,16,1024]{2,1,0:T(8,128)(2,1)}, bf16[16,16,1024]{2,1,0:T(8,128)(2,1)S(1)}, u32[]{:S(2)}, u32[]{:S(2)}) collective-permute-start(bf16[16,16,1024]{2,1,0:T(8,128)(2,1)} %bitcast.29), channel_id=1, source_target_pairs={{0,1},{2,3},{4,5},{6,7},{8,9},{10,11},{12,13},{14,15},{16,17},{18,... | collective-permute-start | bytes 1572872 | tf_op jit(solution)/shard_map/ppermute | solution.py:18
  62.8 3.7 %collective-permute-done = bf16[16,16,1024]{2,1,0:T(8,128)(2,1)S(1)} collective-permute-done((bf16[16,16,1024]{2,1,0:T(8,128)(2,1)}, bf16[16,16,1024]{2,1,0:T(8,128)(2,1)S(1)}, u32[]{:S(2)}, u32[]{:S(2)}) %collective-permute-start) | collective-permute-done | bytes 524320 | tf_op jit(solution)/shard_map/ppermute | solution.py:18
  66.5 0.8 copy-done.2
  67.3 6.2 %shard_map.84.qkv_hbm = bf16[3,256,1024]{2,1,0:T(8,128)(2,1)} custom-call(bf16[256,1024]{1,0:T(8,128)(2,1)} %bitcast.27, bf16[1024,3072]{1,0:T(8,128)(2,1)} %bitcast.20), custom_call_target="tpu_custom_call" | custom-call | tf_op jit(solution)/shard_map/pallas_call | solution.py:161
  73.5 23.3 %shard_map.85 = bf16[256,1024]{1,0:T(8,128)(2,1)} custom-call(s32[32]{0:T(128)} %pad_add_fusion.sel_ref, bf16[256,1024]{1,0:T(8,128)(2,1)} %bitcast.28, f32[1,256]{1,0:T(1,128)} %reshape.113.klive_ref, f32[256,1]{1,0:T(8,128)} %reshape.123.rlive_ref, f32[31,1024]{1,0:T(8,128)} %bitcast.31, bf16[3,256,1024]{2,1,0:T(8,128)(2,1)} %shard_map.84.qkv_hbm, ...), custom_call_target="tpu_custom_call" | custom-call | tf_op jit(solution)/shard_map/pallas_call | solution.py:189
  96.8 1.9 %broadcast_select_fusion.1 = bf16[256,1024]{1,0:T(8,128)(2,1)} fusion(bf16[256,1024]{1,0:T(8,128)(2,1)S(1)} %copy-done.3, bf16[256,1024]{1,0:T(8,128)(2,1)} %shard_map.85, pred[]{:T(512)S(6)} %eq.35), kind=kLoop, calls=%fused_computation.14 | loop fusion | flops 262144 | bytes 1572865 | tf_op jit(solution)/shard_map/jit(_where)/select_n | solution.py:256
  (12 shorter events, 0.0 us)
Async XLA Ops:
  0.0 3.4 %copy-start.4 = (bf16[1,16,30,1024]{3,1,2,0:T(8,128)(2,1)S(1)}, bf16[1,16,30,1024]{3,1,2,0:T(8,128)(2,1)}, u32[]{:S(2)}) copy-start(bf16[1,16,30,1024]{3,1,2,0:T(8,128)(2,1)} %param.12) | copy-start | bytes 2949124
  4.5 1.8 %copy-start = (bf16[16,64,1024]{2,1,0:T(8,128)(2,1)}, bf16[16,64,1024]{2,1,0:T(8,128)(2,1)S(1)}, u32[]{:S(2)}) copy-start(bf16[16,64,1024]{2,1,0:T(8,128)(2,1)S(1)} %fusion.5.state_hbm) | copy-start | bytes 6291460
  5.1 7.6 %copy-start.7 = (s32[128]{0:T(128)S(1)}, s32[128]{0:T(128)}, u32[]{:S(2)}) copy-start(s32[128]{0:T(128)} %param.9) | copy-start | bytes 1540
  5.1 9.1 %copy-start.5 = (f32[1,31,1024]{2,0,1:T(1,128)S(1)}, f32[1,31,1024]{2,0,1:T(1,128)}, u32[]{:S(2)}) copy-start(f32[1,31,1024]{2,0,1:T(1,128)} %param.15) | copy-start | bytes 380932
  6.3 31.0 %all-to-all-start = ((bf16[8,64,1024]{2,1,0:T(8,128)(2,1)}), bf16[8,64,1024]{2,1,0:T(8,128)(2,1)S(1)}, u32[]{:S(2)}, u32[]{:S(2)}) async-start(bf16[8,64,1024]{2,1,0:T(8,128)(2,1)} %broadcast_select_fusion), calls=%async_computation | async-start | bytes 2097152 | tf_op jit(solution)/shard_map/all_to_all | solution.py:220
  14.9 6.2 %copy-start.6 = (s32[128]{0:T(128)S(1)}, s32[128]{0:T(128)}, u32[]{:S(2)}) copy-start(s32[128]{0:T(128)} %param.10) | copy-start | bytes 1540
  37.3 1.0 %copy-start.1 = (bf16[8,64,1024]{2,1,0:T(8,128)(2,1)}, bf16[8,64,1024]{2,1,0:T(8,128)(2,1)S(1)}, u32[]{:S(2)}) copy-start(bf16[8,64,1024]{2,1,0:T(8,128)(2,1)S(1)} %all-to-all-done.recv_hbm) | copy-start | bytes 3145732
  61.5 5.0 %collective-permute-start = (bf16[16,16,1024]{2,1,0:T(8,128)(2,1)}, bf16[16,16,1024]{2,1,0:T(8,128)(2,1)S(1)}, u32[]{:S(2)}, u32[]{:S(2)}) collective-permute-start(bf16[16,16,1024]{2,1,0:T(8,128)(2,1)} %bitcast.29), channel_id=1, source_target_pairs={{0,1},{2,3},{4,5},{6,7},{8,9},{10,11},{12,13},{14,15},{16,17},{18,... | collective-permute-start | bytes 1572872 | tf_op jit(solution)/shard_map/ppermute | solution.py:18
  66.5 0.8 copy-start.2
  73.5 23.3 %copy-start.3 = (bf16[256,1024]{1,0:T(8,128)(2,1)S(1)}, bf16[256,1024]{1,0:T(8,128)(2,1)}, u32[]{:S(2)}) copy-start(bf16[256,1024]{1,0:T(8,128)(2,1)} %shard_map.83) | copy-start | bytes 1572868

commit v6 on v5

--- a/solution.py
+++ b/solution.py
@@ -33,9 +33,86 @@
     out_ref[0] = (part * scale).astype(out_ref.dtype)
 
 
+def conv_rows(conv_ref, pad_ref, cw_ref, tap_rows, frames, origin):
+    width = cw_ref.shape[1]
+    chunk = 128
+
+    def conv_chunk(c, carry):
+        cols = pl.ds(pl.multiple_of(c * chunk, chunk), chunk)
+        for lo in range(0, frames, 8):
+            conv = conv_ref[:, pl.ds(lo, 8), cols]
+            for j, rows in enumerate(tap_rows):
+                if lo in rows:
+                    conv = conv + cw_ref[pl.ds(j, 1), cols].reshape(1, 1, chunk) * pad_ref[
+                        :, pl.ds(origin + j + lo, 8), cols]
+            conv_ref[:, pl.ds(lo, 8), cols] = conv
+        return carry
+
+    lax.fori_loop(0, width // chunk, conv_chunk, 0)
+
+
+def kept_taps(taps, kept, frames):
+    return [[lo for lo in range(0, frames, 8) if lo < kept - j] for j in range(taps)]
+
+
+def new_taps(taps, kept, frames):
+    return [[lo for lo in range(0, frames, 8) if lo + 7 >= kept - j] for j in range(taps)]
+
+
+def kept_conv_kernel(sel_ref, cw_ref, state_hbm, recv_hbm, out_ref, stv, pad_ref, gsem, *,
+                     streams, frames, slot, kept):
+    width = cw_ref.shape[1]
+    rows = pad_ref.shape[1] - frames
+    for j in range(streams):
+        kind = sel_ref[j]
+        idx = sel_ref[streams + j]
+
+        @pl.when(kind == 0)
+        def _():
+            pltpu.make_async_copy(state_hbm.at[idx, pl.ds(2 * slot, rows)], stv.at[j],
+                                  gsem.at[j]).start()
+
+        @pl.when(kind != 0)
+        def _():
+            pltpu.make_async_copy(recv_hbm.at[idx, pl.ds(2 * slot, rows)], stv.at[j],
+                                  gsem.at[j]).start()
+
+    for j in range(streams):
+        pltpu.make_async_copy(state_hbm.at[0, pl.ds(2 * slot, rows)], stv.at[j], gsem.at[j]).wait()
+    pad_ref[:, 0:rows, :] = stv[...].astype(jnp.float32)
+    pad_ref[:, rows:, :] = jnp.zeros((streams, frames, width), jnp.float32)
+    out_ref[...] = jnp.zeros_like(out_ref)
+    taps = cw_ref.shape[0]
+    conv_rows(out_ref, pad_ref, cw_ref, kept_taps(taps, kept, frames), frames, rows - kept)
+
+
+def kept_conv(sel, state, recv, conv_weight, streams, frames, ctx, kept):
+    slot = -(-ctx // 16) * 16
+    rows = state.shape[1] - 2 * slot
+    width = state.shape[2]
+    kernel = functools.partial(kept_conv_kernel, streams=streams, frames=frames, slot=slot,
+                               kept=kept)
+    vmem = pl.BlockSpec(memory_space=pltpu.VMEM)
+    hbm = pl.BlockSpec(memory_space=pl.ANY)
+    return pl.pallas_call(
+        kernel,
+        out_shape=jax.ShapeDtypeStruct((streams, frames, width), jnp.float32),
+        in_specs=[pl.BlockSpec(memory_space=pltpu.SMEM), vmem, hbm, hbm],
+        out_specs=vmem,
+        scratch_shapes=[
+            pltpu.VMEM((streams, rows, width), jnp.bfloat16),
+            pltpu.VMEM((streams, rows + frames, width), jnp.float32),
+            pltpu.SemaphoreType.DMA((streams,)),
+        ],
+    )(sel, conv_weight, state, recv)
+
+
 def layer_kernel(sel_ref, x_ref, klive_ref, rlive_ref, cw_ref, qkv_hbm, wo_hbm, state_hbm,
-                 recv_hbm, out_ref, wobuf, stv, qkv, conv_ref, pad_ref, res_ref, wsem, gsem,
-                 *, streams, frames, ctx, head_size):
+                 recv_hbm, *rest, streams, frames, ctx, head_size, kept_real, early):
+    if early:
+        conv_in_ref, out_ref, wobuf, stv, qkv, conv_ref, pad_ref, res_ref, wsem, gsem = rest
+    else:
+        out_ref, wobuf, stv, qkv, conv_ref, pad_ref, res_ref, wsem, gsem = rest
     tokens = streams * frames
     width = x_ref.shape[1]
     slot = -(-ctx // 16) * 16
@@ -65,23 +142,6 @@
 
     for j in range(streams):
         pltpu.make_async_copy(state_hbm.at[0], stv.at[j], gsem.at[j]).wait()
-    pad_ref[:, 0:kept, :] = stv[:, pl.ds(2 * slot, kept), :].astype(jnp.float32)
-    pad_ref[:, kept:, :] = jnp.zeros((streams, frames, width), jnp.float32)
-
-    def conv_taps(first):
-        def conv_chunk(c, carry):
-            cols = pl.ds(pl.multiple_of(c * chunk, chunk), chunk)
-            conv = conv_ref[:, :, cols]
-            for j in range(first, taps):
-                conv = conv + cw_ref[pl.ds(j, 1), cols].reshape(1, 1, chunk) * pad_ref[
-                    :, pl.ds(kept - taps + 1 + j, frames), cols]
-            conv_ref[:, :, cols] = conv
-            return carry
-
-        lax.fori_loop(0, width // chunk, conv_chunk, 0)
-
-    conv_ref[...] = jnp.zeros_like(conv_ref)
-    conv_taps(0)
 
     copies[0].wait()
 
@@ -119,8 +179,9 @@
                 ec = jnp.exp(sc - top)
                 en = jnp.exp(sn - top)
                 total = jnp.sum(ec, axis=-1, keepdims=True) + jnp.sum(en, axis=-1, keepdims=True)
-                pc = (ec / total).astype(jnp.bfloat16)
-                pn = (en / total).astype(jnp.bfloat16)
+                inv = 1.0 / total
+                pc = (ec * inv).astype(jnp.bfloat16)
+                pn = (en * inv).astype(jnp.bfloat16)
                 oh = jnp.dot(pc, cv, preferred_element_type=jnp.float32) + jnp.dot(
                     pn, v, preferred_element_type=jnp.float32)
                 attended = oh if attended is None else jnp.where(mine, oh, attended)
@@ -134,11 +195,19 @@
     mixed = jnp.dot(qkv[0], wobuf[...], preferred_element_type=jnp.float32)
     residual = x_ref[...].astype(jnp.float32) + mixed
     res_ref[...] = residual
-    pad_ref[:, 0:kept, :] = jnp.zeros((streams, kept, width), jnp.float32)
-    pad_ref[:, kept:, :] = residual.astype(jnp.bfloat16).astype(jnp.float32).reshape(
-        streams, frames, width)
-    first = taps - frames
-    conv_taps(first)
+    rounded = residual.astype(jnp.bfloat16).astype(jnp.float32).reshape(streams, frames, width)
+    origin = kept - kept_real
+    if early:
+        pad_ref[:, 0:kept, :] = jnp.zeros((streams, kept, width), jnp.float32)
+        pad_ref[:, kept:, :] = rounded
+        conv_ref[...] = conv_in_ref[...]
+        conv_rows(conv_ref, pad_ref, cw_ref, new_taps(taps, kept_real, frames), frames, origin)
+    else:
+        pad_ref[:, 0:kept, :] = stv[:, pl.ds(2 * slot, kept), :].astype(jnp.float32)
+        pad_ref[:, kept:, :] = rounded
+        conv_ref[...] = jnp.zeros_like(conv_ref)
+        every = [list(range(0, frames, 8))] * taps
+        conv_rows(conv_ref, pad_ref, cw_ref, every, frames, origin)
     live = rlive_ref[...].reshape(streams, frames, 1)
 
     def finish(c, carry):
@@ -171,7 +240,7 @@
 
 
 def encoder_layer(inputs, valid_counts, sel, state, recv, qkv_weight, out_weight, conv_weight,
-                  ctx):
+                  ctx, kept_real, conv_in=None):
     streams, frames, width = inputs.shape
     taps = conv_weight.shape[0]
     head_size = width // HEADS
@@ -182,15 +251,17 @@
     rlive = live.reshape(tokens, 1)
     x = inputs.reshape(tokens, width)
     kept = state.shape[1] - 2 * slot
+    early = conv_in is not None
     kernel = functools.partial(layer_kernel, streams=streams, frames=frames, ctx=ctx,
-                               head_size=head_size)
+                               head_size=head_size, kept_real=kept_real, early=early)
     vmem = pl.BlockSpec(memory_space=pltpu.VMEM)
     hbm = pl.BlockSpec(memory_space=pl.ANY)
+    extra = [conv_in] if early else []
     out = pl.pallas_call(
         kernel,
         out_shape=jax.ShapeDtypeStruct((tokens, width), jnp.bfloat16),
         in_specs=[pl.BlockSpec(memory_space=pltpu.SMEM), vmem, vmem, vmem, vmem,
-                  hbm, hbm, hbm, hbm],
+                  hbm, hbm, hbm, hbm] + [vmem] * len(extra),
         out_specs=vmem,
         scratch_shapes=[
             pltpu.VMEM((width, width), jnp.bfloat16),
@@ -202,7 +273,7 @@
             pltpu.SemaphoreType.DMA((2, width // CHUNK_ROWS)),
             pltpu.SemaphoreType.DMA((streams,)),
         ],
-    )(sel, x, klive, rlive, conv_weight, project(inputs, qkv_weight), out_weight, state, recv)
+    )(sel, x, klive, rlive, conv_weight, project(inputs, qkv_weight), out_weight, state, recv, *extra)
     return out.reshape(streams, frames, width)
 
 
@@ -249,10 +320,11 @@
     section_index = lax.axis_index("section")
     layer = functools.partial(encoder_layer, valid_counts=valid_here, sel=sel, state=state,
                               recv=recv, qkv_weight=qkv_weight[0], out_weight=out_weight[0],
-                              conv_weight=conv_weight[0], ctx=ctx)
+                              conv_weight=conv_weight[0], ctx=ctx, kept_real=kept)
     first = layer(new_frames)
     inbound = shifted(first, "section", 1)
-    second = layer(inbound)
+    early = kept_conv(sel, state, recv, conv_weight[0], local_count, new_frames.shape[1], ctx, kept)
+    second = layer(inbound, conv_in=early)
     result = jnp.where(section_index == 0, first, second)
     return result[None]
 

time: 99.1 us -> 96.2 us (0.971); the launches traced: 98.7 us -> 94.6 us
  waiting for transfers between devices: 19.2 us -> 15.4 us
    pallas_call x2, Pallas kernels: 46.4 us -> 37.4 us  [encoder_layer(): pl.pallas_call(kernel, out_shape=jax.ShapeDtypeStruct((tokens, width), jn...]
    pallas_call x0 -> x1, Pallas kernels: none -> 8.66 us  [kept_conv(): pl.pallas_call(kernel, out_shape=jax.ShapeDtypeStruct((streams, frames, w...]
    ppermute x1, waiting for transfers between devices: 3.7 us -> 0.01 us  [shifted(): lax.ppermute(value, axis, [(source, source + steps) for source in range(l...]
  transfers between devices with their start and end apart: 2 -> 2, of which waited for: 2 -> 1; matrix products, arithmetic and copies ran while one was open for 3% -> 3% of each run, Pallas kernels for 6% -> 16%
where the time goes in v6:
time: 96.2 us; the launch traced here: 94.6 us
  Pallas kernels  58.5 us (61%)
  waiting for transfers between devices  15.4 us (16%)
  starting transfers between devices  7.68 us (8%)
  local copies, waits for them, and re-layouts  6.79 us (7%)
  other arithmetic  6.08 us (6%)
    pallas_call x2, Pallas kernels, encoder_layer(): pl.pallas_call(kernel, out_shape=jax.ShapeDtypeStruct((tokens, width), jn...  37.4 us
    all_to_all x1, waiting for transfers between devices, migrate(): lax.all_to_all(jnp.take(state, send_slot, axis=0), 'stream', 0, 0, tiled=...  15.4 us
    pallas_call x2, Pallas kernels, project(): pl.pallas_call(kernel, out_shape=jax.ShapeDtypeStruct((3, tokens, width),...  12.4 us
    pallas_call x1, Pallas kernels, kept_conv(): pl.pallas_call(kernel, out_shape=jax.ShapeDtypeStruct((streams, frames, w...  8.66 us
    all_to_all x1, starting transfers between devices, migrate(): lax.all_to_all(jnp.take(state, send_slot, axis=0), 'stream', 0, 0, tiled=...  6.38 us
    unnamed x19, local copies, waits for them, and re-layouts  4.6 us
  transfers between devices with their start and end apart: 2, of which 1 were waited for; matrix products, arithmetic and copies ran while one was open for 3% of the time, Pallas kernels for 16%

profile of v6, /device:TPU:1, one launch (start us, length us, event | category | flops | bytes accessed | tf_op | source)
XLA Modules:
  0.0 94.6 jit_solution(13077851539930453148)
XLA Ops:
  0.0 0.8 select_reduce_fusion
  0.8 0.7 compare_select_fusion.9
  1.6 0.1 select_reduce_fusion.1
  1.7 1.6 %copy.24 = bf16[1,16,12,2048]{3,2,1,0:T(8,128)(2,1)S(1)} copy(bf16[1,16,12,2048]{3,1,2,0:T(8,128)(2,1)} %param.11) | data formatting | bytes 1572864 | tf_op args[3]
  3.3 0.1 fusion.8
  3.4 0.5 copy.23
  4.0 0.5 fusion.5.state_hbm
  4.5 0.0 copy-start
  4.5 0.6 gather_fusion
  5.1 0.0 copy-start.7
  5.1 0.0 copy-start.5
  5.1 1.2 %broadcast_select_fusion = bf16[8,64,1024]{2,1,0:T(8,128)(2,1)} fusion(bf16[8,64,1024]{2,1,0:T(8,128)(2,1)S(1)} %gather_fusion, pred[8]{0:T(512)(128)(4,1)S(1)} %compare_and_fusion), kind=kLoop, calls=%fused_computation.13 | loop fusion | flops 524288 | bytes 2097160 | tf_op jit(solution)/shard_map/jit(_take)/select_n | solution.py:291
  6.3 6.4 %all-to-all-start = ((bf16[8,64,1024]{2,1,0:T(8,128)(2,1)}), bf16[8,64,1024]{2,1,0:T(8,128)(2,1)S(1)}, u32[]{:S(2)}, u32[]{:S(2)}) async-start(bf16[8,64,1024]{2,1,0:T(8,128)(2,1)} %broadcast_select_fusion), calls=%async_computation | async-start | bytes 2097152 | tf_op jit(solution)/shard_map/all_to_all | solution.py:291
  12.7 0.1 dynamic_slice.10
  12.8 0.1 fusion.6
  12.9 0.7 reshape.113.klive_ref
  13.5 0.8 reshape.123.rlive_ref
  14.3 0.7 copy.25
  14.9 6.2 %shard_map.82.qkv_hbm = bf16[3,256,1024]{2,1,0:T(8,128)(2,1)} custom-call(bf16[256,1024]{1,0:T(8,128)(2,1)} %bitcast.28, bf16[1024,3072]{1,0:T(8,128)(2,1)} %bitcast.19), custom_call_target="tpu_custom_call" | custom-call | tf_op jit(solution)/shard_map/pallas_call | solution.py:230
  21.2 0.0 copy-done.6
  21.2 0.1 compare_select_fusion.8
  21.2 0.7 pad_add_fusion.sel_ref
  21.9 15.4 %all-to-all-done.recv_hbm = bf16[8,64,1024]{2,1,0:T(8,128)(2,1)S(1)} async-done(((bf16[8,64,1024]{2,1,0:T(8,128)(2,1)}), bf16[8,64,1024]{2,1,0:T(8,128)(2,1)S(1)}, u32[]{:S(2)}, u32[]{:S(2)}) %all-to-all-start) | async-done | bytes 1048608 | tf_op jit(solution)/shard_map/all_to_all | solution.py:291
  37.3 1.0 %copy-done.1 = bf16[8,64,1024]{2,1,0:T(8,128)(2,1)} copy-done((bf16[8,64,1024]{2,1,0:T(8,128)(2,1)}, bf16[8,64,1024]{2,1,0:T(8,128)(2,1)S(1)}, u32[]{:S(2)}) %copy-start.1) | copy-done | bytes 1048600
  38.3 20.4 %shard_map.83 = bf16[256,1024]{1,0:T(8,128)(2,1)} custom-call(s32[32]{0:T(128)} %pad_add_fusion.sel_ref, bf16[256,1024]{1,0:T(8,128)(2,1)} %bitcast.29, f32[1,256]{1,0:T(1,128)} %reshape.113.klive_ref, f32[256,1]{1,0:T(8,128)} %reshape.123.rlive_ref, f32[31,1024]{1,0:T(8,128)} %bitcast.25, bf16[3,256,1024]{2,1,0:T(8,128)(2,1)} %shard_map.82.qkv_hbm, ...), custom_call_target="tpu_custom_call" | custom-call | tf_op jit(solution)/shard_map/pallas_call | solution.py:260
  58.7 1.3 %collective-permute-start = (bf16[16,16,1024]{2,1,0:T(8,128)(2,1)}, bf16[16,16,1024]{2,1,0:T(8,128)(2,1)S(1)}, u32[]{:S(2)}, u32[]{:S(2)}) collective-permute-start(bf16[16,16,1024]{2,1,0:T(8,128)(2,1)} %bitcast.32), channel_id=1, source_target_pairs={{0,1},{2,3},{4,5},{6,7},{8,9},{10,11},{12,13},{14,15},{16,17},{18,... | collective-permute-start | bytes 1572872 | tf_op jit(solution)/shard_map/ppermute | solution.py:18
  60.0 8.7 %shard_map.85.rest_0_ = f32[16,16,1024]{2,1,0:T(8,128)} custom-call(s32[32]{0:T(128)} %pad_add_fusion.sel_ref, f32[31,1024]{1,0:T(8,128)} %bitcast.26, bf16[16,64,1024]{2,1,0:T(8,128)(2,1)} %copy-done, bf16[8,64,1024]{2,1,0:T(8,128)(2,1)} %copy-done.1), custom_call_target="tpu_custom_call" | custom-call | tf_op jit(solution)/shard_map/pallas_call | solution.py:97
  68.7 0.0 collective-permute-done
  68.7 0.8 copy-done.2
  69.5 6.2 %shard_map.84.qkv_hbm = bf16[3,256,1024]{2,1,0:T(8,128)(2,1)} custom-call(bf16[256,1024]{1,0:T(8,128)(2,1)} %bitcast.30, bf16[1024,3072]{1,0:T(8,128)(2,1)} %bitcast.20), custom_call_target="tpu_custom_call" | custom-call | tf_op jit(solution)/shard_map/pallas_call | solution.py:230
  75.7 17.0 %shard_map.86 = bf16[256,1024]{1,0:T(8,128)(2,1)} custom-call(s32[32]{0:T(128)} %pad_add_fusion.sel_ref, bf16[256,1024]{1,0:T(8,128)(2,1)} %bitcast.31, f32[1,256]{1,0:T(1,128)} %reshape.113.klive_ref, f32[256,1]{1,0:T(8,128)} %reshape.123.rlive_ref, f32[31,1024]{1,0:T(8,128)} %bitcast.27, bf16[3,256,1024]{2,1,0:T(8,128)(2,1)} %shard_map.84.qkv_hbm, ...), custom_call_target="tpu_custom_call" | custom-call | tf_op jit(solution)/shard_map/pallas_call | solution.py:260
  92.7 1.9 %broadcast_select_fusion.1 = bf16[256,1024]{1,0:T(8,128)(2,1)} fusion(bf16[256,1024]{1,0:T(8,128)(2,1)S(1)} %copy-done.3, bf16[256,1024]{1,0:T(8,128)(2,1)} %shard_map.86, pred[]{:T(512)S(6)} %eq.35), kind=kLoop, calls=%fused_computation.14 | loop fusion | flops 262144 | bytes 1572865 | tf_op jit(solution)/shard_map/jit(_where)/select_n | solution.py:328
  (13 shorter events, 0.0 us)
Async XLA Ops:
  0.0 3.4 %copy-start.4 = (bf16[1,16,30,1024]{3,1,2,0:T(8,128)(2,1)S(1)}, bf16[1,16,30,1024]{3,1,2,0:T(8,128)(2,1)}, u32[]{:S(2)}) copy-start(bf16[1,16,30,1024]{3,1,2,0:T(8,128)(2,1)} %param.12) | copy-start | bytes 2949124
  4.5 1.8 %copy-start = (bf16[16,64,1024]{2,1,0:T(8,128)(2,1)}, bf16[16,64,1024]{2,1,0:T(8,128)(2,1)S(1)}, u32[]{:S(2)}) copy-start(bf16[16,64,1024]{2,1,0:T(8,128)(2,1)S(1)} %fusion.5.state_hbm) | copy-start | bytes 6291460
  5.1 7.6 %copy-start.7 = (s32[128]{0:T(128)S(1)}, s32[128]{0:T(128)}, u32[]{:S(2)}) copy-start(s32[128]{0:T(128)} %param.9) | copy-start | bytes 1540
  5.1 9.1 %copy-start.5 = (f32[1,31,1024]{2,0,1:T(1,128)S(1)}, f32[1,31,1024]{2,0,1:T(1,128)}, u32[]{:S(2)}) copy-start(f32[1,31,1024]{2,0,1:T(1,128)} %param.15) | copy-start | bytes 380932
  6.3 31.0 %all-to-all-start = ((bf16[8,64,1024]{2,1,0:T(8,128)(2,1)}), bf16[8,64,1024]{2,1,0:T(8,128)(2,1)S(1)}, u32[]{:S(2)}, u32[]{:S(2)}) async-start(bf16[8,64,1024]{2,1,0:T(8,128)(2,1)} %broadcast_select_fusion), calls=%async_computation | async-start | bytes 2097152 | tf_op jit(solution)/shard_map/all_to_all | solution.py:291
  14.9 6.2 %copy-start.6 = (s32[128]{0:T(128)S(1)}, s32[128]{0:T(128)}, u32[]{:S(2)}) copy-start(s32[128]{0:T(128)} %param.10) | copy-start | bytes 1540
  37.3 1.0 %copy-start.1 = (bf16[8,64,1024]{2,1,0:T(8,128)(2,1)}, bf16[8,64,1024]{2,1,0:T(8,128)(2,1)S(1)}, u32[]{:S(2)}) copy-start(bf16[8,64,1024]{2,1,0:T(8,128)(2,1)S(1)} %all-to-all-done.recv_hbm) | copy-start | bytes 3145732
  58.7 10.0 %collective-permute-start = (bf16[16,16,1024]{2,1,0:T(8,128)(2,1)}, bf16[16,16,1024]{2,1,0:T(8,128)(2,1)S(1)}, u32[]{:S(2)}, u32[]{:S(2)}) collective-permute-start(bf16[16,16,1024]{2,1,0:T(8,128)(2,1)} %bitcast.32), channel_id=1, source_target_pairs={{0,1},{2,3},{4,5},{6,7},{8,9},{10,11},{12,13},{14,15},{16,17},{18,... | collective-permute-start | bytes 1572872 | tf_op jit(solution)/shard_map/ppermute | solution.py:18
  68.7 0.8 copy-start.2
  75.7 17.0 %copy-start.3 = (bf16[256,1024]{1,0:T(8,128)(2,1)S(1)}, bf16[256,1024]{1,0:T(8,128)(2,1)}, u32[]{:S(2)}) copy-start(bf16[256,1024]{1,0:T(8,128)(2,1)} %shard_map.83) | copy-start | bytes 1572868

commit v7 on v6

--- a/solution.py
+++ b/solution.py
@@ -240,7 +240,7 @@
 
 
 def encoder_layer(inputs, valid_counts, sel, state, recv, qkv_weight, out_weight, conv_weight,
-                  ctx, kept_real, conv_in=None):
+                  ctx, kept_real, conv_in=None, projected=None):
     streams, frames, width = inputs.shape
     taps = conv_weight.shape[0]
     head_size = width // HEADS
@@ -273,7 +273,8 @@
             pltpu.SemaphoreType.DMA((2, width // CHUNK_ROWS)),
             pltpu.SemaphoreType.DMA((streams,)),
         ],
-    )(sel, x, klive, rlive, conv_weight, project(inputs, qkv_weight), out_weight, state, recv, *extra)
+    )(sel, x, klive, rlive, conv_weight, project(inputs, qkv_weight) if projected is None else projected,
+      out_weight, state, recv, *extra)
     return out.reshape(streams, frames, width)
 
 
@@ -321,11 +322,20 @@
     layer = functools.partial(encoder_layer, valid_counts=valid_here, sel=sel, state=state,
                               recv=recv, qkv_weight=qkv_weight[0], out_weight=out_weight[0],
                               conv_weight=conv_weight[0], ctx=ctx, kept_real=kept)
-    first = layer(new_frames)
+    on_first = section_index == 0
+    frames = new_frames.shape[1]
+    like = lambda shape, dtype: (lambda: jnp.zeros(shape, dtype))
+    projected = lax.cond(on_first, lambda: project(new_frames, qkv_weight[0]),
+                         like((3, local_count * frames, width), jnp.bfloat16))
+    first = lax.cond(on_first, lambda: layer(new_frames, projected=projected),
+                     like(new_frames.shape, new_frames.dtype))
+    early = lax.cond(on_first, like(new_frames.shape, jnp.float32),
+                     lambda: kept_conv(sel, state, recv, conv_weight[0], local_count, frames, ctx,
+                                       kept))
     inbound = shifted(first, "section", 1)
-    early = kept_conv(sel, state, recv, conv_weight[0], local_count, new_frames.shape[1], ctx, kept)
-    second = layer(inbound, conv_in=early)
-    result = jnp.where(section_index == 0, first, second)
+    second = lax.cond(on_first, like(new_frames.shape, new_frames.dtype),
+                      lambda: layer(inbound, conv_in=early))
+    result = jnp.where(on_first, first, second)
     return result[None]
 
 

time: 96.2 us -> 94.2 us (0.979); the launches traced: 94.6 us -> 93.8 us
  Pallas kernels: 58.5 us -> 33.7 us
  waiting for transfers between devices: 15.4 us -> 39.6 us
    pallas_call x2 -> x1, Pallas kernels: 37.4 us -> 18.5 us  [encoder_layer(): pl.pallas_call(kernel, out_shape=jax.ShapeDtypeStruct((tokens, width), jn...]
    ppermute x1, waiting for transfers between devices: 0.01 us -> 16.6 us  [shifted(): lax.ppermute(value, axis, [(source, source + steps) for source in range(l...]
    all_to_all x1, waiting for transfers between devices: 15.4 us -> 23 us  [migrate(): lax.all_to_all(jnp.take(state, send_slot, axis=0), 'stream', 0, 0, tiled=...]
    pallas_call x2 -> x1, Pallas kernels: 12.4 us -> 6.24 us  [project(): pl.pallas_call(kernel, out_shape=jax.ShapeDtypeStruct((3, tokens, width),...]
    another operation x0 -> x3, local copies, waits for them, and re-layouts: none -> 2.87 us
    unnamed x19 -> x11, local copies, waits for them, and re-layouts: 4.6 us -> 2.17 us
    broadcast_in_dim x0 -> x1, other arithmetic: none -> 1.91 us  [body(): return result[None]]
    select_n x1 -> x0, other arithmetic: 1.9 us -> none  [body(): result = jnp.where(section_index == 0, first, second)]
  transfers between devices with their start and end apart: 2 -> 2, of which waited for: 1 -> 2; matrix products, arithmetic and copies ran while one was open for 3% -> 2% of each run, Pallas kernels for 16% -> 10%
where the time goes in v7:
time: 94.2 us; the launch traced here: 93.8 us
  waiting for transfers between devices  39.6 us (42%)
  Pallas kernels  33.7 us (36%)
  starting transfers between devices  7.66 us (8%)
  local copies, waits for them, and re-layouts  7.19 us (8%)
  other arithmetic  5.48 us (6%)
    all_to_all x1, waiting for transfers between devices, migrate(): lax.all_to_all(jnp.take(state, send_slot, axis=0), 'stream', 0, 0, tiled=...  23 us
    pallas_call x1, Pallas kernels, encoder_layer(): pl.pallas_call(kernel, out_shape=jax.ShapeDtypeStruct((tokens, width), jn...  18.5 us
    ppermute x1, waiting for transfers between devices, shifted(): lax.ppermute(value, axis, [(source, source + steps) for source in range(l...  16.6 us
    pallas_call x1, Pallas kernels, kept_conv(): pl.pallas_call(kernel, out_shape=jax.ShapeDtypeStruct((streams, frames, w...  8.93 us
    all_to_all x1, starting transfers between devices, migrate(): lax.all_to_all(jnp.take(state, send_slot, axis=0), 'stream', 0, 0, tiled=...  6.38 us
    pallas_call x1, Pallas kernels, project(): pl.pallas_call(kernel, out_shape=jax.ShapeDtypeStruct((3, tokens, width),...  6.24 us
    another operation x3, local copies, waits for them, and re-layouts  2.87 us
    unnamed x11, local copies, waits for them, and re-layouts  2.17 us
  transfers between devices with their start and end apart: 2, of which 2 were waited for; matrix products, arithmetic and copies ran while one was open for 2% of the time, Pallas kernels for 10%

profile of v7, /device:TPU:1, one launch (start us, length us, event | category | flops | bytes accessed | tf_op | source)
XLA Modules:
  0.0 93.8 jit_solution(14174203277900431004)
XLA Ops:
  0.0 0.8 select_reduce_fusion
  0.8 0.7 compare_select_fusion.9
  1.6 0.1 select_reduce_fusion.1
  1.7 1.6 %copy.29 = bf16[1,16,12,2048]{3,2,1,0:T(8,128)(2,1)S(1)} copy(bf16[1,16,12,2048]{3,1,2,0:T(8,128)(2,1)} %param.19) | data formatting | bytes 1572864 | tf_op args[3]
  3.3 0.1 fusion.9
  3.4 0.5 copy.28
  4.0 0.5 fusion.7
  4.5 0.6 gather_fusion
  5.1 0.0 copy-start.3
  5.1 0.0 copy-start.1
  5.1 1.1 %broadcast_select_fusion = bf16[8,64,1024]{2,1,0:T(8,128)(2,1)} fusion(bf16[8,64,1024]{2,1,0:T(8,128)(2,1)S(1)} %gather_fusion, pred[8]{0:T(512)(128)(4,1)S(1)} %compare_and_fusion), kind=kLoop, calls=%fused_computation.18 | loop fusion | flops 524288 | bytes 2097160 | tf_op jit(solution)/shard_map/jit(_take)/select_n | solution.py:292
  6.3 6.4 %all-to-all-start = ((bf16[8,64,1024]{2,1,0:T(8,128)(2,1)}), bf16[8,64,1024]{2,1,0:T(8,128)(2,1)S(1)}, u32[]{:S(2)}, u32[]{:S(2)}) async-start(bf16[8,64,1024]{2,1,0:T(8,128)(2,1)} %broadcast_select_fusion), calls=%async_computation | async-start | bytes 2097152 | tf_op jit(solution)/shard_map/all_to_all | solution.py:292
  12.7 0.1 dynamic_slice.9
  12.8 1.4 %conditional.4 = (bf16[3,256,1024]{2,1,0:T(8,128)(2,1)}) conditional(s32[]{:T(128)} %convert_element_type.61, () %tuple.30, (bf16[16,16,1024]{2,1,0:T(8,128)(2,1)}, bf16[1,1024,3072]{2,1,0:T(8,128)(2,1)}) %tuple.31), branch_computations={%region_0.1_spmd, %region_1.2_spmd} | conditional | bytes 1572874 | solution.py:328
  12.8 1.3 %broadcast.78 = bf16[3,256,1024]{2,1,0:T(8,128)(2,1)} broadcast(bf16[]{:T(256)} %constant.46.clone), dimensions={} | broadcast | bytes 1572866 | tf_op jit(solution)/shard_map/broadcast.13
  14.2 0.1 compare_select_fusion.8
  14.2 0.1 pad_add_fusion
  14.3 23.0 %all-to-all-done = bf16[8,64,1024]{2,1,0:T(8,128)(2,1)S(1)} async-done(((bf16[8,64,1024]{2,1,0:T(8,128)(2,1)}), bf16[8,64,1024]{2,1,0:T(8,128)(2,1)S(1)}, u32[]{:S(2)}, u32[]{:S(2)}) %all-to-all-start) | async-done | bytes 1048608 | tf_op jit(solution)/shard_map/all_to_all | solution.py:292
  37.3 0.9 conditional.5
  37.3 0.9 broadcast.79
  38.1 1.3 %collective-permute-start = (bf16[16,16,1024]{2,1,0:T(8,128)(2,1)}, bf16[16,16,1024]{2,1,0:T(8,128)(2,1)}, u32[]{:S(2)}, u32[]{:S(2)}) collective-permute-start(bf16[16,16,1024]{2,1,0:T(8,128)(2,1)} %get-tuple-element.105), channel_id=1, source_target_pairs={{0,1},{2,3},{4,5},{6,7},{8,9},{10,11},{12,13},{14,15},{16,17},{18,... | collective-permute-start | bytes 1572872 | tf_op jit(solution)/shard_map/ppermute | solution.py:18
  39.4 9.6 %conditional.6 = (f32[16,16,1024]{2,1,0:T(8,128)}) conditional(s32[]{:T(128)} %convert_element_type.61, (f32[1,31,1024]{2,0,1:T(1,128)S(1)}, s32[32]{0:T(128)S(1)}, bf16[16,64,1024]{2,1,0:T(8,128)(2,1)S(1)}, bf16[8,64,1024]{2,1,0:T(8,128)(2,1)S(1)}) %tuple.55, () %tuple.34), branch_computations={%region_6.7_spmd, %region_7.8_spmd} | conditional | bytes 1048588 | solution.py:332
  39.4 0.7 copy.27
  40.1 8.9 %branch_0_fun.3 = f32[16,16,1024]{2,1,0:T(8,128)} custom-call(s32[32]{0:T(128)S(1)} %get-tuple-element.74.sel_ref, f32[31,1024]{1,0:T(8,128)} %bitcast.38, bf16[16,64,1024]{2,1,0:T(8,128)(2,1)S(1)} %get-tuple-element.76.state_hbm, bf16[8,64,1024]{2,1,0:T(8,128)(2,1)S(1)} %get-tuple-element.77.recv_hbm), custom_call_target="tpu_custom_call" | custom-call | tf_op jit(solution)/shard_map/cond/branch_0_fun/pallas_call | solution.py:97
  49.0 16.6 %collective-permute-done = bf16[16,16,1024]{2,1,0:T(8,128)(2,1)} collective-permute-done((bf16[16,16,1024]{2,1,0:T(8,128)(2,1)}, bf16[16,16,1024]{2,1,0:T(8,128)(2,1)}, u32[]{:S(2)}, u32[]{:S(2)}) %collective-permute-start) | collective-permute-done | bytes 524320 | tf_op jit(solution)/shard_map/ppermute | solution.py:18
  65.6 26.2 %conditional.7 = (bf16[16,16,1024]{2,1,0:T(8,128)(2,1)}) conditional(s32[]{:T(128)} %convert_element_type.61, (bf16[16,16,1024]{2,1,0:T(8,128)(2,1)}, s32[16]{0:T(128)S(1)}, bf16[1,1024,3072]{2,1,0:T(8,128)(2,1)}, s32[32]{0:T(128)S(1)}, f32[31,1024]{1,0:T(8,128)S(1)}, /*index=5*/bf16[1024,1024]{1,0:T(8,128)(2,1)}, ...), branch_computations={%region_8.9_spmd, %region_9.10_spmd} | conditional | flops 512 | bytes 524298 | solution.py:336
  65.6 0.1 fusion.1
  65.7 0.6 reshape.152.klive_ref
  66.3 0.8 reshape.163.rlive_ref
  67.1 6.2 %branch_0_fun.4.qkv_hbm = bf16[3,256,1024]{2,1,0:T(8,128)(2,1)} custom-call(bf16[256,1024]{1,0:T(8,128)(2,1)} %bitcast.5.x_ref, bf16[1024,3072]{1,0:T(8,128)(2,1)} %bitcast.27), custom_call_target="tpu_custom_call" | custom-call | tf_op jit(solution)/shard_map/cond/branch_0_fun/pallas_call | solution.py:230
  73.3 18.5 %branch_0_fun.5 = bf16[256,1024]{1,0:T(8,128)(2,1)} custom-call(s32[32]{0:T(128)S(1)} %get-tuple-element.78.sel_ref, bf16[256,1024]{1,0:T(8,128)(2,1)} %bitcast.5.x_ref, f32[1,256]{1,0:T(1,128)} %reshape.152.klive_ref, f32[256,1]{1,0:T(8,128)} %reshape.163.rlive_ref, f32[31,1024]{1,0:T(8,128)S(1)} %get-tuple-element.81.cw_ref, ...), custom_call_target="tpu_custom_call" | custom-call | tf_op jit(solution)/shard_map/cond/branch_0_fun/pallas_call | solution.py:260
  91.9 1.9 %select_bitcast_fusion = bf16[1,16,16,1024]{3,2,1,0:T(8,128)(2,1)} fusion(bf16[16,16,1024]{2,1,0:T(8,128)(2,1)} %get-tuple-element.105, bf16[16,16,1024]{2,1,0:T(8,128)(2,1)} %get-tuple-element.107, pred[]{:T(512)S(6)} %eq.35), kind=kLoop, calls=%fused_computation.19 | loop fusion | flops 262144 | bytes 1572865 | tf_op jit(solution)/shard_map/broadcast_in_dim | solution.py:339
  (10 shorter events, 0.1 us)
Async XLA Ops:
  0.0 3.4 %copy-start = (bf16[1,16,30,1024]{3,1,2,0:T(8,128)(2,1)S(1)}, bf16[1,16,30,1024]{3,1,2,0:T(8,128)(2,1)}, u32[]{:S(2)}) copy-start(bf16[1,16,30,1024]{3,1,2,0:T(8,128)(2,1)} %param.20) | copy-start | bytes 2949124
  5.1 7.5 %copy-start.3 = (s32[128]{0:T(128)S(1)}, s32[128]{0:T(128)}, u32[]{:S(2)}) copy-start(s32[128]{0:T(128)} %param.17) | copy-start | bytes 1540
  5.1 7.6 %copy-start.1 = (f32[1,31,1024]{2,0,1:T(1,128)S(1)}, f32[1,31,1024]{2,0,1:T(1,128)}, u32[]{:S(2)}) copy-start(f32[1,31,1024]{2,0,1:T(1,128)} %param.23) | copy-start | bytes 380932
  6.3 31.0 %all-to-all-start = ((bf16[8,64,1024]{2,1,0:T(8,128)(2,1)}), bf16[8,64,1024]{2,1,0:T(8,128)(2,1)S(1)}, u32[]{:S(2)}, u32[]{:S(2)}) async-start(bf16[8,64,1024]{2,1,0:T(8,128)(2,1)} %broadcast_select_fusion), calls=%async_computation | async-start | bytes 2097152 | tf_op jit(solution)/shard_map/all_to_all | solution.py:292
  12.8 1.4 %copy-start.2 = (s32[128]{0:T(128)S(1)}, s32[128]{0:T(128)}, u32[]{:S(2)}) copy-start(s32[128]{0:T(128)} %param.18) | copy-start | bytes 1540
  38.1 27.5 %collective-permute-start = (bf16[16,16,1024]{2,1,0:T(8,128)(2,1)}, bf16[16,16,1024]{2,1,0:T(8,128)(2,1)}, u32[]{:S(2)}, u32[]{:S(2)}) collective-permute-start(bf16[16,16,1024]{2,1,0:T(8,128)(2,1)} %get-tuple-element.105), channel_id=1, source_target_pairs={{0,1},{2,3},{4,5},{6,7},{8,9},{10,11},{12,13},{14,15},{16,17},{18,... | collective-permute-start | bytes 1572872 | tf_op jit(solution)/shard_map/ppermute | solution.py:18

commit v8 on v7

--- a/solution.py
+++ b/solution.py
@@ -278,7 +278,7 @@
     return out.reshape(streams, frames, width)
 
 
-def migrate(anchor, own, count, local_count, state):
+def migrate(anchor, own, count, local_count, packed):
     total = anchor.shape[0]
     every_slot = jnp.arange(total, dtype=jnp.int32)
     newpos = jnp.sum(jnp.where(anchor[None, :] == every_slot[:, None], every_slot[None, :], 0),
@@ -289,7 +289,7 @@
     match = target[None, :] == hosts[:, None]
     send_slot = jnp.sum(jnp.where(match, jnp.arange(local_count, dtype=jnp.int32)[None, :], 0),
                         axis=1)
-    recv = lax.all_to_all(jnp.take(state, send_slot, axis=0), "stream", 0, 0, tiled=True)
+    recv = lax.all_to_all(jnp.take(packed, send_slot, axis=0), "stream", 0, 0, tiled=True)
     mine_old = lax.dynamic_slice_in_dim(anchor, own * local_count, local_count)
     source = mine_old // local_count
     staying = source == own
@@ -316,7 +316,13 @@
         jnp.pad(context[:, :, width:], ((0, 0), (0, slot - ctx), (0, 0))),
         jnp.pad(conv_state[0], ((0, 0), (lead, 0), (0, 0))),
     ], axis=1)
-    sel, recv = migrate(anchor, own, count, local_count, state)
+    packed = jnp.concatenate([context[:, :, :width], context[:, :, width:], conv_state[0]], axis=1)
+    sel, recv = migrate(anchor, own, count, local_count, packed)
+    recv = jnp.concatenate([
+        jnp.pad(recv[:, :ctx], ((0, 0), (0, slot - ctx), (0, 0))),
+        jnp.pad(recv[:, ctx:2 * ctx], ((0, 0), (0, slot - ctx), (0, 0))),
+        jnp.pad(recv[:, 2 * ctx:], ((0, 0), (lead, 0), (0, 0))),
+    ], axis=1)
     valid_here = lax.dynamic_slice_in_dim(valid_counts, own * local_count, local_count)
     section_index = lax.axis_index("section")
     layer = functools.partial(encoder_layer, valid_counts=valid_here, sel=sel, state=state,
@@ -333,9 +339,7 @@
                      lambda: kept_conv(sel, state, recv, conv_weight[0], local_count, frames, ctx,
                                        kept))
     inbound = shifted(first, "section", 1)
-    second = lax.cond(on_first, like(new_frames.shape, new_frames.dtype),
-                      lambda: layer(inbound, conv_in=early))
-    result = jnp.where(on_first, first, second)
+    result = lax.cond(on_first, lambda: first, lambda: layer(inbound, conv_in=early))
     return result[None]
 
 

time: 94.2 us -> 95.7 us (1.016)
  waiting for transfers between devices: 39.6 us -> 35.4 us
  local copies, waits for them, and re-layouts: 7.19 us -> 10.7 us
  other arithmetic: 5.48 us -> 7.45 us
    all_to_all x1, waiting for transfers between devices: 23 us -> 18.9 us  [migrate(): lax.all_to_all(jnp.take(packed, send_slot, axis=0), 'stream', 0, 0, tiled...]
    slice x0 -> x2, local copies, waits for them, and re-layouts: none -> 2.16 us  [the longest x1 1.09 us: body(): recv[:, 2 * ctx:]]
    broadcast_in_dim x1 -> x0, other arithmetic: 1.91 us -> none  [body(): return result[None]]
    unnamed x11 -> x21, local copies, waits for them, and re-layouts: 2.17 us -> 3.66 us
    select_n x2, other arithmetic: 1.14 us -> 2.33 us  [migrate(): jnp.take(packed, send_slot, axis=0)]
    another operation x3, local copies, waits for them, and re-layouts: 2.87 us -> 1.72 us
    pad x0 -> x1, other arithmetic: none -> 1.05 us  [body(): jnp.pad(recv[:, :ctx], ((0, 0), (0, slot - ctx), (0, 0)))]
    concatenate x1, other arithmetic: 0.49 us -> 1.5 us  [body(): jnp.concatenate([jnp.pad(context[:, :, :width], ((0, 0), (0, slot - ctx),...]
  transfers between devices with their start and end apart: 2 -> 2, of which waited for: 2 -> 2; matrix products, arithmetic and copies ran while one was open for 2% -> 3% of each run, Pallas kernels for 10% -> 9%
where the time goes in v8:
time: 95.7 us; the launch traced here: 95.2 us
  waiting for transfers between devices  35.4 us (37%)
  Pallas kernels  33.7 us (35%)
  local copies, waits for them, and re-layouts  10.7 us (11%)
  starting transfers between devices  7.66 us (8%)
  other arithmetic  7.45 us (8%)
    all_to_all x1, waiting for transfers between devices, migrate(): lax.all_to_all(jnp.take(packed, send_slot, axis=0), 'stream', 0, 0, tiled...  18.9 us
    pallas_call x1, Pallas kernels, encoder_layer(): pl.pallas_call(kernel, out_shape=jax.ShapeDtypeStruct((tokens, width), jn...  18.5 us
    ppermute x1, waiting for transfers between devices, shifted(): lax.ppermute(value, axis, [(source, source + steps) for source in range(l...  16.5 us
    pallas_call x1, Pallas kernels, kept_conv(): pl.pallas_call(kernel, out_shape=jax.ShapeDtypeStruct((streams, frames, w...  8.96 us
    all_to_all x1, starting transfers between devices, migrate(): lax.all_to_all(jnp.take(packed, send_slot, axis=0), 'stream', 0, 0, tiled...  6.38 us
    pallas_call x1, Pallas kernels, project(): pl.pallas_call(kernel, out_shape=jax.ShapeDtypeStruct((3, tokens, width),...  6.25 us
    unnamed x21, local copies, waits for them, and re-layouts  3.66 us
    select_n x2, other arithmetic, migrate(): jnp.take(packed, send_slot, axis=0)  2.33 us
  transfers between devices with their start and end apart: 2, of which 2 were waited for; matrix products, arithmetic and copies ran while one was open for 3% of the time, Pallas kernels for 9%

profile of v8, /device:TPU:1, one launch (start us, length us, event | category | flops | bytes accessed | tf_op | source)
XLA Modules:
  0.0 95.2 jit_solution(3657251428742920368)
XLA Ops:
  0.0 0.8 select_reduce_fusion
  0.8 0.7 compare_select_fusion.9
  1.7 1.6 %copy.31 = bf16[1,16,12,2048]{3,2,1,0:T(8,128)(2,1)S(1)} copy(bf16[1,16,12,2048]{3,1,2,0:T(8,128)(2,1)} %param.19) | data formatting | bytes 1572864 | tf_op args[3]
  3.5 0.5 copy.30
  4.0 0.2 copy-done.1
  4.3 0.2 copy-done.2
  4.4 0.4 pad_maximum_fusion
  4.8 1.5 %gather_fusion = bf16[8,54,1024]{2,1,0:T(8,128)(2,1)} fusion(bf16[16,54,1024]{2,1,0:T(8,128)(2,1)S(1)} %pad_maximum_fusion, s32[1024]{0:T(1024)S(1)} %pad_clamp_fusion), kind=kCustom, calls=%fused_computation | custom fusion | bytes 1769504 | tf_op jit(solution)/shard_map/jit(_take)/gather | solution.py:292
  6.4 2.3 %broadcast_select_fusion = bf16[8,54,1024]{2,1,0:T(8,128)(2,1)} fusion(bf16[8,54,1024]{2,1,0:T(8,128)(2,1)} %gather_fusion, pred[8]{0:T(512)(128)(4,1)S(1)} %compare_and_fusion), kind=kLoop, calls=%fused_computation.27 | loop fusion | flops 442368 | bytes 1769480 | tf_op jit(solution)/shard_map/jit(_take)/select_n | solution.py:292
  8.7 6.4 %all-to-all-start = ((bf16[8,54,1024]{2,1,0:T(8,128)(2,1)}), bf16[8,54,1024]{2,1,0:T(8,128)(2,1)}, u32[]{:S(2)}, u32[]{:S(2)}) async-start(bf16[8,54,1024]{2,1,0:T(8,128)(2,1)} %broadcast_select_fusion), calls=%async_computation | async-start | bytes 1835008 | tf_op jit(solution)/shard_map/all_to_all | solution.py:292
  15.3 0.2 conditional.4
  15.3 0.2 broadcast.80
  15.5 0.4 copy-done.6
  16.0 0.7 copy-done
  16.7 1.5 %fusion.7 = bf16[16,64,1024]{2,1,0:T(8,128)(2,1)S(1)} fusion(bf16[16,30,1024]{2,1,0:T(8,128)(2,1)S(1)} %bitcast.28, bf16[16,12,1024]{2,1,0:T(8,128)(2,1)} %copy-done.2, bf16[16,12,1024]{2,1,0:T(8,128)(2,1)} %copy-done.1), kind=kLoop, calls=%fused_computation.17 | loop fusion | flops 14680064 | bytes 3866624 | tf_op jit(solution)/shard_map/concatenate | solution.py:314
  18.2 18.9 %all-to-all-done = bf16[8,54,1024]{2,1,0:T(8,128)(2,1)} async-done(((bf16[8,54,1024]{2,1,0:T(8,128)(2,1)}), bf16[8,54,1024]{2,1,0:T(8,128)(2,1)}, u32[]{:S(2)}, u32[]{:S(2)}) %all-to-all-start) | async-done | bytes 884768 | tf_op jit(solution)/shard_map/all_to_all | solution.py:292
  37.2 1.1 %slice.28 = bf16[8,12,1024]{2,1,0:T(8,128)(2,1)S(1)} slice(bf16[8,54,1024]{2,1,0:T(8,128)(2,1)} %all-to-all-done), slice={[0:8], [12:24], [0:1024]} | slice | bytes 393216 | tf_op jit(solution)/shard_map/slice | solution.py:323
  38.2 1.1 %slice.29 = bf16[8,30,1024]{2,1,0:T(8,128)(2,1)S(1)} slice(bf16[8,54,1024]{2,1,0:T(8,128)(2,1)} %all-to-all-done), slice={[0:8], [24:54], [0:1024]} | slice | bytes 983040 | tf_op jit(solution)/shard_map/slice | solution.py:324
  39.3 1.0 %slice_select_fusion = bf16[8,16,1024]{2,1,0:T(8,128)(2,1)S(1)} fusion(bf16[8,54,1024]{2,1,0:T(8,128)(2,1)} %all-to-all-done, pred[16]{0:T(512)(128)(4,1)S(1)} %copy-done.7), kind=kLoop, calls=%fused_computation.28 | loop fusion | flops 131072 | bytes 524304 | tf_op jit(solution)/shard_map/jit(_pad)/pad | solution.py:322
  40.4 0.2 fusion.12
  40.6 0.9 conditional.5
  40.6 0.9 broadcast.81
  41.5 1.3 %collective-permute-start = (bf16[16,16,1024]{2,1,0:T(8,128)(2,1)}, bf16[16,16,1024]{2,1,0:T(8,128)(2,1)}, u32[]{:S(2)}, u32[]{:S(2)}) collective-permute-start(bf16[16,16,1024]{2,1,0:T(8,128)(2,1)} %get-tuple-element.111), channel_id=1, source_target_pairs={{0,1},{2,3},{4,5},{6,7},{8,9},{10,11},{12,13},{14,15},{16,17},{18,... | collective-permute-start | bytes 1572872 | tf_op jit(solution)/shard_map/ppermute | solution.py:18
  42.8 9.7 %conditional.6 = (f32[16,16,1024]{2,1,0:T(8,128)}) conditional(s32[]{:T(128)} %convert_element_type.66, (f32[1,31,1024]{2,0,1:T(1,128)S(1)}, s32[32]{0:T(128)S(1)}, bf16[16,64,1024]{2,1,0:T(8,128)(2,1)S(1)}, bf16[8,64,1024]{2,1,0:T(8,128)(2,1)S(1)}) %tuple.60, () %tuple.36), branch_computations={%region_6.7_spmd, %region_7.8_spmd} | conditional | bytes 1048588 | solution.py:338
  42.8 0.7 copy.29
  43.4 9.0 %branch_0_fun.3 = f32[16,16,1024]{2,1,0:T(8,128)} custom-call(s32[32]{0:T(128)S(1)} %get-tuple-element.77.sel_ref, f32[31,1024]{1,0:T(8,128)} %bitcast.39, bf16[16,64,1024]{2,1,0:T(8,128)(2,1)S(1)} %get-tuple-element.79.state_hbm, bf16[8,64,1024]{2,1,0:T(8,128)(2,1)S(1)} %get-tuple-element.80.recv_hbm), custom_call_target="tpu_custom_call" | custom-call | tf_op jit(solution)/shard_map/cond/branch_0_fun/pallas_call | solution.py:97
  52.4 16.5 %collective-permute-done = bf16[16,16,1024]{2,1,0:T(8,128)(2,1)} collective-permute-done((bf16[16,16,1024]{2,1,0:T(8,128)(2,1)}, bf16[16,16,1024]{2,1,0:T(8,128)(2,1)}, u32[]{:S(2)}, u32[]{:S(2)}) %collective-permute-start) | collective-permute-done | bytes 524320 | tf_op jit(solution)/shard_map/ppermute | solution.py:18
  68.9 26.2 %conditional.7 = (bf16[1,16,16,1024]{3,2,1,0:T(8,128)(2,1)}) conditional(s32[]{:T(128)} %convert_element_type.66, (bf16[16,16,1024]{2,1,0:T(8,128)(2,1)}, s32[16]{0:T(128)S(1)}, bf16[1,1024,3072]{2,1,0:T(8,128)(2,1)}, s32[32]{0:T(128)S(1)}, f32[31,1024]{1,0:T(8,128)S(1)}, /*index=5*/bf16[1024,1024]{1,0:T(8,128)(2,1)}, ...), branch_computations={%region_8.9_spmd, %region_9.10_spmd} | conditional | flops 512 | bytes 1048584 | solution.py:342
  69.0 0.7 reshape.151.klive_ref
  69.7 0.7 reshape.162.rlive_ref
  70.4 6.2 %branch_0_fun.4.qkv_hbm = bf16[3,256,1024]{2,1,0:T(8,128)(2,1)} custom-call(bf16[256,1024]{1,0:T(8,128)(2,1)} %bitcast.5.x_ref, bf16[1024,3072]{1,0:T(8,128)(2,1)} %bitcast.26), custom_call_target="tpu_custom_call" | custom-call | tf_op jit(solution)/shard_map/cond/branch_0_fun/pallas_call | solution.py:230
  76.7 18.5 %branch_0_fun.5 = bf16[256,1024]{1,0:T(8,128)(2,1)} custom-call(s32[32]{0:T(128)S(1)} %get-tuple-element.81.sel_ref, bf16[256,1024]{1,0:T(8,128)(2,1)} %bitcast.5.x_ref, f32[1,256]{1,0:T(1,128)} %reshape.151.klive_ref, f32[256,1]{1,0:T(8,128)} %reshape.162.rlive_ref, f32[31,1024]{1,0:T(8,128)S(1)} %get-tuple-element.84.cw_ref, ...), custom_call_target="tpu_custom_call" | custom-call | tf_op jit(solution)/shard_map/cond/branch_0_fun/pallas_call | solution.py:260
  (24 shorter events, 0.6 us)
Async XLA Ops:
  0.0 3.4 %copy-start.4 = (bf16[1,16,30,1024]{3,1,2,0:T(8,128)(2,1)S(1)}, bf16[1,16,30,1024]{3,1,2,0:T(8,128)(2,1)}, u32[]{:S(2)}) copy-start(bf16[1,16,30,1024]{3,1,2,0:T(8,128)(2,1)} %param.20) | copy-start | bytes 2949124
  3.4 0.8 copy-start.1
  3.5 1.0 %copy-start.2 = (bf16[16,12,1024]{2,1,0:T(8,128)(2,1)}, bf16[16,12,1024]{2,1,0:T(8,128)(2,1)S(1)}, u32[]{:S(2)}) copy-start(bf16[16,12,1024]{2,1,0:T(8,128)(2,1)S(1)} %get-tuple-element.106) | copy-start | bytes 1179652
  6.4 8.7 %copy-start.8 = (s32[128]{0:T(128)S(1)}, s32[128]{0:T(128)}, u32[]{:S(2)}) copy-start(s32[128]{0:T(128)} %param.17) | copy-start | bytes 1540
  6.4 8.8 %copy-start.5 = (f32[1,31,1024]{2,0,1:T(1,128)S(1)}, f32[1,31,1024]{2,0,1:T(1,128)}, u32[]{:S(2)}) copy-start(f32[1,31,1024]{2,0,1:T(1,128)} %param.23) | copy-start | bytes 380932
  6.4 8.8 %copy-start.3 = (bf16[16,16,1024]{2,1,0:T(8,128)(2,1)S(1)}, bf16[16,16,1024]{2,1,0:T(8,128)(2,1)}, u32[]{:S(2)}) copy-start(bf16[16,16,1024]{2,1,0:T(8,128)(2,1)} %param.16) | copy-start | bytes 1572868
  8.7 28.4 %all-to-all-start = ((bf16[8,54,1024]{2,1,0:T(8,128)(2,1)}), bf16[8,54,1024]{2,1,0:T(8,128)(2,1)}, u32[]{:S(2)}, u32[]{:S(2)}) async-start(bf16[8,54,1024]{2,1,0:T(8,128)(2,1)} %broadcast_select_fusion), calls=%async_computation | async-start | bytes 1835008 | tf_op jit(solution)/shard_map/all_to_all | solution.py:292
  15.2 0.7 copy-start.6
  15.5 1.2 %copy-start = (bf16[3,256,1024]{2,1,0:T(8,128)(2,1)}, bf16[3,256,1024]{2,1,0:T(8,128)(2,1)S(1)}, u32[]{:S(2)}) copy-start(bf16[3,256,1024]{2,1,0:T(8,128)(2,1)S(1)} %get-tuple-element.110) | copy-start | bytes 4718596
  16.7 22.6 %copy-start.7 = (pred[16]{0:T(512)(128)(4,1)S(1)}, pred[16]{0:T(512)(128)(4,1)}, u32[]{:S(2)}) copy-start(pred[16]{0:T(512)(128)(4,1)} %constant.60.clone.1) | copy-start | bytes 52
  41.5 27.5 %collective-permute-start = (bf16[16,16,1024]{2,1,0:T(8,128)(2,1)}, bf16[16,16,1024]{2,1,0:T(8,128)(2,1)}, u32[]{:S(2)}, u32[]{:S(2)}) collective-permute-start(bf16[16,16,1024]{2,1,0:T(8,128)(2,1)} %get-tuple-element.111), channel_id=1, source_target_pairs={{0,1},{2,3},{4,5},{6,7},{8,9},{10,11},{12,13},{14,15},{16,17},{18,... | collective-permute-start | bytes 1572872 | tf_op jit(solution)/shard_map/ppermute | solution.py:18

commit v9 on v7

--- a/solution.py
+++ b/solution.py
@@ -289,14 +289,18 @@
     match = target[None, :] == hosts[:, None]
     send_slot = jnp.sum(jnp.where(match, jnp.arange(local_count, dtype=jnp.int32)[None, :], 0),
                         axis=1)
-    recv = lax.all_to_all(jnp.take(state, send_slot, axis=0), "stream", 0, 0, tiled=True)
+    send = jnp.take(state, jnp.clip(send_slot, 0, local_count - 1), axis=0)
     mine_old = lax.dynamic_slice_in_dim(anchor, own * local_count, local_count)
     source = mine_old // local_count
     staying = source == own
     local_idx = jnp.clip(mine_old - own * local_count, 0, local_count - 1)
     recv_idx = jnp.clip(source, 0, count - 1)
     sel = jnp.concatenate([jnp.where(staying, 0, 1), jnp.where(staying, local_idx, recv_idx)])
-    return sel.astype(jnp.int32), recv
+    return sel.astype(jnp.int32), send
+
+
+def exchange(send):
+    return lax.all_to_all(send, "stream", 0, 0, tiled=True)
 
 
 def body(
@@ -316,26 +320,39 @@
         jnp.pad(context[:, :, width:], ((0, 0), (0, slot - ctx), (0, 0))),
         jnp.pad(conv_state[0], ((0, 0), (lead, 0), (0, 0))),
     ], axis=1)
-    sel, recv = migrate(anchor, own, count, local_count, state)
+    sel, send = migrate(anchor, own, count, local_count, state)
     valid_here = lax.dynamic_slice_in_dim(valid_counts, own * local_count, local_count)
     section_index = lax.axis_index("section")
     layer = functools.partial(encoder_layer, valid_counts=valid_here, sel=sel, state=state,
-                              recv=recv, qkv_weight=qkv_weight[0], out_weight=out_weight[0],
+                              qkv_weight=qkv_weight[0], out_weight=out_weight[0],
                               conv_weight=conv_weight[0], ctx=ctx, kept_real=kept)
     on_first = section_index == 0
     frames = new_frames.shape[1]
     like = lambda shape, dtype: (lambda: jnp.zeros(shape, dtype))
-    projected = lax.cond(on_first, lambda: project(new_frames, qkv_weight[0]),
-                         like((3, local_count * frames, width), jnp.bfloat16))
-    first = lax.cond(on_first, lambda: layer(new_frames, projected=projected),
+
+    def early_branch():
+        return exchange(send), project(new_frames, qkv_weight[0])
+
+    recv0, projected = lax.cond(
+        on_first, early_branch,
+        lambda: (jnp.zeros_like(send), jnp.zeros((3, local_count * frames, width), jnp.bfloat16)))
+    token = shifted(recv0[:1, :8], "section", 1)
+    zero = jnp.where(on_first, 0.0, jnp.sum(token.astype(jnp.float32)) * 0.0)
+    sel0 = sel + zero.astype(sel.dtype)
+    first = lax.cond(on_first,
+                     lambda: layer(new_frames, sel=sel0, recv=recv0, projected=projected),
                      like(new_frames.shape, new_frames.dtype))
-    early = lax.cond(on_first, like(new_frames.shape, jnp.float32),
-                     lambda: kept_conv(sel, state, recv, conv_weight[0], local_count, frames, ctx,
-                                       kept))
+
+    def late_branch():
+        recv1 = exchange(send + zero.astype(send.dtype))
+        return recv1, kept_conv(sel, state, recv1, conv_weight[0], local_count, frames, ctx, kept)
+
+    recv1, early = lax.cond(on_first, lambda: (jnp.zeros_like(send),
+                                               jnp.zeros(new_frames.shape, jnp.float32)),
+                            late_branch)
     inbound = shifted(first, "section", 1)
-    second = lax.cond(on_first, like(new_frames.shape, new_frames.dtype),
-                      lambda: layer(inbound, conv_in=early))
-    result = jnp.where(on_first, first, second)
+    result = lax.cond(on_first, lambda: first,
+                      lambda: layer(inbound, recv=recv1, conv_in=early))
     return result[None]
 
 

time: 94.2 us -> 93.3 us (level)
  waiting for transfers between devices: 39.6 us -> 36 us
  local copies, waits for them, and re-layouts: 7.19 us -> 10 us
  starting transfers between devices: 7.66 us -> 6.12 us
    all_to_all x1, waiting for transfers between devices: 23 us -> 14.2 us  [exchange(): return lax.all_to_all(send, 'stream', 0, 0, tiled=True)]
    ppermute x1 -> x2, waiting for transfers between devices: 16.6 us -> 21.8 us  [shifted(): lax.ppermute(value, axis, [(source, source + steps) for source in range(l...]
    all_to_all x1, starting transfers between devices: 6.38 us -> 3.56 us  [exchange(): return lax.all_to_all(send, 'stream', 0, 0, tiled=True)]
    broadcast_in_dim x1 -> x0, other arithmetic: 1.91 us -> none  [body(): return result[None]]
    ppermute x1 -> x2, starting transfers between devices: 1.28 us -> 2.56 us  [shifted(): lax.ppermute(value, axis, [(source, source + steps) for source in range(l...]
    another operation x3 -> x4, local copies, waits for them, and re-layouts: 2.87 us -> 4.01 us
    add x0 -> x1, other arithmetic: none -> 1.04 us  [late_branch(): recv1 = exchange(send + zero.astype(send.dtype))]
    gather x1, local copies, waits for them, and re-layouts: 0.61 us -> 1.58 us  [migrate(): send = jnp.take(state, jnp.clip(send_slot, 0, local_count - 1), axis=0)]
  transfers between devices with their start and end apart: 2 -> 3, of which waited for: 2 -> 2; matrix products, arithmetic and copies ran while one was open for 2% -> 2% of each run, Pallas kernels for 10% -> 10%
where the time goes in v9:
time: 93.3 us; the launch traced here: 92.8 us
  waiting for transfers between devices  36 us (39%)
  Pallas kernels  33.7 us (36%)
  local copies, waits for them, and re-layouts  10 us (11%)
  other arithmetic  6.13 us (7%)
  starting transfers between devices  6.12 us (7%)
    ppermute x2, waiting for transfers between devices, shifted(): lax.ppermute(value, axis, [(source, source + steps) for source in range(l...  21.8 us
    pallas_call x1, Pallas kernels, encoder_layer(): pl.pallas_call(kernel, out_shape=jax.ShapeDtypeStruct((tokens, width), jn...  18.5 us
    all_to_all x1, waiting for transfers between devices, exchange(): return lax.all_to_all(send, 'stream', 0, 0, tiled=True)  14.2 us
    pallas_call x1, Pallas kernels, kept_conv(): pl.pallas_call(kernel, out_shape=jax.ShapeDtypeStruct((streams, frames, w...  8.93 us
    pallas_call x1, Pallas kernels, project(): pl.pallas_call(kernel, out_shape=jax.ShapeDtypeStruct((3, tokens, width),...  6.24 us
    another operation x4, local copies, waits for them, and re-layouts  4.01 us
    all_to_all x1, starting transfers between devices, exchange(): return lax.all_to_all(send, 'stream', 0, 0, tiled=True)  3.56 us
    ppermute x2, starting transfers between devices, shifted(): lax.ppermute(value, axis, [(source, source + steps) for source in range(l...  2.56 us
  transfers between devices with their start and end apart: 3, of which 2 were waited for; matrix products, arithmetic and copies ran while one was open for 2% of the time, Pallas kernels for 10%

profile of v9, /device:TPU:1, one launch (start us, length us, event | category | flops | bytes accessed | tf_op | source)
XLA Modules:
  0.0 92.8 jit_solution(2216063053778745917)
XLA Ops:
  0.0 0.8 select_reduce_fusion
  0.8 0.7 compare_select_fusion.9
  1.6 0.7 and_select_fusion
  2.3 0.1 select_reduce_fusion.1
  2.5 1.6 %copy.31 = bf16[1,16,12,2048]{3,2,1,0:T(8,128)(2,1)S(1)} copy(bf16[1,16,12,2048]{3,1,2,0:T(8,128)(2,1)} %param.19) | data formatting | bytes 1572864 | tf_op args[3]
  4.1 0.1 fusion.9
  4.2 0.5 copy.30
  4.7 0.5 fusion.7
  5.2 1.6 %gather_fusion = bf16[8,64,1024]{2,1,0:T(8,128)(2,1)} fusion(bf16[16,64,1024]{2,1,0:T(8,128)(2,1)S(1)} %fusion.7, s32[1024]{0:T(1024)S(1)} %pad_clamp_fusion), kind=kCustom, calls=%fused_computation | custom fusion | bytes 2097184 | tf_op jit(solution)/shard_map/jit(_take)/gather | solution.py:292
  6.8 1.4 %broadcast_select_fusion = bf16[8,64,1024]{2,1,0:T(8,128)(2,1)S(1)} fusion(bf16[8,64,1024]{2,1,0:T(8,128)(2,1)} %gather_fusion, pred[8]{0:T(512)(128)(4,1)S(1)} %compare_and_fusion), kind=kLoop, calls=%fused_computation.20 | loop fusion | flops 524288 | bytes 2097160 | tf_op jit(solution)/shard_map/jit(_take)/select_n | solution.py:292
  8.2 2.5 %conditional.4 = (bf16[8,64,1024]{2,1,0:T(8,128)(2,1)}, bf16[3,256,1024]{2,1,0:T(8,128)(2,1)}) conditional(s32[]{:T(128)} %convert_element_type.70, () %tuple.36, (bf16[8,64,1024]{2,1,0:T(8,128)(2,1)S(1)}, bf16[16,16,1024]{2,1,0:T(8,128)(2,1)}, bf16[1,1024,3072]{2,1,0:T(8,128)(2,1)}) %tuple.37), branch_computations={%region_2.3_spmd, %region_3.4_spmd} | conditional | bytes 3145776 | solution.py:336
  8.2 1.1 %broadcast.102 = bf16[8,64,1024]{2,1,0:T(8,128)(2,1)} broadcast(bf16[]{:T(256)} %constant.48.clone), dimensions={} | broadcast | bytes 1048578 | tf_op jit(solution)/shard_map/broadcast.15
  9.4 1.3 %broadcast.103 = bf16[3,256,1024]{2,1,0:T(8,128)(2,1)} broadcast(bf16[]{:T(256)} %constant.48.clone), dimensions={} | broadcast | bytes 1572866 | tf_op jit(solution)/shard_map/broadcast.14
  10.7 0.7 slice.11
  11.4 1.3 %collective-permute-start = (bf16[1,8,1024]{2,1,0:T(8,128)(2,1)S(1)}, bf16[1,8,1024]{2,1,0:T(8,128)(2,1)S(1)}, u32[]{:S(2)}, u32[]{:S(2)}) collective-permute-start(bf16[1,8,1024]{2,1,0:T(8,128)(2,1)S(1)} %slice.11), channel_id=1, source_target_pairs={{0,1},{2,3},{4,5},{6,7},{8,9},{10,11},{12,13},{14,15},{16,17},{18,... | collective-permute-start | bytes 49160 | tf_op jit(solution)/shard_map/ppermute | solution.py:18
  12.7 0.1 pad_add_fusion
  12.9 21.8 %collective-permute-done = bf16[1,8,1024]{2,1,0:T(8,128)(2,1)S(1)} collective-permute-done((bf16[1,8,1024]{2,1,0:T(8,128)(2,1)S(1)}, bf16[1,8,1024]{2,1,0:T(8,128)(2,1)S(1)}, u32[]{:S(2)}, u32[]{:S(2)}) %collective-permute-start) | collective-permute-done | bytes 16416 | tf_op jit(solution)/shard_map/ppermute | solution.py:18
  34.7 0.6 convert_reduce_fusion
  36.0 0.9 conditional.5
  36.0 0.9 broadcast.104
  36.8 1.3 %collective-permute-start.1 = (bf16[16,16,1024]{2,1,0:T(8,128)(2,1)}, bf16[16,16,1024]{2,1,0:T(8,128)(2,1)}, u32[]{:S(2)}, u32[]{:S(2)}) collective-permute-start(bf16[16,16,1024]{2,1,0:T(8,128)(2,1)} %get-tuple-element.133), channel_id=1, source_target_pairs={{0,1},{2,3},{4,5},{6,7},{8,9},{10,11},{12,13},{14,15},{16,17},{18,... | collective-permute-start | bytes 1572872 | tf_op jit(solution)/shard_map/ppermute | solution.py:18
  38.1 28.5 %conditional.6 = (bf16[8,64,1024]{2,1,0:T(8,128)(2,1)S(1)}, f32[16,16,1024]{2,1,0:T(8,128)}) conditional(s32[]{:T(128)} %convert_element_type.70, (f32[]{:T(128)}, bf16[8,64,1024]{2,1,0:T(8,128)(2,1)S(1)}, f32[1,31,1024]{2,0,1:T(1,128)S(1)}, s32[32]{0:T(128)S(1)}, bf16[16,64,1024]{2,1,0:T(8,128)(2,1)S(1)}) %tuple.62, () %tuple.40), branch_computations={%region_7.8_spmd, %region_8.9_spmd} | conditional | flops 524289 | bytes 5496888 | solution.py:350
  38.2 1.0 %broadcast_add_fusion.1 = bf16[8,64,1024]{2,1,0:T(8,128)(2,1)} fusion(bf16[8,64,1024]{2,1,0:T(8,128)(2,1)S(1)} %get-tuple-element.76, bf16[]{:T(256)S(6)} %convert_element_type.62), kind=kLoop, calls=%fused_computation.4 | loop fusion | flops 524288 | bytes 2097154 | tf_op jit(solution)/shard_map/cond/branch_0_fun/add | solution.py:347
  39.2 3.6 %all-to-all-start.1 = ((bf16[8,64,1024]{2,1,0:T(8,128)(2,1)}), bf16[8,64,1024]{2,1,0:T(8,128)(2,1)S(1)}, u32[]{:S(2)}, u32[]{:S(2)}) async-start(bf16[8,64,1024]{2,1,0:T(8,128)(2,1)} %broadcast_add_fusion.1), calls=%async_computation.1 | async-start | bytes 2097152 | tf_op jit(solution)/shard_map/cond/branch_0_fun/all_to_all | solution.py:303
  42.8 0.7 copy.29
  43.4 14.2 %all-to-all-done.1.recv_hbm = bf16[8,64,1024]{2,1,0:T(8,128)(2,1)S(1)} async-done(((bf16[8,64,1024]{2,1,0:T(8,128)(2,1)}), bf16[8,64,1024]{2,1,0:T(8,128)(2,1)S(1)}, u32[]{:S(2)}, u32[]{:S(2)}) %all-to-all-start.1) | async-done | bytes 1048608 | tf_op jit(solution)/shard_map/cond/branch_0_fun/all_to_all | solution.py:303
  57.7 8.9 %branch_0_fun.3 = f32[16,16,1024]{2,1,0:T(8,128)} custom-call(s32[32]{0:T(128)S(1)} %get-tuple-element.78.sel_ref, f32[31,1024]{1,0:T(8,128)} %bitcast.38, bf16[16,64,1024]{2,1,0:T(8,128)(2,1)S(1)} %get-tuple-element.80.state_hbm, bf16[8,64,1024]{2,1,0:T(8,128)(2,1)S(1)} %all-to-all-done.1.recv_hbm), custom_call_target="tpu_custom_call" | custom-call | tf_op jit(solution)/shard_map/cond/branch_0_fun/pallas_call | solution.py:97
  66.6 26.2 %conditional.7 = (bf16[1,16,16,1024]{3,2,1,0:T(8,128)(2,1)}) conditional(s32[]{:T(128)} %convert_element_type.70, (bf16[16,16,1024]{2,1,0:T(8,128)(2,1)}, s32[16]{0:T(128)S(1)}, bf16[1,1024,3072]{2,1,0:T(8,128)(2,1)}, s32[32]{0:T(128)S(1)}, f32[31,1024]{1,0:T(8,128)S(1)}, /*index=5*/bf16[1024,1024]{1,0:T(8,128)(2,1)}, ...), branch_computations={%region_9.10_spmd, %region_10.11_spmd} | conditional | flops 512 | bytes 1048584 | solution.py:354
  66.7 0.6 reshape.157.klive_ref
  67.3 0.8 reshape.168.rlive_ref
  68.1 6.2 %branch_0_fun.4.qkv_hbm = bf16[3,256,1024]{2,1,0:T(8,128)(2,1)} custom-call(bf16[256,1024]{1,0:T(8,128)(2,1)} %bitcast.5.x_ref, bf16[1024,3072]{1,0:T(8,128)(2,1)} %bitcast.26), custom_call_target="tpu_custom_call" | custom-call | tf_op jit(solution)/shard_map/cond/branch_0_fun/pallas_call | solution.py:230
  74.3 18.5 %branch_0_fun.5 = bf16[256,1024]{1,0:T(8,128)(2,1)} custom-call(s32[32]{0:T(128)S(1)} %get-tuple-element.81.sel_ref, bf16[256,1024]{1,0:T(8,128)(2,1)} %bitcast.5.x_ref, f32[1,256]{1,0:T(1,128)} %reshape.157.klive_ref, f32[256,1]{1,0:T(8,128)} %reshape.168.rlive_ref, f32[31,1024]{1,0:T(8,128)S(1)} %get-tuple-element.84.cw_ref, ...), custom_call_target="tpu_custom_call" | custom-call | tf_op jit(solution)/shard_map/cond/branch_0_fun/pallas_call | solution.py:260
  (13 shorter events, 0.2 us)
Async XLA Ops:
  0.0 4.2 %copy-start = (bf16[1,16,30,1024]{3,1,2,0:T(8,128)(2,1)S(1)}, bf16[1,16,30,1024]{3,1,2,0:T(8,128)(2,1)}, u32[]{:S(2)}) copy-start(bf16[1,16,30,1024]{3,1,2,0:T(8,128)(2,1)} %param.20) | copy-start | bytes 2949124
  8.2 4.6 %copy-start.2 = (s32[128]{0:T(128)S(1)}, s32[128]{0:T(128)}, u32[]{:S(2)}) copy-start(s32[128]{0:T(128)} %param.17) | copy-start | bytes 1540
  8.2 4.6 %copy-start.1 = (f32[1,31,1024]{2,0,1:T(1,128)S(1)}, f32[1,31,1024]{2,0,1:T(1,128)}, u32[]{:S(2)}) copy-start(f32[1,31,1024]{2,0,1:T(1,128)} %param.23) | copy-start | bytes 380932
  11.4 23.3 %collective-permute-start = (bf16[1,8,1024]{2,1,0:T(8,128)(2,1)S(1)}, bf16[1,8,1024]{2,1,0:T(8,128)(2,1)S(1)}, u32[]{:S(2)}, u32[]{:S(2)}) collective-permute-start(bf16[1,8,1024]{2,1,0:T(8,128)(2,1)S(1)} %slice.11), channel_id=1, source_target_pairs={{0,1},{2,3},{4,5},{6,7},{8,9},{10,11},{12,13},{14,15},{16,17},{18,... | collective-permute-start | bytes 49160 | tf_op jit(solution)/shard_map/ppermute | solution.py:18
  36.8 29.8 %collective-permute-start.1 = (bf16[16,16,1024]{2,1,0:T(8,128)(2,1)}, bf16[16,16,1024]{2,1,0:T(8,128)(2,1)}, u32[]{:S(2)}, u32[]{:S(2)}) collective-permute-start(bf16[16,16,1024]{2,1,0:T(8,128)(2,1)} %get-tuple-element.133), channel_id=1, source_target_pairs={{0,1},{2,3},{4,5},{6,7},{8,9},{10,11},{12,13},{14,15},{16,17},{18,... | collective-permute-start | bytes 1572872 | tf_op jit(solution)/shard_map/ppermute | solution.py:18
  39.2 18.5 %all-to-all-start.1 = ((bf16[8,64,1024]{2,1,0:T(8,128)(2,1)}), bf16[8,64,1024]{2,1,0:T(8,128)(2,1)S(1)}, u32[]{:S(2)}, u32[]{:S(2)}) async-start(bf16[8,64,1024]{2,1,0:T(8,128)(2,1)} %broadcast_add_fusion.1), calls=%async_computation.1 | async-start | bytes 2097152 | tf_op jit(solution)/shard_map/cond/branch_0_fun/all_to_all | solution.py:303

commit v10 on v9

--- a/solution.py
+++ b/solution.py
@@ -289,7 +289,7 @@
     match = target[None, :] == hosts[:, None]
     send_slot = jnp.sum(jnp.where(match, jnp.arange(local_count, dtype=jnp.int32)[None, :], 0),
                         axis=1)
-    send = jnp.take(state, jnp.clip(send_slot, 0, local_count - 1), axis=0)
+    send = jnp.take(state, jnp.clip(send_slot, 0, local_count - 1), axis=0, mode="clip")
     mine_old = lax.dynamic_slice_in_dim(anchor, own * local_count, local_count)
     source = mine_old // local_count
     staying = source == own
@@ -343,16 +343,10 @@
                      lambda: layer(new_frames, sel=sel0, recv=recv0, projected=projected),
                      like(new_frames.shape, new_frames.dtype))
 
-    def late_branch():
-        recv1 = exchange(send + zero.astype(send.dtype))
-        return recv1, kept_conv(sel, state, recv1, conv_weight[0], local_count, frames, ctx, kept)
-
-    recv1, early = lax.cond(on_first, lambda: (jnp.zeros_like(send),
-                                               jnp.zeros(new_frames.shape, jnp.float32)),
-                            late_branch)
+    recv1 = lax.cond(on_first, lambda: jnp.zeros_like(send),
+                     lambda: exchange(send + zero.astype(send.dtype)))
     inbound = shifted(first, "section", 1)
-    result = lax.cond(on_first, lambda: first,
-                      lambda: layer(inbound, recv=recv1, conv_in=early))
+    result = lax.cond(on_first, lambda: first, lambda: layer(inbound, recv=recv1))
     return result[None]
 
 

time: 93.3 us -> 91.3 us (0.979)
  blocking collectives: 0 us -> 17.5 us
  waiting for transfers between devices: 36 us -> 27.8 us
  Pallas kernels: 33.7 us -> 28 us
  starting transfers between devices: 6.12 us -> 2.56 us
  other arithmetic: 6.13 us -> 4.77 us
    all_to_all x0 -> x1, blocking collectives: none -> 17.5 us  [exchange(): return lax.all_to_all(send, 'stream', 0, 0, tiled=True)]
    all_to_all x1 -> x0, waiting for transfers between devices: 14.2 us -> none  [exchange(): return lax.all_to_all(send, 'stream', 0, 0, tiled=True)]
    pallas_call x1 -> x0, Pallas kernels: 8.93 us -> none  [kept_conv(): pl.pallas_call(kernel, out_shape=jax.ShapeDtypeStruct((streams, frames, w...]
    ppermute x2, waiting for transfers between devices: 21.8 us -> 27.8 us  [shifted(): lax.ppermute(value, axis, [(source, source + steps) for source in range(l...]
    all_to_all x1 -> x0, starting transfers between devices: 3.56 us -> none  [exchange(): return lax.all_to_all(send, 'stream', 0, 0, tiled=True)]
    pallas_call x1, Pallas kernels: 18.5 us -> 21.7 us  [encoder_layer(): pl.pallas_call(kernel, out_shape=jax.ShapeDtypeStruct((tokens, width), jn...]
    select_n x2 -> x0, other arithmetic: 1.39 us -> none  [migrate(): send = jnp.take(state, jnp.clip(send_slot, 0, local_count - 1), axis=0)]
    concatenate x1, other arithmetic: 0.49 us -> 1.49 us  [body(): jnp.concatenate([jnp.pad(context[:, :, :width], ((0, 0), (0, slot - ctx),...]
  transfers between devices with their start and end apart: 3 -> 2, of which waited for: 2 -> 2; matrix products, arithmetic and copies ran while one was open for 2% -> 0% of each run, Pallas kernels for 10% -> 0%
where the time goes in v10:
time: 91.3 us; the launch traced here: 90.8 us
  Pallas kernels  28 us (31%)
  waiting for transfers between devices  27.8 us (30%)
  blocking collectives  17.5 us (19%)
  local copies, waits for them, and re-layouts  9.37 us (10%)
  other arithmetic  4.77 us (5%)
  starting transfers between devices  2.56 us (3%)
    ppermute x2, waiting for transfers between devices, shifted(): lax.ppermute(value, axis, [(source, source + steps) for source in range(l...  27.8 us
    pallas_call x1, Pallas kernels, encoder_layer(): pl.pallas_call(kernel, out_shape=jax.ShapeDtypeStruct((tokens, width), jn...  21.7 us
    all_to_all x1, blocking collectives, exchange(): return lax.all_to_all(send, 'stream', 0, 0, tiled=True)  17.5 us
    pallas_call x1, Pallas kernels, project(): pl.pallas_call(kernel, out_shape=jax.ShapeDtypeStruct((3, tokens, width),...  6.24 us
    another operation x3, local copies, waits for them, and re-layouts  3.3 us
    ppermute x2, starting transfers between devices, shifted(): lax.ppermute(value, axis, [(source, source + steps) for source in range(l...  2.56 us
    unnamed x9, local copies, waits for them, and re-layouts  2.17 us
  transfers between devices with their start and end apart: 2, of which 2 were waited for; matrix products, arithmetic and copies ran while one was open for 0% of the time, Pallas kernels for 0%

profile of v10, /device:TPU:1, one launch (start us, length us, event | category | flops | bytes accessed | tf_op | source)
XLA Modules:
  0.0 90.8 jit_solution(707087706446157807)
XLA Ops:
  0.0 0.8 select_reduce_fusion
  0.8 0.7 compare_select_fusion.7
  1.6 0.7 and_select_fusion
  2.3 0.1 select_reduce_fusion.1
  2.5 1.6 %copy.26 = bf16[1,16,12,2048]{3,2,1,0:T(8,128)(2,1)S(1)} copy(bf16[1,16,12,2048]{3,1,2,0:T(8,128)(2,1)} %param.19) | data formatting | bytes 1572864 | tf_op args[3]
  4.1 1.1 %fusion.8 = (bf16[16,12,1024]{2,1,0:T(8,128)(2,1)}, bf16[16,12,1024]{2,1,0:T(8,128)(2,1)}) fusion(bf16[16,12,2048]{2,1,0:T(8,128)(2,1)S(1)} %bitcast.22), kind=kLoop, calls=%fused_computation.38 | loop fusion | bytes 1572864 | tf_op jit(solution)/shard_map/slice | solution.py:319
  5.1 0.5 copy.25
  5.7 1.5 %fusion.7 = bf16[16,64,1024]{2,1,0:T(8,128)(2,1)S(1)} fusion(bf16[16,30,1024]{2,1,0:T(8,128)(2,1)S(1)} %bitcast.23, bf16[16,12,1024]{2,1,0:T(8,128)(2,1)} %get-tuple-element.92, bf16[16,12,1024]{2,1,0:T(8,128)(2,1)} %get-tuple-element.91), kind=kLoop, calls=%fused_computation.16 | loop fusion | flops 14680064 | bytes 3866624 | tf_op jit(solution)/shard_map/concatenate | solution.py:318
  7.2 0.6 gather_fusion
  7.8 0.0 copy-start.1
  7.8 2.5 %conditional.4 = (bf16[8,64,1024]{2,1,0:T(8,128)(2,1)}, bf16[3,256,1024]{2,1,0:T(8,128)(2,1)}) conditional(s32[]{:T(128)} %convert_element_type.70, () %tuple.34, (bf16[8,64,1024]{2,1,0:T(8,128)(2,1)S(1)}, bf16[16,16,1024]{2,1,0:T(8,128)(2,1)}, bf16[1,1024,3072]{2,1,0:T(8,128)(2,1)}) %tuple.35), branch_computations={%region_2.3_spmd, %region_3.4_spmd} | conditional | bytes 3145776 | solution.py:336
  7.8 1.3 %broadcast.65 = bf16[3,256,1024]{2,1,0:T(8,128)(2,1)} broadcast(bf16[]{:T(256)} %constant.35.clone), dimensions={} | broadcast | bytes 1572866 | tf_op jit(solution)/shard_map/broadcast.6
  9.2 1.1 %broadcast.64 = bf16[8,64,1024]{2,1,0:T(8,128)(2,1)} broadcast(bf16[]{:T(256)} %constant.35.clone), dimensions={} | broadcast | bytes 1048578 | tf_op jit(solution)/shard_map/broadcast.7
  10.3 0.7 slice.11
  11.0 1.3 %collective-permute-start = (bf16[1,8,1024]{2,1,0:T(8,128)(2,1)S(1)}, bf16[1,8,1024]{2,1,0:T(8,128)(2,1)S(1)}, u32[]{:S(2)}, u32[]{:S(2)}) collective-permute-start(bf16[1,8,1024]{2,1,0:T(8,128)(2,1)S(1)} %slice.11), channel_id=1, source_target_pairs={{0,1},{2,3},{4,5},{6,7},{8,9},{10,11},{12,13},{14,15},{16,17},{18,... | collective-permute-start | bytes 49160 | tf_op jit(solution)/shard_map/ppermute | solution.py:18
  12.3 0.1 pad_add_fusion
  12.4 0.1 dynamic_slice.9
  12.5 21.8 %collective-permute-done = bf16[1,8,1024]{2,1,0:T(8,128)(2,1)S(1)} collective-permute-done((bf16[1,8,1024]{2,1,0:T(8,128)(2,1)S(1)}, bf16[1,8,1024]{2,1,0:T(8,128)(2,1)S(1)}, u32[]{:S(2)}, u32[]{:S(2)}) %collective-permute-start) | collective-permute-done | bytes 16416 | tf_op jit(solution)/shard_map/ppermute | solution.py:18
  34.3 0.6 convert_reduce_fusion
  35.5 0.9 conditional.5
  35.6 0.9 broadcast.66
  36.4 1.3 %collective-permute-start.1 = (bf16[16,16,1024]{2,1,0:T(8,128)(2,1)}, bf16[16,16,1024]{2,1,0:T(8,128)(2,1)}, u32[]{:S(2)}, u32[]{:S(2)}) collective-permute-start(bf16[16,16,1024]{2,1,0:T(8,128)(2,1)} %get-tuple-element.101), channel_id=1, source_target_pairs={{0,1},{2,3},{4,5},{6,7},{8,9},{10,11},{12,13},{14,15},{16,17},{18,... | collective-permute-start | bytes 1572872 | tf_op jit(solution)/shard_map/ppermute | solution.py:18
  37.7 17.6 %conditional.6 = (bf16[8,64,1024]{2,1,0:T(8,128)(2,1)S(1)}) conditional(s32[]{:T(128)} %convert_element_type.70, (f32[]{:T(128)}, bf16[8,64,1024]{2,1,0:T(8,128)(2,1)S(1)}) %tuple.37, () %tuple.38), branch_computations={%region_7.8_spmd, %region_8.9_spmd} | conditional | flops 524289 | bytes 4194320 | solution.py:346
  37.7 0.1 broadcast_add_fusion.1
  37.8 17.5 %all_to_all.8 = bf16[8,64,1024]{2,1,0:T(8,128)(2,1)S(1)} all-to-all(bf16[8,64,1024]{2,1,0:T(8,128)(2,1)S(1)} %broadcast_add_fusion.1), channel_id=1, replica_groups=mesh['groups'=2,'stream'=8,'section'=2] {'stream'}, dimensions={0} | all-to-all | bytes 2097152 | tf_op jit(solution)/shard_map/cond/branch_0_fun/all_to_all | solution.py:303
  55.3 6.0 %collective-permute-done.1 = bf16[16,16,1024]{2,1,0:T(8,128)(2,1)} collective-permute-done((bf16[16,16,1024]{2,1,0:T(8,128)(2,1)}, bf16[16,16,1024]{2,1,0:T(8,128)(2,1)}, u32[]{:S(2)}, u32[]{:S(2)}) %collective-permute-start.1) | collective-permute-done | bytes 524320 | tf_op jit(solution)/shard_map/ppermute | solution.py:18
  61.3 29.5 %conditional.7 = (bf16[1,16,16,1024]{3,2,1,0:T(8,128)(2,1)}) conditional(s32[]{:T(128)} %convert_element_type.70, (bf16[16,16,1024]{2,1,0:T(8,128)(2,1)}, s32[16]{0:T(128)S(1)}, bf16[1,1024,3072]{2,1,0:T(8,128)(2,1)}, s32[32]{0:T(128)S(1)}, f32[31,1024]{1,0:T(8,128)S(1)}, /*index=5*/bf16[1024,1024]{1,0:T(8,128)(2,1)}, ...), branch_computations={%region_9.10_spmd, %region_10.11_spmd} | conditional | flops 512 | bytes 1048584 | solution.py:349
  61.3 6.2 %branch_0_fun.2.qkv_hbm = bf16[3,256,1024]{2,1,0:T(8,128)(2,1)} custom-call(bf16[256,1024]{1,0:T(8,128)(2,1)} %bitcast.4.x_ref, bf16[1024,3072]{1,0:T(8,128)(2,1)} %bitcast.19), custom_call_target="tpu_custom_call" | custom-call | tf_op jit(solution)/shard_map/cond/branch_0_fun/pallas_call | solution.py:230
  67.6 0.1 fusion.1
  67.6 0.8 reshape.155.rlive_ref
  68.4 0.7 reshape.143.klive_ref
  69.1 21.7 %branch_0_fun.3 = bf16[256,1024]{1,0:T(8,128)(2,1)} custom-call(s32[32]{0:T(128)S(1)} %get-tuple-element.73.sel_ref, bf16[256,1024]{1,0:T(8,128)(2,1)} %bitcast.4.x_ref, f32[1,256]{1,0:T(1,128)} %reshape.143.klive_ref, f32[256,1]{1,0:T(8,128)} %reshape.155.rlive_ref, f32[31,1024]{1,0:T(8,128)S(1)} %get-tuple-element.76.cw_ref, ...), custom_call_target="tpu_custom_call" | custom-call | tf_op jit(solution)/shard_map/cond/branch_0_fun/pallas_call | solution.py:260
  (8 shorter events, 0.1 us)
Async XLA Ops:
  0.0 5.1 %copy-start = (bf16[1,16,30,1024]{3,1,2,0:T(8,128)(2,1)S(1)}, bf16[1,16,30,1024]{3,1,2,0:T(8,128)(2,1)}, u32[]{:S(2)}) copy-start(bf16[1,16,30,1024]{3,1,2,0:T(8,128)(2,1)} %param.20) | copy-start | bytes 2949124
  7.8 4.6 %copy-start.2 = (s32[128]{0:T(128)S(1)}, s32[128]{0:T(128)}, u32[]{:S(2)}) copy-start(s32[128]{0:T(128)} %param.17) | copy-start | bytes 1540
  7.8 4.6 %copy-start.1 = (f32[1,31,1024]{2,0,1:T(1,128)S(1)}, f32[1,31,1024]{2,0,1:T(1,128)}, u32[]{:S(2)}) copy-start(f32[1,31,1024]{2,0,1:T(1,128)} %param.23) | copy-start | bytes 380932
  11.0 23.3 %collective-permute-start = (bf16[1,8,1024]{2,1,0:T(8,128)(2,1)S(1)}, bf16[1,8,1024]{2,1,0:T(8,128)(2,1)S(1)}, u32[]{:S(2)}, u32[]{:S(2)}) collective-permute-start(bf16[1,8,1024]{2,1,0:T(8,128)(2,1)S(1)} %slice.11), channel_id=1, source_target_pairs={{0,1},{2,3},{4,5},{6,7},{8,9},{10,11},{12,13},{14,15},{16,17},{18,... | collective-permute-start | bytes 49160 | tf_op jit(solution)/shard_map/ppermute | solution.py:18
  36.4 24.9 %collective-permute-start.1 = (bf16[16,16,1024]{2,1,0:T(8,128)(2,1)}, bf16[16,16,1024]{2,1,0:T(8,128)(2,1)}, u32[]{:S(2)}, u32[]{:S(2)}) collective-permute-start(bf16[16,16,1024]{2,1,0:T(8,128)(2,1)} %get-tuple-element.101), channel_id=1, source_target_pairs={{0,1},{2,3},{4,5},{6,7},{8,9},{10,11},{12,13},{14,15},{16,17},{18,... | collective-permute-start | bytes 1572872 | tf_op jit(solution)/shard_map/ppermute | solution.py:18

commit v11 on v10

--- a/solution.py
+++ b/solution.py
@@ -179,11 +179,10 @@
                 ec = jnp.exp(sc - top)
                 en = jnp.exp(sn - top)
                 total = jnp.sum(ec, axis=-1, keepdims=True) + jnp.sum(en, axis=-1, keepdims=True)
-                inv = 1.0 / total
-                pc = (ec * inv).astype(jnp.bfloat16)
-                pn = (en * inv).astype(jnp.bfloat16)
-                oh = jnp.dot(pc, cv, preferred_element_type=jnp.float32) + jnp.dot(
-                    pn, v, preferred_element_type=jnp.float32)
+                pc = ec.astype(jnp.bfloat16)
+                pn = en.astype(jnp.bfloat16)
+                oh = (jnp.dot(pc, cv, preferred_element_type=jnp.float32) + jnp.dot(
+                    pn, v, preferred_element_type=jnp.float32)) * (1.0 / total)
                 attended = oh if attended is None else jnp.where(mine, oh, attended)
             qkv[0, rows, cols] = attended.astype(jnp.bfloat16)
             return carry

time: 91.3 us -> 89 us (0.975)
  Pallas kernels: 28 us -> 26.7 us
  waiting for transfers between devices: 27.8 us -> 26.5 us
    ppermute x2, waiting for transfers between devices: 27.8 us -> 26.5 us  [shifted(): lax.ppermute(value, axis, [(source, source + steps) for source in range(l...]
    pallas_call x1, Pallas kernels: 21.7 us -> 20.4 us  [encoder_layer(): pl.pallas_call(kernel, out_shape=jax.ShapeDtypeStruct((tokens, width), jn...]
where the time goes in v11:
time: 89 us; the launch traced here: 88.2 us
  Pallas kernels  26.7 us (30%)
  waiting for transfers between devices  26.5 us (30%)
  blocking collectives  17.5 us (20%)
  local copies, waits for them, and re-layouts  9.37 us (11%)
  other arithmetic  4.77 us (5%)
  starting transfers between devices  2.56 us (3%)
    ppermute x2, waiting for transfers between devices, shifted(): lax.ppermute(value, axis, [(source, source + steps) for source in range(l...  26.5 us
    pallas_call x1, Pallas kernels, encoder_layer(): pl.pallas_call(kernel, out_shape=jax.ShapeDtypeStruct((tokens, width), jn...  20.4 us
    all_to_all x1, blocking collectives, exchange(): return lax.all_to_all(send, 'stream', 0, 0, tiled=True)  17.5 us
    pallas_call x1, Pallas kernels, project(): pl.pallas_call(kernel, out_shape=jax.ShapeDtypeStruct((3, tokens, width),...  6.24 us
    another operation x3, local copies, waits for them, and re-layouts  3.3 us
    ppermute x2, starting transfers between devices, shifted(): lax.ppermute(value, axis, [(source, source + steps) for source in range(l...  2.56 us
    unnamed x9, local copies, waits for them, and re-layouts  2.17 us
  transfers between devices with their start and end apart: 2, of which 2 were waited for; matrix products, arithmetic and copies ran while one was open for 0% of the time, Pallas kernels for 0%

profile of v11, /device:TPU:1, one launch (start us, length us, event | category | flops | bytes accessed | tf_op | source)
XLA Modules:
  0.0 88.2 jit_solution(12440178483792236639)
XLA Ops:
  0.0 0.8 select_reduce_fusion
  0.8 0.7 compare_select_fusion.7
  1.6 0.7 and_select_fusion
  2.3 0.1 select_reduce_fusion.1
  2.5 1.6 %copy.26 = bf16[1,16,12,2048]{3,2,1,0:T(8,128)(2,1)S(1)} copy(bf16[1,16,12,2048]{3,1,2,0:T(8,128)(2,1)} %param.19) | data formatting | bytes 1572864 | tf_op args[3]
  4.1 1.1 %fusion.8 = (bf16[16,12,1024]{2,1,0:T(8,128)(2,1)}, bf16[16,12,1024]{2,1,0:T(8,128)(2,1)}) fusion(bf16[16,12,2048]{2,1,0:T(8,128)(2,1)S(1)} %bitcast.22), kind=kLoop, calls=%fused_computation.38 | loop fusion | bytes 1572864 | tf_op jit(solution)/shard_map/slice | solution.py:318
  5.1 0.5 copy.25
  5.7 1.5 %fusion.7 = bf16[16,64,1024]{2,1,0:T(8,128)(2,1)S(1)} fusion(bf16[16,30,1024]{2,1,0:T(8,128)(2,1)S(1)} %bitcast.23, bf16[16,12,1024]{2,1,0:T(8,128)(2,1)} %get-tuple-element.92, bf16[16,12,1024]{2,1,0:T(8,128)(2,1)} %get-tuple-element.91), kind=kLoop, calls=%fused_computation.16 | loop fusion | flops 14680064 | bytes 3866624 | tf_op jit(solution)/shard_map/concatenate | solution.py:317
  7.2 0.6 gather_fusion
  7.8 0.0 copy-start.1
  7.8 2.5 %conditional.4 = (bf16[8,64,1024]{2,1,0:T(8,128)(2,1)}, bf16[3,256,1024]{2,1,0:T(8,128)(2,1)}) conditional(s32[]{:T(128)} %convert_element_type.70, () %tuple.34, (bf16[8,64,1024]{2,1,0:T(8,128)(2,1)S(1)}, bf16[16,16,1024]{2,1,0:T(8,128)(2,1)}, bf16[1,1024,3072]{2,1,0:T(8,128)(2,1)}) %tuple.35), branch_computations={%region_2.3_spmd, %region_3.4_spmd} | conditional | bytes 3145776 | solution.py:335
  7.8 1.3 %broadcast.65 = bf16[3,256,1024]{2,1,0:T(8,128)(2,1)} broadcast(bf16[]{:T(256)} %constant.35.clone), dimensions={} | broadcast | bytes 1572866 | tf_op jit(solution)/shard_map/broadcast.6
  9.2 1.1 %broadcast.64 = bf16[8,64,1024]{2,1,0:T(8,128)(2,1)} broadcast(bf16[]{:T(256)} %constant.35.clone), dimensions={} | broadcast | bytes 1048578 | tf_op jit(solution)/shard_map/broadcast.7
  10.3 0.7 slice.11
  11.0 1.3 %collective-permute-start = (bf16[1,8,1024]{2,1,0:T(8,128)(2,1)S(1)}, bf16[1,8,1024]{2,1,0:T(8,128)(2,1)S(1)}, u32[]{:S(2)}, u32[]{:S(2)}) collective-permute-start(bf16[1,8,1024]{2,1,0:T(8,128)(2,1)S(1)} %slice.11), channel_id=1, source_target_pairs={{0,1},{2,3},{4,5},{6,7},{8,9},{10,11},{12,13},{14,15},{16,17},{18,... | collective-permute-start | bytes 49160 | tf_op jit(solution)/shard_map/ppermute | solution.py:18
  12.3 0.1 pad_add_fusion
  12.4 0.1 dynamic_slice.9
  12.5 21.8 %collective-permute-done = bf16[1,8,1024]{2,1,0:T(8,128)(2,1)S(1)} collective-permute-done((bf16[1,8,1024]{2,1,0:T(8,128)(2,1)S(1)}, bf16[1,8,1024]{2,1,0:T(8,128)(2,1)S(1)}, u32[]{:S(2)}, u32[]{:S(2)}) %collective-permute-start) | collective-permute-done | bytes 16416 | tf_op jit(solution)/shard_map/ppermute | solution.py:18
  34.3 0.6 convert_reduce_fusion
  35.5 0.9 conditional.5
  35.6 0.9 broadcast.66
  36.4 1.3 %collective-permute-start.1 = (bf16[16,16,1024]{2,1,0:T(8,128)(2,1)}, bf16[16,16,1024]{2,1,0:T(8,128)(2,1)}, u32[]{:S(2)}, u32[]{:S(2)}) collective-permute-start(bf16[16,16,1024]{2,1,0:T(8,128)(2,1)} %get-tuple-element.101), channel_id=1, source_target_pairs={{0,1},{2,3},{4,5},{6,7},{8,9},{10,11},{12,13},{14,15},{16,17},{18,... | collective-permute-start | bytes 1572872 | tf_op jit(solution)/shard_map/ppermute | solution.py:18
  37.7 17.6 %conditional.6 = (bf16[8,64,1024]{2,1,0:T(8,128)(2,1)S(1)}) conditional(s32[]{:T(128)} %convert_element_type.70, (f32[]{:T(128)}, bf16[8,64,1024]{2,1,0:T(8,128)(2,1)S(1)}) %tuple.37, () %tuple.38), branch_computations={%region_7.8_spmd, %region_8.9_spmd} | conditional | flops 524289 | bytes 4194320 | solution.py:345
  37.7 0.1 broadcast_add_fusion.1
  37.8 17.5 %all_to_all.8 = bf16[8,64,1024]{2,1,0:T(8,128)(2,1)S(1)} all-to-all(bf16[8,64,1024]{2,1,0:T(8,128)(2,1)S(1)} %broadcast_add_fusion.1), channel_id=1, replica_groups=mesh['groups'=2,'stream'=8,'section'=2] {'stream'}, dimensions={0} | all-to-all | bytes 2097152 | tf_op jit(solution)/shard_map/cond/branch_0_fun/all_to_all | solution.py:302
  55.3 4.7 %collective-permute-done.1 = bf16[16,16,1024]{2,1,0:T(8,128)(2,1)} collective-permute-done((bf16[16,16,1024]{2,1,0:T(8,128)(2,1)}, bf16[16,16,1024]{2,1,0:T(8,128)(2,1)}, u32[]{:S(2)}, u32[]{:S(2)}) %collective-permute-start.1) | collective-permute-done | bytes 524320 | tf_op jit(solution)/shard_map/ppermute | solution.py:18
  60.0 28.2 %conditional.7 = (bf16[1,16,16,1024]{3,2,1,0:T(8,128)(2,1)}) conditional(s32[]{:T(128)} %convert_element_type.70, (bf16[16,16,1024]{2,1,0:T(8,128)(2,1)}, s32[16]{0:T(128)S(1)}, bf16[1,1024,3072]{2,1,0:T(8,128)(2,1)}, s32[32]{0:T(128)S(1)}, f32[31,1024]{1,0:T(8,128)S(1)}, /*index=5*/bf16[1024,1024]{1,0:T(8,128)(2,1)}, ...), branch_computations={%region_9.10_spmd, %region_10.11_spmd} | conditional | flops 512 | bytes 1048584 | solution.py:348
  60.0 6.2 %branch_0_fun.2.qkv_hbm = bf16[3,256,1024]{2,1,0:T(8,128)(2,1)} custom-call(bf16[256,1024]{1,0:T(8,128)(2,1)} %bitcast.4.x_ref, bf16[1024,3072]{1,0:T(8,128)(2,1)} %bitcast.19), custom_call_target="tpu_custom_call" | custom-call | tf_op jit(solution)/shard_map/cond/branch_0_fun/pallas_call | solution.py:229
  66.3 0.1 fusion.1
  66.3 0.8 reshape.155.rlive_ref
  67.1 0.7 reshape.143.klive_ref
  67.8 20.4 %branch_0_fun.3 = bf16[256,1024]{1,0:T(8,128)(2,1)} custom-call(s32[32]{0:T(128)S(1)} %get-tuple-element.73.sel_ref, bf16[256,1024]{1,0:T(8,128)(2,1)} %bitcast.4.x_ref, f32[1,256]{1,0:T(1,128)} %reshape.143.klive_ref, f32[256,1]{1,0:T(8,128)} %reshape.155.rlive_ref, f32[31,1024]{1,0:T(8,128)S(1)} %get-tuple-element.76.cw_ref, ...), custom_call_target="tpu_custom_call" | custom-call | tf_op jit(solution)/shard_map/cond/branch_0_fun/pallas_call | solution.py:259
  (8 shorter events, 0.1 us)
Async XLA Ops:
  0.0 5.1 %copy-start = (bf16[1,16,30,1024]{3,1,2,0:T(8,128)(2,1)S(1)}, bf16[1,16,30,1024]{3,1,2,0:T(8,128)(2,1)}, u32[]{:S(2)}) copy-start(bf16[1,16,30,1024]{3,1,2,0:T(8,128)(2,1)} %param.20) | copy-start | bytes 2949124
  7.8 4.6 %copy-start.2 = (s32[128]{0:T(128)S(1)}, s32[128]{0:T(128)}, u32[]{:S(2)}) copy-start(s32[128]{0:T(128)} %param.17) | copy-start | bytes 1540
  7.8 4.6 %copy-start.1 = (f32[1,31,1024]{2,0,1:T(1,128)S(1)}, f32[1,31,1024]{2,0,1:T(1,128)}, u32[]{:S(2)}) copy-start(f32[1,31,1024]{2,0,1:T(1,128)} %param.23) | copy-start | bytes 380932
  11.0 23.3 %collective-permute-start = (bf16[1,8,1024]{2,1,0:T(8,128)(2,1)S(1)}, bf16[1,8,1024]{2,1,0:T(8,128)(2,1)S(1)}, u32[]{:S(2)}, u32[]{:S(2)}) collective-permute-start(bf16[1,8,1024]{2,1,0:T(8,128)(2,1)S(1)} %slice.11), channel_id=1, source_target_pairs={{0,1},{2,3},{4,5},{6,7},{8,9},{10,11},{12,13},{14,15},{16,17},{18,... | collective-permute-start | bytes 49160 | tf_op jit(solution)/shard_map/ppermute | solution.py:18
  36.4 23.6 %collective-permute-start.1 = (bf16[16,16,1024]{2,1,0:T(8,128)(2,1)}, bf16[16,16,1024]{2,1,0:T(8,128)(2,1)}, u32[]{:S(2)}, u32[]{:S(2)}) collective-permute-start(bf16[16,16,1024]{2,1,0:T(8,128)(2,1)} %get-tuple-element.101), channel_id=1, source_target_pairs={{0,1},{2,3},{4,5},{6,7},{8,9},{10,11},{12,13},{14,15},{16,17},{18,... | collective-permute-start | bytes 1572872 | tf_op jit(solution)/shard_map/ppermute | solution.py:18

commit v12 on v11

--- a/solution.py
+++ b/solution.py
@@ -120,30 +120,41 @@
     taps = cw_ref.shape[0]
     chunk = 128
 
-    for j in range(streams):
-        kind = sel_ref[j]
-        idx = sel_ref[streams + j]
-
-        @pl.when(kind == 0)
-        def _():
-            pltpu.make_async_copy(state_hbm.at[idx], stv.at[j], gsem.at[j]).start()
-
-        @pl.when(kind != 0)
-        def _():
-            pltpu.make_async_copy(recv_hbm.at[idx], stv.at[j], gsem.at[j]).start()
+    keys_rows = pl.ds(0, 2 * slot)
+    conv_part = pl.ds(2 * slot, stv.shape[1] - 2 * slot)
+
+    def gather(part, which):
+        for j in range(streams):
+            kind = sel_ref[j]
+            idx = sel_ref[streams + j]
+
+            @pl.when(kind == 0)
+            def _():
+                pltpu.make_async_copy(state_hbm.at[idx, part], stv.at[j, part],
+                                      gsem.at[which, j]).start()
+
+            @pl.when(kind != 0)
+            def _():
+                pltpu.make_async_copy(recv_hbm.at[idx, part], stv.at[j, part],
+                                      gsem.at[which, j]).start()
+
+    def gather_wait(part, which):
+        for j in range(streams):
+            pltpu.make_async_copy(state_hbm.at[0, part], stv.at[j, part], gsem.at[which, j]).wait()
 
     rows_w = wo_hbm.shape[0]
     copies = [pltpu.make_async_copy(qkv_hbm, qkv, wsem.at[0, 0])]
     for r in range(rows_w // CHUNK_ROWS):
         part = pl.ds(r * CHUNK_ROWS, CHUNK_ROWS)
         copies.append(pltpu.make_async_copy(wo_hbm.at[part], wobuf.at[part], wsem.at[1, r]))
-    for c in copies:
+    copies[0].start()
+    gather(keys_rows, 0)
+    for c in copies[1:]:
         c.start()
-
-    for j in range(streams):
-        pltpu.make_async_copy(state_hbm.at[0], stv.at[j], gsem.at[j]).wait()
+    gather(conv_part, 1)
 
     copies[0].wait()
+    gather_wait(keys_rows, 0)
 
     rows_g = GROUP * frames
     cols_g = GROUP * slot
@@ -195,6 +206,7 @@
     residual = x_ref[...].astype(jnp.float32) + mixed
     res_ref[...] = residual
     rounded = residual.astype(jnp.bfloat16).astype(jnp.float32).reshape(streams, frames, width)
+    gather_wait(conv_part, 1)
     origin = kept - kept_real
     if early:
         pad_ref[:, 0:kept, :] = jnp.zeros((streams, kept, width), jnp.float32)
@@ -270,7 +282,7 @@
             pltpu.VMEM((streams, kept + frames, width), jnp.float32),
             pltpu.VMEM((tokens, width), jnp.float32),
             pltpu.SemaphoreType.DMA((2, width // CHUNK_ROWS)),
-            pltpu.SemaphoreType.DMA((streams,)),
+            pltpu.SemaphoreType.DMA((2, streams)),
         ],
     )(sel, x, klive, rlive, conv_weight, project(inputs, qkv_weight) if projected is None else projected,
       out_weight, state, recv, *extra)

time: 89 us -> 87.3 us (0.981)
  Pallas kernels: 26.7 us -> 25.7 us
    pallas_call x1, Pallas kernels: 20.4 us -> 19.5 us  [encoder_layer(): pl.pallas_call(kernel, out_shape=jax.ShapeDtypeStruct((tokens, width), jn...]
where the time goes in v12:
time: 87.3 us; the launch traced here: 86.8 us
  waiting for transfers between devices  26.1 us (30%)
  Pallas kernels  25.7 us (29%)
  blocking collectives  17.5 us (20%)
  local copies, waits for them, and re-layouts  9.37 us (11%)
  other arithmetic  4.77 us (5%)
  starting transfers between devices  2.56 us (3%)
    ppermute x2, waiting for transfers between devices, shifted(): lax.ppermute(value, axis, [(source, source + steps) for source in range(l...  26.1 us
    pallas_call x1, Pallas kernels, encoder_layer(): pl.pallas_call(kernel, out_shape=jax.ShapeDtypeStruct((tokens, width), jn...  19.5 us
    all_to_all x1, blocking collectives, exchange(): return lax.all_to_all(send, 'stream', 0, 0, tiled=True)  17.5 us
    pallas_call x1, Pallas kernels, project(): pl.pallas_call(kernel, out_shape=jax.ShapeDtypeStruct((3, tokens, width),...  6.24 us
    another operation x3, local copies, waits for them, and re-layouts  3.3 us
    ppermute x2, starting transfers between devices, shifted(): lax.ppermute(value, axis, [(source, source + steps) for source in range(l...  2.56 us
    unnamed x9, local copies, waits for them, and re-layouts  2.17 us
  transfers between devices with their start and end apart: 2, of which 2 were waited for; matrix products, arithmetic and copies ran while one was open for 0% of the time, Pallas kernels for 0%

profile of v12, /device:TPU:1, one launch (start us, length us, event | category | flops | bytes accessed | tf_op | source)
XLA Modules:
  0.0 86.8 jit_solution(4438412213311111264)
XLA Ops:
  0.0 0.8 select_reduce_fusion
  0.8 0.7 compare_select_fusion.7
  1.6 0.7 and_select_fusion
  2.3 0.1 select_reduce_fusion.1
  2.5 1.6 %copy.26 = bf16[1,16,12,2048]{3,2,1,0:T(8,128)(2,1)S(1)} copy(bf16[1,16,12,2048]{3,1,2,0:T(8,128)(2,1)} %param.19) | data formatting | bytes 1572864 | tf_op args[3]
  4.1 1.1 %fusion.8 = (bf16[16,12,1024]{2,1,0:T(8,128)(2,1)}, bf16[16,12,1024]{2,1,0:T(8,128)(2,1)}) fusion(bf16[16,12,2048]{2,1,0:T(8,128)(2,1)S(1)} %bitcast.22), kind=kLoop, calls=%fused_computation.38 | loop fusion | bytes 1572864 | tf_op jit(solution)/shard_map/slice | solution.py:330
  5.1 0.5 copy.25
  5.7 1.5 %fusion.7 = bf16[16,64,1024]{2,1,0:T(8,128)(2,1)S(1)} fusion(bf16[16,30,1024]{2,1,0:T(8,128)(2,1)S(1)} %bitcast.23, bf16[16,12,1024]{2,1,0:T(8,128)(2,1)} %get-tuple-element.92, bf16[16,12,1024]{2,1,0:T(8,128)(2,1)} %get-tuple-element.91), kind=kLoop, calls=%fused_computation.16 | loop fusion | flops 14680064 | bytes 3866624 | tf_op jit(solution)/shard_map/concatenate | solution.py:329
  7.2 0.6 gather_fusion
  7.8 0.0 copy-start.2
  7.8 2.5 %conditional.4 = (bf16[8,64,1024]{2,1,0:T(8,128)(2,1)}, bf16[3,256,1024]{2,1,0:T(8,128)(2,1)}) conditional(s32[]{:T(128)} %convert_element_type.70, () %tuple.34, (bf16[8,64,1024]{2,1,0:T(8,128)(2,1)S(1)}, bf16[16,16,1024]{2,1,0:T(8,128)(2,1)}, bf16[1,1024,3072]{2,1,0:T(8,128)(2,1)}) %tuple.35), branch_computations={%region_2.3_spmd, %region_3.4_spmd} | conditional | bytes 3145776 | solution.py:347
  7.8 1.3 %broadcast.65 = bf16[3,256,1024]{2,1,0:T(8,128)(2,1)} broadcast(bf16[]{:T(256)} %constant.35.clone), dimensions={} | broadcast | bytes 1572866 | tf_op jit(solution)/shard_map/broadcast.6
  9.2 1.1 %broadcast.64 = bf16[8,64,1024]{2,1,0:T(8,128)(2,1)} broadcast(bf16[]{:T(256)} %constant.35.clone), dimensions={} | broadcast | bytes 1048578 | tf_op jit(solution)/shard_map/broadcast.7
  10.3 0.7 slice.11
  11.0 1.3 %collective-permute-start = (bf16[1,8,1024]{2,1,0:T(8,128)(2,1)S(1)}, bf16[1,8,1024]{2,1,0:T(8,128)(2,1)S(1)}, u32[]{:S(2)}, u32[]{:S(2)}) collective-permute-start(bf16[1,8,1024]{2,1,0:T(8,128)(2,1)S(1)} %slice.11), channel_id=1, source_target_pairs={{0,1},{2,3},{4,5},{6,7},{8,9},{10,11},{12,13},{14,15},{16,17},{18,... | collective-permute-start | bytes 49160 | tf_op jit(solution)/shard_map/ppermute | solution.py:18
  12.3 0.1 pad_add_fusion
  12.4 0.1 dynamic_slice.9
  12.5 21.8 %collective-permute-done = bf16[1,8,1024]{2,1,0:T(8,128)(2,1)S(1)} collective-permute-done((bf16[1,8,1024]{2,1,0:T(8,128)(2,1)S(1)}, bf16[1,8,1024]{2,1,0:T(8,128)(2,1)S(1)}, u32[]{:S(2)}, u32[]{:S(2)}) %collective-permute-start) | collective-permute-done | bytes 16416 | tf_op jit(solution)/shard_map/ppermute | solution.py:18
  34.3 0.6 convert_reduce_fusion
  35.5 0.9 %conditional.5 = (bf16[16,16,1024]{2,1,0:T(8,128)(2,1)}) conditional(s32[]{:T(128)} %convert_element_type.70, () %tuple.33, (bf16[16,16,1024]{2,1,0:T(8,128)(2,1)}, s32[16]{0:T(128)S(1)}, s32[32]{0:T(128)S(1)}, f32[31,1024]{1,0:T(8,128)S(1)}, bf16[3,256,1024]{2,1,0:T(8,128)(2,1)}, /*index=5*/bf16[1024,1024]{1,0:T(8,128)(2,1)}, ...), branch_computations={%region_5.6_spmd, %region_6.7_spmd} | conditional | flops 544 | bytes 524298 | solution.py:353
  35.6 0.9 broadcast.66
  36.4 1.3 %collective-permute-start.1 = (bf16[16,16,1024]{2,1,0:T(8,128)(2,1)}, bf16[16,16,1024]{2,1,0:T(8,128)(2,1)}, u32[]{:S(2)}, u32[]{:S(2)}) collective-permute-start(bf16[16,16,1024]{2,1,0:T(8,128)(2,1)} %get-tuple-element.101), channel_id=1, source_target_pairs={{0,1},{2,3},{4,5},{6,7},{8,9},{10,11},{12,13},{14,15},{16,17},{18,... | collective-permute-start | bytes 1572872 | tf_op jit(solution)/shard_map/ppermute | solution.py:18
  37.7 17.6 %conditional.6 = (bf16[8,64,1024]{2,1,0:T(8,128)(2,1)S(1)}) conditional(s32[]{:T(128)} %convert_element_type.70, (f32[]{:T(128)}, bf16[8,64,1024]{2,1,0:T(8,128)(2,1)S(1)}) %tuple.37, () %tuple.38), branch_computations={%region_7.8_spmd, %region_8.9_spmd} | conditional | flops 524289 | bytes 4194320 | solution.py:357
  37.7 0.1 broadcast_add_fusion.1
  37.8 17.5 %all_to_all.8 = bf16[8,64,1024]{2,1,0:T(8,128)(2,1)S(1)} all-to-all(bf16[8,64,1024]{2,1,0:T(8,128)(2,1)S(1)} %broadcast_add_fusion.1), channel_id=1, replica_groups=mesh['groups'=2,'stream'=8,'section'=2] {'stream'}, dimensions={0} | all-to-all | bytes 2097152 | tf_op jit(solution)/shard_map/cond/branch_0_fun/all_to_all | solution.py:314
  55.3 4.3 %collective-permute-done.1 = bf16[16,16,1024]{2,1,0:T(8,128)(2,1)} collective-permute-done((bf16[16,16,1024]{2,1,0:T(8,128)(2,1)}, bf16[16,16,1024]{2,1,0:T(8,128)(2,1)}, u32[]{:S(2)}, u32[]{:S(2)}) %collective-permute-start.1) | collective-permute-done | bytes 524320 | tf_op jit(solution)/shard_map/ppermute | solution.py:18
  59.6 27.2 %conditional.7 = (bf16[1,16,16,1024]{3,2,1,0:T(8,128)(2,1)}) conditional(s32[]{:T(128)} %convert_element_type.70, (bf16[16,16,1024]{2,1,0:T(8,128)(2,1)}, s32[16]{0:T(128)S(1)}, bf16[1,1024,3072]{2,1,0:T(8,128)(2,1)}, s32[32]{0:T(128)S(1)}, f32[31,1024]{1,0:T(8,128)S(1)}, /*index=5*/bf16[1024,1024]{1,0:T(8,128)(2,1)}, ...), branch_computations={%region_9.10_spmd, %region_10.11_spmd} | conditional | flops 512 | bytes 1048584 | solution.py:360
  59.6 6.2 %branch_0_fun.2.qkv_hbm = bf16[3,256,1024]{2,1,0:T(8,128)(2,1)} custom-call(bf16[256,1024]{1,0:T(8,128)(2,1)} %bitcast.4.x_ref, bf16[1024,3072]{1,0:T(8,128)(2,1)} %bitcast.19), custom_call_target="tpu_custom_call" | custom-call | tf_op jit(solution)/shard_map/cond/branch_0_fun/pallas_call | solution.py:241
  65.8 0.1 fusion.1
  65.9 0.8 reshape.155.rlive_ref
  66.7 0.7 reshape.143.klive_ref
  67.3 19.5 %branch_0_fun.3 = bf16[256,1024]{1,0:T(8,128)(2,1)} custom-call(s32[32]{0:T(128)S(1)} %get-tuple-element.73.sel_ref, bf16[256,1024]{1,0:T(8,128)(2,1)} %bitcast.4.x_ref, f32[1,256]{1,0:T(1,128)} %reshape.143.klive_ref, f32[256,1]{1,0:T(8,128)} %reshape.155.rlive_ref, f32[31,1024]{1,0:T(8,128)S(1)} %get-tuple-element.76.cw_ref, ...), custom_call_target="tpu_custom_call" | custom-call | tf_op jit(solution)/shard_map/cond/branch_0_fun/pallas_call | solution.py:271
  (8 shorter events, 0.1 us)
Async XLA Ops:
  0.0 5.1 %copy-start = (bf16[1,16,30,1024]{3,1,2,0:T(8,128)(2,1)S(1)}, bf16[1,16,30,1024]{3,1,2,0:T(8,128)(2,1)}, u32[]{:S(2)}) copy-start(bf16[1,16,30,1024]{3,1,2,0:T(8,128)(2,1)} %param.20) | copy-start | bytes 2949124
  7.8 4.6 %copy-start.2 = (s32[128]{0:T(128)S(1)}, s32[128]{0:T(128)}, u32[]{:S(2)}) copy-start(s32[128]{0:T(128)} %param.17) | copy-start | bytes 1540
  7.8 4.6 %copy-start.1 = (f32[1,31,1024]{2,0,1:T(1,128)S(1)}, f32[1,31,1024]{2,0,1:T(1,128)}, u32[]{:S(2)}) copy-start(f32[1,31,1024]{2,0,1:T(1,128)} %param.23) | copy-start | bytes 380932
  11.0 23.3 %collective-permute-start = (bf16[1,8,1024]{2,1,0:T(8,128)(2,1)S(1)}, bf16[1,8,1024]{2,1,0:T(8,128)(2,1)S(1)}, u32[]{:S(2)}, u32[]{:S(2)}) collective-permute-start(bf16[1,8,1024]{2,1,0:T(8,128)(2,1)S(1)} %slice.11), channel_id=1, source_target_pairs={{0,1},{2,3},{4,5},{6,7},{8,9},{10,11},{12,13},{14,15},{16,17},{18,... | collective-permute-start | bytes 49160 | tf_op jit(solution)/shard_map/ppermute | solution.py:18
  36.4 23.2 %collective-permute-start.1 = (bf16[16,16,1024]{2,1,0:T(8,128)(2,1)}, bf16[16,16,1024]{2,1,0:T(8,128)(2,1)}, u32[]{:S(2)}, u32[]{:S(2)}) collective-permute-start(bf16[16,16,1024]{2,1,0:T(8,128)(2,1)} %get-tuple-element.101), channel_id=1, source_target_pairs={{0,1},{2,3},{4,5},{6,7},{8,9},{10,11},{12,13},{14,15},{16,17},{18,... | collective-permute-start | bytes 1572872 | tf_op jit(solution)/shard_map/ppermute | solution.py:18

commit v13 on v12

--- a/solution.py
+++ b/solution.py
@@ -289,7 +289,7 @@
     return out.reshape(streams, frames, width)
 
 
-def migrate(anchor, own, count, local_count, state):
+def migrate(anchor, own, count, local_count, build):
     total = anchor.shape[0]
     every_slot = jnp.arange(total, dtype=jnp.int32)
     newpos = jnp.sum(jnp.where(anchor[None, :] == every_slot[:, None], every_slot[None, :], 0),
@@ -300,7 +300,7 @@
     match = target[None, :] == hosts[:, None]
     send_slot = jnp.sum(jnp.where(match, jnp.arange(local_count, dtype=jnp.int32)[None, :], 0),
                         axis=1)
-    send = jnp.take(state, jnp.clip(send_slot, 0, local_count - 1), axis=0, mode="clip")
+    send = build(jnp.clip(send_slot, 0, local_count - 1))
     mine_old = lax.dynamic_slice_in_dim(anchor, own * local_count, local_count)
     source = mine_old // local_count
     staying = source == own
@@ -326,12 +326,17 @@
     kept = conv_state.shape[2]
     lead = (-kept) % 16
     context = context_cache[0]
-    state = jnp.concatenate([
-        jnp.pad(context[:, :, :width], ((0, 0), (0, slot - ctx), (0, 0))),
-        jnp.pad(context[:, :, width:], ((0, 0), (0, slot - ctx), (0, 0))),
-        jnp.pad(conv_state[0], ((0, 0), (lead, 0), (0, 0))),
-    ], axis=1)
-    sel, send = migrate(anchor, own, count, local_count, state)
+    def slab(context, conv):
+        return jnp.concatenate([
+            jnp.pad(context[:, :, :width], ((0, 0), (0, slot - ctx), (0, 0))),
+            jnp.pad(context[:, :, width:], ((0, 0), (0, slot - ctx), (0, 0))),
+            jnp.pad(conv, ((0, 0), (lead, 0), (0, 0))),
+        ], axis=1)
+
+    state = slab(context, conv_state[0])
+    build = lambda rows: slab(jnp.take(context, rows, axis=0, mode="clip"),
+                              jnp.take(conv_state[0], rows, axis=0, mode="clip"))
+    sel, send = migrate(anchor, own, count, local_count, build)
     valid_here = lax.dynamic_slice_in_dim(valid_counts, own * local_count, local_count)
     section_index = lax.axis_index("section")
     layer = functools.partial(encoder_layer, valid_counts=valid_here, sel=sel, state=state,

time: 87.3 us -> 88.4 us (1.013)
  local copies, waits for them, and re-layouts: 9.37 us -> 10.7 us
    gather x1 -> x2, local copies, waits for them, and re-layouts: 0.61 us -> 1.95 us  [the longest x1 1.37 us: body(): jnp.take(conv_state[0], rows, axis=0, mode='clip')]
    concatenate x1 -> x2, other arithmetic: 1.49 us -> 1.8 us  [slab(): jnp.concatenate([jnp.pad(context[:, :, :width], ((0, 0), (0, slot - ctx),...]
    unnamed x9 -> x13, local copies, waits for them, and re-layouts: 2.17 us -> 2.42 us
  transfers between devices with their start and end apart: 2 -> 2, of which waited for: 2 -> 2; matrix products, arithmetic and copies ran while one was open for 0% -> 1% of each run, Pallas kernels for 0% -> 0%
where the time goes in v13:
time: 88.4 us; the launch traced here: 87.9 us
  Pallas kernels  25.7 us (29%)
  waiting for transfers between devices  25.4 us (29%)
  blocking collectives  17.5 us (20%)
  local copies, waits for them, and re-layouts  10.7 us (12%)
  other arithmetic  5.08 us (6%)
  starting transfers between devices  2.56 us (3%)
    ppermute x2, waiting for transfers between devices, shifted(): lax.ppermute(value, axis, [(source, source + steps) for source in range(l...  25.4 us
    pallas_call x1, Pallas kernels, encoder_layer(): pl.pallas_call(kernel, out_shape=jax.ShapeDtypeStruct((tokens, width), jn...  19.5 us
    all_to_all x1, blocking collectives, exchange(): return lax.all_to_all(send, 'stream', 0, 0, tiled=True)  17.5 us
    pallas_call x1, Pallas kernels, project(): pl.pallas_call(kernel, out_shape=jax.ShapeDtypeStruct((3, tokens, width),...  6.25 us
    another operation x3, local copies, waits for them, and re-layouts  3.33 us
    ppermute x2, starting transfers between devices, shifted(): lax.ppermute(value, axis, [(source, source + steps) for source in range(l...  2.56 us
    unnamed x13, local copies, waits for them, and re-layouts  2.42 us
    concatenate x2, other arithmetic, slab(): jnp.concatenate([jnp.pad(context[:, :, :width], ((0, 0), (0, slot - ctx),...  1.8 us
  transfers between devices with their start and end apart: 2, of which 2 were waited for; matrix products, arithmetic and copies ran while one was open for 1% of the time, Pallas kernels for 0%

profile of v13, /device:TPU:1, one launch (start us, length us, event | category | flops | bytes accessed | tf_op | source)
XLA Modules:
  0.0 87.9 jit_solution(3575050523796780589)
XLA Ops:
  0.0 0.8 select_reduce_fusion
  0.8 0.7 compare_select_fusion.7
  1.6 0.7 and_select_fusion
  2.3 0.1 select_reduce_fusion.1
  2.5 1.6 %copy.26 = bf16[1,16,12,2048]{3,2,1,0:T(8,128)(2,1)S(1)} copy(bf16[1,16,12,2048]{3,1,2,0:T(8,128)(2,1)} %param.19) | data formatting | bytes 1572864 | tf_op args[3]
  4.1 0.6 gather_fusion
  4.6 0.7 fusion.15
  5.4 0.5 copy.25
  5.9 1.4 %gather_fusion.1 = bf16[8,30,1024]{2,1,0:T(8,128)(2,1)} fusion(bf16[16,30,1024]{2,1,0:T(8,128)(2,1)S(1)} %bitcast.24, s32[1024]{0:T(1024)S(1)} %pad_clamp_fusion), kind=kCustom, calls=%fused_computation.1 | custom fusion | bytes 983072 | tf_op jit(solution)/shard_map/jit(_take)/gather | solution.py:338
  7.3 1.3 %fusion.13 = bf16[8,64,1024]{2,1,0:T(8,128)(2,1)S(1)} fusion(bf16[8,30,1024]{2,1,0:T(8,128)(2,1)} %gather_fusion.1, bf16[8,12,1024]{2,1,0:T(8,128)(2,1)} %get-tuple-element.94, bf16[8,12,1024]{2,1,0:T(8,128)(2,1)S(1)} %get-tuple-element.93), kind=kLoop, calls=%fused_computation.27 | loop fusion | flops 7340032 | bytes 1933312 | tf_op jit(solution)/shard_map/concatenate | solution.py:330
  8.6 2.5 %conditional.4 = (bf16[8,64,1024]{2,1,0:T(8,128)(2,1)}, bf16[3,256,1024]{2,1,0:T(8,128)(2,1)}) conditional(s32[]{:T(128)} %convert_element_type.75, () %tuple.34, (bf16[8,64,1024]{2,1,0:T(8,128)(2,1)S(1)}, bf16[16,16,1024]{2,1,0:T(8,128)(2,1)}, bf16[1,1024,3072]{2,1,0:T(8,128)(2,1)}) %tuple.35), branch_computations={%region_2.3_spmd, %region_3.4_spmd} | conditional | bytes 5242956 | solution.py:352
  8.7 1.4 %broadcast.65 = bf16[3,256,1024]{2,1,0:T(8,128)(2,1)} broadcast(bf16[]{:T(256)} %constant.35.clone), dimensions={} | broadcast | bytes 1572866 | tf_op jit(solution)/shard_map/broadcast.6
  10.0 1.1 %broadcast.64 = bf16[8,64,1024]{2,1,0:T(8,128)(2,1)} broadcast(bf16[]{:T(256)} %constant.35.clone), dimensions={} | broadcast | bytes 1048578 | tf_op jit(solution)/shard_map/broadcast.7
  11.1 0.8 slice.17
  11.9 1.3 %collective-permute-start = (bf16[1,8,1024]{2,1,0:T(8,128)(2,1)S(1)}, bf16[1,8,1024]{2,1,0:T(8,128)(2,1)S(1)}, u32[]{:S(2)}, u32[]{:S(2)}) collective-permute-start(bf16[1,8,1024]{2,1,0:T(8,128)(2,1)S(1)} %slice.17), channel_id=1, source_target_pairs={{0,1},{2,3},{4,5},{6,7},{8,9},{10,11},{12,13},{14,15},{16,17},{18,... | collective-permute-start | bytes 49160 | tf_op jit(solution)/shard_map/ppermute | solution.py:18
  13.2 0.1 fusion.14
  13.3 0.5 fusion.7
  13.8 0.1 pad_add_fusion
  14.1 0.2 copy-done.4
  14.3 20.9 %collective-permute-done = bf16[1,8,1024]{2,1,0:T(8,128)(2,1)S(1)} collective-permute-done((bf16[1,8,1024]{2,1,0:T(8,128)(2,1)S(1)}, bf16[1,8,1024]{2,1,0:T(8,128)(2,1)S(1)}, u32[]{:S(2)}, u32[]{:S(2)}) %collective-permute-start) | collective-permute-done | bytes 16416 | tf_op jit(solution)/shard_map/ppermute | solution.py:18
  35.2 0.6 convert_reduce_fusion
  36.5 0.9 conditional.5
  36.5 0.9 broadcast.66
  37.3 1.3 %collective-permute-start.1 = (bf16[16,16,1024]{2,1,0:T(8,128)(2,1)}, bf16[16,16,1024]{2,1,0:T(8,128)(2,1)}, u32[]{:S(2)}, u32[]{:S(2)}) collective-permute-start(bf16[16,16,1024]{2,1,0:T(8,128)(2,1)} %get-tuple-element.103), channel_id=1, source_target_pairs={{0,1},{2,3},{4,5},{6,7},{8,9},{10,11},{12,13},{14,15},{16,17},{18,... | collective-permute-start | bytes 1572872 | tf_op jit(solution)/shard_map/ppermute | solution.py:18
  38.6 17.6 %conditional.6 = (bf16[8,64,1024]{2,1,0:T(8,128)(2,1)S(1)}) conditional(s32[]{:T(128)} %convert_element_type.75, (f32[]{:T(128)}, bf16[8,64,1024]{2,1,0:T(8,128)(2,1)S(1)}) %tuple.37, () %tuple.38), branch_computations={%region_7.8_spmd, %region_8.9_spmd} | conditional | flops 524289 | bytes 4194320 | solution.py:362
  38.7 17.5 %all_to_all.8 = bf16[8,64,1024]{2,1,0:T(8,128)(2,1)S(1)} all-to-all(bf16[8,64,1024]{2,1,0:T(8,128)(2,1)S(1)} %broadcast_add_fusion.1), channel_id=1, replica_groups=mesh['groups'=2,'stream'=8,'section'=2] {'stream'}, dimensions={0} | all-to-all | bytes 2097152 | tf_op jit(solution)/shard_map/cond/branch_0_fun/all_to_all | solution.py:314
  56.2 4.5 %collective-permute-done.1 = bf16[16,16,1024]{2,1,0:T(8,128)(2,1)} collective-permute-done((bf16[16,16,1024]{2,1,0:T(8,128)(2,1)}, bf16[16,16,1024]{2,1,0:T(8,128)(2,1)}, u32[]{:S(2)}, u32[]{:S(2)}) %collective-permute-start.1) | collective-permute-done | bytes 524320 | tf_op jit(solution)/shard_map/ppermute | solution.py:18
  60.8 27.2 %conditional.7 = (bf16[1,16,16,1024]{3,2,1,0:T(8,128)(2,1)}) conditional(s32[]{:T(128)} %convert_element_type.75, (bf16[16,16,1024]{2,1,0:T(8,128)(2,1)}, s32[16]{0:T(128)S(1)}, bf16[1,1024,3072]{2,1,0:T(8,128)(2,1)}, s32[32]{0:T(128)S(1)}, f32[31,1024]{1,0:T(8,128)S(1)}, /*index=5*/bf16[1024,1024]{1,0:T(8,128)(2,1)}, ...), branch_computations={%region_9.10_spmd, %region_10.11_spmd} | conditional | flops 512 | bytes 1048584 | solution.py:365
  60.8 6.3 %branch_0_fun.2.qkv_hbm = bf16[3,256,1024]{2,1,0:T(8,128)(2,1)} custom-call(bf16[256,1024]{1,0:T(8,128)(2,1)} %bitcast.4.x_ref, bf16[1024,3072]{1,0:T(8,128)(2,1)} %bitcast.19), custom_call_target="tpu_custom_call" | custom-call | tf_op jit(solution)/shard_map/cond/branch_0_fun/pallas_call | solution.py:241
  67.1 0.7 reshape.164.rlive_ref
  67.8 0.6 reshape.143.klive_ref
  68.4 19.5 %branch_0_fun.3 = bf16[256,1024]{1,0:T(8,128)(2,1)} custom-call(s32[32]{0:T(128)S(1)} %get-tuple-element.73.sel_ref, bf16[256,1024]{1,0:T(8,128)(2,1)} %bitcast.4.x_ref, f32[1,256]{1,0:T(1,128)} %reshape.143.klive_ref, f32[256,1]{1,0:T(8,128)} %reshape.164.rlive_ref, f32[31,1024]{1,0:T(8,128)S(1)} %get-tuple-element.76.cw_ref, ...), custom_call_target="tpu_custom_call" | custom-call | tf_op jit(solution)/shard_map/cond/branch_0_fun/pallas_call | solution.py:271
  (15 shorter events, 0.3 us)
Async XLA Ops:
  0.0 5.4 %copy-start.3 = (bf16[1,16,30,1024]{3,1,2,0:T(8,128)(2,1)S(1)}, bf16[1,16,30,1024]{3,1,2,0:T(8,128)(2,1)}, u32[]{:S(2)}) copy-start(bf16[1,16,30,1024]{3,1,2,0:T(8,128)(2,1)} %param.20) | copy-start | bytes 2949124
  5.9 2.7 %copy-start = (bf16[1,16,30,1024]{3,2,1,0:T(8,128)(2,1)}, bf16[1,16,30,1024]{3,2,1,0:T(8,128)(2,1)S(1)}, u32[]{:S(2)}) copy-start(bf16[1,16,30,1024]{3,2,1,0:T(8,128)(2,1)S(1)} %copy.25) | copy-start | bytes 2949124
  11.1 2.2 %copy-start.1 = (bf16[1,16,30,1024]{3,2,1,0:T(8,128)(2,1)S(1)}, bf16[1,16,30,1024]{3,2,1,0:T(8,128)(2,1)}, u32[]{:S(2)}) copy-start(bf16[1,16,30,1024]{3,2,1,0:T(8,128)(2,1)} %copy-done) | copy-start | bytes 2949124
  11.9 23.3 %collective-permute-start = (bf16[1,8,1024]{2,1,0:T(8,128)(2,1)S(1)}, bf16[1,8,1024]{2,1,0:T(8,128)(2,1)S(1)}, u32[]{:S(2)}, u32[]{:S(2)}) collective-permute-start(bf16[1,8,1024]{2,1,0:T(8,128)(2,1)S(1)} %slice.17), channel_id=1, source_target_pairs={{0,1},{2,3},{4,5},{6,7},{8,9},{10,11},{12,13},{14,15},{16,17},{18,... | collective-permute-start | bytes 49160 | tf_op jit(solution)/shard_map/ppermute | solution.py:18
  13.3 0.7 copy-start.5
  13.3 0.9 %copy-start.4 = (f32[1,31,1024]{2,0,1:T(1,128)S(1)}, f32[1,31,1024]{2,0,1:T(1,128)}, u32[]{:S(2)}) copy-start(f32[1,31,1024]{2,0,1:T(1,128)} %param.23) | copy-start | bytes 380932
  37.3 23.4 %collective-permute-start.1 = (bf16[16,16,1024]{2,1,0:T(8,128)(2,1)}, bf16[16,16,1024]{2,1,0:T(8,128)(2,1)}, u32[]{:S(2)}, u32[]{:S(2)}) collective-permute-start(bf16[16,16,1024]{2,1,0:T(8,128)(2,1)} %get-tuple-element.103), channel_id=1, source_target_pairs={{0,1},{2,3},{4,5},{6,7},{8,9},{10,11},{12,13},{14,15},{16,17},{18,... | collective-permute-start | bytes 1572872 | tf_op jit(solution)/shard_map/ppermute | solution.py:18

commit v14 on v12

--- a/solution.py
+++ b/solution.py
@@ -108,7 +108,10 @@
 
 
 def layer_kernel(sel_ref, x_ref, klive_ref, rlive_ref, cw_ref, qkv_hbm, wo_hbm, state_hbm,
-                 recv_hbm, *rest, streams, frames, ctx, head_size, kept_real, early):
+                 recv_hbm, *rest, streams, frames, ctx, head_size, kept_real, early, fused):
+    if fused:
+        wbuf = rest[-1]
+        rest = rest[:-1]
     if early:
         conv_in_ref, out_ref, wobuf, stv, qkv, conv_ref, pad_ref, res_ref, wsem, gsem = rest
     else:
@@ -143,17 +146,38 @@
             pltpu.make_async_copy(state_hbm.at[0, part], stv.at[j, part], gsem.at[which, j]).wait()
 
     rows_w = wo_hbm.shape[0]
-    copies = [pltpu.make_async_copy(qkv_hbm, qkv, wsem.at[0, 0])]
+    if fused:
+        first = []
+        for r in range(rows_w // CHUNK_ROWS):
+            part = pl.ds(r * CHUNK_ROWS, CHUNK_ROWS)
+            first.append(pltpu.make_async_copy(qkv_hbm.at[part], wbuf.at[part], wsem.at[0, r]))
+    else:
+        first = [pltpu.make_async_copy(qkv_hbm, qkv, wsem.at[0, 0])]
+    copies = []
     for r in range(rows_w // CHUNK_ROWS):
         part = pl.ds(r * CHUNK_ROWS, CHUNK_ROWS)
         copies.append(pltpu.make_async_copy(wo_hbm.at[part], wobuf.at[part], wsem.at[1, r]))
-    copies[0].start()
+    for c in first:
+        c.start()
     gather(keys_rows, 0)
-    for c in copies[1:]:
+    for c in copies:
         c.start()
     gather(conv_part, 1)
 
-    copies[0].wait()
+    if fused:
+        floats = x_ref[...].astype(jnp.float32)
+        centred = floats - jnp.mean(floats, axis=-1, keepdims=True)
+        variance = jnp.mean(centred * centred, axis=-1, keepdims=True)
+        normed = (centred * lax.rsqrt(variance + 1e-05)).astype(jnp.bfloat16)
+    for c in first:
+        c.wait()
+    if fused:
+        for i in range(3):
+            part = jnp.dot(normed, wbuf[:, pl.ds(i * width, width)],
+                           preferred_element_type=jnp.float32)
+            if i == 0:
+                part = part * (head_size ** -0.5)
+            qkv[i] = part.astype(jnp.bfloat16)
     gather_wait(keys_rows, 0)
 
     rows_g = GROUP * frames
@@ -200,7 +224,7 @@
 
         lax.fori_loop(0, width // pair, head_pair, 0)
 
-    for c in copies[1:]:
+    for c in copies:
         c.wait()
     mixed = jnp.dot(qkv[0], wobuf[...], preferred_element_type=jnp.float32)
     residual = x_ref[...].astype(jnp.float32) + mixed
@@ -251,7 +275,7 @@
 
 
 def encoder_layer(inputs, valid_counts, sel, state, recv, qkv_weight, out_weight, conv_weight,
-                  ctx, kept_real, conv_in=None, projected=None):
+                  ctx, kept_real, conv_in=None, projected=None, fused=False):
     streams, frames, width = inputs.shape
     taps = conv_weight.shape[0]
     head_size = width // HEADS
@@ -264,7 +288,8 @@
     kept = state.shape[1] - 2 * slot
     early = conv_in is not None
     kernel = functools.partial(layer_kernel, streams=streams, frames=frames, ctx=ctx,
-                               head_size=head_size, kept_real=kept_real, early=early)
+                               head_size=head_size, kept_real=kept_real, early=early,
+                               fused=fused)
     vmem = pl.BlockSpec(memory_space=pltpu.VMEM)
     hbm = pl.BlockSpec(memory_space=pl.ANY)
     extra = [conv_in] if early else []
@@ -283,8 +308,9 @@
             pltpu.VMEM((tokens, width), jnp.float32),
             pltpu.SemaphoreType.DMA((2, width // CHUNK_ROWS)),
             pltpu.SemaphoreType.DMA((2, streams)),
-        ],
-    )(sel, x, klive, rlive, conv_weight, project(inputs, qkv_weight) if projected is None else projected,
+        ] + ([pltpu.VMEM((width, 3 * width), jnp.bfloat16)] if fused else []),
+    )(sel, x, klive, rlive, conv_weight,
+      qkv_weight if fused else (project(inputs, qkv_weight) if projected is None else projected),
       out_weight, state, recv, *extra)
     return out.reshape(streams, frames, width)
 
@@ -357,7 +383,7 @@
     recv1 = lax.cond(on_first, lambda: jnp.zeros_like(send),
                      lambda: exchange(send + zero.astype(send.dtype)))
     inbound = shifted(first, "section", 1)
-    result = lax.cond(on_first, lambda: first, lambda: layer(inbound, recv=recv1))
+    result = lax.cond(on_first, lambda: first, lambda: layer(inbound, recv=recv1, fused=True))
     return result[None]
 
 

time: 87.3 us -> 82.6 us (0.946)
  Pallas kernels: 25.7 us -> 21.7 us
    pallas_call x1 -> x0, Pallas kernels: 6.24 us -> none  [project(): pl.pallas_call(kernel, out_shape=jax.ShapeDtypeStruct((3, tokens, width),...]
    pallas_call x1, Pallas kernels: 19.5 us -> 21.7 us  [encoder_layer(): pl.pallas_call(kernel, out_shape=jax.ShapeDtypeStruct((tokens, width), jn...]
where the time goes in v14:
time: 82.6 us; the launch traced here: 82.1 us
  waiting for transfers between devices  25.5 us (31%)
  Pallas kernels  21.7 us (26%)
  blocking collectives  17.5 us (21%)
  local copies, waits for them, and re-layouts  9.33 us (11%)
  other arithmetic  4.77 us (6%)
  starting transfers between devices  2.56 us (3%)
    ppermute x2, waiting for transfers between devices, shifted(): lax.ppermute(value, axis, [(source, source + steps) for source in range(l...  25.5 us
    pallas_call x1, Pallas kernels, encoder_layer(): pl.pallas_call(kernel, out_shape=jax.ShapeDtypeStruct((tokens, width), jn...  21.7 us
    all_to_all x1, blocking collectives, exchange(): return lax.all_to_all(send, 'stream', 0, 0, tiled=True)  17.5 us
    another operation x3, local copies, waits for them, and re-layouts  3.3 us
    ppermute x2, starting transfers between devices, shifted(): lax.ppermute(value, axis, [(source, source + steps) for source in range(l...  2.56 us
    unnamed x9, local copies, waits for them, and re-layouts  2.17 us
  transfers between devices with their start and end apart: 2, of which 2 were waited for; matrix products, arithmetic and copies ran while one was open for 0% of the time, Pallas kernels for 0%

profile of v14, /device:TPU:1, one launch (start us, length us, event | category | flops | bytes accessed | tf_op | source)
XLA Modules:
  0.0 82.1 jit_solution(12461388620548255921)
XLA Ops:
  0.0 0.8 %select_reduce_fusion = s32[128]{0:T(128)S(1)} fusion(s32[128]{0:T(128)} %param.18), kind=kLoop, calls=%fused_computation.20 | loop fusion | flops 49024 | bytes 1024 | tf_op jit(solution)/shard_map/reduce_sum | solution.py:321
  0.8 0.7 compare_select_fusion.7
  1.6 0.7 and_select_fusion
  2.3 0.1 select_reduce_fusion.1
  2.5 1.6 %copy.26 = bf16[1,16,12,2048]{3,2,1,0:T(8,128)(2,1)S(1)} copy(bf16[1,16,12,2048]{3,1,2,0:T(8,128)(2,1)} %param.19) | data formatting | bytes 1572864 | tf_op args[3]
  4.1 1.1 %fusion.8 = (bf16[16,12,1024]{2,1,0:T(8,128)(2,1)}, bf16[16,12,1024]{2,1,0:T(8,128)(2,1)}) fusion(bf16[16,12,2048]{2,1,0:T(8,128)(2,1)S(1)} %bitcast.22), kind=kLoop, calls=%fused_computation.38 | loop fusion | bytes 1572864 | tf_op jit(solution)/shard_map/slice | solution.py:356
  5.1 0.5 copy.25
  5.7 1.5 %fusion.7 = bf16[16,64,1024]{2,1,0:T(8,128)(2,1)S(1)} fusion(bf16[16,30,1024]{2,1,0:T(8,128)(2,1)S(1)} %bitcast.23, bf16[16,12,1024]{2,1,0:T(8,128)(2,1)} %get-tuple-element.92, bf16[16,12,1024]{2,1,0:T(8,128)(2,1)} %get-tuple-element.91), kind=kLoop, calls=%fused_computation.16 | loop fusion | flops 14680064 | bytes 3866624 | tf_op jit(solution)/shard_map/concatenate | solution.py:355
  7.2 0.6 gather_fusion
  7.8 0.0 copy-start.2
  7.8 0.0 copy-start.1
  7.8 2.5 %conditional.4 = (bf16[8,64,1024]{2,1,0:T(8,128)(2,1)}, bf16[3,256,1024]{2,1,0:T(8,128)(2,1)}) conditional(s32[]{:T(128)} %convert_element_type.70, () %tuple.34, (bf16[8,64,1024]{2,1,0:T(8,128)(2,1)S(1)}, bf16[16,16,1024]{2,1,0:T(8,128)(2,1)}, bf16[1,1024,3072]{2,1,0:T(8,128)(2,1)}) %tuple.35), branch_computations={%region_2.3_spmd, %region_3.4_spmd} | conditional | bytes 3145776 | solution.py:373
  7.8 1.3 %broadcast.65 = bf16[3,256,1024]{2,1,0:T(8,128)(2,1)} broadcast(bf16[]{:T(256)} %constant.35.clone), dimensions={} | broadcast | bytes 1572866 | tf_op jit(solution)/shard_map/broadcast.6
  9.2 1.1 %broadcast.64 = bf16[8,64,1024]{2,1,0:T(8,128)(2,1)} broadcast(bf16[]{:T(256)} %constant.35.clone), dimensions={} | broadcast | bytes 1048578 | tf_op jit(solution)/shard_map/broadcast.7
  10.3 0.7 slice.11
  11.0 1.3 %collective-permute-start = (bf16[1,8,1024]{2,1,0:T(8,128)(2,1)S(1)}, bf16[1,8,1024]{2,1,0:T(8,128)(2,1)S(1)}, u32[]{:S(2)}, u32[]{:S(2)}) collective-permute-start(bf16[1,8,1024]{2,1,0:T(8,128)(2,1)S(1)} %slice.11), channel_id=1, source_target_pairs={{0,1},{2,3},{4,5},{6,7},{8,9},{10,11},{12,13},{14,15},{16,17},{18,... | collective-permute-start | bytes 49160 | tf_op jit(solution)/shard_map/ppermute | solution.py:18
  12.3 0.1 pad_add_fusion
  12.4 0.1 dynamic_slice.9
  12.5 21.8 %collective-permute-done = bf16[1,8,1024]{2,1,0:T(8,128)(2,1)S(1)} collective-permute-done((bf16[1,8,1024]{2,1,0:T(8,128)(2,1)S(1)}, bf16[1,8,1024]{2,1,0:T(8,128)(2,1)S(1)}, u32[]{:S(2)}, u32[]{:S(2)}) %collective-permute-start) | collective-permute-done | bytes 16416 | tf_op jit(solution)/shard_map/ppermute | solution.py:18
  34.3 0.6 convert_reduce_fusion
  35.5 0.9 %conditional.5 = (bf16[16,16,1024]{2,1,0:T(8,128)(2,1)}) conditional(s32[]{:T(128)} %convert_element_type.70, () %tuple.33, (bf16[16,16,1024]{2,1,0:T(8,128)(2,1)}, s32[16]{0:T(128)S(1)}, s32[32]{0:T(128)S(1)}, f32[31,1024]{1,0:T(8,128)S(1)}, bf16[3,256,1024]{2,1,0:T(8,128)(2,1)}, /*index=5*/bf16[1024,1024]{1,0:T(8,128)(2,1)}, ...), branch_computations={%region_5.6_spmd, %region_6.7_spmd} | conditional | flops 544 | bytes 524298 | solution.py:379
  35.6 0.9 %broadcast.66 = bf16[16,16,1024]{2,1,0:T(8,128)(2,1)} broadcast(bf16[]{:T(256)} %constant.36.clone), dimensions={} | broadcast | bytes 524290 | tf_op jit(solution)/shard_map/broadcast.9
  36.4 1.3 %collective-permute-start.1 = (bf16[16,16,1024]{2,1,0:T(8,128)(2,1)}, bf16[16,16,1024]{2,1,0:T(8,128)(2,1)}, u32[]{:S(2)}, u32[]{:S(2)}) collective-permute-start(bf16[16,16,1024]{2,1,0:T(8,128)(2,1)} %get-tuple-element.101), channel_id=1, source_target_pairs={{0,1},{2,3},{4,5},{6,7},{8,9},{10,11},{12,13},{14,15},{16,17},{18,... | collective-permute-start | bytes 1572872 | tf_op jit(solution)/shard_map/ppermute | solution.py:18
  37.7 17.6 %conditional.6 = (bf16[8,64,1024]{2,1,0:T(8,128)(2,1)S(1)}) conditional(s32[]{:T(128)} %convert_element_type.70, (f32[]{:T(128)}, bf16[8,64,1024]{2,1,0:T(8,128)(2,1)S(1)}) %tuple.37, () %tuple.38), branch_computations={%region_7.8_spmd, %region_8.9_spmd} | conditional | flops 524289 | bytes 4194320 | solution.py:383
  37.7 0.1 broadcast_add_fusion.1
  37.8 17.5 %all_to_all.8 = bf16[8,64,1024]{2,1,0:T(8,128)(2,1)S(1)} all-to-all(bf16[8,64,1024]{2,1,0:T(8,128)(2,1)S(1)} %broadcast_add_fusion.1), channel_id=1, replica_groups=mesh['groups'=2,'stream'=8,'section'=2] {'stream'}, dimensions={0} | all-to-all | bytes 2097152 | tf_op jit(solution)/shard_map/cond/branch_0_fun/all_to_all | solution.py:340
  55.3 3.7 %collective-permute-done.1 = bf16[16,16,1024]{2,1,0:T(8,128)(2,1)} collective-permute-done((bf16[16,16,1024]{2,1,0:T(8,128)(2,1)}, bf16[16,16,1024]{2,1,0:T(8,128)(2,1)}, u32[]{:S(2)}, u32[]{:S(2)}) %collective-permute-start.1) | collective-permute-done | bytes 524320 | tf_op jit(solution)/shard_map/ppermute | solution.py:18
  59.0 23.1 %conditional.7 = (bf16[1,16,16,1024]{3,2,1,0:T(8,128)(2,1)}) conditional(s32[]{:T(128)} %convert_element_type.70, (bf16[16,16,1024]{2,1,0:T(8,128)(2,1)}, s32[16]{0:T(128)S(1)}, bf16[1,1024,3072]{2,1,0:T(8,128)(2,1)}, s32[32]{0:T(128)S(1)}, f32[31,1024]{1,0:T(8,128)S(1)}, /*index=5*/bf16[1024,1024]{1,0:T(8,128)(2,1)}, ...), branch_computations={%region_9.10_spmd, %region_10.11_spmd} | conditional | flops 512 | bytes 1048584 | solution.py:386
  59.0 0.1 fusion.1
  59.1 0.7 reshape.154.rlive_ref
  59.8 0.6 reshape.142.klive_ref
  60.5 21.7 %branch_0_fun.1 = bf16[256,1024]{1,0:T(8,128)(2,1)} custom-call(s32[32]{0:T(128)S(1)} %get-tuple-element.73.sel_ref, bf16[256,1024]{1,0:T(8,128)(2,1)} %bitcast.4.x_ref, f32[1,256]{1,0:T(1,128)} %reshape.142.klive_ref, f32[256,1]{1,0:T(8,128)} %reshape.154.rlive_ref, f32[31,1024]{1,0:T(8,128)S(1)} %get-tuple-element.76.cw_ref, bf16[1024,3072]{1,0:T(8,128)(2,1)} %bitcast.19, ...), custom_call_target="tpu_custom_call" | custom-call | tf_op jit(solution)/shard_map/cond/branch_0_fun/pallas_call | solution.py:296
  (7 shorter events, 0.0 us)
Async XLA Ops:
  0.0 5.1 %copy-start = (bf16[1,16,30,1024]{3,1,2,0:T(8,128)(2,1)S(1)}, bf16[1,16,30,1024]{3,1,2,0:T(8,128)(2,1)}, u32[]{:S(2)}) copy-start(bf16[1,16,30,1024]{3,1,2,0:T(8,128)(2,1)} %param.20) | copy-start | bytes 2949124
  7.8 4.6 %copy-start.2 = (s32[128]{0:T(128)S(1)}, s32[128]{0:T(128)}, u32[]{:S(2)}) copy-start(s32[128]{0:T(128)} %param.17) | copy-start | bytes 1540
  7.8 4.6 %copy-start.1 = (f32[1,31,1024]{2,0,1:T(1,128)S(1)}, f32[1,31,1024]{2,0,1:T(1,128)}, u32[]{:S(2)}) copy-start(f32[1,31,1024]{2,0,1:T(1,128)} %param.23) | copy-start | bytes 380932
  11.0 23.3 %collective-permute-start = (bf16[1,8,1024]{2,1,0:T(8,128)(2,1)S(1)}, bf16[1,8,1024]{2,1,0:T(8,128)(2,1)S(1)}, u32[]{:S(2)}, u32[]{:S(2)}) collective-permute-start(bf16[1,8,1024]{2,1,0:T(8,128)(2,1)S(1)} %slice.11), channel_id=1, source_target_pairs={{0,1},{2,3},{4,5},{6,7},{8,9},{10,11},{12,13},{14,15},{16,17},{18,... | collective-permute-start | bytes 49160 | tf_op jit(solution)/shard_map/ppermute | solution.py:18
  36.4 22.6 %collective-permute-start.1 = (bf16[16,16,1024]{2,1,0:T(8,128)(2,1)}, bf16[16,16,1024]{2,1,0:T(8,128)(2,1)}, u32[]{:S(2)}, u32[]{:S(2)}) collective-permute-start(bf16[16,16,1024]{2,1,0:T(8,128)(2,1)} %get-tuple-element.101), channel_id=1, source_target_pairs={{0,1},{2,3},{4,5},{6,7},{8,9},{10,11},{12,13},{14,15},{16,17},{18,... | collective-permute-start | bytes 1572872 | tf_op jit(solution)/shard_map/ppermute | solution.py:18

commit v15 on v14

--- a/solution.py
+++ b/solution.py
@@ -157,18 +157,30 @@
     for r in range(rows_w // CHUNK_ROWS):
         part = pl.ds(r * CHUNK_ROWS, CHUNK_ROWS)
         copies.append(pltpu.make_async_copy(wo_hbm.at[part], wobuf.at[part], wsem.at[1, r]))
-    for c in first:
-        c.start()
-    gather(keys_rows, 0)
-    for c in copies:
-        c.start()
-    gather(conv_part, 1)
-
+    origin = kept - kept_real
     if fused:
+        gather(conv_part, 1)
+        for c in first:
+            c.start()
+        gather(keys_rows, 0)
+        for c in copies:
+            c.start()
         floats = x_ref[...].astype(jnp.float32)
         centred = floats - jnp.mean(floats, axis=-1, keepdims=True)
         variance = jnp.mean(centred * centred, axis=-1, keepdims=True)
         normed = (centred * lax.rsqrt(variance + 1e-05)).astype(jnp.bfloat16)
+        gather_wait(conv_part, 1)
+        pad_ref[:, 0:kept, :] = stv[:, pl.ds(2 * slot, kept), :].astype(jnp.float32)
+        pad_ref[:, kept:, :] = jnp.zeros((streams, frames, width), jnp.float32)
+        conv_ref[...] = jnp.zeros_like(conv_ref)
+        conv_rows(conv_ref, pad_ref, cw_ref, kept_taps(taps, kept_real, frames), frames, origin)
+    else:
+        for c in first:
+            c.start()
+        gather(keys_rows, 0)
+        for c in copies:
+            c.start()
+        gather(conv_part, 1)
     for c in first:
         c.wait()
     if fused:
@@ -230,9 +242,13 @@
     residual = x_ref[...].astype(jnp.float32) + mixed
     res_ref[...] = residual
     rounded = residual.astype(jnp.bfloat16).astype(jnp.float32).reshape(streams, frames, width)
-    gather_wait(conv_part, 1)
-    origin = kept - kept_real
-    if early:
+    if not fused:
+        gather_wait(conv_part, 1)
+    if fused:
+        pad_ref[:, 0:kept, :] = jnp.zeros((streams, kept, width), jnp.float32)
+        pad_ref[:, kept:, :] = rounded
+        conv_rows(conv_ref, pad_ref, cw_ref, new_taps(taps, kept_real, frames), frames, origin)
+    elif early:
         pad_ref[:, 0:kept, :] = jnp.zeros((streams, kept, width), jnp.float32)
         pad_ref[:, kept:, :] = rounded
         conv_ref[...] = conv_in_ref[...]

time: 82.6 us -> 84.5 us (1.023)
  Pallas kernels: 21.7 us -> 23.2 us
    pallas_call x1, Pallas kernels: 21.7 us -> 23.2 us  [encoder_layer(): pl.pallas_call(kernel, out_shape=jax.ShapeDtypeStruct((tokens, width), jn...]
where the time goes in v15:
time: 84.5 us; the launch traced here: 83.7 us
  waiting for transfers between devices  25.5 us (30%)
  Pallas kernels  23.2 us (27%)
  blocking collectives  17.5 us (21%)
  local copies, waits for them, and re-layouts  9.33 us (11%)
  other arithmetic  4.77 us (6%)
  starting transfers between devices  2.56 us (3%)
    ppermute x2, waiting for transfers between devices, shifted(): lax.ppermute(value, axis, [(source, source + steps) for source in range(l...  25.5 us
    pallas_call x1, Pallas kernels, encoder_layer(): pl.pallas_call(kernel, out_shape=jax.ShapeDtypeStruct((tokens, width), jn...  23.2 us
    all_to_all x1, blocking collectives, exchange(): return lax.all_to_all(send, 'stream', 0, 0, tiled=True)  17.5 us
    another operation x3, local copies, waits for them, and re-layouts  3.3 us
    ppermute x2, starting transfers between devices, shifted(): lax.ppermute(value, axis, [(source, source + steps) for source in range(l...  2.56 us
    unnamed x9, local copies, waits for them, and re-layouts  2.17 us
  transfers between devices with their start and end apart: 2, of which 2 were waited for; matrix products, arithmetic and copies ran while one was open for 0% of the time, Pallas kernels for 0%

profile of v15, /device:TPU:1, one launch (start us, length us, event | category | flops | bytes accessed | tf_op | source)
XLA Modules:
  0.0 83.7 jit_solution(9844920104953896244)
XLA Ops:
  0.0 0.8 %select_reduce_fusion = s32[128]{0:T(128)S(1)} fusion(s32[128]{0:T(128)} %param.18), kind=kLoop, calls=%fused_computation.20 | loop fusion | flops 49024 | bytes 1024 | tf_op jit(solution)/shard_map/reduce_sum | solution.py:337
  0.8 0.7 compare_select_fusion.7
  1.6 0.7 and_select_fusion
  2.3 0.1 select_reduce_fusion.1
  2.5 1.6 %copy.26 = bf16[1,16,12,2048]{3,2,1,0:T(8,128)(2,1)S(1)} copy(bf16[1,16,12,2048]{3,1,2,0:T(8,128)(2,1)} %param.19) | data formatting | bytes 1572864 | tf_op args[3]
  4.1 1.1 %fusion.8 = (bf16[16,12,1024]{2,1,0:T(8,128)(2,1)}, bf16[16,12,1024]{2,1,0:T(8,128)(2,1)}) fusion(bf16[16,12,2048]{2,1,0:T(8,128)(2,1)S(1)} %bitcast.22), kind=kLoop, calls=%fused_computation.38 | loop fusion | bytes 1572864 | tf_op jit(solution)/shard_map/slice | solution.py:372
  5.1 0.5 copy.25
  5.7 1.5 %fusion.7 = bf16[16,64,1024]{2,1,0:T(8,128)(2,1)S(1)} fusion(bf16[16,30,1024]{2,1,0:T(8,128)(2,1)S(1)} %bitcast.23, bf16[16,12,1024]{2,1,0:T(8,128)(2,1)} %get-tuple-element.92, bf16[16,12,1024]{2,1,0:T(8,128)(2,1)} %get-tuple-element.91), kind=kLoop, calls=%fused_computation.16 | loop fusion | flops 14680064 | bytes 3866624 | tf_op jit(solution)/shard_map/concatenate | solution.py:371
  7.2 0.6 gather_fusion
  7.8 0.0 copy-start.2
  7.8 0.0 copy-start.1
  7.8 2.5 %conditional.4 = (bf16[8,64,1024]{2,1,0:T(8,128)(2,1)}, bf16[3,256,1024]{2,1,0:T(8,128)(2,1)}) conditional(s32[]{:T(128)} %convert_element_type.70, () %tuple.34, (bf16[8,64,1024]{2,1,0:T(8,128)(2,1)S(1)}, bf16[16,16,1024]{2,1,0:T(8,128)(2,1)}, bf16[1,1024,3072]{2,1,0:T(8,128)(2,1)}) %tuple.35), branch_computations={%region_2.3_spmd, %region_3.4_spmd} | conditional | bytes 3145776 | solution.py:389
  7.8 1.3 %broadcast.65 = bf16[3,256,1024]{2,1,0:T(8,128)(2,1)} broadcast(bf16[]{:T(256)} %constant.35.clone), dimensions={} | broadcast | bytes 1572866 | tf_op jit(solution)/shard_map/broadcast.6
  9.2 1.1 %broadcast.64 = bf16[8,64,1024]{2,1,0:T(8,128)(2,1)} broadcast(bf16[]{:T(256)} %constant.35.clone), dimensions={} | broadcast | bytes 1048578 | tf_op jit(solution)/shard_map/broadcast.7
  10.3 0.7 slice.11
  11.0 1.3 %collective-permute-start = (bf16[1,8,1024]{2,1,0:T(8,128)(2,1)S(1)}, bf16[1,8,1024]{2,1,0:T(8,128)(2,1)S(1)}, u32[]{:S(2)}, u32[]{:S(2)}) collective-permute-start(bf16[1,8,1024]{2,1,0:T(8,128)(2,1)S(1)} %slice.11), channel_id=1, source_target_pairs={{0,1},{2,3},{4,5},{6,7},{8,9},{10,11},{12,13},{14,15},{16,17},{18,... | collective-permute-start | bytes 49160 | tf_op jit(solution)/shard_map/ppermute | solution.py:18
  12.3 0.1 pad_add_fusion
  12.4 0.1 dynamic_slice.9
  12.5 21.8 %collective-permute-done = bf16[1,8,1024]{2,1,0:T(8,128)(2,1)S(1)} collective-permute-done((bf16[1,8,1024]{2,1,0:T(8,128)(2,1)S(1)}, bf16[1,8,1024]{2,1,0:T(8,128)(2,1)S(1)}, u32[]{:S(2)}, u32[]{:S(2)}) %collective-permute-start) | collective-permute-done | bytes 16416 | tf_op jit(solution)/shard_map/ppermute | solution.py:18
  34.3 0.6 convert_reduce_fusion
  35.5 0.9 %conditional.5 = (bf16[16,16,1024]{2,1,0:T(8,128)(2,1)}) conditional(s32[]{:T(128)} %convert_element_type.70, () %tuple.33, (bf16[16,16,1024]{2,1,0:T(8,128)(2,1)}, s32[16]{0:T(128)S(1)}, s32[32]{0:T(128)S(1)}, f32[31,1024]{1,0:T(8,128)S(1)}, bf16[3,256,1024]{2,1,0:T(8,128)(2,1)}, /*index=5*/bf16[1024,1024]{1,0:T(8,128)(2,1)}, ...), branch_computations={%region_5.6_spmd, %region_6.7_spmd} | conditional | flops 544 | bytes 524298 | solution.py:395
  35.6 0.9 %broadcast.66 = bf16[16,16,1024]{2,1,0:T(8,128)(2,1)} broadcast(bf16[]{:T(256)} %constant.36.clone), dimensions={} | broadcast | bytes 524290 | tf_op jit(solution)/shard_map/broadcast.9
  36.4 1.3 %collective-permute-start.1 = (bf16[16,16,1024]{2,1,0:T(8,128)(2,1)}, bf16[16,16,1024]{2,1,0:T(8,128)(2,1)}, u32[]{:S(2)}, u32[]{:S(2)}) collective-permute-start(bf16[16,16,1024]{2,1,0:T(8,128)(2,1)} %get-tuple-element.101), channel_id=1, source_target_pairs={{0,1},{2,3},{4,5},{6,7},{8,9},{10,11},{12,13},{14,15},{16,17},{18,... | collective-permute-start | bytes 1572872 | tf_op jit(solution)/shard_map/ppermute | solution.py:18
  37.7 17.6 %conditional.6 = (bf16[8,64,1024]{2,1,0:T(8,128)(2,1)S(1)}) conditional(s32[]{:T(128)} %convert_element_type.70, (f32[]{:T(128)}, bf16[8,64,1024]{2,1,0:T(8,128)(2,1)S(1)}) %tuple.37, () %tuple.38), branch_computations={%region_7.8_spmd, %region_8.9_spmd} | conditional | flops 524289 | bytes 4194320 | solution.py:399
  37.7 0.1 broadcast_add_fusion.1
  37.8 17.5 %all_to_all.8 = bf16[8,64,1024]{2,1,0:T(8,128)(2,1)S(1)} all-to-all(bf16[8,64,1024]{2,1,0:T(8,128)(2,1)S(1)} %broadcast_add_fusion.1), channel_id=1, replica_groups=mesh['groups'=2,'stream'=8,'section'=2] {'stream'}, dimensions={0} | all-to-all | bytes 2097152 | tf_op jit(solution)/shard_map/cond/branch_0_fun/all_to_all | solution.py:356
  55.3 3.7 %collective-permute-done.1 = bf16[16,16,1024]{2,1,0:T(8,128)(2,1)} collective-permute-done((bf16[16,16,1024]{2,1,0:T(8,128)(2,1)}, bf16[16,16,1024]{2,1,0:T(8,128)(2,1)}, u32[]{:S(2)}, u32[]{:S(2)}) %collective-permute-start.1) | collective-permute-done | bytes 524320 | tf_op jit(solution)/shard_map/ppermute | solution.py:18
  59.0 24.7 %conditional.7 = (bf16[1,16,16,1024]{3,2,1,0:T(8,128)(2,1)}) conditional(s32[]{:T(128)} %convert_element_type.70, (bf16[16,16,1024]{2,1,0:T(8,128)(2,1)}, s32[16]{0:T(128)S(1)}, bf16[1,1024,3072]{2,1,0:T(8,128)(2,1)}, s32[32]{0:T(128)S(1)}, f32[31,1024]{1,0:T(8,128)S(1)}, /*index=5*/bf16[1024,1024]{1,0:T(8,128)(2,1)}, ...), branch_computations={%region_9.10_spmd, %region_10.11_spmd} | conditional | flops 512 | bytes 1048584 | solution.py:402
  59.0 0.1 fusion.1
  59.1 0.7 reshape.154.rlive_ref
  59.8 0.6 reshape.142.klive_ref
  60.5 23.2 %branch_0_fun.1 = bf16[256,1024]{1,0:T(8,128)(2,1)} custom-call(s32[32]{0:T(128)S(1)} %get-tuple-element.73.sel_ref, bf16[256,1024]{1,0:T(8,128)(2,1)} %bitcast.4.x_ref, f32[1,256]{1,0:T(1,128)} %reshape.142.klive_ref, f32[256,1]{1,0:T(8,128)} %reshape.154.rlive_ref, f32[31,1024]{1,0:T(8,128)S(1)} %get-tuple-element.76.cw_ref, bf16[1024,3072]{1,0:T(8,128)(2,1)} %bitcast.19, ...), custom_call_target="tpu_custom_call" | custom-call | tf_op jit(solution)/shard_map/cond/branch_0_fun/pallas_call | solution.py:312
  (7 shorter events, 0.0 us)
Async XLA Ops:
  0.0 5.1 %copy-start = (bf16[1,16,30,1024]{3,1,2,0:T(8,128)(2,1)S(1)}, bf16[1,16,30,1024]{3,1,2,0:T(8,128)(2,1)}, u32[]{:S(2)}) copy-start(bf16[1,16,30,1024]{3,1,2,0:T(8,128)(2,1)} %param.20) | copy-start | bytes 2949124
  7.8 4.6 %copy-start.2 = (s32[128]{0:T(128)S(1)}, s32[128]{0:T(128)}, u32[]{:S(2)}) copy-start(s32[128]{0:T(128)} %param.17) | copy-start | bytes 1540
  7.8 4.6 %copy-start.1 = (f32[1,31,1024]{2,0,1:T(1,128)S(1)}, f32[1,31,1024]{2,0,1:T(1,128)}, u32[]{:S(2)}) copy-start(f32[1,31,1024]{2,0,1:T(1,128)} %param.23) | copy-start | bytes 380932
  11.0 23.3 %collective-permute-start = (bf16[1,8,1024]{2,1,0:T(8,128)(2,1)S(1)}, bf16[1,8,1024]{2,1,0:T(8,128)(2,1)S(1)}, u32[]{:S(2)}, u32[]{:S(2)}) collective-permute-start(bf16[1,8,1024]{2,1,0:T(8,128)(2,1)S(1)} %slice.11), channel_id=1, source_target_pairs={{0,1},{2,3},{4,5},{6,7},{8,9},{10,11},{12,13},{14,15},{16,17},{18,... | collective-permute-start | bytes 49160 | tf_op jit(solution)/shard_map/ppermute | solution.py:18
  36.4 22.6 %collective-permute-start.1 = (bf16[16,16,1024]{2,1,0:T(8,128)(2,1)}, bf16[16,16,1024]{2,1,0:T(8,128)(2,1)}, u32[]{:S(2)}, u32[]{:S(2)}) collective-permute-start(bf16[16,16,1024]{2,1,0:T(8,128)(2,1)} %get-tuple-element.101), channel_id=1, source_target_pairs={{0,1},{2,3},{4,5},{6,7},{8,9},{10,11},{12,13},{14,15},{16,17},{18,... | collective-permute-start | bytes 1572872 | tf_op jit(solution)/shard_map/ppermute | solution.py:18

commit v16 on v14

--- a/solution.py
+++ b/solution.py
@@ -318,9 +318,8 @@
 def migrate(anchor, own, count, local_count, state):
     total = anchor.shape[0]
     every_slot = jnp.arange(total, dtype=jnp.int32)
-    newpos = jnp.sum(jnp.where(anchor[None, :] == every_slot[:, None], every_slot[None, :], 0),
-                     axis=1)
-    mine_new = lax.dynamic_slice_in_dim(newpos, own * local_count, local_count)
+    mine = own * local_count + jnp.arange(local_count, dtype=jnp.int32)
+    mine_new = jnp.sum(jnp.where(anchor[None, :] == mine[:, None], every_slot[None, :], 0), axis=1)
     target = mine_new // local_count
     hosts = jnp.arange(count, dtype=jnp.int32)
     match = target[None, :] == hosts[:, None]

time: 82.6 us -> 83.3 us (level)
  no operation moved by 1% of the time
where the time goes in v16:
time: 83.3 us; the launch traced here: 82.8 us
  waiting for transfers between devices  26.1 us (31%)
  Pallas kernels  21.7 us (26%)
  blocking collectives  17.5 us (21%)
  local copies, waits for them, and re-layouts  9.33 us (11%)
  other arithmetic  4.85 us (6%)
  starting transfers between devices  2.56 us (3%)
    ppermute x2, waiting for transfers between devices, shifted(): lax.ppermute(value, axis, [(source, source + steps) for source in range(l...  26.1 us
    pallas_call x1, Pallas kernels, encoder_layer(): pl.pallas_call(kernel, out_shape=jax.ShapeDtypeStruct((tokens, width), jn...  21.7 us
    all_to_all x1, blocking collectives, exchange(): return lax.all_to_all(send, 'stream', 0, 0, tiled=True)  17.5 us
    another operation x3, local copies, waits for them, and re-layouts  3.3 us
    ppermute x2, starting transfers between devices, shifted(): lax.ppermute(value, axis, [(source, source + steps) for source in range(l...  2.56 us
    unnamed x9, local copies, waits for them, and re-layouts  2.17 us
  transfers between devices with their start and end apart: 2, of which 2 were waited for; matrix products, arithmetic and copies ran while one was open for 0% of the time, Pallas kernels for 0%

profile of v16, /device:TPU:1, one launch (start us, length us, event | category | flops | bytes accessed | tf_op | source)
XLA Modules:
  0.0 82.8 jit_solution(18341642367099664322)
XLA Ops:
  0.0 0.8 compare_select_fusion.7
  0.8 0.7 compare_select_fusion.6
  1.6 0.8 %select_reduce_fusion = s32[16]{0:T(128)S(1)} fusion(s32[128]{0:T(128)} %param.18, s32[16]{0:T(128)S(1)} %get-tuple-element.94), kind=kLoop, calls=%fused_computation.21 | loop fusion | flops 6128 | bytes 640 | tf_op jit(solution)/shard_map/reduce_sum | solution.py:322
  2.4 0.1 select_reduce_fusion.1
  2.5 1.6 %copy.26 = bf16[1,16,12,2048]{3,2,1,0:T(8,128)(2,1)S(1)} copy(bf16[1,16,12,2048]{3,1,2,0:T(8,128)(2,1)} %param.19) | data formatting | bytes 1572864 | tf_op args[3]
  4.1 1.1 %fusion.8 = (bf16[16,12,1024]{2,1,0:T(8,128)(2,1)}, bf16[16,12,1024]{2,1,0:T(8,128)(2,1)}) fusion(bf16[16,12,2048]{2,1,0:T(8,128)(2,1)S(1)} %bitcast.22), kind=kLoop, calls=%fused_computation.38 | loop fusion | bytes 1572864 | tf_op jit(solution)/shard_map/slice | solution.py:355
  5.2 0.5 copy.25
  5.8 1.5 %fusion.7 = bf16[16,64,1024]{2,1,0:T(8,128)(2,1)S(1)} fusion(bf16[16,30,1024]{2,1,0:T(8,128)(2,1)S(1)} %bitcast.23, bf16[16,12,1024]{2,1,0:T(8,128)(2,1)} %get-tuple-element.92, bf16[16,12,1024]{2,1,0:T(8,128)(2,1)} %get-tuple-element.91), kind=kLoop, calls=%fused_computation.16 | loop fusion | flops 14680064 | bytes 3866624 | tf_op jit(solution)/shard_map/concatenate | solution.py:354
  7.3 0.6 gather_fusion
  7.9 0.0 copy-start.2
  7.9 0.0 copy-start.1
  7.9 2.5 %conditional.4 = (bf16[8,64,1024]{2,1,0:T(8,128)(2,1)}, bf16[3,256,1024]{2,1,0:T(8,128)(2,1)}) conditional(s32[]{:T(128)} %convert_element_type.70, () %tuple.34, (bf16[8,64,1024]{2,1,0:T(8,128)(2,1)S(1)}, bf16[16,16,1024]{2,1,0:T(8,128)(2,1)}, bf16[1,1024,3072]{2,1,0:T(8,128)(2,1)}) %tuple.35), branch_computations={%region_2.3_spmd, %region_3.4_spmd} | conditional | bytes 3145776 | solution.py:372
  7.9 1.3 %broadcast.93 = bf16[3,256,1024]{2,1,0:T(8,128)(2,1)} broadcast(bf16[]{:T(256)} %constant.35.clone), dimensions={} | broadcast | bytes 1572866 | tf_op jit(solution)/shard_map/broadcast.6
  9.3 1.1 %broadcast.92 = bf16[8,64,1024]{2,1,0:T(8,128)(2,1)} broadcast(bf16[]{:T(256)} %constant.35.clone), dimensions={} | broadcast | bytes 1048578 | tf_op jit(solution)/shard_map/broadcast.7
  10.4 0.7 slice.11
  11.1 1.3 %collective-permute-start = (bf16[1,8,1024]{2,1,0:T(8,128)(2,1)S(1)}, bf16[1,8,1024]{2,1,0:T(8,128)(2,1)S(1)}, u32[]{:S(2)}, u32[]{:S(2)}) collective-permute-start(bf16[1,8,1024]{2,1,0:T(8,128)(2,1)S(1)} %slice.11), channel_id=1, source_target_pairs={{0,1},{2,3},{4,5},{6,7},{8,9},{10,11},{12,13},{14,15},{16,17},{18,... | collective-permute-start | bytes 49160 | tf_op jit(solution)/shard_map/ppermute | solution.py:18
  12.4 0.1 pad_add_fusion
  12.4 0.1 dynamic_slice.6
  12.6 21.8 %collective-permute-done = bf16[1,8,1024]{2,1,0:T(8,128)(2,1)S(1)} collective-permute-done((bf16[1,8,1024]{2,1,0:T(8,128)(2,1)S(1)}, bf16[1,8,1024]{2,1,0:T(8,128)(2,1)S(1)}, u32[]{:S(2)}, u32[]{:S(2)}) %collective-permute-start) | collective-permute-done | bytes 16416 | tf_op jit(solution)/shard_map/ppermute | solution.py:18
  34.4 0.6 convert_reduce_fusion
  35.6 0.9 %conditional.5 = (bf16[16,16,1024]{2,1,0:T(8,128)(2,1)}) conditional(s32[]{:T(128)} %convert_element_type.70, () %tuple.33, (bf16[16,16,1024]{2,1,0:T(8,128)(2,1)}, s32[16]{0:T(128)S(1)}, s32[32]{0:T(128)S(1)}, f32[31,1024]{1,0:T(8,128)S(1)}, bf16[3,256,1024]{2,1,0:T(8,128)(2,1)}, /*index=5*/bf16[1024,1024]{1,0:T(8,128)(2,1)}, ...), branch_computations={%region_5.6_spmd, %region_6.7_spmd} | conditional | flops 544 | bytes 524298 | solution.py:378
  35.6 0.9 %broadcast.94 = bf16[16,16,1024]{2,1,0:T(8,128)(2,1)} broadcast(bf16[]{:T(256)} %constant.36.clone), dimensions={} | broadcast | bytes 524290 | tf_op jit(solution)/shard_map/broadcast.9
  36.5 1.3 %collective-permute-start.1 = (bf16[16,16,1024]{2,1,0:T(8,128)(2,1)}, bf16[16,16,1024]{2,1,0:T(8,128)(2,1)}, u32[]{:S(2)}, u32[]{:S(2)}) collective-permute-start(bf16[16,16,1024]{2,1,0:T(8,128)(2,1)} %get-tuple-element.101), channel_id=1, source_target_pairs={{0,1},{2,3},{4,5},{6,7},{8,9},{10,11},{12,13},{14,15},{16,17},{18,... | collective-permute-start | bytes 1572872 | tf_op jit(solution)/shard_map/ppermute | solution.py:18
  37.8 17.6 %conditional.6 = (bf16[8,64,1024]{2,1,0:T(8,128)(2,1)S(1)}) conditional(s32[]{:T(128)} %convert_element_type.70, (f32[]{:T(128)}, bf16[8,64,1024]{2,1,0:T(8,128)(2,1)S(1)}) %tuple.37, () %tuple.38), branch_computations={%region_7.8_spmd, %region_8.9_spmd} | conditional | flops 524289 | bytes 4194320 | solution.py:382
  37.8 0.1 broadcast_add_fusion.1
  37.9 17.5 %all_to_all.8 = bf16[8,64,1024]{2,1,0:T(8,128)(2,1)S(1)} all-to-all(bf16[8,64,1024]{2,1,0:T(8,128)(2,1)S(1)} %broadcast_add_fusion.1), channel_id=1, replica_groups=mesh['groups'=2,'stream'=8,'section'=2] {'stream'}, dimensions={0} | all-to-all | bytes 2097152 | tf_op jit(solution)/shard_map/cond/branch_0_fun/all_to_all | solution.py:339
  55.4 4.3 %collective-permute-done.1 = bf16[16,16,1024]{2,1,0:T(8,128)(2,1)} collective-permute-done((bf16[16,16,1024]{2,1,0:T(8,128)(2,1)}, bf16[16,16,1024]{2,1,0:T(8,128)(2,1)}, u32[]{:S(2)}, u32[]{:S(2)}) %collective-permute-start.1) | collective-permute-done | bytes 524320 | tf_op jit(solution)/shard_map/ppermute | solution.py:18
  59.7 23.1 %conditional.7 = (bf16[1,16,16,1024]{3,2,1,0:T(8,128)(2,1)}) conditional(s32[]{:T(128)} %convert_element_type.70, (bf16[16,16,1024]{2,1,0:T(8,128)(2,1)}, s32[16]{0:T(128)S(1)}, bf16[1,1024,3072]{2,1,0:T(8,128)(2,1)}, s32[32]{0:T(128)S(1)}, f32[31,1024]{1,0:T(8,128)S(1)}, /*index=5*/bf16[1024,1024]{1,0:T(8,128)(2,1)}, ...), branch_computations={%region_9.10_spmd, %region_10.11_spmd} | conditional | flops 512 | bytes 1048584 | solution.py:385
  59.7 0.1 fusion.1
  59.8 0.7 reshape.174.rlive_ref
  60.5 0.6 reshape.162.klive_ref
  61.2 21.7 %branch_0_fun.1 = bf16[256,1024]{1,0:T(8,128)(2,1)} custom-call(s32[32]{0:T(128)S(1)} %get-tuple-element.73.sel_ref, bf16[256,1024]{1,0:T(8,128)(2,1)} %bitcast.4.x_ref, f32[1,256]{1,0:T(1,128)} %reshape.162.klive_ref, f32[256,1]{1,0:T(8,128)} %reshape.174.rlive_ref, f32[31,1024]{1,0:T(8,128)S(1)} %get-tuple-element.76.cw_ref, bf16[1024,3072]{1,0:T(8,128)(2,1)} %bitcast.19, ...), custom_call_target="tpu_custom_call" | custom-call | tf_op jit(solution)/shard_map/cond/branch_0_fun/pallas_call | solution.py:296
  (8 shorter events, 0.1 us)
Async XLA Ops:
  0.0 5.2 %copy-start = (bf16[1,16,30,1024]{3,1,2,0:T(8,128)(2,1)S(1)}, bf16[1,16,30,1024]{3,1,2,0:T(8,128)(2,1)}, u32[]{:S(2)}) copy-start(bf16[1,16,30,1024]{3,1,2,0:T(8,128)(2,1)} %param.20) | copy-start | bytes 2949124
  7.9 4.6 %copy-start.2 = (s32[128]{0:T(128)S(1)}, s32[128]{0:T(128)}, u32[]{:S(2)}) copy-start(s32[128]{0:T(128)} %param.17) | copy-start | bytes 1540
  7.9 4.6 %copy-start.1 = (f32[1,31,1024]{2,0,1:T(1,128)S(1)}, f32[1,31,1024]{2,0,1:T(1,128)}, u32[]{:S(2)}) copy-start(f32[1,31,1024]{2,0,1:T(1,128)} %param.23) | copy-start | bytes 380932
  11.1 23.3 %collective-permute-start = (bf16[1,8,1024]{2,1,0:T(8,128)(2,1)S(1)}, bf16[1,8,1024]{2,1,0:T(8,128)(2,1)S(1)}, u32[]{:S(2)}, u32[]{:S(2)}) collective-permute-start(bf16[1,8,1024]{2,1,0:T(8,128)(2,1)S(1)} %slice.11), channel_id=1, source_target_pairs={{0,1},{2,3},{4,5},{6,7},{8,9},{10,11},{12,13},{14,15},{16,17},{18,... | collective-permute-start | bytes 49160 | tf_op jit(solution)/shard_map/ppermute | solution.py:18
  36.5 23.2 %collective-permute-start.1 = (bf16[16,16,1024]{2,1,0:T(8,128)(2,1)}, bf16[16,16,1024]{2,1,0:T(8,128)(2,1)}, u32[]{:S(2)}, u32[]{:S(2)}) collective-permute-start(bf16[16,16,1024]{2,1,0:T(8,128)(2,1)} %get-tuple-element.101), channel_id=1, source_target_pairs={{0,1},{2,3},{4,5},{6,7},{8,9},{10,11},{12,13},{14,15},{16,17},{18,... | collective-permute-start | bytes 1572872 | tf_op jit(solution)/shard_map/ppermute | solution.py:18

commit v17 on v16

--- a/solution.py
+++ b/solution.py
@@ -148,9 +148,10 @@
     rows_w = wo_hbm.shape[0]
     if fused:
         first = []
-        for r in range(rows_w // CHUNK_ROWS):
-            part = pl.ds(r * CHUNK_ROWS, CHUNK_ROWS)
-            first.append(pltpu.make_async_copy(qkv_hbm.at[part], wbuf.at[part], wsem.at[0, r]))
+        for i in range(3):
+            part = pl.ds(i * width, width)
+            first.append(pltpu.make_async_copy(qkv_hbm.at[:, part], wbuf.at[:, part],
+                                               wsem.at[0, i]))
     else:
         first = [pltpu.make_async_copy(qkv_hbm, qkv, wsem.at[0, 0])]
     copies = []
@@ -169,10 +170,11 @@
         centred = floats - jnp.mean(floats, axis=-1, keepdims=True)
         variance = jnp.mean(centred * centred, axis=-1, keepdims=True)
         normed = (centred * lax.rsqrt(variance + 1e-05)).astype(jnp.bfloat16)
-    for c in first:
-        c.wait()
+    if not fused:
+        first[0].wait()
     if fused:
         for i in range(3):
+            first[i].wait()
             part = jnp.dot(normed, wbuf[:, pl.ds(i * width, width)],
                            preferred_element_type=jnp.float32)
             if i == 0:

time: 83.3 us -> 83.3 us (level)
  no operation moved by 1% of the time
where the time goes in v17:
time: 83.3 us; the launch traced here: 82.5 us
  waiting for transfers between devices  25.5 us (31%)
  Pallas kernels  22 us (26%)
  blocking collectives  17.5 us (21%)
  local copies, waits for them, and re-layouts  9.33 us (11%)
  other arithmetic  4.85 us (6%)
  starting transfers between devices  2.56 us (3%)
    ppermute x2, waiting for transfers between devices, shifted(): lax.ppermute(value, axis, [(source, source + steps) for source in range(l...  25.5 us
    pallas_call x1, Pallas kernels, encoder_layer(): pl.pallas_call(kernel, out_shape=jax.ShapeDtypeStruct((tokens, width), jn...  22 us
    all_to_all x1, blocking collectives, exchange(): return lax.all_to_all(send, 'stream', 0, 0, tiled=True)  17.5 us
    another operation x3, local copies, waits for them, and re-layouts  3.3 us
    ppermute x2, starting transfers between devices, shifted(): lax.ppermute(value, axis, [(source, source + steps) for source in range(l...  2.56 us
    unnamed x9, local copies, waits for them, and re-layouts  2.17 us
  transfers between devices with their start and end apart: 2, of which 2 were waited for; matrix products, arithmetic and copies ran while one was open for 0% of the time, Pallas kernels for 0%

profile of v17, /device:TPU:1, one launch (start us, length us, event | category | flops | bytes accessed | tf_op | source)
XLA Modules:
  0.0 82.5 jit_solution(9785850053054164859)
XLA Ops:
  0.0 0.8 compare_select_fusion.7
  0.8 0.7 compare_select_fusion.6
  1.6 0.8 %select_reduce_fusion = s32[16]{0:T(128)S(1)} fusion(s32[128]{0:T(128)} %param.18, s32[16]{0:T(128)S(1)} %get-tuple-element.94), kind=kLoop, calls=%fused_computation.21 | loop fusion | flops 6128 | bytes 640 | tf_op jit(solution)/shard_map/reduce_sum | solution.py:324
  2.4 0.1 select_reduce_fusion.1
  2.5 1.6 %copy.26 = bf16[1,16,12,2048]{3,2,1,0:T(8,128)(2,1)S(1)} copy(bf16[1,16,12,2048]{3,1,2,0:T(8,128)(2,1)} %param.19) | data formatting | bytes 1572864 | tf_op args[3]
  4.1 1.1 %fusion.8 = (bf16[16,12,1024]{2,1,0:T(8,128)(2,1)}, bf16[16,12,1024]{2,1,0:T(8,128)(2,1)}) fusion(bf16[16,12,2048]{2,1,0:T(8,128)(2,1)S(1)} %bitcast.22), kind=kLoop, calls=%fused_computation.38 | loop fusion | bytes 1572864 | tf_op jit(solution)/shard_map/slice | solution.py:357
  5.2 0.5 copy.25
  5.8 1.5 %fusion.7 = bf16[16,64,1024]{2,1,0:T(8,128)(2,1)S(1)} fusion(bf16[16,30,1024]{2,1,0:T(8,128)(2,1)S(1)} %bitcast.23, bf16[16,12,1024]{2,1,0:T(8,128)(2,1)} %get-tuple-element.92, bf16[16,12,1024]{2,1,0:T(8,128)(2,1)} %get-tuple-element.91), kind=kLoop, calls=%fused_computation.16 | loop fusion | flops 14680064 | bytes 3866624 | tf_op jit(solution)/shard_map/concatenate | solution.py:356
  7.3 0.6 gather_fusion
  7.9 0.0 copy-start.2
  7.9 0.0 copy-start.1
  7.9 2.5 %conditional.4 = (bf16[8,64,1024]{2,1,0:T(8,128)(2,1)}, bf16[3,256,1024]{2,1,0:T(8,128)(2,1)}) conditional(s32[]{:T(128)} %convert_element_type.70, () %tuple.34, (bf16[8,64,1024]{2,1,0:T(8,128)(2,1)S(1)}, bf16[16,16,1024]{2,1,0:T(8,128)(2,1)}, bf16[1,1024,3072]{2,1,0:T(8,128)(2,1)}) %tuple.35), branch_computations={%region_2.3_spmd, %region_3.4_spmd} | conditional | bytes 3145776 | solution.py:374
  7.9 1.3 %broadcast.93 = bf16[3,256,1024]{2,1,0:T(8,128)(2,1)} broadcast(bf16[]{:T(256)} %constant.35.clone), dimensions={} | broadcast | bytes 1572866 | tf_op jit(solution)/shard_map/broadcast.6
  9.3 1.1 %broadcast.92 = bf16[8,64,1024]{2,1,0:T(8,128)(2,1)} broadcast(bf16[]{:T(256)} %constant.35.clone), dimensions={} | broadcast | bytes 1048578 | tf_op jit(solution)/shard_map/broadcast.7
  10.4 0.7 slice.11
  11.1 1.3 %collective-permute-start = (bf16[1,8,1024]{2,1,0:T(8,128)(2,1)S(1)}, bf16[1,8,1024]{2,1,0:T(8,128)(2,1)S(1)}, u32[]{:S(2)}, u32[]{:S(2)}) collective-permute-start(bf16[1,8,1024]{2,1,0:T(8,128)(2,1)S(1)} %slice.11), channel_id=1, source_target_pairs={{0,1},{2,3},{4,5},{6,7},{8,9},{10,11},{12,13},{14,15},{16,17},{18,... | collective-permute-start | bytes 49160 | tf_op jit(solution)/shard_map/ppermute | solution.py:18
  12.4 0.1 pad_add_fusion
  12.4 0.1 dynamic_slice.6
  12.6 21.8 %collective-permute-done = bf16[1,8,1024]{2,1,0:T(8,128)(2,1)S(1)} collective-permute-done((bf16[1,8,1024]{2,1,0:T(8,128)(2,1)S(1)}, bf16[1,8,1024]{2,1,0:T(8,128)(2,1)S(1)}, u32[]{:S(2)}, u32[]{:S(2)}) %collective-permute-start) | collective-permute-done | bytes 16416 | tf_op jit(solution)/shard_map/ppermute | solution.py:18
  34.4 0.6 convert_reduce_fusion
  35.6 0.9 %conditional.5 = (bf16[16,16,1024]{2,1,0:T(8,128)(2,1)}) conditional(s32[]{:T(128)} %convert_element_type.70, () %tuple.33, (bf16[16,16,1024]{2,1,0:T(8,128)(2,1)}, s32[16]{0:T(128)S(1)}, s32[32]{0:T(128)S(1)}, f32[31,1024]{1,0:T(8,128)S(1)}, bf16[3,256,1024]{2,1,0:T(8,128)(2,1)}, /*index=5*/bf16[1024,1024]{1,0:T(8,128)(2,1)}, ...), branch_computations={%region_5.6_spmd, %region_6.7_spmd} | conditional | flops 544 | bytes 524298 | solution.py:380
  35.6 0.9 %broadcast.94 = bf16[16,16,1024]{2,1,0:T(8,128)(2,1)} broadcast(bf16[]{:T(256)} %constant.36.clone), dimensions={} | broadcast | bytes 524290 | tf_op jit(solution)/shard_map/broadcast.9
  36.5 1.3 %collective-permute-start.1 = (bf16[16,16,1024]{2,1,0:T(8,128)(2,1)}, bf16[16,16,1024]{2,1,0:T(8,128)(2,1)}, u32[]{:S(2)}, u32[]{:S(2)}) collective-permute-start(bf16[16,16,1024]{2,1,0:T(8,128)(2,1)} %get-tuple-element.101), channel_id=1, source_target_pairs={{0,1},{2,3},{4,5},{6,7},{8,9},{10,11},{12,13},{14,15},{16,17},{18,... | collective-permute-start | bytes 1572872 | tf_op jit(solution)/shard_map/ppermute | solution.py:18
  37.8 17.6 %conditional.6 = (bf16[8,64,1024]{2,1,0:T(8,128)(2,1)S(1)}) conditional(s32[]{:T(128)} %convert_element_type.70, (f32[]{:T(128)}, bf16[8,64,1024]{2,1,0:T(8,128)(2,1)S(1)}) %tuple.37, () %tuple.38), branch_computations={%region_7.8_spmd, %region_8.9_spmd} | conditional | flops 524289 | bytes 4194320 | solution.py:384
  37.8 0.1 broadcast_add_fusion.1
  37.9 17.5 %all_to_all.8 = bf16[8,64,1024]{2,1,0:T(8,128)(2,1)S(1)} all-to-all(bf16[8,64,1024]{2,1,0:T(8,128)(2,1)S(1)} %broadcast_add_fusion.1), channel_id=1, replica_groups=mesh['groups'=2,'stream'=8,'section'=2] {'stream'}, dimensions={0} | all-to-all | bytes 2097152 | tf_op jit(solution)/shard_map/cond/branch_0_fun/all_to_all | solution.py:341
  55.4 3.7 %collective-permute-done.1 = bf16[16,16,1024]{2,1,0:T(8,128)(2,1)} collective-permute-done((bf16[16,16,1024]{2,1,0:T(8,128)(2,1)}, bf16[16,16,1024]{2,1,0:T(8,128)(2,1)}, u32[]{:S(2)}, u32[]{:S(2)}) %collective-permute-start.1) | collective-permute-done | bytes 524320 | tf_op jit(solution)/shard_map/ppermute | solution.py:18
  59.1 23.5 %conditional.7 = (bf16[1,16,16,1024]{3,2,1,0:T(8,128)(2,1)}) conditional(s32[]{:T(128)} %convert_element_type.70, (bf16[16,16,1024]{2,1,0:T(8,128)(2,1)}, s32[16]{0:T(128)S(1)}, bf16[1,1024,3072]{2,1,0:T(8,128)(2,1)}, s32[32]{0:T(128)S(1)}, f32[31,1024]{1,0:T(8,128)S(1)}, /*index=5*/bf16[1024,1024]{1,0:T(8,128)(2,1)}, ...), branch_computations={%region_9.10_spmd, %region_10.11_spmd} | conditional | flops 512 | bytes 1048584 | solution.py:387
  59.1 0.1 fusion.1
  59.2 0.7 reshape.174.rlive_ref
  59.9 0.6 reshape.162.klive_ref
  60.5 22.0 %branch_0_fun.1 = bf16[256,1024]{1,0:T(8,128)(2,1)} custom-call(s32[32]{0:T(128)S(1)} %get-tuple-element.73.sel_ref, bf16[256,1024]{1,0:T(8,128)(2,1)} %bitcast.4.x_ref, f32[1,256]{1,0:T(1,128)} %reshape.162.klive_ref, f32[256,1]{1,0:T(8,128)} %reshape.174.rlive_ref, f32[31,1024]{1,0:T(8,128)S(1)} %get-tuple-element.76.cw_ref, bf16[1024,3072]{1,0:T(8,128)(2,1)} %bitcast.19, ...), custom_call_target="tpu_custom_call" | custom-call | tf_op jit(solution)/shard_map/cond/branch_0_fun/pallas_call | solution.py:298
  (8 shorter events, 0.1 us)
Async XLA Ops:
  0.0 5.2 %copy-start = (bf16[1,16,30,1024]{3,1,2,0:T(8,128)(2,1)S(1)}, bf16[1,16,30,1024]{3,1,2,0:T(8,128)(2,1)}, u32[]{:S(2)}) copy-start(bf16[1,16,30,1024]{3,1,2,0:T(8,128)(2,1)} %param.20) | copy-start | bytes 2949124
  7.9 4.6 %copy-start.2 = (s32[128]{0:T(128)S(1)}, s32[128]{0:T(128)}, u32[]{:S(2)}) copy-start(s32[128]{0:T(128)} %param.17) | copy-start | bytes 1540
  7.9 4.6 %copy-start.1 = (f32[1,31,1024]{2,0,1:T(1,128)S(1)}, f32[1,31,1024]{2,0,1:T(1,128)}, u32[]{:S(2)}) copy-start(f32[1,31,1024]{2,0,1:T(1,128)} %param.23) | copy-start | bytes 380932
  11.1 23.3 %collective-permute-start = (bf16[1,8,1024]{2,1,0:T(8,128)(2,1)S(1)}, bf16[1,8,1024]{2,1,0:T(8,128)(2,1)S(1)}, u32[]{:S(2)}, u32[]{:S(2)}) collective-permute-start(bf16[1,8,1024]{2,1,0:T(8,128)(2,1)S(1)} %slice.11), channel_id=1, source_target_pairs={{0,1},{2,3},{4,5},{6,7},{8,9},{10,11},{12,13},{14,15},{16,17},{18,... | collective-permute-start | bytes 49160 | tf_op jit(solution)/shard_map/ppermute | solution.py:18
  36.5 22.6 %collective-permute-start.1 = (bf16[16,16,1024]{2,1,0:T(8,128)(2,1)}, bf16[16,16,1024]{2,1,0:T(8,128)(2,1)}, u32[]{:S(2)}, u32[]{:S(2)}) collective-permute-start(bf16[16,16,1024]{2,1,0:T(8,128)(2,1)} %get-tuple-element.101), channel_id=1, source_target_pairs={{0,1},{2,3},{4,5},{6,7},{8,9},{10,11},{12,13},{14,15},{16,17},{18,... | collective-permute-start | bytes 1572872 | tf_op jit(solution)/shard_map/ppermute | solution.py:18

commit v18 on v16

--- a/solution.py
+++ b/solution.py
@@ -222,7 +222,7 @@
             qkv[0, rows, cols] = attended.astype(jnp.bfloat16)
             return carry
 
-        lax.fori_loop(0, width // pair, head_pair, 0)
+        lax.fori_loop(0, width // pair, head_pair, 0, unroll=2)
 
     for c in copies:
         c.wait()

time: 83.3 us -> 83.7 us (level)
  no operation moved by 1% of the time
where the time goes in v18:
time: 83.7 us; the launch traced here: 82.9 us
  waiting for transfers between devices  25.5 us (30%)
  Pallas kernels  21.9 us (26%)
  blocking collectives  17.5 us (21%)
  local copies, waits for them, and re-layouts  9.33 us (11%)
  other arithmetic  4.85 us (6%)
  starting transfers between devices  2.56 us (3%)
  between operations  0.93 us (1%)
    ppermute x2, waiting for transfers between devices, shifted(): lax.ppermute(value, axis, [(source, source + steps) for source in range(l...  25.5 us
    pallas_call x1, Pallas kernels, encoder_layer(): pl.pallas_call(kernel, out_shape=jax.ShapeDtypeStruct((tokens, width), jn...  21.9 us
    all_to_all x1, blocking collectives, exchange(): return lax.all_to_all(send, 'stream', 0, 0, tiled=True)  17.5 us
    another operation x3, local copies, waits for them, and re-layouts  3.3 us
    ppermute x2, starting transfers between devices, shifted(): lax.ppermute(value, axis, [(source, source + steps) for source in range(l...  2.56 us
    unnamed x9, local copies, waits for them, and re-layouts  2.17 us
  transfers between devices with their start and end apart: 2, of which 2 were waited for; matrix products, arithmetic and copies ran while one was open for 0% of the time, Pallas kernels for 0%

profile of v18, /device:TPU:1, one launch (start us, length us, event | category | flops | bytes accessed | tf_op | source)
XLA Modules:
  0.0 82.9 jit_solution(1362116079801152471)
XLA Ops:
  0.0 0.8 compare_select_fusion.7
  0.8 0.7 compare_select_fusion.6
  1.6 0.8 %select_reduce_fusion = s32[16]{0:T(128)S(1)} fusion(s32[128]{0:T(128)} %param.18, s32[16]{0:T(128)S(1)} %get-tuple-element.94), kind=kLoop, calls=%fused_computation.21 | loop fusion | flops 6128 | bytes 640 | tf_op jit(solution)/shard_map/reduce_sum | solution.py:322
  2.4 0.1 select_reduce_fusion.1
  2.5 1.6 %copy.26 = bf16[1,16,12,2048]{3,2,1,0:T(8,128)(2,1)S(1)} copy(bf16[1,16,12,2048]{3,1,2,0:T(8,128)(2,1)} %param.19) | data formatting | bytes 1572864 | tf_op args[3]
  4.1 1.1 %fusion.8 = (bf16[16,12,1024]{2,1,0:T(8,128)(2,1)}, bf16[16,12,1024]{2,1,0:T(8,128)(2,1)}) fusion(bf16[16,12,2048]{2,1,0:T(8,128)(2,1)S(1)} %bitcast.22), kind=kLoop, calls=%fused_computation.38 | loop fusion | bytes 1572864 | tf_op jit(solution)/shard_map/slice | solution.py:355
  5.2 0.5 copy.25
  5.8 1.5 %fusion.7 = bf16[16,64,1024]{2,1,0:T(8,128)(2,1)S(1)} fusion(bf16[16,30,1024]{2,1,0:T(8,128)(2,1)S(1)} %bitcast.23, bf16[16,12,1024]{2,1,0:T(8,128)(2,1)} %get-tuple-element.92, bf16[16,12,1024]{2,1,0:T(8,128)(2,1)} %get-tuple-element.91), kind=kLoop, calls=%fused_computation.16 | loop fusion | flops 14680064 | bytes 3866624 | tf_op jit(solution)/shard_map/concatenate | solution.py:354
  7.3 0.6 gather_fusion
  7.9 0.0 copy-start.2
  7.9 0.0 copy-start.1
  7.9 2.5 %conditional.4 = (bf16[8,64,1024]{2,1,0:T(8,128)(2,1)}, bf16[3,256,1024]{2,1,0:T(8,128)(2,1)}) conditional(s32[]{:T(128)} %convert_element_type.70, () %tuple.34, (bf16[8,64,1024]{2,1,0:T(8,128)(2,1)S(1)}, bf16[16,16,1024]{2,1,0:T(8,128)(2,1)}, bf16[1,1024,3072]{2,1,0:T(8,128)(2,1)}) %tuple.35), branch_computations={%region_2.3_spmd, %region_3.4_spmd} | conditional | bytes 3145776 | solution.py:372
  7.9 1.3 %broadcast.93 = bf16[3,256,1024]{2,1,0:T(8,128)(2,1)} broadcast(bf16[]{:T(256)} %constant.35.clone), dimensions={} | broadcast | bytes 1572866 | tf_op jit(solution)/shard_map/broadcast.6
  9.3 1.1 %broadcast.92 = bf16[8,64,1024]{2,1,0:T(8,128)(2,1)} broadcast(bf16[]{:T(256)} %constant.35.clone), dimensions={} | broadcast | bytes 1048578 | tf_op jit(solution)/shard_map/broadcast.7
  10.4 0.7 slice.11
  11.1 1.3 %collective-permute-start = (bf16[1,8,1024]{2,1,0:T(8,128)(2,1)S(1)}, bf16[1,8,1024]{2,1,0:T(8,128)(2,1)S(1)}, u32[]{:S(2)}, u32[]{:S(2)}) collective-permute-start(bf16[1,8,1024]{2,1,0:T(8,128)(2,1)S(1)} %slice.11), channel_id=1, source_target_pairs={{0,1},{2,3},{4,5},{6,7},{8,9},{10,11},{12,13},{14,15},{16,17},{18,... | collective-permute-start | bytes 49160 | tf_op jit(solution)/shard_map/ppermute | solution.py:18
  12.4 0.1 pad_add_fusion
  12.4 0.1 dynamic_slice.6
  12.6 21.8 %collective-permute-done = bf16[1,8,1024]{2,1,0:T(8,128)(2,1)S(1)} collective-permute-done((bf16[1,8,1024]{2,1,0:T(8,128)(2,1)S(1)}, bf16[1,8,1024]{2,1,0:T(8,128)(2,1)S(1)}, u32[]{:S(2)}, u32[]{:S(2)}) %collective-permute-start) | collective-permute-done | bytes 16416 | tf_op jit(solution)/shard_map/ppermute | solution.py:18
  34.4 0.6 convert_reduce_fusion
  35.6 0.9 %conditional.5 = (bf16[16,16,1024]{2,1,0:T(8,128)(2,1)}) conditional(s32[]{:T(128)} %convert_element_type.70, () %tuple.33, (bf16[16,16,1024]{2,1,0:T(8,128)(2,1)}, s32[16]{0:T(128)S(1)}, s32[32]{0:T(128)S(1)}, f32[31,1024]{1,0:T(8,128)S(1)}, bf16[3,256,1024]{2,1,0:T(8,128)(2,1)}, /*index=5*/bf16[1024,1024]{1,0:T(8,128)(2,1)}, ...), branch_computations={%region_5.6_spmd, %region_6.7_spmd} | conditional | flops 544 | bytes 524298 | solution.py:378
  35.6 0.9 %broadcast.94 = bf16[16,16,1024]{2,1,0:T(8,128)(2,1)} broadcast(bf16[]{:T(256)} %constant.36.clone), dimensions={} | broadcast | bytes 524290 | tf_op jit(solution)/shard_map/broadcast.9
  36.5 1.3 %collective-permute-start.1 = (bf16[16,16,1024]{2,1,0:T(8,128)(2,1)}, bf16[16,16,1024]{2,1,0:T(8,128)(2,1)}, u32[]{:S(2)}, u32[]{:S(2)}) collective-permute-start(bf16[16,16,1024]{2,1,0:T(8,128)(2,1)} %get-tuple-element.101), channel_id=1, source_target_pairs={{0,1},{2,3},{4,5},{6,7},{8,9},{10,11},{12,13},{14,15},{16,17},{18,... | collective-permute-start | bytes 1572872 | tf_op jit(solution)/shard_map/ppermute | solution.py:18
  37.8 17.6 %conditional.6 = (bf16[8,64,1024]{2,1,0:T(8,128)(2,1)S(1)}) conditional(s32[]{:T(128)} %convert_element_type.70, (f32[]{:T(128)}, bf16[8,64,1024]{2,1,0:T(8,128)(2,1)S(1)}) %tuple.37, () %tuple.38), branch_computations={%region_7.8_spmd, %region_8.9_spmd} | conditional | flops 524289 | bytes 4194320 | solution.py:382
  37.8 0.1 broadcast_add_fusion.1
  37.9 17.5 %all_to_all.8 = bf16[8,64,1024]{2,1,0:T(8,128)(2,1)S(1)} all-to-all(bf16[8,64,1024]{2,1,0:T(8,128)(2,1)S(1)} %broadcast_add_fusion.1), channel_id=1, replica_groups=mesh['groups'=2,'stream'=8,'section'=2] {'stream'}, dimensions={0} | all-to-all | bytes 2097152 | tf_op jit(solution)/shard_map/cond/branch_0_fun/all_to_all | solution.py:339
  55.4 3.7 %collective-permute-done.1 = bf16[16,16,1024]{2,1,0:T(8,128)(2,1)} collective-permute-done((bf16[16,16,1024]{2,1,0:T(8,128)(2,1)}, bf16[16,16,1024]{2,1,0:T(8,128)(2,1)}, u32[]{:S(2)}, u32[]{:S(2)}) %collective-permute-start.1) | collective-permute-done | bytes 524320 | tf_op jit(solution)/shard_map/ppermute | solution.py:18
  59.1 23.6 %conditional.7 = (bf16[1,16,16,1024]{3,2,1,0:T(8,128)(2,1)}) conditional(s32[]{:T(128)} %convert_element_type.70, (bf16[16,16,1024]{2,1,0:T(8,128)(2,1)}, s32[16]{0:T(128)S(1)}, bf16[1,1024,3072]{2,1,0:T(8,128)(2,1)}, s32[32]{0:T(128)S(1)}, f32[31,1024]{1,0:T(8,128)S(1)}, /*index=5*/bf16[1024,1024]{1,0:T(8,128)(2,1)}, ...), branch_computations={%region_9.10_spmd, %region_10.11_spmd} | conditional | flops 512 | bytes 1048584 | solution.py:385
  59.1 0.1 fusion.1
  59.2 0.7 reshape.174.rlive_ref
  59.9 0.6 reshape.162.klive_ref
  60.6 21.9 %branch_0_fun.1 = bf16[256,1024]{1,0:T(8,128)(2,1)} custom-call(s32[32]{0:T(128)S(1)} %get-tuple-element.73.sel_ref, bf16[256,1024]{1,0:T(8,128)(2,1)} %bitcast.4.x_ref, f32[1,256]{1,0:T(1,128)} %reshape.162.klive_ref, f32[256,1]{1,0:T(8,128)} %reshape.174.rlive_ref, f32[31,1024]{1,0:T(8,128)S(1)} %get-tuple-element.76.cw_ref, bf16[1024,3072]{1,0:T(8,128)(2,1)} %bitcast.19, ...), custom_call_target="tpu_custom_call" | custom-call | tf_op jit(solution)/shard_map/cond/branch_0_fun/pallas_call | solution.py:296
  (8 shorter events, 0.1 us)
Async XLA Ops:
  0.0 5.2 %copy-start = (bf16[1,16,30,1024]{3,1,2,0:T(8,128)(2,1)S(1)}, bf16[1,16,30,1024]{3,1,2,0:T(8,128)(2,1)}, u32[]{:S(2)}) copy-start(bf16[1,16,30,1024]{3,1,2,0:T(8,128)(2,1)} %param.20) | copy-start | bytes 2949124
  7.9 4.6 %copy-start.2 = (s32[128]{0:T(128)S(1)}, s32[128]{0:T(128)}, u32[]{:S(2)}) copy-start(s32[128]{0:T(128)} %param.17) | copy-start | bytes 1540
  7.9 4.6 %copy-start.1 = (f32[1,31,1024]{2,0,1:T(1,128)S(1)}, f32[1,31,1024]{2,0,1:T(1,128)}, u32[]{:S(2)}) copy-start(f32[1,31,1024]{2,0,1:T(1,128)} %param.23) | copy-start | bytes 380932
  11.1 23.3 %collective-permute-start = (bf16[1,8,1024]{2,1,0:T(8,128)(2,1)S(1)}, bf16[1,8,1024]{2,1,0:T(8,128)(2,1)S(1)}, u32[]{:S(2)}, u32[]{:S(2)}) collective-permute-start(bf16[1,8,1024]{2,1,0:T(8,128)(2,1)S(1)} %slice.11), channel_id=1, source_target_pairs={{0,1},{2,3},{4,5},{6,7},{8,9},{10,11},{12,13},{14,15},{16,17},{18,... | collective-permute-start | bytes 49160 | tf_op jit(solution)/shard_map/ppermute | solution.py:18
  36.5 22.6 %collective-permute-start.1 = (bf16[16,16,1024]{2,1,0:T(8,128)(2,1)}, bf16[16,16,1024]{2,1,0:T(8,128)(2,1)}, u32[]{:S(2)}, u32[]{:S(2)}) collective-permute-start(bf16[16,16,1024]{2,1,0:T(8,128)(2,1)} %get-tuple-element.101), channel_id=1, source_target_pairs={{0,1},{2,3},{4,5},{6,7},{8,9},{10,11},{12,13},{14,15},{16,17},{18,... | collective-permute-start | bytes 1572872 | tf_op jit(solution)/shard_map/ppermute | solution.py:18

commit v19 on v16

--- a/solution.py
+++ b/solution.py
@@ -372,7 +372,7 @@
     recv0, projected = lax.cond(
         on_first, early_branch,
         lambda: (jnp.zeros_like(send), jnp.zeros((3, local_count * frames, width), jnp.bfloat16)))
-    token = shifted(recv0[:1, :8], "section", 1)
+    token = shifted(recv0[:1, :8, :128], "section", 1)
     zero = jnp.where(on_first, 0.0, jnp.sum(token.astype(jnp.float32)) * 0.0)
     sel0 = sel + zero.astype(sel.dtype)
     first = lax.cond(on_first,

time: 83.3 us -> 83.2 us (level)
  no operation moved by 1% of the time
where the time goes in v19:
time: 83.2 us; the launch traced here: 82.8 us
  waiting for transfers between devices  26.1 us (31%)
  Pallas kernels  21.7 us (26%)
  blocking collectives  17.5 us (21%)
  local copies, waits for them, and re-layouts  9.3 us (11%)
  other arithmetic  4.84 us (6%)
  starting transfers between devices  2.56 us (3%)
    ppermute x2, waiting for transfers between devices, shifted(): lax.ppermute(value, axis, [(source, source + steps) for source in range(l...  26.1 us
    pallas_call x1, Pallas kernels, encoder_layer(): pl.pallas_call(kernel, out_shape=jax.ShapeDtypeStruct((tokens, width), jn...  21.7 us
    all_to_all x1, blocking collectives, exchange(): return lax.all_to_all(send, 'stream', 0, 0, tiled=True)  17.5 us
    another operation x3, local copies, waits for them, and re-layouts  3.3 us
    ppermute x2, starting transfers between devices, shifted(): lax.ppermute(value, axis, [(source, source + steps) for source in range(l...  2.56 us
    unnamed x9, local copies, waits for them, and re-layouts  2.17 us
  transfers between devices with their start and end apart: 2, of which 2 were waited for; matrix products, arithmetic and copies ran while one was open for 0% of the time, Pallas kernels for 0%

profile of v19, /device:TPU:1, one launch (start us, length us, event | category | flops | bytes accessed | tf_op | source)
XLA Modules:
  0.0 82.8 jit_solution(14613309206856916158)
XLA Ops:
  0.0 0.8 compare_select_fusion.7
  0.8 0.7 compare_select_fusion.6
  1.6 0.8 %select_reduce_fusion = s32[16]{0:T(128)S(1)} fusion(s32[128]{0:T(128)} %param.18, s32[16]{0:T(128)S(1)} %get-tuple-element.94), kind=kLoop, calls=%fused_computation.20 | loop fusion | flops 6128 | bytes 640 | tf_op jit(solution)/shard_map/reduce_sum | solution.py:322
  2.4 0.1 select_reduce_fusion.1
  2.5 1.6 %copy.26 = bf16[1,16,12,2048]{3,2,1,0:T(8,128)(2,1)S(1)} copy(bf16[1,16,12,2048]{3,1,2,0:T(8,128)(2,1)} %param.19) | data formatting | bytes 1572864 | tf_op args[3]
  4.1 1.1 %fusion.8 = (bf16[16,12,1024]{2,1,0:T(8,128)(2,1)}, bf16[16,12,1024]{2,1,0:T(8,128)(2,1)}) fusion(bf16[16,12,2048]{2,1,0:T(8,128)(2,1)S(1)} %bitcast.22), kind=kLoop, calls=%fused_computation.38 | loop fusion | bytes 1572864 | tf_op jit(solution)/shard_map/slice | solution.py:355
  5.2 0.5 copy.25
  5.8 1.5 %fusion.7 = bf16[16,64,1024]{2,1,0:T(8,128)(2,1)S(1)} fusion(bf16[16,30,1024]{2,1,0:T(8,128)(2,1)S(1)} %bitcast.23, bf16[16,12,1024]{2,1,0:T(8,128)(2,1)} %get-tuple-element.92, bf16[16,12,1024]{2,1,0:T(8,128)(2,1)} %get-tuple-element.91), kind=kLoop, calls=%fused_computation.16 | loop fusion | flops 14680064 | bytes 3866624 | tf_op jit(solution)/shard_map/concatenate | solution.py:354
  7.3 0.6 gather_fusion
  7.9 0.0 copy-start.2
  7.9 0.0 copy-start.1
  7.9 2.5 %conditional.4 = (bf16[8,64,1024]{2,1,0:T(8,128)(2,1)}, bf16[3,256,1024]{2,1,0:T(8,128)(2,1)}) conditional(s32[]{:T(128)} %convert_element_type.70, () %tuple.34, (bf16[8,64,1024]{2,1,0:T(8,128)(2,1)S(1)}, bf16[16,16,1024]{2,1,0:T(8,128)(2,1)}, bf16[1,1024,3072]{2,1,0:T(8,128)(2,1)}) %tuple.35), branch_computations={%region_2.3_spmd, %region_3.4_spmd} | conditional | bytes 3145776 | solution.py:372
  7.9 1.3 %broadcast.93 = bf16[3,256,1024]{2,1,0:T(8,128)(2,1)} broadcast(bf16[]{:T(256)} %constant.35.clone), dimensions={} | broadcast | bytes 1572866 | tf_op jit(solution)/shard_map/broadcast.6
  9.3 1.1 %broadcast.92 = bf16[8,64,1024]{2,1,0:T(8,128)(2,1)} broadcast(bf16[]{:T(256)} %constant.35.clone), dimensions={} | broadcast | bytes 1048578 | tf_op jit(solution)/shard_map/broadcast.7
  10.4 0.7 slice.11
  11.0 1.3 %collective-permute-start = (bf16[1,8,128]{2,1,0:T(8,128)(2,1)S(1)}, bf16[1,8,128]{2,1,0:T(8,128)(2,1)S(1)}, u32[]{:S(2)}, u32[]{:S(2)}) collective-permute-start(bf16[1,8,128]{2,1,0:T(8,128)(2,1)S(1)} %slice.11), channel_id=1, source_target_pairs={{0,1},{2,3},{4,5},{6,7},{8,9},{10,11},{12,13},{14,15},{16,17},{18,... | collective-permute-start | bytes 6152 | tf_op jit(solution)/shard_map/ppermute | solution.py:18
  12.3 0.1 pad_add_fusion
  12.4 0.1 dynamic_slice.6
  12.5 21.8 %collective-permute-done = bf16[1,8,128]{2,1,0:T(8,128)(2,1)S(1)} collective-permute-done((bf16[1,8,128]{2,1,0:T(8,128)(2,1)S(1)}, bf16[1,8,128]{2,1,0:T(8,128)(2,1)S(1)}, u32[]{:S(2)}, u32[]{:S(2)}) %collective-permute-start) | collective-permute-done | bytes 2080 | tf_op jit(solution)/shard_map/ppermute | solution.py:18
  34.3 0.6 convert_reduce_fusion
  35.6 0.9 %conditional.5 = (bf16[16,16,1024]{2,1,0:T(8,128)(2,1)}) conditional(s32[]{:T(128)} %convert_element_type.70, () %tuple.33, (bf16[16,16,1024]{2,1,0:T(8,128)(2,1)}, s32[16]{0:T(128)S(1)}, s32[32]{0:T(128)S(1)}, f32[31,1024]{1,0:T(8,128)S(1)}, bf16[3,256,1024]{2,1,0:T(8,128)(2,1)}, /*index=5*/bf16[1024,1024]{1,0:T(8,128)(2,1)}, ...), branch_computations={%region_5.6_spmd, %region_6.7_spmd} | conditional | flops 544 | bytes 524298 | solution.py:378
  35.6 0.9 %broadcast.94 = bf16[16,16,1024]{2,1,0:T(8,128)(2,1)} broadcast(bf16[]{:T(256)} %constant.36.clone), dimensions={} | broadcast | bytes 524290 | tf_op jit(solution)/shard_map/broadcast.9
  36.4 1.3 %collective-permute-start.1 = (bf16[16,16,1024]{2,1,0:T(8,128)(2,1)}, bf16[16,16,1024]{2,1,0:T(8,128)(2,1)}, u32[]{:S(2)}, u32[]{:S(2)}) collective-permute-start(bf16[16,16,1024]{2,1,0:T(8,128)(2,1)} %get-tuple-element.101), channel_id=1, source_target_pairs={{0,1},{2,3},{4,5},{6,7},{8,9},{10,11},{12,13},{14,15},{16,17},{18,... | collective-permute-start | bytes 1572872 | tf_op jit(solution)/shard_map/ppermute | solution.py:18
  37.7 17.6 %conditional.6 = (bf16[8,64,1024]{2,1,0:T(8,128)(2,1)S(1)}) conditional(s32[]{:T(128)} %convert_element_type.70, (f32[]{:T(128)}, bf16[8,64,1024]{2,1,0:T(8,128)(2,1)S(1)}) %tuple.37, () %tuple.38), branch_computations={%region_7.8_spmd, %region_8.9_spmd} | conditional | flops 524289 | bytes 4194320 | solution.py:382
  37.7 0.1 broadcast_add_fusion.1
  37.8 17.5 %all_to_all.8 = bf16[8,64,1024]{2,1,0:T(8,128)(2,1)S(1)} all-to-all(bf16[8,64,1024]{2,1,0:T(8,128)(2,1)S(1)} %broadcast_add_fusion.1), channel_id=1, replica_groups=mesh['groups'=2,'stream'=8,'section'=2] {'stream'}, dimensions={0} | all-to-all | bytes 2097152 | tf_op jit(solution)/shard_map/cond/branch_0_fun/all_to_all | solution.py:339
  55.3 4.3 %collective-permute-done.1 = bf16[16,16,1024]{2,1,0:T(8,128)(2,1)} collective-permute-done((bf16[16,16,1024]{2,1,0:T(8,128)(2,1)}, bf16[16,16,1024]{2,1,0:T(8,128)(2,1)}, u32[]{:S(2)}, u32[]{:S(2)}) %collective-permute-start.1) | collective-permute-done | bytes 524320 | tf_op jit(solution)/shard_map/ppermute | solution.py:18
  59.6 23.1 %conditional.7 = (bf16[1,16,16,1024]{3,2,1,0:T(8,128)(2,1)}) conditional(s32[]{:T(128)} %convert_element_type.70, (bf16[16,16,1024]{2,1,0:T(8,128)(2,1)}, s32[16]{0:T(128)S(1)}, bf16[1,1024,3072]{2,1,0:T(8,128)(2,1)}, s32[32]{0:T(128)S(1)}, f32[31,1024]{1,0:T(8,128)S(1)}, /*index=5*/bf16[1024,1024]{1,0:T(8,128)(2,1)}, ...), branch_computations={%region_9.10_spmd, %region_10.11_spmd} | conditional | flops 512 | bytes 1048584 | solution.py:385
  59.6 0.1 fusion.1
  59.7 0.7 reshape.174.rlive_ref
  60.4 0.6 reshape.162.klive_ref
  61.1 21.7 %branch_0_fun.1 = bf16[256,1024]{1,0:T(8,128)(2,1)} custom-call(s32[32]{0:T(128)S(1)} %get-tuple-element.73.sel_ref, bf16[256,1024]{1,0:T(8,128)(2,1)} %bitcast.4.x_ref, f32[1,256]{1,0:T(1,128)} %reshape.162.klive_ref, f32[256,1]{1,0:T(8,128)} %reshape.174.rlive_ref, f32[31,1024]{1,0:T(8,128)S(1)} %get-tuple-element.76.cw_ref, bf16[1024,3072]{1,0:T(8,128)(2,1)} %bitcast.19, ...), custom_call_target="tpu_custom_call" | custom-call | tf_op jit(solution)/shard_map/cond/branch_0_fun/pallas_call | solution.py:296
  (8 shorter events, 0.1 us)
Async XLA Ops:
  0.0 5.2 %copy-start = (bf16[1,16,30,1024]{3,1,2,0:T(8,128)(2,1)S(1)}, bf16[1,16,30,1024]{3,1,2,0:T(8,128)(2,1)}, u32[]{:S(2)}) copy-start(bf16[1,16,30,1024]{3,1,2,0:T(8,128)(2,1)} %param.20) | copy-start | bytes 2949124
  7.9 4.5 %copy-start.2 = (s32[128]{0:T(128)S(1)}, s32[128]{0:T(128)}, u32[]{:S(2)}) copy-start(s32[128]{0:T(128)} %param.17) | copy-start | bytes 1540
  7.9 4.6 %copy-start.1 = (f32[1,31,1024]{2,0,1:T(1,128)S(1)}, f32[1,31,1024]{2,0,1:T(1,128)}, u32[]{:S(2)}) copy-start(f32[1,31,1024]{2,0,1:T(1,128)} %param.23) | copy-start | bytes 380932
  11.0 23.3 %collective-permute-start = (bf16[1,8,128]{2,1,0:T(8,128)(2,1)S(1)}, bf16[1,8,128]{2,1,0:T(8,128)(2,1)S(1)}, u32[]{:S(2)}, u32[]{:S(2)}) collective-permute-start(bf16[1,8,128]{2,1,0:T(8,128)(2,1)S(1)} %slice.11), channel_id=1, source_target_pairs={{0,1},{2,3},{4,5},{6,7},{8,9},{10,11},{12,13},{14,15},{16,17},{18,... | collective-permute-start | bytes 6152 | tf_op jit(solution)/shard_map/ppermute | solution.py:18
  36.4 23.2 %collective-permute-start.1 = (bf16[16,16,1024]{2,1,0:T(8,128)(2,1)}, bf16[16,16,1024]{2,1,0:T(8,128)(2,1)}, u32[]{:S(2)}, u32[]{:S(2)}) collective-permute-start(bf16[16,16,1024]{2,1,0:T(8,128)(2,1)} %get-tuple-element.101), channel_id=1, source_target_pairs={{0,1},{2,3},{4,5},{6,7},{8,9},{10,11},{12,13},{14,15},{16,17},{18,... | collective-permute-start | bytes 1572872 | tf_op jit(solution)/shard_map/ppermute | solution.py:18

commit v20 on v16

--- a/solution.py
+++ b/solution.py
@@ -35,7 +35,7 @@
 
 def conv_rows(conv_ref, pad_ref, cw_ref, tap_rows, frames, origin):
     width = cw_ref.shape[1]
-    chunk = 128
+    chunk = 256
 
     def conv_chunk(c, carry):
         cols = pl.ds(pl.multiple_of(c * chunk, chunk), chunk)

time: 83.3 us -> 84.1 us (level)
  no operation moved by 1% of the time
where the time goes in v20:
time: 84.1 us; the launch traced here: 83.3 us
  waiting for transfers between devices  25.7 us (31%)
  Pallas kernels  22.1 us (26%)
  blocking collectives  17.5 us (21%)
  local copies, waits for them, and re-layouts  9.33 us (11%)
  other arithmetic  4.85 us (6%)
  starting transfers between devices  2.56 us (3%)
  between operations  0.93 us (1%)
    ppermute x2, waiting for transfers between devices, shifted(): lax.ppermute(value, axis, [(source, source + steps) for source in range(l...  25.7 us
    pallas_call x1, Pallas kernels, encoder_layer(): pl.pallas_call(kernel, out_shape=jax.ShapeDtypeStruct((tokens, width), jn...  22.1 us
    all_to_all x1, blocking collectives, exchange(): return lax.all_to_all(send, 'stream', 0, 0, tiled=True)  17.5 us
    another operation x3, local copies, waits for them, and re-layouts  3.3 us
    ppermute x2, starting transfers between devices, shifted(): lax.ppermute(value, axis, [(source, source + steps) for source in range(l...  2.56 us
    unnamed x9, local copies, waits for them, and re-layouts  2.17 us
  transfers between devices with their start and end apart: 2, of which 2 were waited for; matrix products, arithmetic and copies ran while one was open for 0% of the time, Pallas kernels for 0%

profile of v20, /device:TPU:1, one launch (start us, length us, event | category | flops | bytes accessed | tf_op | source)
XLA Modules:
  0.0 83.3 jit_solution(5560361834414503713)
XLA Ops:
  0.0 0.8 compare_select_fusion.7
  0.8 0.7 compare_select_fusion.6
  1.6 0.8 %select_reduce_fusion = s32[16]{0:T(128)S(1)} fusion(s32[128]{0:T(128)} %param.18, s32[16]{0:T(128)S(1)} %get-tuple-element.94), kind=kLoop, calls=%fused_computation.21 | loop fusion | flops 6128 | bytes 640 | tf_op jit(solution)/shard_map/reduce_sum | solution.py:322
  2.4 0.1 select_reduce_fusion.1
  2.5 1.6 %copy.26 = bf16[1,16,12,2048]{3,2,1,0:T(8,128)(2,1)S(1)} copy(bf16[1,16,12,2048]{3,1,2,0:T(8,128)(2,1)} %param.19) | data formatting | bytes 1572864 | tf_op args[3]
  4.1 1.1 %fusion.8 = (bf16[16,12,1024]{2,1,0:T(8,128)(2,1)}, bf16[16,12,1024]{2,1,0:T(8,128)(2,1)}) fusion(bf16[16,12,2048]{2,1,0:T(8,128)(2,1)S(1)} %bitcast.22), kind=kLoop, calls=%fused_computation.38 | loop fusion | bytes 1572864 | tf_op jit(solution)/shard_map/slice | solution.py:355
  5.2 0.5 copy.25
  5.8 1.5 %fusion.7 = bf16[16,64,1024]{2,1,0:T(8,128)(2,1)S(1)} fusion(bf16[16,30,1024]{2,1,0:T(8,128)(2,1)S(1)} %bitcast.23, bf16[16,12,1024]{2,1,0:T(8,128)(2,1)} %get-tuple-element.92, bf16[16,12,1024]{2,1,0:T(8,128)(2,1)} %get-tuple-element.91), kind=kLoop, calls=%fused_computation.16 | loop fusion | flops 14680064 | bytes 3866624 | tf_op jit(solution)/shard_map/concatenate | solution.py:354
  7.3 0.6 gather_fusion
  7.9 0.0 copy-start.2
  7.9 0.0 copy-start.1
  7.9 2.5 %conditional.4 = (bf16[8,64,1024]{2,1,0:T(8,128)(2,1)}, bf16[3,256,1024]{2,1,0:T(8,128)(2,1)}) conditional(s32[]{:T(128)} %convert_element_type.70, () %tuple.34, (bf16[8,64,1024]{2,1,0:T(8,128)(2,1)S(1)}, bf16[16,16,1024]{2,1,0:T(8,128)(2,1)}, bf16[1,1024,3072]{2,1,0:T(8,128)(2,1)}) %tuple.35), branch_computations={%region_2.3_spmd, %region_3.4_spmd} | conditional | bytes 3145776 | solution.py:372
  7.9 1.3 %broadcast.93 = bf16[3,256,1024]{2,1,0:T(8,128)(2,1)} broadcast(bf16[]{:T(256)} %constant.35.clone), dimensions={} | broadcast | bytes 1572866 | tf_op jit(solution)/shard_map/broadcast.6
  9.3 1.1 %broadcast.92 = bf16[8,64,1024]{2,1,0:T(8,128)(2,1)} broadcast(bf16[]{:T(256)} %constant.35.clone), dimensions={} | broadcast | bytes 1048578 | tf_op jit(solution)/shard_map/broadcast.7
  10.4 0.7 slice.11
  11.1 1.3 %collective-permute-start = (bf16[1,8,1024]{2,1,0:T(8,128)(2,1)S(1)}, bf16[1,8,1024]{2,1,0:T(8,128)(2,1)S(1)}, u32[]{:S(2)}, u32[]{:S(2)}) collective-permute-start(bf16[1,8,1024]{2,1,0:T(8,128)(2,1)S(1)} %slice.11), channel_id=1, source_target_pairs={{0,1},{2,3},{4,5},{6,7},{8,9},{10,11},{12,13},{14,15},{16,17},{18,... | collective-permute-start | bytes 49160 | tf_op jit(solution)/shard_map/ppermute | solution.py:18
  12.4 0.1 pad_add_fusion
  12.4 0.1 dynamic_slice.6
  12.6 21.8 %collective-permute-done = bf16[1,8,1024]{2,1,0:T(8,128)(2,1)S(1)} collective-permute-done((bf16[1,8,1024]{2,1,0:T(8,128)(2,1)S(1)}, bf16[1,8,1024]{2,1,0:T(8,128)(2,1)S(1)}, u32[]{:S(2)}, u32[]{:S(2)}) %collective-permute-start) | collective-permute-done | bytes 16416 | tf_op jit(solution)/shard_map/ppermute | solution.py:18
  34.4 0.6 convert_reduce_fusion
  35.6 0.9 %conditional.5 = (bf16[16,16,1024]{2,1,0:T(8,128)(2,1)}) conditional(s32[]{:T(128)} %convert_element_type.70, () %tuple.33, (bf16[16,16,1024]{2,1,0:T(8,128)(2,1)}, s32[16]{0:T(128)S(1)}, s32[32]{0:T(128)S(1)}, f32[31,1024]{1,0:T(8,128)S(1)}, bf16[3,256,1024]{2,1,0:T(8,128)(2,1)}, /*index=5*/bf16[1024,1024]{1,0:T(8,128)(2,1)}, ...), branch_computations={%region_5.6_spmd, %region_6.7_spmd} | conditional | flops 544 | bytes 524298 | solution.py:378
  35.6 0.9 %broadcast.94 = bf16[16,16,1024]{2,1,0:T(8,128)(2,1)} broadcast(bf16[]{:T(256)} %constant.36.clone), dimensions={} | broadcast | bytes 524290 | tf_op jit(solution)/shard_map/broadcast.9
  36.5 1.3 %collective-permute-start.1 = (bf16[16,16,1024]{2,1,0:T(8,128)(2,1)}, bf16[16,16,1024]{2,1,0:T(8,128)(2,1)}, u32[]{:S(2)}, u32[]{:S(2)}) collective-permute-start(bf16[16,16,1024]{2,1,0:T(8,128)(2,1)} %get-tuple-element.101), channel_id=1, source_target_pairs={{0,1},{2,3},{4,5},{6,7},{8,9},{10,11},{12,13},{14,15},{16,17},{18,... | collective-permute-start | bytes 1572872 | tf_op jit(solution)/shard_map/ppermute | solution.py:18
  37.8 17.6 %conditional.6 = (bf16[8,64,1024]{2,1,0:T(8,128)(2,1)S(1)}) conditional(s32[]{:T(128)} %convert_element_type.70, (f32[]{:T(128)}, bf16[8,64,1024]{2,1,0:T(8,128)(2,1)S(1)}) %tuple.37, () %tuple.38), branch_computations={%region_7.8_spmd, %region_8.9_spmd} | conditional | flops 524289 | bytes 4194320 | solution.py:382
  37.8 0.1 broadcast_add_fusion.1
  37.9 17.5 %all_to_all.8 = bf16[8,64,1024]{2,1,0:T(8,128)(2,1)S(1)} all-to-all(bf16[8,64,1024]{2,1,0:T(8,128)(2,1)S(1)} %broadcast_add_fusion.1), channel_id=1, replica_groups=mesh['groups'=2,'stream'=8,'section'=2] {'stream'}, dimensions={0} | all-to-all | bytes 2097152 | tf_op jit(solution)/shard_map/cond/branch_0_fun/all_to_all | solution.py:339
  55.4 3.9 %collective-permute-done.1 = bf16[16,16,1024]{2,1,0:T(8,128)(2,1)} collective-permute-done((bf16[16,16,1024]{2,1,0:T(8,128)(2,1)}, bf16[16,16,1024]{2,1,0:T(8,128)(2,1)}, u32[]{:S(2)}, u32[]{:S(2)}) %collective-permute-start.1) | collective-permute-done | bytes 524320 | tf_op jit(solution)/shard_map/ppermute | solution.py:18
  59.3 23.8 %conditional.7 = (bf16[1,16,16,1024]{3,2,1,0:T(8,128)(2,1)}) conditional(s32[]{:T(128)} %convert_element_type.70, (bf16[16,16,1024]{2,1,0:T(8,128)(2,1)}, s32[16]{0:T(128)S(1)}, bf16[1,1024,3072]{2,1,0:T(8,128)(2,1)}, s32[32]{0:T(128)S(1)}, f32[31,1024]{1,0:T(8,128)S(1)}, /*index=5*/bf16[1024,1024]{1,0:T(8,128)(2,1)}, ...), branch_computations={%region_9.10_spmd, %region_10.11_spmd} | conditional | flops 512 | bytes 1048584 | solution.py:385
  59.3 0.1 fusion.1
  59.4 0.7 reshape.174.rlive_ref
  60.2 0.6 reshape.162.klive_ref
  60.8 22.1 %branch_0_fun.1 = bf16[256,1024]{1,0:T(8,128)(2,1)} custom-call(s32[32]{0:T(128)S(1)} %get-tuple-element.73.sel_ref, bf16[256,1024]{1,0:T(8,128)(2,1)} %bitcast.4.x_ref, f32[1,256]{1,0:T(1,128)} %reshape.162.klive_ref, f32[256,1]{1,0:T(8,128)} %reshape.174.rlive_ref, f32[31,1024]{1,0:T(8,128)S(1)} %get-tuple-element.76.cw_ref, bf16[1024,3072]{1,0:T(8,128)(2,1)} %bitcast.19, ...), custom_call_target="tpu_custom_call" | custom-call | tf_op jit(solution)/shard_map/cond/branch_0_fun/pallas_call | solution.py:296
  (8 shorter events, 0.1 us)
Async XLA Ops:
  0.0 5.2 %copy-start = (bf16[1,16,30,1024]{3,1,2,0:T(8,128)(2,1)S(1)}, bf16[1,16,30,1024]{3,1,2,0:T(8,128)(2,1)}, u32[]{:S(2)}) copy-start(bf16[1,16,30,1024]{3,1,2,0:T(8,128)(2,1)} %param.20) | copy-start | bytes 2949124
  7.9 4.6 %copy-start.2 = (s32[128]{0:T(128)S(1)}, s32[128]{0:T(128)}, u32[]{:S(2)}) copy-start(s32[128]{0:T(128)} %param.17) | copy-start | bytes 1540
  7.9 4.6 %copy-start.1 = (f32[1,31,1024]{2,0,1:T(1,128)S(1)}, f32[1,31,1024]{2,0,1:T(1,128)}, u32[]{:S(2)}) copy-start(f32[1,31,1024]{2,0,1:T(1,128)} %param.23) | copy-start | bytes 380932
  11.1 23.3 %collective-permute-start = (bf16[1,8,1024]{2,1,0:T(8,128)(2,1)S(1)}, bf16[1,8,1024]{2,1,0:T(8,128)(2,1)S(1)}, u32[]{:S(2)}, u32[]{:S(2)}) collective-permute-start(bf16[1,8,1024]{2,1,0:T(8,128)(2,1)S(1)} %slice.11), channel_id=1, source_target_pairs={{0,1},{2,3},{4,5},{6,7},{8,9},{10,11},{12,13},{14,15},{16,17},{18,... | collective-permute-start | bytes 49160 | tf_op jit(solution)/shard_map/ppermute | solution.py:18
  36.5 22.8 %collective-permute-start.1 = (bf16[16,16,1024]{2,1,0:T(8,128)(2,1)}, bf16[16,16,1024]{2,1,0:T(8,128)(2,1)}, u32[]{:S(2)}, u32[]{:S(2)}) collective-permute-start(bf16[16,16,1024]{2,1,0:T(8,128)(2,1)} %get-tuple-element.101), channel_id=1, source_target_pairs={{0,1},{2,3},{4,5},{6,7},{8,9},{10,11},{12,13},{14,15},{16,17},{18,... | collective-permute-start | bytes 1572872 | tf_op jit(solution)/shard_map/ppermute | solution.py:18

commit v21 on v16

--- a/solution.py
+++ b/solution.py
@@ -9,7 +9,7 @@
 
 HEADS = 16
 GROUP = 16
-CHUNK_ROWS = 128
+CHUNK_ROWS = 512
 
 
 def shifted(value, axis, steps):

time: 83.3 us -> 82.8 us (level)
  no operation moved by 1% of the time
where the time goes in v21:
time: 82.8 us; the launch traced here: 82.3 us
  waiting for transfers between devices  25.7 us (31%)
  Pallas kernels  21.5 us (26%)
  blocking collectives  17.5 us (21%)
  local copies, waits for them, and re-layouts  9.33 us (11%)
  other arithmetic  4.85 us (6%)
  starting transfers between devices  2.56 us (3%)
    ppermute x2, waiting for transfers between devices, shifted(): lax.ppermute(value, axis, [(source, source + steps) for source in range(l...  25.7 us
    pallas_call x1, Pallas kernels, encoder_layer(): pl.pallas_call(kernel, out_shape=jax.ShapeDtypeStruct((tokens, width), jn...  21.5 us
    all_to_all x1, blocking collectives, exchange(): return lax.all_to_all(send, 'stream', 0, 0, tiled=True)  17.5 us
    another operation x3, local copies, waits for them, and re-layouts  3.3 us
    ppermute x2, starting transfers between devices, shifted(): lax.ppermute(value, axis, [(source, source + steps) for source in range(l...  2.56 us
    unnamed x9, local copies, waits for them, and re-layouts  2.17 us
  transfers between devices with their start and end apart: 2, of which 2 were waited for; matrix products, arithmetic and copies ran while one was open for 0% of the time, Pallas kernels for 0%

profile of v21, /device:TPU:1, one launch (start us, length us, event | category | flops | bytes accessed | tf_op | source)
XLA Modules:
  0.0 82.3 jit_solution(17138020446459441508)
XLA Ops:
  0.0 0.8 compare_select_fusion.7
  0.8 0.7 compare_select_fusion.6
  1.6 0.8 %select_reduce_fusion = s32[16]{0:T(128)S(1)} fusion(s32[128]{0:T(128)} %param.18, s32[16]{0:T(128)S(1)} %get-tuple-element.94), kind=kLoop, calls=%fused_computation.21 | loop fusion | flops 6128 | bytes 640 | tf_op jit(solution)/shard_map/reduce_sum | solution.py:322
  2.4 0.1 select_reduce_fusion.1
  2.5 1.6 %copy.26 = bf16[1,16,12,2048]{3,2,1,0:T(8,128)(2,1)S(1)} copy(bf16[1,16,12,2048]{3,1,2,0:T(8,128)(2,1)} %param.19) | data formatting | bytes 1572864 | tf_op args[3]
  4.1 1.1 %fusion.8 = (bf16[16,12,1024]{2,1,0:T(8,128)(2,1)}, bf16[16,12,1024]{2,1,0:T(8,128)(2,1)}) fusion(bf16[16,12,2048]{2,1,0:T(8,128)(2,1)S(1)} %bitcast.22), kind=kLoop, calls=%fused_computation.38 | loop fusion | bytes 1572864 | tf_op jit(solution)/shard_map/slice | solution.py:355
  5.2 0.5 copy.25
  5.8 1.5 %fusion.7 = bf16[16,64,1024]{2,1,0:T(8,128)(2,1)S(1)} fusion(bf16[16,30,1024]{2,1,0:T(8,128)(2,1)S(1)} %bitcast.23, bf16[16,12,1024]{2,1,0:T(8,128)(2,1)} %get-tuple-element.92, bf16[16,12,1024]{2,1,0:T(8,128)(2,1)} %get-tuple-element.91), kind=kLoop, calls=%fused_computation.16 | loop fusion | flops 14680064 | bytes 3866624 | tf_op jit(solution)/shard_map/concatenate | solution.py:354
  7.3 0.6 gather_fusion
  7.9 0.0 copy-start.2
  7.9 0.0 copy-start.1
  7.9 2.5 %conditional.4 = (bf16[8,64,1024]{2,1,0:T(8,128)(2,1)}, bf16[3,256,1024]{2,1,0:T(8,128)(2,1)}) conditional(s32[]{:T(128)} %convert_element_type.70, () %tuple.34, (bf16[8,64,1024]{2,1,0:T(8,128)(2,1)S(1)}, bf16[16,16,1024]{2,1,0:T(8,128)(2,1)}, bf16[1,1024,3072]{2,1,0:T(8,128)(2,1)}) %tuple.35), branch_computations={%region_2.3_spmd, %region_3.4_spmd} | conditional | bytes 3145776 | solution.py:372
  7.9 1.3 %broadcast.93 = bf16[3,256,1024]{2,1,0:T(8,128)(2,1)} broadcast(bf16[]{:T(256)} %constant.35.clone), dimensions={} | broadcast | bytes 1572866 | tf_op jit(solution)/shard_map/broadcast.6
  9.3 1.1 %broadcast.92 = bf16[8,64,1024]{2,1,0:T(8,128)(2,1)} broadcast(bf16[]{:T(256)} %constant.35.clone), dimensions={} | broadcast | bytes 1048578 | tf_op jit(solution)/shard_map/broadcast.7
  10.4 0.7 slice.11
  11.1 1.3 %collective-permute-start = (bf16[1,8,1024]{2,1,0:T(8,128)(2,1)S(1)}, bf16[1,8,1024]{2,1,0:T(8,128)(2,1)S(1)}, u32[]{:S(2)}, u32[]{:S(2)}) collective-permute-start(bf16[1,8,1024]{2,1,0:T(8,128)(2,1)S(1)} %slice.11), channel_id=1, source_target_pairs={{0,1},{2,3},{4,5},{6,7},{8,9},{10,11},{12,13},{14,15},{16,17},{18,... | collective-permute-start | bytes 49160 | tf_op jit(solution)/shard_map/ppermute | solution.py:18
  12.4 0.1 pad_add_fusion
  12.4 0.1 dynamic_slice.6
  12.6 21.8 %collective-permute-done = bf16[1,8,1024]{2,1,0:T(8,128)(2,1)S(1)} collective-permute-done((bf16[1,8,1024]{2,1,0:T(8,128)(2,1)S(1)}, bf16[1,8,1024]{2,1,0:T(8,128)(2,1)S(1)}, u32[]{:S(2)}, u32[]{:S(2)}) %collective-permute-start) | collective-permute-done | bytes 16416 | tf_op jit(solution)/shard_map/ppermute | solution.py:18
  34.4 0.6 convert_reduce_fusion
  35.6 0.9 %conditional.5 = (bf16[16,16,1024]{2,1,0:T(8,128)(2,1)}) conditional(s32[]{:T(128)} %convert_element_type.70, () %tuple.33, (bf16[16,16,1024]{2,1,0:T(8,128)(2,1)}, s32[16]{0:T(128)S(1)}, s32[32]{0:T(128)S(1)}, f32[31,1024]{1,0:T(8,128)S(1)}, bf16[3,256,1024]{2,1,0:T(8,128)(2,1)}, /*index=5*/bf16[1024,1024]{1,0:T(8,128)(2,1)}, ...), branch_computations={%region_5.6_spmd, %region_6.7_spmd} | conditional | flops 544 | bytes 524298 | solution.py:378
  35.6 0.9 %broadcast.94 = bf16[16,16,1024]{2,1,0:T(8,128)(2,1)} broadcast(bf16[]{:T(256)} %constant.36.clone), dimensions={} | broadcast | bytes 524290 | tf_op jit(solution)/shard_map/broadcast.9
  36.5 1.3 %collective-permute-start.1 = (bf16[16,16,1024]{2,1,0:T(8,128)(2,1)}, bf16[16,16,1024]{2,1,0:T(8,128)(2,1)}, u32[]{:S(2)}, u32[]{:S(2)}) collective-permute-start(bf16[16,16,1024]{2,1,0:T(8,128)(2,1)} %get-tuple-element.101), channel_id=1, source_target_pairs={{0,1},{2,3},{4,5},{6,7},{8,9},{10,11},{12,13},{14,15},{16,17},{18,... | collective-permute-start | bytes 1572872 | tf_op jit(solution)/shard_map/ppermute | solution.py:18
  37.8 17.6 %conditional.6 = (bf16[8,64,1024]{2,1,0:T(8,128)(2,1)S(1)}) conditional(s32[]{:T(128)} %convert_element_type.70, (f32[]{:T(128)}, bf16[8,64,1024]{2,1,0:T(8,128)(2,1)S(1)}) %tuple.37, () %tuple.38), branch_computations={%region_7.8_spmd, %region_8.9_spmd} | conditional | flops 524289 | bytes 4194320 | solution.py:382
  37.8 0.1 broadcast_add_fusion.1
  37.9 17.5 %all_to_all.8 = bf16[8,64,1024]{2,1,0:T(8,128)(2,1)S(1)} all-to-all(bf16[8,64,1024]{2,1,0:T(8,128)(2,1)S(1)} %broadcast_add_fusion.1), channel_id=1, replica_groups=mesh['groups'=2,'stream'=8,'section'=2] {'stream'}, dimensions={0} | all-to-all | bytes 2097152 | tf_op jit(solution)/shard_map/cond/branch_0_fun/all_to_all | solution.py:339
  55.4 3.9 %collective-permute-done.1 = bf16[16,16,1024]{2,1,0:T(8,128)(2,1)} collective-permute-done((bf16[16,16,1024]{2,1,0:T(8,128)(2,1)}, bf16[16,16,1024]{2,1,0:T(8,128)(2,1)}, u32[]{:S(2)}, u32[]{:S(2)}) %collective-permute-start.1) | collective-permute-done | bytes 524320 | tf_op jit(solution)/shard_map/ppermute | solution.py:18
  59.3 23.0 %conditional.7 = (bf16[1,16,16,1024]{3,2,1,0:T(8,128)(2,1)}) conditional(s32[]{:T(128)} %convert_element_type.70, (bf16[16,16,1024]{2,1,0:T(8,128)(2,1)}, s32[16]{0:T(128)S(1)}, bf16[1,1024,3072]{2,1,0:T(8,128)(2,1)}, s32[32]{0:T(128)S(1)}, f32[31,1024]{1,0:T(8,128)S(1)}, /*index=5*/bf16[1024,1024]{1,0:T(8,128)(2,1)}, ...), branch_computations={%region_9.10_spmd, %region_10.11_spmd} | conditional | flops 512 | bytes 1048584 | solution.py:385
  59.3 0.1 fusion.1
  59.4 0.7 reshape.174.rlive_ref
  60.1 0.6 reshape.162.klive_ref
  60.8 21.5 %branch_0_fun.1 = bf16[256,1024]{1,0:T(8,128)(2,1)} custom-call(s32[32]{0:T(128)S(1)} %get-tuple-element.73.sel_ref, bf16[256,1024]{1,0:T(8,128)(2,1)} %bitcast.4.x_ref, f32[1,256]{1,0:T(1,128)} %reshape.162.klive_ref, f32[256,1]{1,0:T(8,128)} %reshape.174.rlive_ref, f32[31,1024]{1,0:T(8,128)S(1)} %get-tuple-element.76.cw_ref, bf16[1024,3072]{1,0:T(8,128)(2,1)} %bitcast.19, ...), custom_call_target="tpu_custom_call" | custom-call | tf_op jit(solution)/shard_map/cond/branch_0_fun/pallas_call | solution.py:296
  (8 shorter events, 0.1 us)
Async XLA Ops:
  0.0 5.2 %copy-start = (bf16[1,16,30,1024]{3,1,2,0:T(8,128)(2,1)S(1)}, bf16[1,16,30,1024]{3,1,2,0:T(8,128)(2,1)}, u32[]{:S(2)}) copy-start(bf16[1,16,30,1024]{3,1,2,0:T(8,128)(2,1)} %param.20) | copy-start | bytes 2949124
  7.9 4.6 %copy-start.2 = (s32[128]{0:T(128)S(1)}, s32[128]{0:T(128)}, u32[]{:S(2)}) copy-start(s32[128]{0:T(128)} %param.17) | copy-start | bytes 1540
  7.9 4.6 %copy-start.1 = (f32[1,31,1024]{2,0,1:T(1,128)S(1)}, f32[1,31,1024]{2,0,1:T(1,128)}, u32[]{:S(2)}) copy-start(f32[1,31,1024]{2,0,1:T(1,128)} %param.23) | copy-start | bytes 380932
  11.1 23.3 %collective-permute-start = (bf16[1,8,1024]{2,1,0:T(8,128)(2,1)S(1)}, bf16[1,8,1024]{2,1,0:T(8,128)(2,1)S(1)}, u32[]{:S(2)}, u32[]{:S(2)}) collective-permute-start(bf16[1,8,1024]{2,1,0:T(8,128)(2,1)S(1)} %slice.11), channel_id=1, source_target_pairs={{0,1},{2,3},{4,5},{6,7},{8,9},{10,11},{12,13},{14,15},{16,17},{18,... | collective-permute-start | bytes 49160 | tf_op jit(solution)/shard_map/ppermute | solution.py:18
  36.5 22.8 %collective-permute-start.1 = (bf16[16,16,1024]{2,1,0:T(8,128)(2,1)}, bf16[16,16,1024]{2,1,0:T(8,128)(2,1)}, u32[]{:S(2)}, u32[]{:S(2)}) collective-permute-start(bf16[16,16,1024]{2,1,0:T(8,128)(2,1)} %get-tuple-element.101), channel_id=1, source_target_pairs={{0,1},{2,3},{4,5},{6,7},{8,9},{10,11},{12,13},{14,15},{16,17},{18,... | collective-permute-start | bytes 1572872 | tf_op jit(solution)/shard_map/ppermute | solution.py:18
